TPU v7x, 128 devices: a whole 4x4x4 slice. The times are simulated.
128 devices in a mesh: dp: 4 (over z), outer: 16 (over x, y), inner: 2 (over core).
Axes of the slice: x: 4, y: 4, z: 4, core: 2. Of those that a mesh axis runs over, the one named last changes fastest.
Arguments:
- tokens: bfloat16 [4096, 4096], P(('dp', 'outer', 'inner')), may hold values from -6 to 6
- expert_ids: int32 [4096, 8], P(('dp', 'outer', 'inner')), may hold values from 0 to 31, all different within a row; in each aligned block of 32 rows (0 to 31, 32 to 63, ...) at most 12 rows name the same one
- gate_values: float32 [4096, 8], P(('dp', 'outer', 'inner')), may hold values from 0.02 to 0.5
- upstream: bfloat16 [4096, 4096], P(('dp', 'outer', 'inner')), may hold values from -1.5 to 1.5
- w_gate: bfloat16 [32, 4096, 768], P(('outer', 'inner')), may hold values from -0.09375 to 0.09375
- w_up: bfloat16 [32, 4096, 768], P(('outer', 'inner')), may hold values from -0.09375 to 0.09375
- w_down: bfloat16 [32, 768, 4096], P(('outer', 'inner')), may hold values from -0.21875 to 0.21875
Outputs:
- output: bfloat16 [4096, 4096], P(('dp', 'outer', 'inner'))
- grad_tokens: bfloat16 [4096, 4096], P(('dp', 'outer', 'inner'))
- grad_gates: float32 [4096, 8], P(('dp', 'outer', 'inner'))
- grad_w_gate: bfloat16 [32, 4096, 768], P(('outer', 'inner'), 'dp')
- grad_w_up: bfloat16 [32, 4096, 768], P(('outer', 'inner'), 'dp')
- grad_w_down: bfloat16 [32, 768, 4096], P(('outer', 'inner'), None, 'dp')
Inputs may be any that keep to these rules, and one draw needn't show every extreme that they name: `expert_ids`: each token names 8 different experts. Among the 32 tokens of one device (aligned blocks of rows), no expert is named more than 12 times, a bound that some block reaches.
All inputs are finite; a program needn't handle non-finite values.
Results may differ from a plain program's by a relative error of at most 0.013.
Values may be sent and summed in bfloat16 or wider, within the bound.
No kernel may reach another device: no remote copies, remote signals or barrier semaphores. Data moves between devices by JAX's collectives and lax.ppermute only.
A program may use at most 192 MiB of HBM per device.

v0:
```python
import jax
import jax.numpy as jnp
from jax import lax
from jax.sharding import PartitionSpec as P


def contract_last(left, right):
    return lax.dot_general(
        left, right, (((1,), (1,)), ((), ())), preferred_element_type=jnp.float32
    )


def contract_first(left, right):
    return lax.dot_general(
        left, right, (((0,), (0,)), ((), ())), preferred_element_type=jnp.float32
    )


def expert_rows(rows_in, grads_in, gate_mat, up_mat, down_mat):
    gate_pre = jnp.dot(rows_in, gate_mat, preferred_element_type=jnp.float32)
    up_pre = jnp.dot(rows_in, up_mat, preferred_element_type=jnp.float32)
    sigma = jax.nn.sigmoid(gate_pre)
    silu_value = gate_pre * sigma
    hidden = (silu_value * up_pre).astype(jnp.bfloat16)
    expert_out = jnp.dot(hidden, down_mat, preferred_element_type=jnp.float32).astype(jnp.bfloat16)
    grad_hidden = contract_last(grads_in, down_mat)
    slope = sigma * (1.0 + gate_pre * (1.0 - sigma))
    grad_gate_pre = (grad_hidden * up_pre * slope).astype(jnp.bfloat16)
    grad_up_pre = (grad_hidden * silu_value).astype(jnp.bfloat16)
    pair_grad = (
        contract_last(grad_gate_pre, gate_mat) + contract_last(grad_up_pre, up_mat)
    ).astype(jnp.bfloat16)
    return (hidden, expert_out, grad_gate_pre, grad_up_pre, pair_grad)


def local(tokens, expert_ids, gate_values, upstream, w_gate, w_up, w_down):
    local_tokens = tokens.shape[0]
    width = tokens.shape[1]
    top_count = expert_ids.shape[1]
    ff_width = w_gate.shape[2]
    outer_count = lax.axis_size("outer")
    inner_count = lax.axis_size("inner")
    expert_count = outer_count * inner_count
    capacity = min(local_tokens, 3 * local_tokens * top_count // (2 * expert_count))
    pair_count = local_tokens * top_count
    flat_ids = expert_ids.reshape(-1)
    flat_gates = gate_values.reshape(-1)
    onehot = (flat_ids[:, None] == jnp.arange(expert_count, dtype=jnp.int32)[None, :]).astype(
        jnp.int32
    )
    slot_rank = jnp.sum((jnp.cumsum(onehot, axis=0) - onehot) * onehot, axis=1)
    pair_slot = flat_ids * capacity + slot_rank
    slot_pair = (
        jnp.full((expert_count * capacity,), pair_count, jnp.int32)
        .at[pair_slot]
        .set(jnp.arange(pair_count, dtype=jnp.int32))
    )
    slot_token = jnp.where(slot_pair < pair_count, slot_pair // top_count, local_tokens)
    token_pad = jnp.concatenate([tokens, jnp.zeros((1, width), jnp.bfloat16)], axis=0)
    upstream_pad = jnp.concatenate([upstream, jnp.zeros((1, width), jnp.bfloat16)], axis=0)
    gate_pad = jnp.concatenate([flat_gates, jnp.zeros((1,), jnp.float32)], axis=0)
    send_rows = token_pad[slot_token]
    send_grads = (
        gate_pad[slot_pair][:, None] * upstream_pad[slot_token].astype(jnp.float32)
    ).astype(jnp.bfloat16)
    flat_shape = (expert_count, capacity, width)
    got_rows, got_grads = (
        lax.all_to_all(
            send_rows.reshape(flat_shape),
            ("outer", "inner"),
            split_axis=0,
            concat_axis=0,
            tiled=True,
        ),
        lax.all_to_all(
            send_grads.reshape(flat_shape),
            ("outer", "inner"),
            split_axis=0,
            concat_axis=0,
            tiled=True,
        ),
    )
    rows_in = got_rows.reshape(-1, width)
    grads_in = got_grads.reshape(-1, width)
    hidden, expert_out, grad_gate_pre, grad_up_pre, pair_grad = expert_rows(
        rows_in, grads_in, w_gate[0], w_up[0], w_down[0]
    )
    back_out, back_grad = (
        lax.all_to_all(
            expert_out.reshape(flat_shape),
            ("outer", "inner"),
            split_axis=0,
            concat_axis=0,
            tiled=True,
        ),
        lax.all_to_all(
            pair_grad.reshape(flat_shape),
            ("outer", "inner"),
            split_axis=0,
            concat_axis=0,
            tiled=True,
        ),
    )
    joined_grads = jnp.concatenate([grad_gate_pre, grad_up_pre], axis=1)
    columns = rows_in
    grad_joined = lax.psum_scatter(
        contract_first(columns, joined_grads).astype(jnp.bfloat16),
        "dp",
        scatter_dimension=0,
        tiled=True,
    ).astype(jnp.float32)
    columns = grads_in
    grad_down = (
        lax.psum_scatter(
            contract_first(columns, hidden).astype(jnp.bfloat16),
            "dp",
            scatter_dimension=0,
            tiled=True,
        )
        .astype(jnp.float32)
        .T
    )
    pair_out = back_out.reshape(-1, width)[pair_slot].reshape(local_tokens, top_count, width)
    pair_back = back_grad.reshape(-1, width)[pair_slot].reshape(local_tokens, top_count, width)
    output = jnp.sum(gate_values[:, :, None] * pair_out.astype(jnp.float32), axis=1).astype(
        jnp.bfloat16
    )
    grad_tokens = jnp.sum(pair_back.astype(jnp.float32), axis=1).astype(jnp.bfloat16)
    grad_gates = jnp.einsum("tkd,td->tk", pair_out, upstream, preferred_element_type=jnp.float32)
    grad_w_gate = grad_joined[:, :ff_width].astype(jnp.bfloat16)[None]
    grad_w_up = grad_joined[:, ff_width:].astype(jnp.bfloat16)[None]
    grad_w_down = grad_down.astype(jnp.bfloat16)[None]
    return (output, grad_tokens, grad_gates, grad_w_gate, grad_w_up, grad_w_down)


def solution(mesh):
    placed = (
        P(("dp", "outer", "inner"), None),
        P(("dp", "outer", "inner"), None),
        P(("dp", "outer", "inner"), None),
        P(("dp", "outer", "inner"), None),
        P(("outer", "inner"), None, None),
        P(("outer", "inner"), None, None),
        P(("outer", "inner"), None, None),
    )
    return jax.shard_map(
        local,
        mesh=mesh,
        in_specs=placed,
        out_specs=(
            P(("dp", "outer", "inner"), None),
            P(("dp", "outer", "inner"), None),
            P(("dp", "outer", "inner"), None),
            P(("outer", "inner"), "dp", None),
            P(("outer", "inner"), "dp", None),
            P(("outer", "inner"), None, "dp"),
        ),
        check_vma=False,
    )
```

profile of v0, /device:TPU:8, one launch (start us, length us, event | category | flops | bytes accessed | tf_op | source)
XLA Modules:
  0.0 356.5 jit_solution(8191160591773802458)
XLA Ops:
  18.4 7.7 %all-to-all-start = ((bf16[32,12,4096]{2,1,0:T(8,128)(2,1)}), bf16[32,12,4096]{2,1,0:T(8,128)(2,1)}, u32[]{:S(2)}, u32[]{:S(2)}) async-start(bf16[32,12,4096]{2,1,0:T(8,128)(2,1)} %reshape.100), calls=%async_computation | async-start | bytes 8388608 | tf_op jit(solution)/shard_map/all_to_all | solution.py:68
  36.1 6.5 %multiply_convert_fusion = bf16[32,12,4096]{2,1,0:T(8,128)(2,1)} fusion(f32[32,12,4096]{2,1,0:T(8,128)} %reshape.110, f32[32,12]{1,0:T(8,128)S(1)} %mul.67), kind=kLoop, calls=%fused_computation.7 | loop fusion | flops 3145728 | bytes 9438720 | tf_op jit(solution)/shard_map/convert_element_type | solution.py:65
  42.7 37.9 %all-to-all-done = bf16[32,12,4096]{2,1,0:T(8,128)(2,1)} async-done(((bf16[32,12,4096]{2,1,0:T(8,128)(2,1)}), bf16[32,12,4096]{2,1,0:T(8,128)(2,1)}, u32[]{:S(2)}, u32[]{:S(2)}) %all-to-all-start) | async-done | bytes 3145760 | tf_op jit(solution)/shard_map/all_to_all | solution.py:68
  80.6 4.8 %all-to-all-start.2 = ((bf16[32,12,4096]{2,1,0:T(8,128)(2,1)}), bf16[32,12,4096]{2,1,0:T(8,128)(2,1)}, u32[]{:S(2)}, u32[]{:S(2)}) async-start(bf16[32,12,4096]{2,1,0:T(8,128)(2,1)} %multiply_convert_fusion), calls=%async_computation.2 | async-start | bytes 8388608 | tf_op jit(solution)/shard_map/all_to_all | solution.py:75
  85.7 4.0 %reshape.101 = bf16[384,4096]{1,0:T(8,128)(2,1)S(1)} reshape(bf16[32,12,4096]{2,1,0:T(8,128)(2,1)} %all-to-all-done) | data formatting | bytes 6291456 | tf_op jit(solution)/shard_map/reshape | solution.py:83
  89.7 6.4 %fusion.6 = f32[384,768]{1,0:T(8,128)} fusion(bf16[384,4096]{1,0:T(8,128)(2,1)S(1)} %reshape.101, bf16[1,4096,768]{2,1,0:T(8,128)(2,1)} %param.12), kind=kOutput, calls=%fused_computation.15 | convolution fusion | flops 2415919104 | bytes 10616832 | tf_op jit(solution)/shard_map/dot_general | solution.py:21
  96.1 43.9 %all-to-all-done.2 = bf16[32,12,4096]{2,1,0:T(8,128)(2,1)} async-done(((bf16[32,12,4096]{2,1,0:T(8,128)(2,1)}), bf16[32,12,4096]{2,1,0:T(8,128)(2,1)}, u32[]{:S(2)}, u32[]{:S(2)}) %all-to-all-start.2) | async-done | bytes 3145760 | tf_op jit(solution)/shard_map/all_to_all | solution.py:75
  140.0 5.6 %reshape.106 = bf16[384,4096]{1,0:T(8,128)(2,1)} reshape(bf16[32,12,4096]{2,1,0:T(8,128)(2,1)} %all-to-all-done.2) | data formatting | bytes 6291456 | tf_op jit(solution)/shard_map/reshape | solution.py:84
  145.6 6.5 %fusion = f32[384,768]{1,0:T(8,128)S(1)} fusion(bf16[384,4096]{1,0:T(8,128)(2,1)} %reshape.106, bf16[1,768,4096]{2,1,0:T(8,128)(2,1)} %param.13), kind=kOutput, calls=%fused_computation.9 | convolution fusion | flops 2415919104 | bytes 10616832 | tf_op jit(solution)/shard_map/dot_general | solution.py:8
  152.1 7.0 %multiply_convert_fusion.2 = (bf16[384,768]{1,0:T(8,128)(2,1)}, bf16[384,768]{1,0:T(8,128)(2,1)}, bf16[384,768]{1,0:T(8,128)(2,1)S(1)}) fusion(f32[384,768]{1,0:T(8,128)S(1)} %fusion, f32[384,768]{1,0:T(8,128)S(1)} %copy-done.8, bf16[384,4096]{1,0:T(8,128)(2,1)S(1)} %reshape.101, bf16[1,4096,768]{2,1,0:T(8,128)(2,1)} %param.11), kind=kOutput, calls=%fused_computation.33 | convolution fusion | flops 2420342784 | bytes 13565952 | tf_op jit(solution)/shard_map/dot_general | solution.py:20
  159.9 5.4 %convolution_convert_fusion.1 = bf16[4096,768]{1,0:T(8,128)(2,1)} fusion(bf16[384,4096]{1,0:T(8,128)(2,1)S(1)} %copy-done.1, bf16[384,768]{1,0:T(8,128)(2,1)S(1)} %get-tuple-element.22), kind=kOutput, calls=%fused_computation.8 | convolution fusion | flops 2419064832 | bytes 10027008 | tf_op jit(solution)/shard_map/dot_general | solution.py:14
  165.5 10.9 %convolution_convert_fusion = bf16[4096,1536]{1,0:T(8,128)(2,1)} fusion(bf16[384,4096]{1,0:T(8,128)(2,1)S(1)} %reshape.101, bf16[384,768]{1,0:T(8,128)(2,1)} %get-tuple-element.21, bf16[384,768]{1,0:T(8,128)(2,1)} %get-tuple-element.20), kind=kOutput, calls=%fused_computation.6 | convolution fusion | flops 4840488960 | bytes 16908288 | tf_op jit(solution)/shard_map/dot_general | solution.py:14
  176.5 5.6 %fusion.14 = bf16[384,4096]{1,0:T(8,128)(2,1)S(1)} fusion(bf16[384,768]{1,0:T(8,128)(2,1)} %copy-done.6, bf16[1,768,4096]{2,1,0:T(8,128)(2,1)} %param.13), kind=kOutput, calls=%fused_computation.22 | convolution fusion | flops 2417491968 | bytes 10027008 | tf_op jit(solution)/shard_map/dot_general | solution.py:25
  184.8 5.5 %all-to-all-start.1 = ((bf16[32,12,4096]{2,1,0:T(8,128)(2,1)}), bf16[32,12,4096]{2,1,0:T(8,128)(2,1)}, u32[]{:S(2)}, u32[]{:S(2)}) async-start(bf16[32,12,4096]{2,1,0:T(8,128)(2,1)} %reshape.102), calls=%async_computation.1 | async-start | bytes 8388608 | tf_op jit(solution)/shard_map/all_to_all | solution.py:89
  190.3 4.9 %fusion.4 = f32[384,4096]{1,0:T(8,128)S(1)} fusion(bf16[384,768]{1,0:T(8,128)(2,1)S(1)} %copy-done.5, bf16[1,4096,768]{2,1,0:T(8,128)(2,1)} %param.12), kind=kOutput, calls=%fused_computation.13 | convolution fusion | flops 2415919104 | bytes 13172736 | tf_op jit(solution)/shard_map/dot_general | solution.py:8
  195.3 7.3 %add_convert_fusion = bf16[384,4096]{1,0:T(8,128)(2,1)S(1)} fusion(f32[384,4096]{1,0:T(8,128)S(1)} %fusion.4, bf16[384,768]{1,0:T(8,128)(2,1)S(1)} %copy-done.7, bf16[1,4096,768]{2,1,0:T(8,128)(2,1)} %param.11), kind=kOutput, calls=%fused_computation.21 | convolution fusion | flops 2419064832 | bytes 16318464 | tf_op jit(solution)/shard_map/dot_general | solution.py:8
  205.3 39.5 %all-to-all-done.1 = bf16[32,12,4096]{2,1,0:T(8,128)(2,1)} async-done(((bf16[32,12,4096]{2,1,0:T(8,128)(2,1)}), bf16[32,12,4096]{2,1,0:T(8,128)(2,1)}, u32[]{:S(2)}, u32[]{:S(2)}) %all-to-all-start.1) | async-done | bytes 3145760 | tf_op jit(solution)/shard_map/all_to_all | solution.py:89
  244.8 4.9 %all-to-all-start.3 = ((bf16[32,12,4096]{2,1,0:T(8,128)(2,1)}), bf16[32,12,4096]{2,1,0:T(8,128)(2,1)}, u32[]{:S(2)}, u32[]{:S(2)}) async-start(bf16[32,12,4096]{2,1,0:T(8,128)(2,1)} %reshape.107), calls=%async_computation.3 | async-start | bytes 8388608 | tf_op jit(solution)/shard_map/all_to_all | solution.py:96
  249.7 4.0 %reshape.103 = bf16[384,4096]{1,0:T(8,128)(2,1)S(1)} reshape(bf16[32,12,4096]{2,1,0:T(8,128)(2,1)} %all-to-all-done.1) | data formatting | bytes 6291456 | tf_op jit(solution)/shard_map/reshape | solution.py:123
  260.7 43.1 %all-to-all-done.3 = bf16[32,12,4096]{2,1,0:T(8,128)(2,1)} async-done(((bf16[32,12,4096]{2,1,0:T(8,128)(2,1)}), bf16[32,12,4096]{2,1,0:T(8,128)(2,1)}, u32[]{:S(2)}, u32[]{:S(2)}) %all-to-all-start.3) | async-done | bytes 3145760 | tf_op jit(solution)/shard_map/all_to_all | solution.py:96
  303.8 4.0 %reshape.108 = bf16[384,4096]{1,0:T(8,128)(2,1)S(1)} reshape(bf16[32,12,4096]{2,1,0:T(8,128)(2,1)} %all-to-all-done.3) | data formatting | bytes 6291456 | tf_op jit(solution)/shard_map/reshape | solution.py:124
  311.0 3.9 %bitcast_reduce_fusion = bf16[32,4096]{1,0:T(8,128)(2,1)} fusion(bf16[256,4096]{1,0:T(8,128)(2,1)} %gather_fusion.4), kind=kLoop, calls=%fused_computation.24 | loop fusion | flops 917504 | bytes 2359296 | tf_op jit(solution)/shard_map/reduce_sum | solution.py:128
  319.8 26.2 %reduce-scatter.3.cloned.1.call-done = bf16[1024,1536]{1,0:T(8,128)(2,1)} async-done(((bf16[4096,1536]{1,0:T(8,128)(2,1)}), bf16[1024,1536]{1,0:T(8,128)(2,1)}) %reduce-scatter.3.cloned.1.call-update) | async-done | bytes 3145744 | tf_op jit(solution)/shard_map/reduce_scatter | solution.py:106
  345.9 3.7 %slice_bitcast_fusion = (bf16[1,1024,768]{2,1,0:T(8,128)(2,1)}, bf16[1,1024,768]{2,1,0:T(8,128)(2,1)}) fusion(bf16[1024,1536]{1,0:T(8,128)(2,1)} %reduce-scatter.3.cloned.1.call-done), kind=kLoop, calls=%fused_computation.27 | loop fusion | bytes 6291456 | tf_op jit(solution)/shard_map/broadcast_in_dim | solution.py:131
  (60 shorter events, 42.9 us)
Async XLA Ops:
  18.3 7.7 %copy-start.4 = (f32[32,8]{0,1:T(8,128)S(1)}, f32[32,8]{0,1:T(8,128)}, u32[]{:S(2)}) copy-start(f32[32,8]{0,1:T(8,128)} %param.9) | copy-start | bytes 3076
  18.3 10.8 %copy-start.2 = (bf16[32,4096]{1,0:T(8,128)(2,1)S(1)}, bf16[32,4096]{1,0:T(8,128)(2,1)}, u32[]{:S(2)}) copy-start(bf16[32,4096]{1,0:T(8,128)(2,1)} %param.10) | copy-start | bytes 786436
  18.4 62.3 %all-to-all-start = ((bf16[32,12,4096]{2,1,0:T(8,128)(2,1)}), bf16[32,12,4096]{2,1,0:T(8,128)(2,1)}, u32[]{:S(2)}, u32[]{:S(2)}) async-start(bf16[32,12,4096]{2,1,0:T(8,128)(2,1)} %reshape.100), calls=%async_computation | async-start | bytes 8388608 | tf_op jit(solution)/shard_map/all_to_all | solution.py:68
  80.6 59.4 %all-to-all-start.2 = ((bf16[32,12,4096]{2,1,0:T(8,128)(2,1)}), bf16[32,12,4096]{2,1,0:T(8,128)(2,1)}, u32[]{:S(2)}, u32[]{:S(2)}) async-start(bf16[32,12,4096]{2,1,0:T(8,128)(2,1)} %multiply_convert_fusion), calls=%async_computation.2 | async-start | bytes 8388608 | tf_op jit(solution)/shard_map/all_to_all | solution.py:75
  85.5 231.7 %reduce-scatter.5.cloned.1.call-start = ((), (), s32[]{:S(2)}) async-start(), calls=%async_computation.7 | async-start | bytes 7864320 | tf_op jit(solution)/shard_map/reduce_scatter | solution.py:114
  145.6 6.5 %copy-start.8 = (f32[384,768]{1,0:T(8,128)S(1)}, f32[384,768]{1,0:T(8,128)}, u32[]{:S(2)}) copy-start(f32[384,768]{1,0:T(8,128)} %fusion.6) | copy-start | bytes 3538948
  152.1 7.8 %copy-start.1 = (bf16[384,4096]{1,0:T(8,128)(2,1)S(1)}, bf16[384,4096]{1,0:T(8,128)(2,1)}, u32[]{:S(2)}) copy-start(bf16[384,4096]{1,0:T(8,128)(2,1)} %reshape.106) | copy-start | bytes 9437188
  159.1 0.8 copy-start.6
  165.3 180.7 %reduce-scatter.3.cloned.1.call-start = ((), (), s32[]{:S(2)}) async-start(), calls=%async_computation.6 | async-start | bytes 15728640 | tf_op jit(solution)/shard_map/reduce_scatter | solution.py:106
  184.8 5.5 %copy-start.5 = (bf16[384,768]{1,0:T(8,128)(2,1)S(1)}, bf16[384,768]{1,0:T(8,128)(2,1)}, u32[]{:S(2)}) copy-start(bf16[384,768]{1,0:T(8,128)(2,1)} %get-tuple-element.21) | copy-start | bytes 1769476
  184.8 60.0 %all-to-all-start.1 = ((bf16[32,12,4096]{2,1,0:T(8,128)(2,1)}), bf16[32,12,4096]{2,1,0:T(8,128)(2,1)}, u32[]{:S(2)}, u32[]{:S(2)}) async-start(bf16[32,12,4096]{2,1,0:T(8,128)(2,1)} %reshape.102), calls=%async_computation.1 | async-start | bytes 8388608 | tf_op jit(solution)/shard_map/all_to_all | solution.py:89
  190.3 5.0 %copy-start.7 = (bf16[384,768]{1,0:T(8,128)(2,1)S(1)}, bf16[384,768]{1,0:T(8,128)(2,1)}, u32[]{:S(2)}) copy-start(bf16[384,768]{1,0:T(8,128)(2,1)} %get-tuple-element.20) | copy-start | bytes 1769476
  244.8 59.0 %all-to-all-start.3 = ((bf16[32,12,4096]{2,1,0:T(8,128)(2,1)}), bf16[32,12,4096]{2,1,0:T(8,128)(2,1)}, u32[]{:S(2)}, u32[]{:S(2)}) async-start(bf16[32,12,4096]{2,1,0:T(8,128)(2,1)} %reshape.107), calls=%async_computation.3 | async-start | bytes 8388608 | tf_op jit(solution)/shard_map/all_to_all | solution.py:96
  253.7 3.2 copy-start.3
  311.0 3.9 %copy-start = (bf16[256,4096]{1,0:T(8,128)(2,1)S(1)}, bf16[256,4096]{1,0:T(8,128)(2,1)}, u32[]{:S(2)}) copy-start(bf16[256,4096]{1,0:T(8,128)(2,1)} %gather_fusion.1) | copy-start | bytes 6291460
Sparse Core Ops, SparseCore 0:
  165.4 63.7 reduce-scatter.4
  231.6 114.2 reduce-scatter.2
where the time goes:
time: 358 us; the launch traced here: 357 us
  waiting for transfers between devices  191 us (53%)
  matrix products  57.1 us (16%)
  local copies, waits for them, and re-layouts  56.8 us (16%)
  starting transfers between devices  23.4 us (7%)
  between operations  14.3 us (4%)
  other arithmetic  14.2 us (4%)
    all_to_all x1, waiting for transfers between devices, local(): lax.all_to_all(send_grads.reshape(flat_shape), ('outer', 'inner'), split_...  43.9 us
    all_to_all x1, waiting for transfers between devices, local(): lax.all_to_all(pair_grad.reshape(flat_shape), ('outer', 'inner'), split_a...  43.1 us
    all_to_all x1, waiting for transfers between devices, local(): lax.all_to_all(expert_out.reshape(flat_shape), ('outer', 'inner'), split_...  39.5 us
    all_to_all x1, waiting for transfers between devices, local(): lax.all_to_all(send_rows.reshape(flat_shape), ('outer', 'inner'), split_a...  37.9 us
    reduce_scatter x1, waiting for transfers between devices, local(): lax.psum_scatter(contract_first(columns, joined_grads).astype(jnp.bfloat1...  26.2 us
    dot_general x3, matrix products, contract_last(): lax.dot_general(left, right, (((1,), (1,)), ((), ())), preferred_element_...  18.7 us
    dot_general x2, matrix products, contract_first(): lax.dot_general(left, right, (((0,), (0,)), ((), ())), preferred_element_...  16.3 us
    all_to_all x1, starting transfers between devices, local(): lax.all_to_all(send_rows.reshape(flat_shape), ('outer', 'inner'), split_a...  7.72 us
  transfers between devices with their start and end apart: 6, of which 5 were waited for; matrix products, arithmetic and copies ran while one was open for 25% of the time, Pallas kernels for 0%

commit v1 on v0

--- a/solution.py
+++ b/solution.py
@@ -101,25 +101,22 @@
             tiled=True,
         ),
     )
+    dp_count = lax.axis_size("dp")
+    slot_total = rows_in.shape[0]
+    piece = width // dp_count
+
+    def spread_columns(block):
+        return lax.all_to_all(
+            block.reshape(slot_total, dp_count, piece), "dp", split_axis=1, concat_axis=0, tiled=True
+        ).reshape(dp_count * slot_total, piece)
+
     joined_grads = jnp.concatenate([grad_gate_pre, grad_up_pre], axis=1)
-    columns = rows_in
-    grad_joined = lax.psum_scatter(
-        contract_first(columns, joined_grads).astype(jnp.bfloat16),
-        "dp",
-        scatter_dimension=0,
-        tiled=True,
-    ).astype(jnp.float32)
-    columns = grads_in
-    grad_down = (
-        lax.psum_scatter(
-            contract_first(columns, hidden).astype(jnp.bfloat16),
-            "dp",
-            scatter_dimension=0,
-            tiled=True,
-        )
-        .astype(jnp.float32)
-        .T
-    )
+    rows_all = spread_columns(rows_in)
+    grads_all = spread_columns(grads_in)
+    joined_all = lax.all_gather(joined_grads, "dp", axis=0, tiled=True)
+    hidden_all = lax.all_gather(hidden, "dp", axis=0, tiled=True)
+    grad_joined = contract_first(rows_all, joined_all)
+    grad_down = contract_first(hidden_all, grads_all)
     pair_out = back_out.reshape(-1, width)[pair_slot].reshape(local_tokens, top_count, width)
     pair_back = back_grad.reshape(-1, width)[pair_slot].reshape(local_tokens, top_count, width)
     output = jnp.sum(gate_values[:, :, None] * pair_out.astype(jnp.float32), axis=1).astype(

time: 358 us -> 394 us (1.10)
  starting transfers between devices: 23.4 us -> 41.2 us
  local copies, waits for them, and re-layouts: 56.8 us -> 69.1 us
  waiting for transfers between devices: 191 us -> 196 us
    reduce_scatter x2 -> x0, waiting for transfers between devices: 26.2 us -> none  [the longest x1 26.2 us: local(): lax.psum_scatter(contract_first(columns, joined_grads).astype(jnp.bfloat1...]
    all_to_all x0 -> x2, waiting for transfers between devices: none -> 24.3 us  [spread_columns(): lax.all_to_all(block.reshape(slot_total, dp_count, piece), 'dp', split_ax...]
    another operation x1 -> x5, local copies, waits for them, and re-layouts: 0.01 us -> 19.2 us  [the longest x4 19.2 us: spread_columns(): block.reshape(slot_total, dp_count, piece)]
    all_to_all x0 -> x2, starting transfers between devices: none -> 18.6 us  [spread_columns(): lax.all_to_all(block.reshape(slot_total, dp_count, piece), 'dp', split_ax...]
    all_to_all x1, waiting for transfers between devices: 39.5 us -> 45 us  [local(): lax.all_to_all(expert_out.reshape(flat_shape), ('outer', 'inner'), split_...]
    all_to_all x1, waiting for transfers between devices: 43.9 us -> 48.5 us  [local(): lax.all_to_all(send_grads.reshape(flat_shape), ('outer', 'inner'), split_...]
  transfers between devices with their start and end apart: 6 -> 8, of which waited for: 5 -> 6; matrix products, arithmetic and copies ran while one was open for 25% -> 27% of each run, Pallas kernels for 0% -> 0%
where the time goes in v1:
time: 394 us; the launch traced here: 389 us
  waiting for transfers between devices  196 us (50%)
  local copies, waits for them, and re-layouts  69.1 us (18%)
  matrix products  54.4 us (14%)
  starting transfers between devices  41.2 us (10%)
  between operations  14.7 us (4%)
  other arithmetic  13.6 us (3%)
    all_to_all x1, waiting for transfers between devices, local(): lax.all_to_all(send_grads.reshape(flat_shape), ('outer', 'inner'), split_...  48.5 us
    all_to_all x1, waiting for transfers between devices, local(): lax.all_to_all(expert_out.reshape(flat_shape), ('outer', 'inner'), split_...  45 us
    all_to_all x1, waiting for transfers between devices, local(): lax.all_to_all(pair_grad.reshape(flat_shape), ('outer', 'inner'), split_a...  43.4 us
    all_to_all x1, waiting for transfers between devices, local(): lax.all_to_all(send_rows.reshape(flat_shape), ('outer', 'inner'), split_a...  34.5 us
    all_to_all x2, waiting for transfers between devices, spread_columns(): lax.all_to_all(block.reshape(slot_total, dp_count, piece), 'dp', split_ax...  24.3 us
    another operation x4, local copies, waits for them, and re-layouts, spread_columns(): block.reshape(slot_total, dp_count, piece)  19.2 us
    dot_general x3, matrix products, contract_last(): lax.dot_general(left, right, (((1,), (1,)), ((), ())), preferred_element_...  18.6 us
    all_to_all x2, starting transfers between devices, spread_columns(): lax.all_to_all(block.reshape(slot_total, dp_count, piece), 'dp', split_ax...  18.6 us
  transfers between devices with their start and end apart: 8, of which 6 were waited for; matrix products, arithmetic and copies ran while one was open for 27% of the time, Pallas kernels for 0%

profile of v1, /device:TPU:8, one launch (start us, length us, event | category | flops | bytes accessed | tf_op | source)
XLA Modules:
  0.0 388.6 jit_solution(16836146155975204668)
XLA Ops:
  22.4 6.6 %multiply_convert_fusion = bf16[32,12,4096]{2,1,0:T(8,128)(2,1)} fusion(f32[32,12,4096]{2,1,0:T(8,128)} %reshape.120, f32[32,12]{1,0:T(8,128)S(1)} %mul.67), kind=kLoop, calls=%fused_computation.6 | loop fusion | flops 3145728 | bytes 9438720 | tf_op jit(solution)/shard_map/convert_element_type | solution.py:65
  28.9 7.7 %all-to-all-start.2 = ((bf16[32,12,4096]{2,1,0:T(8,128)(2,1)}), bf16[32,12,4096]{2,1,0:T(8,128)(2,1)}, u32[]{:S(2)}, u32[]{:S(2)}) async-start(bf16[32,12,4096]{2,1,0:T(8,128)(2,1)} %multiply_convert_fusion), calls=%async_computation.2 | async-start | bytes 8388608 | tf_op jit(solution)/shard_map/all_to_all | solution.py:75
  42.7 48.5 %all-to-all-done.2 = bf16[32,12,4096]{2,1,0:T(8,128)(2,1)} async-done(((bf16[32,12,4096]{2,1,0:T(8,128)(2,1)}), bf16[32,12,4096]{2,1,0:T(8,128)(2,1)}, u32[]{:S(2)}, u32[]{:S(2)}) %all-to-all-start.2) | async-done | bytes 3145760 | tf_op jit(solution)/shard_map/all_to_all | solution.py:75
  91.2 4.8 %all-to-all-start = ((bf16[32,12,4096]{2,1,0:T(8,128)(2,1)}), bf16[32,12,4096]{2,1,0:T(8,128)(2,1)}, u32[]{:S(2)}, u32[]{:S(2)}) async-start(bf16[32,12,4096]{2,1,0:T(8,128)(2,1)} %reshape.108), calls=%async_computation | async-start | bytes 8388608 | tf_op jit(solution)/shard_map/all_to_all | solution.py:68
  96.0 6.9 %reshape_reshape.7 = bf16[384,4,1024]{2,1,0:T(4,128)(2,1)S(1)} reshape(bf16[32,12,4096]{2,1,0:T(8,128)(2,1)} %all-to-all-done.2) | data formatting | bytes 6291456 | tf_op jit(solution)/shard_map/reshape;reshape | solution.py:110
  109.6 6.4 %fusion = f32[384,768]{1,0:T(8,128)} fusion(bf16[384,4096]{1,0:T(8,128)(2,1)S(1)} %reshape.114, bf16[1,768,4096]{2,1,0:T(8,128)(2,1)} %param.13), kind=kOutput, calls=%fused_computation.7 | convolution fusion | flops 2415919104 | bytes 10616832 | tf_op jit(solution)/shard_map/dot_general | solution.py:8
  116.1 34.5 %all-to-all-done = bf16[32,12,4096]{2,1,0:T(8,128)(2,1)} async-done(((bf16[32,12,4096]{2,1,0:T(8,128)(2,1)}), bf16[32,12,4096]{2,1,0:T(8,128)(2,1)}, u32[]{:S(2)}, u32[]{:S(2)}) %all-to-all-start) | async-done | bytes 3145760 | tf_op jit(solution)/shard_map/all_to_all | solution.py:68
  150.6 13.8 %all-to-all-start.5 = ((bf16[384,4,1024]{2,0,1:T(8,128)(2,1)}), bf16[384,4,1024]{2,0,1:T(8,128)(2,1)}, u32[]{:S(2)}, u32[]{:S(2)}) async-start(bf16[384,4,1024]{2,0,1:T(8,128)(2,1)} %copy.29), calls=%async_computation.5 | async-start | bytes 6291456 | tf_op jit(solution)/shard_map/all_to_all | solution.py:109
  164.4 4.0 %reshape.109 = bf16[384,4096]{1,0:T(8,128)(2,1)S(1)} reshape(bf16[32,12,4096]{2,1,0:T(8,128)(2,1)} %all-to-all-done) | data formatting | bytes 6291456 | tf_op jit(solution)/shard_map/reshape | solution.py:83
  168.4 5.5 %fusion.6 = f32[384,768]{1,0:T(8,128)S(1)} fusion(bf16[384,4096]{1,0:T(8,128)(2,1)S(1)} %reshape.109, bf16[1,4096,768]{2,1,0:T(8,128)(2,1)} %param.12), kind=kOutput, calls=%fused_computation.13 | convolution fusion | flops 2415919104 | bytes 10616832 | tf_op jit(solution)/shard_map/dot_general | solution.py:21
  173.9 7.0 %multiply_convert_fusion.2 = (bf16[384,768]{1,0:T(8,128)(2,1)}, bf16[384,768]{1,0:T(8,128)(2,1)}, bf16[384,768]{1,0:T(8,128)(2,1)}) fusion(f32[384,768]{1,0:T(8,128)S(1)} %copy-done.8, f32[384,768]{1,0:T(8,128)S(1)} %fusion.6, bf16[384,4096]{1,0:T(8,128)(2,1)S(1)} %reshape.109, bf16[1,4096,768]{2,1,0:T(8,128)(2,1)} %param.11), kind=kOutput, calls=%fused_computation.32 | convolution fusion | flops 2420342784 | bytes 13565952 | tf_op jit(solution)/shard_map/dot_general | solution.py:20
  180.9 4.9 %fusion.4 = f32[384,4096]{1,0:T(8,128)S(1)} fusion(bf16[384,768]{1,0:T(8,128)(2,1)} %get-tuple-element.9, bf16[1,4096,768]{2,1,0:T(8,128)(2,1)} %param.12), kind=kOutput, calls=%fused_computation.11 | convolution fusion | flops 2415919104 | bytes 13172736 | tf_op jit(solution)/shard_map/dot_general | solution.py:8
  185.8 7.3 %add_convert_fusion = bf16[384,4096]{1,0:T(8,128)(2,1)S(1)} fusion(f32[384,4096]{1,0:T(8,128)S(1)} %fusion.4, bf16[384,768]{1,0:T(8,128)(2,1)S(1)} %copy-done.2, bf16[1,4096,768]{2,1,0:T(8,128)(2,1)} %param.11), kind=kOutput, calls=%fused_computation.19 | convolution fusion | flops 2419064832 | bytes 16318464 | tf_op jit(solution)/shard_map/dot_general | solution.py:8
  195.8 15.8 %all-to-all-done.5 = bf16[384,4,1024]{2,0,1:T(8,128)(2,1)} async-done(((bf16[384,4,1024]{2,0,1:T(8,128)(2,1)}), bf16[384,4,1024]{2,0,1:T(8,128)(2,1)}, u32[]{:S(2)}, u32[]{:S(2)}) %all-to-all-start.5) | async-done | bytes 3145760 | tf_op jit(solution)/shard_map/all_to_all | solution.py:109
  211.6 4.6 %all-to-all-start.3 = ((bf16[32,12,4096]{2,1,0:T(8,128)(2,1)}), bf16[32,12,4096]{2,1,0:T(8,128)(2,1)}, u32[]{:S(2)}, u32[]{:S(2)}) async-start(bf16[32,12,4096]{2,1,0:T(8,128)(2,1)} %reshape.115), calls=%async_computation.3 | async-start | bytes 8388608 | tf_op jit(solution)/shard_map/all_to_all | solution.py:96
  217.4 5.6 %fusion.14 = bf16[384,4096]{1,0:T(8,128)(2,1)S(1)} fusion(bf16[384,768]{1,0:T(8,128)(2,1)} %get-tuple-element.10, bf16[1,768,4096]{2,1,0:T(8,128)(2,1)} %param.13), kind=kOutput, calls=%fused_computation.20 | convolution fusion | flops 2417491968 | bytes 10027008 | tf_op jit(solution)/shard_map/dot_general | solution.py:25
  225.8 43.4 %all-to-all-done.3 = bf16[32,12,4096]{2,1,0:T(8,128)(2,1)} async-done(((bf16[32,12,4096]{2,1,0:T(8,128)(2,1)}), bf16[32,12,4096]{2,1,0:T(8,128)(2,1)}, u32[]{:S(2)}, u32[]{:S(2)}) %all-to-all-start.3) | async-done | bytes 3145760 | tf_op jit(solution)/shard_map/all_to_all | solution.py:96
  269.2 5.3 %all-to-all-start.1 = ((bf16[32,12,4096]{2,1,0:T(8,128)(2,1)}), bf16[32,12,4096]{2,1,0:T(8,128)(2,1)}, u32[]{:S(2)}, u32[]{:S(2)}) async-start(bf16[32,12,4096]{2,1,0:T(8,128)(2,1)} %reshape.110), calls=%async_computation.1 | async-start | bytes 8388608 | tf_op jit(solution)/shard_map/all_to_all | solution.py:89
  274.5 6.9 %reshape_reshape.6 = bf16[384,4,1024]{2,1,0:T(4,128)(2,1)S(1)} reshape(bf16[32,12,4096]{2,1,0:T(8,128)(2,1)} %all-to-all-done) | data formatting | bytes 6291456 | tf_op jit(solution)/shard_map/reshape;reshape | solution.py:110
  284.1 45.0 %all-to-all-done.1 = bf16[32,12,4096]{2,1,0:T(8,128)(2,1)} async-done(((bf16[32,12,4096]{2,1,0:T(8,128)(2,1)}), bf16[32,12,4096]{2,1,0:T(8,128)(2,1)}, u32[]{:S(2)}, u32[]{:S(2)}) %all-to-all-start.1) | async-done | bytes 3145760 | tf_op jit(solution)/shard_map/all_to_all | solution.py:89
  329.1 4.8 %all-to-all-start.4 = ((bf16[384,4,1024]{2,0,1:T(8,128)(2,1)}), bf16[384,4,1024]{2,0,1:T(8,128)(2,1)}, u32[]{:S(2)}, u32[]{:S(2)}) async-start(bf16[384,4,1024]{2,0,1:T(8,128)(2,1)} %copy.28), calls=%async_computation.4 | async-start | bytes 6291456 | tf_op jit(solution)/shard_map/all_to_all | solution.py:109
  356.5 6.4 %fusion.19 = bf16[1,768,1024]{2,1,0:T(8,128)(2,1)} fusion(bf16[1536,768]{1,0:T(8,128)(2,1)} %all-gather.5.cloned.1.call-done, bf16[1536,1024]{1,0:T(8,128)(2,1)} %bitcast.17), kind=kOutput, calls=%fused_computation.29 | convolution fusion | flops 2416705536 | bytes 7077888 | tf_op jit(solution)/shard_map/dot_general | solution.py:14
  362.9 8.5 %all-to-all-done.4 = bf16[384,4,1024]{2,0,1:T(8,128)(2,1)} async-done(((bf16[384,4,1024]{2,0,1:T(8,128)(2,1)}), bf16[384,4,1024]{2,0,1:T(8,128)(2,1)}, u32[]{:S(2)}, u32[]{:S(2)}) %all-to-all-start.4) | async-done | bytes 3145760 | tf_op jit(solution)/shard_map/all_to_all | solution.py:109
  371.4 8.1 %convolution_convert_fusion = bf16[1024,1536]{1,0:T(8,128)(2,1)S(1)} fusion(bf16[1536,1024]{1,0:T(8,128)(2,1)} %bitcast.12, bf16[1536,1536]{1,0:T(8,128)(2,1)} %all-gather.3.cloned.1.call-done), kind=kOutput, calls=%fused_computation.22 | convolution fusion | flops 4833411072 | bytes 11010048 | tf_op jit(solution)/shard_map/dot_general | solution.py:14
  (68 shorter events, 61.6 us)
Async XLA Ops:
  15.6 3.6 copy-start.7
  28.9 7.7 %copy-start.5 = (bf16[32,4096]{1,0:T(8,128)(2,1)S(1)}, bf16[32,4096]{1,0:T(8,128)(2,1)}, u32[]{:S(2)}) copy-start(bf16[32,4096]{1,0:T(8,128)(2,1)} %param.7) | copy-start | bytes 786436
  28.9 62.3 %all-to-all-start.2 = ((bf16[32,12,4096]{2,1,0:T(8,128)(2,1)}), bf16[32,12,4096]{2,1,0:T(8,128)(2,1)}, u32[]{:S(2)}, u32[]{:S(2)}) async-start(bf16[32,12,4096]{2,1,0:T(8,128)(2,1)} %multiply_convert_fusion), calls=%async_computation.2 | async-start | bytes 8388608 | tf_op jit(solution)/shard_map/all_to_all | solution.py:75
  91.2 59.4 %all-to-all-start = ((bf16[32,12,4096]{2,1,0:T(8,128)(2,1)}), bf16[32,12,4096]{2,1,0:T(8,128)(2,1)}, u32[]{:S(2)}, u32[]{:S(2)}) async-start(bf16[32,12,4096]{2,1,0:T(8,128)(2,1)} %reshape.108), calls=%async_computation | async-start | bytes 8388608 | tf_op jit(solution)/shard_map/all_to_all | solution.py:68
  150.6 61.0 %all-to-all-start.5 = ((bf16[384,4,1024]{2,0,1:T(8,128)(2,1)}), bf16[384,4,1024]{2,0,1:T(8,128)(2,1)}, u32[]{:S(2)}, u32[]{:S(2)}) async-start(bf16[384,4,1024]{2,0,1:T(8,128)(2,1)} %copy.29), calls=%async_computation.5 | async-start | bytes 6291456 | tf_op jit(solution)/shard_map/all_to_all | solution.py:109
  164.4 192.2 %all-gather.5.cloned.1.call-start = ((), (), s32[]{:S(2)}) async-start(), calls=%async_computation.7 | async-start | bytes 2949120 | tf_op jit(solution)/shard_map/all_gather | solution.py:117
  168.4 5.5 %copy-start.8 = (f32[384,768]{1,0:T(8,128)S(1)}, f32[384,768]{1,0:T(8,128)}, u32[]{:S(2)}) copy-start(f32[384,768]{1,0:T(8,128)} %fusion) | copy-start | bytes 3538948
  180.9 5.0 %copy-start.2 = (bf16[384,768]{1,0:T(8,128)(2,1)S(1)}, bf16[384,768]{1,0:T(8,128)(2,1)}, u32[]{:S(2)}) copy-start(bf16[384,768]{1,0:T(8,128)(2,1)} %get-tuple-element.8) | copy-start | bytes 1769476
  195.8 20.5 %copy-start.3 = (bf16[384,768]{1,0:T(8,128)(2,1)S(1)}, bf16[384,768]{1,0:T(8,128)(2,1)}, u32[]{:S(2)}) copy-start(bf16[384,768]{1,0:T(8,128)(2,1)} %get-tuple-element.8) | copy-start | bytes 1769476
  195.8 20.5 %copy-start.4 = (bf16[384,768]{1,0:T(8,128)(2,1)S(1)}, bf16[384,768]{1,0:T(8,128)(2,1)}, u32[]{:S(2)}) copy-start(bf16[384,768]{1,0:T(8,128)(2,1)} %get-tuple-element.9) | copy-start | bytes 1769476
  211.6 57.6 %all-to-all-start.3 = ((bf16[32,12,4096]{2,1,0:T(8,128)(2,1)}), bf16[32,12,4096]{2,1,0:T(8,128)(2,1)}, u32[]{:S(2)}, u32[]{:S(2)}) async-start(bf16[32,12,4096]{2,1,0:T(8,128)(2,1)} %reshape.115), calls=%async_computation.3 | async-start | bytes 8388608 | tf_op jit(solution)/shard_map/all_to_all | solution.py:96
  216.3 155.2 %all-gather.3.cloned.1.call-start = ((), (), s32[]{:S(2)}) async-start(), calls=%async_computation.6 | async-start | bytes 5898240 | tf_op jit(solution)/shard_map/all_gather | solution.py:116
  269.2 59.9 %all-to-all-start.1 = ((bf16[32,12,4096]{2,1,0:T(8,128)(2,1)}), bf16[32,12,4096]{2,1,0:T(8,128)(2,1)}, u32[]{:S(2)}, u32[]{:S(2)}) async-start(bf16[32,12,4096]{2,1,0:T(8,128)(2,1)} %reshape.110), calls=%async_computation.1 | async-start | bytes 8388608 | tf_op jit(solution)/shard_map/all_to_all | solution.py:89
  329.1 42.4 %all-to-all-start.4 = ((bf16[384,4,1024]{2,0,1:T(8,128)(2,1)}), bf16[384,4,1024]{2,0,1:T(8,128)(2,1)}, u32[]{:S(2)}, u32[]{:S(2)}) async-start(bf16[384,4,1024]{2,0,1:T(8,128)(2,1)} %copy.28), calls=%async_computation.4 | async-start | bytes 6291456 | tf_op jit(solution)/shard_map/all_to_all | solution.py:109
  345.1 3.2 copy-start.6
  348.2 3.9 copy-start
  352.1 2.1 copy-start.1
Sparse Core Ops, SparseCore 0:
  181.0 41.0 all-gather.4
  224.3 49.8 all-gather.2

commit v2 on v1

v2 whole, which is shorter than its diff:
```python
import jax
import jax.numpy as jnp
from jax import lax
from jax.sharding import PartitionSpec as P


def contract_last(left, right):
    return lax.dot_general(
        left, right, (((1,), (1,)), ((), ())), preferred_element_type=jnp.float32
    )


def contract_first(left, right):
    return lax.dot_general(
        left, right, (((0,), (0,)), ((), ())), preferred_element_type=jnp.float32
    )


def expert_rows(rows_in, grads_in, gate_mat, up_mat, down_mat):
    gate_pre = jnp.dot(rows_in, gate_mat, preferred_element_type=jnp.float32)
    up_pre = jnp.dot(rows_in, up_mat, preferred_element_type=jnp.float32)
    sigma = jax.nn.sigmoid(gate_pre)
    silu_value = gate_pre * sigma
    hidden = (silu_value * up_pre).astype(jnp.bfloat16)
    expert_out = jnp.dot(hidden, down_mat, preferred_element_type=jnp.float32).astype(jnp.bfloat16)
    grad_hidden = contract_last(grads_in, down_mat)
    slope = sigma * (1.0 + gate_pre * (1.0 - sigma))
    grad_gate_pre = (grad_hidden * up_pre * slope).astype(jnp.bfloat16)
    grad_up_pre = (grad_hidden * silu_value).astype(jnp.bfloat16)
    pair_grad = (
        contract_last(grad_gate_pre, gate_mat) + contract_last(grad_up_pre, up_mat)
    ).astype(jnp.bfloat16)
    return (hidden, expert_out, grad_gate_pre, grad_up_pre, pair_grad)


def local(tokens, expert_ids, gate_values, upstream, w_gate, w_up, w_down):
    local_tokens = tokens.shape[0]
    width = tokens.shape[1]
    top_count = expert_ids.shape[1]
    ff_width = w_gate.shape[2]
    outer_count = lax.axis_size("outer")
    inner_count = lax.axis_size("inner")
    dp_count = lax.axis_size("dp")
    expert_count = outer_count * inner_count
    group = ("outer", "inner")
    me = lax.axis_index("outer") * inner_count + lax.axis_index("inner")
    group_tokens = expert_count * local_tokens
    capacity = min(local_tokens, 3 * local_tokens * top_count // (2 * expert_count))
    slot_total = expert_count * capacity

    ids_all = lax.all_gather(expert_ids, group, axis=0, tiled=True)
    gates_all = lax.all_gather(gate_values, group, axis=0, tiled=True)
    tokens_all = lax.all_gather(tokens, group, axis=0, tiled=True)
    upstream_all = lax.all_gather(upstream, group, axis=0, tiled=True)

    chosen = ids_all == me
    picked = jnp.any(chosen, axis=1)
    token_gate = jnp.sum(jnp.where(chosen, gates_all, 0.0), axis=1)
    position = jnp.cumsum(picked.astype(jnp.int32)) - 1
    token_slot = jnp.where(picked, position, slot_total)
    slot_token = (
        jnp.full((slot_total + 1,), group_tokens, jnp.int32)
        .at[token_slot]
        .set(jnp.arange(group_tokens, dtype=jnp.int32))[:slot_total]
    )
    token_pad = jnp.concatenate([tokens_all, jnp.zeros((1, width), jnp.bfloat16)], axis=0)
    upstream_pad = jnp.concatenate([upstream_all, jnp.zeros((1, width), jnp.bfloat16)], axis=0)
    gate_pad = jnp.concatenate([token_gate, jnp.zeros((1,), jnp.float32)], axis=0)
    rows_in = token_pad[slot_token]
    up_rows = upstream_pad[slot_token]
    grads_in = (gate_pad[slot_token][:, None] * up_rows.astype(jnp.float32)).astype(jnp.bfloat16)

    hidden, expert_out, grad_gate_pre, grad_up_pre, pair_grad = expert_rows(
        rows_in, grads_in, w_gate[0], w_up[0], w_down[0]
    )

    slot_gates_grad = jnp.sum(
        up_rows.astype(jnp.float32) * expert_out.astype(jnp.float32), axis=1
    )
    out_pad = jnp.concatenate([expert_out, jnp.zeros((1, width), jnp.bfloat16)], axis=0)
    back_pad = jnp.concatenate([pair_grad, jnp.zeros((1, width), jnp.bfloat16)], axis=0)
    gg_pad = jnp.concatenate([slot_gates_grad, jnp.zeros((1,), jnp.float32)], axis=0)
    out_share = (token_gate[:, None] * out_pad[token_slot].astype(jnp.float32)).astype(jnp.bfloat16)
    back_share = back_pad[token_slot]
    gg_share = jnp.where(chosen, gg_pad[token_slot][:, None], 0.0)
    output = lax.psum_scatter(out_share, group, scatter_dimension=0, tiled=True)
    grad_tokens = lax.psum_scatter(back_share, group, scatter_dimension=0, tiled=True)
    grad_gates = lax.psum_scatter(gg_share, group, scatter_dimension=0, tiled=True)

    piece = width // dp_count

    def spread_columns(block):
        return lax.all_to_all(
            block.reshape(slot_total, dp_count, piece), "dp", split_axis=1, concat_axis=0, tiled=True
        ).reshape(dp_count * slot_total, piece)

    joined_grads = jnp.concatenate([grad_gate_pre, grad_up_pre], axis=1)
    rows_all = spread_columns(rows_in)
    grads_all = spread_columns(grads_in)
    joined_all = lax.all_gather(joined_grads, "dp", axis=0, tiled=True)
    hidden_all = lax.all_gather(hidden, "dp", axis=0, tiled=True)
    grad_joined = contract_first(rows_all, joined_all)
    grad_down = contract_first(hidden_all, grads_all)
    grad_w_gate = grad_joined[:, :ff_width].astype(jnp.bfloat16)[None]
    grad_w_up = grad_joined[:, ff_width:].astype(jnp.bfloat16)[None]
    grad_w_down = grad_down.astype(jnp.bfloat16)[None]
    return (output, grad_tokens, grad_gates, grad_w_gate, grad_w_up, grad_w_down)


def solution(mesh):
    placed = (
        P(("dp", "outer", "inner"), None),
        P(("dp", "outer", "inner"), None),
        P(("dp", "outer", "inner"), None),
        P(("dp", "outer", "inner"), None),
        P(("outer", "inner"), None, None),
        P(("outer", "inner"), None, None),
        P(("outer", "inner"), None, None),
    )
    return jax.shard_map(
        local,
        mesh=mesh,
        in_specs=placed,
        out_specs=(
            P(("dp", "outer", "inner"), None),
            P(("dp", "outer", "inner"), None),
            P(("dp", "outer", "inner"), None),
            P(("outer", "inner"), "dp", None),
            P(("outer", "inner"), "dp", None),
            P(("outer", "inner"), None, "dp"),
        ),
        check_vma=False,
    )
```

time: 394 us -> 564 us (1.43)
  waiting for transfers between devices: 196 us -> 338 us
  blocking collectives: 0 us -> 47 us
  starting transfers between devices: 41.2 us -> 9.17 us
  local copies, waits for them, and re-layouts: 69.1 us -> 81.5 us
    reduce_scatter x0 -> x2, waiting for transfers between devices: none -> 183 us  [the longest x1 96.8 us: local(): output = lax.psum_scatter(out_share, group, scatter_dimension=0, tiled=True)]
    all_to_all x4 -> x0, waiting for transfers between devices: 171 us -> none  [the longest x1 48.5 us: local(): lax.all_to_all(send_grads.reshape(flat_shape), ('outer', 'inner'), split_...]
    all_gather x0 -> x2, blocking collectives: none -> 47 us  [the longest x1 24.5 us: local(): ids_all = lax.all_gather(expert_ids, group, axis=0, tiled=True)]
    all_gather x1, waiting for transfers between devices: 0.01 us -> 35.7 us  [local(): joined_all = lax.all_gather(joined_grads, 'dp', axis=0, tiled=True)]
    all_gather x0 -> x2, waiting for transfers between devices: none -> 35.5 us  [the longest x1 34.1 us: local(): tokens_all = lax.all_gather(tokens, group, axis=0, tiled=True)]
    gather x5 -> x6, local copies, waits for them, and re-layouts: 15.7 us -> 49.8 us  [the longest x1 12.7 us: local(): up_rows = upstream_pad[slot_token]]
    all_to_all x2, waiting for transfers between devices: 24.3 us -> 53.2 us  [spread_columns(): lax.all_to_all(block.reshape(slot_total, dp_count, piece), 'dp', split_ax...]
    all_gather x1, waiting for transfers between devices: 0.01 us -> 28.1 us  [local(): hidden_all = lax.all_gather(hidden, 'dp', axis=0, tiled=True)]
  transfers between devices with their start and end apart: 8 -> 9, of which waited for: 6 -> 8; matrix products, arithmetic and copies ran while one was open for 27% -> 17% of each run, Pallas kernels for 0% -> 0%
where the time goes in v2:
time: 564 us; the launch traced here: 559 us
  waiting for transfers between devices  338 us (60%)
  local copies, waits for them, and re-layouts  81.5 us (14%)
  matrix products  53.8 us (10%)
  blocking collectives  47 us (8%)
  other arithmetic  15.1 us (3%)
  between operations  14.7 us (3%)
  starting transfers between devices  9.17 us (2%)
    reduce_scatter x1, waiting for transfers between devices, local(): output = lax.psum_scatter(out_share, group, scatter_dimension=0, tiled=True)  96.8 us
    reduce_scatter x1, waiting for transfers between devices, local(): lax.psum_scatter(back_share, group, scatter_dimension=0, tiled=True)  86.6 us
    all_to_all x2, waiting for transfers between devices, spread_columns(): lax.all_to_all(block.reshape(slot_total, dp_count, piece), 'dp', split_ax...  53.2 us
    all_gather x1, waiting for transfers between devices, local(): joined_all = lax.all_gather(joined_grads, 'dp', axis=0, tiled=True)  35.7 us
    all_gather x1, waiting for transfers between devices, local(): tokens_all = lax.all_gather(tokens, group, axis=0, tiled=True)  34.1 us
    all_gather x1, waiting for transfers between devices, local(): hidden_all = lax.all_gather(hidden, 'dp', axis=0, tiled=True)  28.1 us
    all_gather x1, blocking collectives, local(): ids_all = lax.all_gather(expert_ids, group, axis=0, tiled=True)  24.5 us
    all_gather x1, blocking collectives, local(): gates_all = lax.all_gather(gate_values, group, axis=0, tiled=True)  22.5 us
  transfers between devices with their start and end apart: 9, of which 8 were waited for; matrix products, arithmetic and copies ran while one was open for 17% of the time, Pallas kernels for 0%

profile of v2, /device:TPU:8, one launch (start us, length us, event | category | flops | bytes accessed | tf_op | source)
XLA Modules:
  0.0 559.0 jit_solution(16613166208065047491)
XLA Ops:
  8.7 24.5 %all-gather = s32[32,32,8]{1,2,0:T(8,128)S(1)} all-gather(s32[1,32,8]{1,2,0:T(8,128)} %bitcast.73), channel_id=1, replica_groups=mesh['dp'=4,'outer'=16,'inner'=2] {'outer','inner'}, dimensions={0}, use_global_device_ids=true | all-gather | bytes 33792 | tf_op jit(solution)/shard_map/all_gather | solution.py:51
  34.0 22.5 %all-gather.1 = f32[32,32,8]{1,2,0:T(8,128)S(1)} all-gather(f32[1,32,8]{1,2,0:T(8,128)} %bitcast.74), channel_id=1, replica_groups=mesh['dp'=4,'outer'=16,'inner'=2] {'outer','inner'}, dimensions={0}, use_global_device_ids=true | all-gather | bytes 33792 | tf_op jit(solution)/shard_map/all_gather | solution.py:52
  65.6 7.7 %concatenate.24 = bf16[1025,4096]{1,0:T(8,128)(2,1)} pad(bf16[1024,4096]{1,0:T(8,128)(2,1)} %all-gather.9.cloned.1.call-done, bf16[]{:T(256)} %constant.7.clone.1), padding=0_1x0_0 | pad | bytes 16785410 | tf_op jit(solution)/shard_map/concatenate | solution.py:67
  73.3 12.7 %gather_fusion.3 = bf16[384,4096]{1,0:T(8,128)(2,1)} fusion(bf16[1025,4096]{1,0:T(8,128)(2,1)} %concatenate.24, s32[1024]{0:T(1024)S(1)} %pad_clamp_fusion), kind=kCustom, calls=%fused_computation.3 | custom fusion | bytes 6292992 | tf_op jit(solution)/shard_map/gather | solution.py:70
  86.0 34.1 %all-gather.7.cloned.1.call-done = bf16[1024,4096]{1,0:T(8,128)(2,1)} async-done(((bf16[32,4096]{1,0:T(8,128)(2,1)}), bf16[1024,4096]{1,0:T(8,128)(2,1)}) %all-gather.7.cloned.1.call-update) | async-done | bytes 8388624 | tf_op jit(solution)/shard_map/all_gather | solution.py:53
  120.2 7.7 %concatenate.21 = bf16[1025,4096]{1,0:T(8,128)(2,1)} pad(bf16[1024,4096]{1,0:T(8,128)(2,1)} %all-gather.7.cloned.1.call-done, bf16[]{:T(256)} %constant.7.clone.1), padding=0_1x0_0 | pad | bytes 16785410 | tf_op jit(solution)/shard_map/concatenate | solution.py:66
  127.9 12.2 %gather_fusion = bf16[384,4096]{1,0:T(8,128)(2,1)S(1)} fusion(bf16[1025,4096]{1,0:T(8,128)(2,1)} %concatenate.21, s32[1024]{0:T(1024)S(1)} %pad_clamp_fusion), kind=kCustom, calls=%fused_computation | custom fusion | bytes 6292992 | tf_op jit(solution)/shard_map/gather | solution.py:69
  140.1 6.6 %fusion.7 = f32[384,768]{1,0:T(8,128)S(1)} fusion(bf16[384,4096]{1,0:T(8,128)(2,1)S(1)} %gather_fusion, bf16[1,4096,768]{2,1,0:T(8,128)(2,1)} %param.12), kind=kOutput, calls=%fused_computation.16 | convolution fusion | flops 2415919104 | bytes 10616832 | tf_op jit(solution)/shard_map/dot_general | solution.py:21
  146.7 5.6 %fusion.1 = f32[384,768]{1,0:T(8,128)S(1)} fusion(bf16[1,768,4096]{2,1,0:T(8,128)(2,1)} %param.13, bf16[384,4096]{1,0:T(8,128)(2,1)S(1)} %copy-done.2, f32[384]{0:T(512)S(1)} %gather_fusion.2), kind=kOutput, calls=%fused_computation.10 | convolution fusion | flops 2420637696 | bytes 10618368 | tf_op jit(solution)/shard_map/dot_general | solution.py:8
  152.3 7.0 %multiply_convert_fusion.4 = (bf16[384,768]{1,0:T(8,128)(2,1)}, bf16[384,768]{1,0:T(8,128)(2,1)}, bf16[384,768]{1,0:T(8,128)(2,1)}) fusion(f32[384,768]{1,0:T(8,128)S(1)} %fusion.1, f32[384,768]{1,0:T(8,128)S(1)} %fusion.7, bf16[384,4096]{1,0:T(8,128)(2,1)S(1)} %gather_fusion, bf16[1,4096,768]{2,1,0:T(8,128)(2,1)} %param.11), kind=kOutput, calls=%fused_computation.36 | convolution fusion | flops 2420342784 | bytes 13565952 | tf_op jit(solution)/shard_map/dot_general | solution.py:20
  159.3 8.2 %multiply_reduce_fusion = (f32[384]{0:T(512)S(1)}, bf16[384,4096]{1,0:T(8,128)(2,1)}) fusion(bf16[384,4096]{1,0:T(8,128)(2,1)} %gather_fusion.3, bf16[384,768]{1,0:T(8,128)(2,1)} %get-tuple-element.12, bf16[1,768,4096]{2,1,0:T(8,128)(2,1)} %param.13), kind=kOutput, calls=%fused_computation.22 | convolution fusion | flops 2423782912 | bytes 13174272 | tf_op jit(solution)/shard_map/dot_general | solution.py:25
  167.6 6.9 %gather_fusion.5 = f32[1024]{0:T(1024)S(1)} fusion(f32[385]{0:T(512)S(1)} %pad_maximum_fusion.2, s32[1024]{0:T(1024)S(1)} %broadcast_clamp_fusion), kind=kCustom, calls=%fused_computation.5 | custom fusion | bytes 12288 | tf_op jit(solution)/shard_map/gather | solution.py:85
  182.3 7.3 %add_convert_fusion = bf16[384,4096]{1,0:T(8,128)(2,1)S(1)} fusion(f32[384,4096]{1,0:T(8,128)S(1)} %fusion.5, bf16[384,768]{1,0:T(8,128)(2,1)S(1)} %copy-done.4, bf16[1,4096,768]{2,1,0:T(8,128)(2,1)} %param.11), kind=kOutput, calls=%fused_computation.23 | convolution fusion | flops 2419064832 | bytes 16318464 | tf_op jit(solution)/shard_map/dot_general | solution.py:8
  189.9 7.8 %gather_fusion.4 = bf16[1024,4096]{1,0:T(8,128)(2,1)} fusion(bf16[385,4096]{1,0:T(8,128)(2,1)S(1)} %concatenate.25, s32[1024]{0:T(1024)S(1)} %broadcast_clamp_fusion), kind=kCustom, calls=%fused_computation.4 | custom fusion | bytes 16781312 | tf_op jit(solution)/shard_map/gather | solution.py:84
  199.9 7.8 %gather_fusion.1 = bf16[1024,4096]{1,0:T(8,128)(2,1)} fusion(bf16[385,4096]{1,0:T(8,128)(2,1)S(1)} %concatenate.22, s32[1024]{0:T(1024)S(1)} %broadcast_clamp_fusion), kind=kCustom, calls=%fused_computation.1 | custom fusion | bytes 16781312 | tf_op jit(solution)/shard_map/gather | solution.py:83
  207.7 10.0 %multiply_convert_fusion = bf16[1024,4096]{1,0:T(8,128)(2,1)} fusion(bf16[1024,4096]{1,0:T(8,128)(2,1)} %gather_fusion.1, f32[1024]{0:T(1024)S(1)} %select_reduce_fusion), kind=kLoop, calls=%fused_computation.7 | loop fusion | flops 12582912 | bytes 16781312 | tf_op jit(solution)/shard_map/convert_element_type | solution.py:83
  230.3 36.1 %all-to-all-done.1 = bf16[384,4,1024]{2,0,1:T(8,128)(2,1)} async-done(((bf16[384,4,1024]{2,0,1:T(8,128)(2,1)}), bf16[384,4,1024]{2,0,1:T(8,128)(2,1)}, u32[]{:S(2)}, u32[]{:S(2)}) %all-to-all-start.1) | async-done | bytes 3145760 | tf_op jit(solution)/shard_map/all_to_all | solution.py:93
  271.8 28.1 %all-gather.13.cloned.1.call-done = bf16[1536,768]{1,0:T(8,128)(2,1)} async-done(((bf16[384,768]{1,0:T(8,128)(2,1)}), bf16[1536,768]{1,0:T(8,128)(2,1)}) %all-gather.13.cloned.1.call-update) | async-done | bytes 2359312 | tf_op jit(solution)/shard_map/all_gather | solution.py:101
  299.8 6.4 %fusion.20 = bf16[1,768,1024]{2,1,0:T(8,128)(2,1)} fusion(bf16[1536,768]{1,0:T(8,128)(2,1)} %all-gather.13.cloned.1.call-done, bf16[1536,1024]{1,0:T(8,128)(2,1)} %bitcast.14), kind=kOutput, calls=%fused_computation.33 | convolution fusion | flops 2416705536 | bytes 7077888 | tf_op jit(solution)/shard_map/dot_general | solution.py:14
  306.2 17.1 %all-to-all-done = bf16[384,4,1024]{2,0,1:T(8,128)(2,1)S(1)} async-done(((bf16[384,4,1024]{2,0,1:T(8,128)(2,1)}), bf16[384,4,1024]{2,0,1:T(8,128)(2,1)S(1)}, u32[]{:S(2)}, u32[]{:S(2)}) %all-to-all-start) | async-done | bytes 3145760 | tf_op jit(solution)/shard_map/all_to_all | solution.py:93
  323.3 35.7 %all-gather.11.cloned.1.call-done = bf16[1536,1536]{1,0:T(8,128)(2,1)} async-done(((bf16[384,1536]{1,0:T(8,128)(2,1)}), bf16[1536,1536]{1,0:T(8,128)(2,1)}) %all-gather.11.cloned.1.call-update) | async-done | bytes 4718608 | tf_op jit(solution)/shard_map/all_gather | solution.py:100
  359.0 7.7 %convolution_convert_fusion = bf16[1024,1536]{1,0:T(8,128)(2,1)S(1)} fusion(bf16[1536,1024]{1,0:T(8,128)(2,1)S(1)} %bitcast.69, bf16[1536,1536]{1,0:T(8,128)(2,1)} %all-gather.11.cloned.1.call-done), kind=kOutput, calls=%fused_computation.26 | convolution fusion | flops 4833411072 | bytes 11010048 | tf_op jit(solution)/shard_map/dot_general | solution.py:14
  368.5 86.6 %reduce-scatter.8.cloned.1.call-done = bf16[32,4096]{1,0:T(8,128)(2,1)} async-done(((bf16[1024,4096]{1,0:T(8,128)(2,1)}), bf16[32,4096]{1,0:T(8,128)(2,1)}) %reduce-scatter.8.cloned.1.call-update) | async-done | bytes 262160 | tf_op jit(solution)/shard_map/reduce_scatter | solution.py:87
  455.1 96.8 %reduce-scatter.6.cloned.1.call-done = bf16[32,4096]{1,0:T(8,128)(2,1)} async-done(((bf16[1024,4096]{1,0:T(8,128)(2,1)}), bf16[32,4096]{1,0:T(8,128)(2,1)}) %reduce-scatter.6.cloned.1.call-update) | async-done | bytes 262160 | tf_op jit(solution)/shard_map/reduce_scatter | solution.py:86
  (64 shorter events, 41.4 us)
Async XLA Ops:
  7.2 58.4 %all-gather.9.cloned.1.call-start = ((), (), s32[]{:S(2)}) async-start(), calls=%async_computation.7 | async-start | bytes 8650752 | tf_op jit(solution)/shard_map/all_gather | solution.py:54
  7.9 112.3 %all-gather.7.cloned.1.call-start = ((), (), s32[]{:S(2)}) async-start(), calls=%async_computation.5 | async-start | bytes 8650752 | tf_op jit(solution)/shard_map/all_gather | solution.py:53
  8.6 261.7 %reduce-scatter.10.cloned.1.call-start = ((), (), s32[]{:S(2)}) async-start(), calls=%async_computation.11 | async-start | bytes 540672
  140.1 12.2 %copy-start = (bf16[384,4096]{1,0:T(8,128)(2,1)}, bf16[384,4096]{1,0:T(8,128)(2,1)S(1)}, u32[]{:S(2)}) copy-start(bf16[384,4096]{1,0:T(8,128)(2,1)S(1)} %gather_fusion) | copy-start | bytes 9437188
  140.1 6.6 %copy-start.2 = (bf16[384,4096]{1,0:T(8,128)(2,1)S(1)}, bf16[384,4096]{1,0:T(8,128)(2,1)}, u32[]{:S(2)}) copy-start(bf16[384,4096]{1,0:T(8,128)(2,1)} %gather_fusion.3) | copy-start | bytes 9437188
  167.6 8.6 %copy-start.4 = (bf16[384,768]{1,0:T(8,128)(2,1)S(1)}, bf16[384,768]{1,0:T(8,128)(2,1)}, u32[]{:S(2)}) copy-start(bf16[384,768]{1,0:T(8,128)(2,1)} %get-tuple-element.10) | copy-start | bytes 1769476
  167.6 8.6 %copy-start.5 = (bf16[384,768]{1,0:T(8,128)(2,1)S(1)}, bf16[384,768]{1,0:T(8,128)(2,1)}, u32[]{:S(2)}) copy-start(bf16[384,768]{1,0:T(8,128)(2,1)} %get-tuple-element.11) | copy-start | bytes 1769476
  175.5 124.3 %all-gather.13.cloned.1.call-start = ((), (), s32[]{:S(2)}) async-start(), calls=%async_computation.10 | async-start | bytes 2949120 | tf_op jit(solution)/shard_map/all_gather | solution.py:101
  176.1 182.8 %all-gather.11.cloned.1.call-start = ((), (), s32[]{:S(2)}) async-start(), calls=%async_computation.9 | async-start | bytes 5898240 | tf_op jit(solution)/shard_map/all_gather | solution.py:100
  177.3 277.8 %reduce-scatter.8.cloned.1.call-start = ((), (), s32[]{:S(2)}) async-start(), calls=%async_computation.8 | async-start | bytes 8650752 | tf_op jit(solution)/shard_map/reduce_scatter | solution.py:87
  197.7 354.2 %reduce-scatter.6.cloned.1.call-start = ((), (), s32[]{:S(2)}) async-start(), calls=%async_computation.6 | async-start | bytes 8650752 | tf_op jit(solution)/shard_map/reduce_scatter | solution.py:86
  217.7 1.9 copy-start.3
  223.1 5.0 copy-start.1
  223.1 43.3 %all-to-all-start.1 = ((bf16[384,4,1024]{2,0,1:T(8,128)(2,1)}), bf16[384,4,1024]{2,0,1:T(8,128)(2,1)}, u32[]{:S(2)}, u32[]{:S(2)}) async-start(bf16[384,4,1024]{2,0,1:T(8,128)(2,1)} %fusion), calls=%async_computation.3 | async-start | bytes 6291456 | tf_op jit(solution)/shard_map/all_to_all | solution.py:93
  266.4 56.9 %all-to-all-start = ((bf16[384,4,1024]{2,0,1:T(8,128)(2,1)}), bf16[384,4,1024]{2,0,1:T(8,128)(2,1)S(1)}, u32[]{:S(2)}, u32[]{:S(2)}) async-start(bf16[384,4,1024]{2,0,1:T(8,128)(2,1)} %bitcast.68), calls=%async_computation.2 | async-start | bytes 6291456 | tf_op jit(solution)/shard_map/all_to_all | solution.py:93
Sparse Core Ops, SparseCore 0:
  10.3 55.2 all-gather.8
  67.8 52.2 all-gather.6
  175.6 76.3 reduce-scatter.9
  254.2 45.6 all-gather.12
  301.9 56.9 all-gather.10
  363.1 91.9 reduce-scatter.7
  459.9 91.9 reduce-scatter.5

commit v3 on v1

--- a/solution.py
+++ b/solution.py
@@ -63,62 +63,47 @@
     send_grads = (
         gate_pad[slot_pair][:, None] * upstream_pad[slot_token].astype(jnp.float32)
     ).astype(jnp.bfloat16)
-    flat_shape = (expert_count, capacity, width)
-    got_rows, got_grads = (
-        lax.all_to_all(
-            send_rows.reshape(flat_shape),
-            ("outer", "inner"),
-            split_axis=0,
-            concat_axis=0,
-            tiled=True,
-        ),
-        lax.all_to_all(
-            send_grads.reshape(flat_shape),
-            ("outer", "inner"),
-            split_axis=0,
-            concat_axis=0,
-            tiled=True,
-        ),
-    )
-    rows_in = got_rows.reshape(-1, width)
-    grads_in = got_grads.reshape(-1, width)
+    flat_shape = (expert_count, capacity, 2 * width)
+    got = lax.all_to_all(
+        jnp.concatenate([send_rows, send_grads], axis=1).reshape(flat_shape),
+        ("outer", "inner"),
+        split_axis=0,
+        concat_axis=0,
+        tiled=True,
+    ).reshape(-1, 2 * width)
+    rows_in = got[:, :width]
+    grads_in = got[:, width:]
     hidden, expert_out, grad_gate_pre, grad_up_pre, pair_grad = expert_rows(
         rows_in, grads_in, w_gate[0], w_up[0], w_down[0]
     )
-    back_out, back_grad = (
-        lax.all_to_all(
-            expert_out.reshape(flat_shape),
-            ("outer", "inner"),
-            split_axis=0,
-            concat_axis=0,
-            tiled=True,
-        ),
-        lax.all_to_all(
-            pair_grad.reshape(flat_shape),
-            ("outer", "inner"),
-            split_axis=0,
-            concat_axis=0,
-            tiled=True,
-        ),
-    )
+    back = lax.all_to_all(
+        jnp.concatenate([expert_out, pair_grad], axis=1).reshape(flat_shape),
+        ("outer", "inner"),
+        split_axis=0,
+        concat_axis=0,
+        tiled=True,
+    ).reshape(-1, 2 * width)
     dp_count = lax.axis_size("dp")
     slot_total = rows_in.shape[0]
     piece = width // dp_count
 
-    def spread_columns(block):
-        return lax.all_to_all(
-            block.reshape(slot_total, dp_count, piece), "dp", split_axis=1, concat_axis=0, tiled=True
-        ).reshape(dp_count * slot_total, piece)
-
     joined_grads = jnp.concatenate([grad_gate_pre, grad_up_pre], axis=1)
-    rows_all = spread_columns(rows_in)
-    grads_all = spread_columns(grads_in)
+    both_all = lax.all_to_all(
+        got.reshape(slot_total, 2, dp_count, piece).transpose(0, 2, 1, 3),
+        "dp",
+        split_axis=1,
+        concat_axis=0,
+        tiled=True,
+    ).reshape(dp_count * slot_total, 2, piece)
+    rows_all = both_all[:, 0]
+    grads_all = both_all[:, 1]
     joined_all = lax.all_gather(joined_grads, "dp", axis=0, tiled=True)
     hidden_all = lax.all_gather(hidden, "dp", axis=0, tiled=True)
     grad_joined = contract_first(rows_all, joined_all)
     grad_down = contract_first(hidden_all, grads_all)
-    pair_out = back_out.reshape(-1, width)[pair_slot].reshape(local_tokens, top_count, width)
-    pair_back = back_grad.reshape(-1, width)[pair_slot].reshape(local_tokens, top_count, width)
+    pair_both = back[pair_slot]
+    pair_out = pair_both[:, :width].reshape(local_tokens, top_count, width)
+    pair_back = pair_both[:, width:].reshape(local_tokens, top_count, width)
     output = jnp.sum(gate_values[:, :, None] * pair_out.astype(jnp.float32), axis=1).astype(
         jnp.bfloat16
     )

time: 394 us -> 499 us (1.27)
  blocking collectives: 0 us -> 102 us
  starting transfers between devices: 41.2 us -> 12.5 us
  local copies, waits for them, and re-layouts: 69.1 us -> 93.8 us
  other arithmetic: 13.6 us -> 28.4 us
  waiting for transfers between devices: 196 us -> 187 us
    all_to_all x0 -> x1, blocking collectives: none -> 102 us  [local(): lax.all_to_all(jnp.concatenate([send_rows, send_grads], axis=1).reshape(f...]
    all_to_all x6 -> x2, starting transfers between devices: 41.1 us -> 12.2 us  [the longest x1 6.91 us: local(): lax.all_to_all(jnp.concatenate([expert_out, pair_grad], axis=1).reshape(f...]
    concatenate x0 -> x2, other arithmetic: none -> 11.6 us  [the longest x1 8.27 us: local(): jnp.concatenate([send_rows, send_grads], axis=1).reshape(flat_shape)]
    transpose x0 -> x1, local copies, waits for them, and re-layouts: none -> 10.2 us  [local(): got.reshape(slot_total, 2, dp_count, piece).transpose(0, 2, 1, 3)]
    all_to_all x6 -> x2, waiting for transfers between devices: 196 us -> 187 us  [the longest x1 110 us: local(): lax.all_to_all(jnp.concatenate([expert_out, pair_grad], axis=1).reshape(f...]
    all_to_all x0 -> x1, local copies, waits for them, and re-layouts: none -> 7.47 us  [local(): lax.all_to_all(got.reshape(slot_total, 2, dp_count, piece).transpose(0, 2...]
    gather x2 -> x1, local copies, waits for them, and re-layouts: 6.33 us -> 12.6 us  [local(): pair_both = back[pair_slot]]
    another operation x5 -> x2, local copies, waits for them, and re-layouts: 19.2 us -> 14 us  [the longest x1 14 us: local(): got.reshape(slot_total, 2, dp_count, piece).transpose(0, 2, 1, 3)]
  transfers between devices with their start and end apart: 8 -> 4, of which waited for: 6 -> 2; matrix products, arithmetic and copies ran while one was open for 27% -> 21% of each run, Pallas kernels for 0% -> 0%
where the time goes in v3:
time: 499 us; the launch traced here: 491 us
  waiting for transfers between devices  187 us (37%)
  blocking collectives  102 us (20%)
  local copies, waits for them, and re-layouts  93.8 us (19%)
  matrix products  53.3 us (11%)
  other arithmetic  28.4 us (6%)
  between operations  14.7 us (3%)
  starting transfers between devices  12.5 us (3%)
    all_to_all x1, waiting for transfers between devices, local(): lax.all_to_all(jnp.concatenate([expert_out, pair_grad], axis=1).reshape(f...  110 us
    all_to_all x1, blocking collectives, local(): lax.all_to_all(jnp.concatenate([send_rows, send_grads], axis=1).reshape(f...  102 us
    all_to_all x1, waiting for transfers between devices, local(): lax.all_to_all(got.reshape(slot_total, 2, dp_count, piece).transpose(0, 2...  76.6 us
    dot_general x3, matrix products, contract_last(): lax.dot_general(left, right, (((1,), (1,)), ((), ())), preferred_element_...  20.7 us
    dot_general x2, matrix products, contract_first(): lax.dot_general(left, right, (((0,), (0,)), ((), ())), preferred_element_...  14.5 us
    another operation x1, local copies, waits for them, and re-layouts, local(): got.reshape(slot_total, 2, dp_count, piece).transpose(0, 2, 1, 3)  14 us
    gather x1, local copies, waits for them, and re-layouts, local(): pair_both = back[pair_slot]  12.6 us
    transpose x1, local copies, waits for them, and re-layouts, local(): got.reshape(slot_total, 2, dp_count, piece).transpose(0, 2, 1, 3)  10.2 us
  transfers between devices with their start and end apart: 4, of which 2 were waited for; matrix products, arithmetic and copies ran while one was open for 21% of the time, Pallas kernels for 0%

profile of v3, /device:TPU:8, one launch (start us, length us, event | category | flops | bytes accessed | tf_op | source)
XLA Modules:
  0.0 491.4 jit_solution(5942732665524686287)
XLA Ops:
  29.4 6.5 %multiply_convert_fusion = bf16[32,12,4096]{2,1,0:T(8,128)(2,1)} fusion(f32[32,12,4096]{2,1,0:T(8,128)} %reshape.101, f32[32,12]{1,0:T(8,128)S(1)} %mul.64), kind=kLoop, calls=%fused_computation.6 | loop fusion | flops 3145728 | bytes 9438720 | tf_op jit(solution)/shard_map/convert_element_type | solution.py:65
  35.9 8.3 %pad_maximum_fusion = bf16[32,12,8192]{2,1,0:T(8,128)(2,1)} fusion(bf16[32,12,4096]{2,1,0:T(8,128)(2,1)} %multiply_convert_fusion, bf16[32,12,4096]{2,1,0:T(8,128)(2,1)} %concatenate.22), kind=kLoop, calls=%fused_computation.5 | loop fusion | flops 12582912 | bytes 12582912 | tf_op jit(solution)/shard_map/concatenate | solution.py:68
  44.2 102.1 %all_to_all.25 = bf16[32,12,8192]{2,1,0:T(8,128)(2,1)} all-to-all(bf16[32,12,8192]{2,1,0:T(8,128)(2,1)} %pad_maximum_fusion), channel_id=1, replica_groups=mesh['dp'=4,'outer'=16,'inner'=2] {'outer','inner'}, dimensions={0} | all-to-all | bytes 12582912 | tf_op jit(solution)/shard_map/all_to_all | solution.py:67
  146.3 8.7 %reshape.95 = bf16[384,8192]{1,0:T(8,128)(2,1)} reshape(bf16[32,12,8192]{2,1,0:T(8,128)(2,1)} %all_to_all.25) | data formatting | bytes 12582912 | tf_op jit(solution)/shard_map/reshape | solution.py:73
  155.0 6.5 %fusion = f32[384,768]{1,0:T(8,128)S(1)} fusion(bf16[1,768,4096]{2,1,0:T(8,128)(2,1)} %param.13, bf16[384,8192]{1,0:T(8,128)(2,1)} %reshape.95), kind=kOutput, calls=%fused_computation.8 | convolution fusion | flops 2415919104 | bytes 10616832 | tf_op jit(solution)/shard_map/dot_general | solution.py:8
  161.6 5.6 %fusion.10 = f32[384,768]{1,0:T(8,128)S(1)} fusion(bf16[1,4096,768]{2,1,0:T(8,128)(2,1)} %param.11, bf16[384,8192]{1,0:T(8,128)(2,1)S(1)} %copy-done), kind=kOutput, calls=%fused_computation.18 | convolution fusion | flops 2415919104 | bytes 10616832 | tf_op jit(solution)/shard_map/dot_general | solution.py:20
  167.2 3.7 multiply_convert_fusion.3
  170.9 14.0 %reshape_reshape.3 = bf16[384,2,4,1024]{3,2,1,0:T(4,128)(2,1)} reshape(bf16[32,12,8192]{2,1,0:T(8,128)(2,1)} %all_to_all.25) | data formatting | bytes 12582912 | tf_op jit(solution)/shard_map/reshape;reshape | solution.py:92
  184.9 10.2 %copy.27 = bf16[384,4,2,1024]{3,2,0,1:T(2,128)(2,1)} copy(bf16[384,4,2,1024]{3,1,2,0:T(4,128)(2,1)} %bitcast.80) | data formatting | bytes 12582912 | tf_op jit(solution)/shard_map/transpose | solution.py:92
  195.1 5.3 %all-to-all-start.2 = ((bf16[384,4,2,1024]{3,2,0,1:T(2,128)(2,1)}), bf16[384,4,2,1024]{3,2,0,1:T(2,128)(2,1)}, u32[]{:S(2)}, u32[]{:S(2)}) async-start(bf16[384,4,2,1024]{3,2,0,1:T(2,128)(2,1)} %copy.27), calls=%async_computation.2 | async-start | bytes 12582912 | tf_op jit(solution)/shard_map/all_to_all | solution.py:91
  201.8 9.0 %fusion.4 = f32[384,4096]{1,0:T(8,128)} fusion(bf16[384,768]{1,0:T(8,128)(2,1)S(1)} %get-tuple-element.10, bf16[1,4096,768]{2,1,0:T(8,128)(2,1)} %param.12), kind=kOutput, calls=%fused_computation.12 | convolution fusion | flops 2415919104 | bytes 13172736 | tf_op jit(solution)/shard_map/dot_general | solution.py:8
  210.8 5.8 %fusion.14 = bf16[384,4096]{1,0:T(8,128)(2,1)S(1)} fusion(bf16[384,768]{1,0:T(8,128)(2,1)S(1)} %copy-done.1, bf16[1,768,4096]{2,1,0:T(8,128)(2,1)} %param.13), kind=kOutput, calls=%fused_computation.21 | convolution fusion | flops 2417491968 | bytes 10027008 | tf_op jit(solution)/shard_map/dot_general | solution.py:25
  216.6 5.2 %add_convert_fusion = bf16[384,4096]{1,0:T(8,128)(2,1)S(1)} fusion(f32[384,4096]{1,0:T(8,128)} %fusion.4, bf16[384,768]{1,0:T(8,128)(2,1)S(1)} %get-tuple-element.9, bf16[1,4096,768]{2,1,0:T(8,128)(2,1)S(1)} %bitcast.91), kind=kOutput, calls=%fused_computation.20 | convolution fusion | flops 2419064832 | bytes 16318464 | tf_op jit(solution)/shard_map/dot_general | solution.py:8
  225.1 8.6 %reshape.96 = bf16[32,12,8192]{2,1,0:T(8,128)(2,1)} reshape(bf16[384,8192]{1,0:T(8,128)(2,1)} %pad_maximum_fusion.1) | data formatting | bytes 12582912 | tf_op jit(solution)/shard_map/reshape | solution.py:80
  233.7 76.6 %all-to-all-done.2 = bf16[384,4,2,1024]{3,2,0,1:T(2,128)(2,1)} async-done(((bf16[384,4,2,1024]{3,2,0,1:T(2,128)(2,1)}), bf16[384,4,2,1024]{3,2,0,1:T(2,128)(2,1)}, u32[]{:S(2)}, u32[]{:S(2)}) %all-to-all-start.2) | async-done | bytes 6291488 | tf_op jit(solution)/shard_map/all_to_all | solution.py:91
  310.3 6.9 %all-to-all-start.1 = ((bf16[32,12,8192]{2,1,0:T(8,128)(2,1)}), bf16[32,12,8192]{2,1,0:T(8,128)(2,1)}, u32[]{:S(2)}, u32[]{:S(2)}) async-start(bf16[32,12,8192]{2,1,0:T(8,128)(2,1)} %reshape.96), calls=%async_computation.1 | async-start | bytes 16777216 | tf_op jit(solution)/shard_map/all_to_all | solution.py:79
  317.2 7.5 %copy.28 = bf16[384,4,2,1024]{3,0,1,2:T(8,128)(2,1)} copy(bf16[384,4,2,1024]{3,2,0,1:T(2,128)(2,1)} %all-to-all-done.2) | data formatting | bytes 12582912 | tf_op jit(solution)/shard_map/all_to_all | solution.py:91
  324.7 6.4 %fusion.24 = bf16[1,768,1024]{2,1,0:T(8,128)(2,1)} fusion(bf16[1536,768]{1,0:T(8,128)(2,1)} %all-gather.5.cloned.1.call-done, bf16[1536,2,1024]{2,0,1:T(8,128)(2,1)} %bitcast.81), kind=kOutput, calls=%fused_computation.37 | convolution fusion | flops 2416705536 | bytes 7077888 | tf_op jit(solution)/shard_map/dot_general | solution.py:14
  331.1 110.1 %all-to-all-done.1 = bf16[32,12,8192]{2,1,0:T(8,128)(2,1)} async-done(((bf16[32,12,8192]{2,1,0:T(8,128)(2,1)}), bf16[32,12,8192]{2,1,0:T(8,128)(2,1)}, u32[]{:S(2)}, u32[]{:S(2)}) %all-to-all-start.1) | async-done | bytes 6291488 | tf_op jit(solution)/shard_map/all_to_all | solution.py:79
  441.2 9.0 %reshape.97 = bf16[384,8192]{1,0:T(8,128)(2,1)} reshape(bf16[32,12,8192]{2,1,0:T(8,128)(2,1)} %all-to-all-done.1) | data formatting | bytes 12582912 | tf_op jit(solution)/shard_map/reshape | solution.py:85
  450.2 12.6 %gather_fusion.3 = bf16[256,8192]{1,0:T(8,128)(2,1)} fusion(bf16[384,8192]{1,0:T(8,128)(2,1)} %reshape.97, s32[1024]{0:T(1024)S(1)} %pad_clamp_fusion), kind=kCustom, calls=%fused_computation.3 | custom fusion | bytes 8389632 | tf_op jit(solution)/shard_map/gather | solution.py:104
  466.4 3.7 fusion.21
  470.2 3.9 multiply_reduce_fusion
  474.1 8.1 %convolution_convert_fusion = bf16[1024,1536]{1,0:T(8,128)(2,1)S(1)} fusion(bf16[1536,1536]{1,0:T(8,128)(2,1)} %all-gather.3.cloned.1.call-done, bf16[1536,2,1024]{2,0,1:T(8,128)(2,1)} %bitcast.82), kind=kOutput, calls=%fused_computation.23 | convolution fusion | flops 4833411072 | bytes 11010048 | tf_op jit(solution)/shard_map/dot_general | solution.py:14
  (58 shorter events, 32.5 us)
Async XLA Ops:
  7.2 317.5 %all-gather.5.cloned.1.call-start = ((), (), s32[]{:S(2)}) async-start(), calls=%async_computation.4 | async-start | bytes 2949120 | tf_op jit(solution)/shard_map/all_gather | solution.py:101
  15.7 3.7 copy-start.3
  155.0 6.5 %copy-start = (bf16[384,8192]{1,0:T(8,128)(2,1)S(1)}, bf16[384,8192]{1,0:T(8,128)(2,1)}, u32[]{:S(2)}) copy-start(bf16[384,8192]{1,0:T(8,128)(2,1)} %reshape.95) | copy-start | bytes 18874372
  155.0 12.1 %slice-start = ((s8[6291456]{0:T(1024)(128)(4,1)}), s8[4194304]{0:T(1024)(128)(4,1)S(1)}, s32[]{:S(2)}) async-start(s8[6291456]{0:T(1024)(128)(4,1)} %bitcast.88), calls=%async_computation.5 | async-start | bytes 8388608
  161.6 5.6 %slice-start.1 = ((s8[6291456]{0:T(1024)(128)(4,1)}), s8[2097152]{0:T(1024)(128)(4,1)S(1)}, s32[]{:S(2)}) async-start(s8[6291456]{0:T(1024)(128)(4,1)} %bitcast.88), calls=%async_computation.6 | async-start | bytes 4194304
  195.1 115.2 %all-to-all-start.2 = ((bf16[384,4,2,1024]{3,2,0,1:T(2,128)(2,1)}), bf16[384,4,2,1024]{3,2,0,1:T(2,128)(2,1)}, u32[]{:S(2)}, u32[]{:S(2)}) async-start(bf16[384,4,2,1024]{3,2,0,1:T(2,128)(2,1)} %copy.27), calls=%async_computation.2 | async-start | bytes 12582912 | tf_op jit(solution)/shard_map/all_to_all | solution.py:91
  200.4 273.7 %all-gather.3.cloned.1.call-start = ((), (), s32[]{:S(2)}) async-start(), calls=%async_computation.3 | async-start | bytes 5898240 | tf_op jit(solution)/shard_map/all_gather | solution.py:100
  201.8 9.0 %copy-start.1 = (bf16[384,768]{1,0:T(8,128)(2,1)S(1)}, bf16[384,768]{1,0:T(8,128)(2,1)}, u32[]{:S(2)}) copy-start(bf16[384,768]{1,0:T(8,128)(2,1)} %get-tuple-element.8) | copy-start | bytes 1769476
  201.8 14.8 %slice-start.2 = ((s8[6291456]{0:T(1024)(128)(4,1)}), s8[4194304]{0:T(1024)(128)(4,1)S(1)}, s32[]{:S(2)}) async-start(s8[6291456]{0:T(1024)(128)(4,1)} %bitcast.90), calls=%async_computation.7 | async-start | bytes 8388608
  210.8 5.8 %slice-start.3 = ((s8[6291456]{0:T(1024)(128)(4,1)}), s8[2097152]{0:T(1024)(128)(4,1)S(1)}, s32[]{:S(2)}) async-start(s8[6291456]{0:T(1024)(128)(4,1)} %bitcast.90), calls=%async_computation.8 | async-start | bytes 4194304
  310.3 130.9 %all-to-all-start.1 = ((bf16[32,12,8192]{2,1,0:T(8,128)(2,1)}), bf16[32,12,8192]{2,1,0:T(8,128)(2,1)}, u32[]{:S(2)}, u32[]{:S(2)}) async-start(bf16[32,12,8192]{2,1,0:T(8,128)(2,1)} %reshape.96), calls=%async_computation.1 | async-start | bytes 16777216 | tf_op jit(solution)/shard_map/all_to_all | solution.py:79
  450.1 12.6 %copy-start.2 = (bf16[32,4096]{1,0:T(8,128)(2,1)S(1)}, bf16[32,4096]{1,0:T(8,128)(2,1)}, u32[]{:S(2)}) copy-start(bf16[32,4096]{1,0:T(8,128)(2,1)} %param.10) | copy-start | bytes 786436
Sparse Core Ops, SparseCore 0:
  171.0 33.2 all-gather.4
  206.6 104.0 all-gather.2

commit v4 on v1

--- a/solution.py
+++ b/solution.py
@@ -102,21 +102,29 @@
         ),
     )
     dp_count = lax.axis_size("dp")
+    dp_index = lax.axis_index("dp")
     slot_total = rows_in.shape[0]
     piece = width // dp_count
-
-    def spread_columns(block):
-        return lax.all_to_all(
-            block.reshape(slot_total, dp_count, piece), "dp", split_axis=1, concat_axis=0, tiled=True
-        ).reshape(dp_count * slot_total, piece)
-
+    both_in = jnp.concatenate(
+        [rows_in.reshape(slot_total, dp_count, piece), grads_in.reshape(slot_total, dp_count, piece)], axis=2
+    )
+    pieces = [lax.dynamic_index_in_dim(both_in, dp_index, axis=1, keepdims=False)]
+    for shift in range(1, dp_count):
+        outgoing = lax.dynamic_index_in_dim(both_in, (dp_index + shift) % dp_count, axis=1, keepdims=False)
+        pieces.append(
+            lax.ppermute(outgoing, "dp", [(j, (j + shift) % dp_count) for j in range(dp_count)])
+        )
+    both_all = jnp.concatenate(pieces, axis=0)
+    source_order = (dp_index - jnp.arange(dp_count)) % dp_count
     joined_grads = jnp.concatenate([grad_gate_pre, grad_up_pre], axis=1)
-    rows_all = spread_columns(rows_in)
-    grads_all = spread_columns(grads_in)
-    joined_all = lax.all_gather(joined_grads, "dp", axis=0, tiled=True)
-    hidden_all = lax.all_gather(hidden, "dp", axis=0, tiled=True)
-    grad_joined = contract_first(rows_all, joined_all)
-    grad_down = contract_first(hidden_all, grads_all)
+    joined_all = jnp.take(
+        lax.all_gather(joined_grads, "dp", axis=0, tiled=False), source_order, axis=0
+    ).reshape(dp_count * slot_total, -1)
+    hidden_all = jnp.take(
+        lax.all_gather(hidden, "dp", axis=0, tiled=False), source_order, axis=0
+    ).reshape(dp_count * slot_total, -1)
+    grad_joined = contract_first(both_all[:, :piece], joined_all)
+    grad_down = contract_first(hidden_all, both_all[:, piece:])
     pair_out = back_out.reshape(-1, width)[pair_slot].reshape(local_tokens, top_count, width)
     pair_back = back_grad.reshape(-1, width)[pair_slot].reshape(local_tokens, top_count, width)
     output = jnp.sum(gate_values[:, :, None] * pair_out.astype(jnp.float32), axis=1).astype(

time: 394 us -> 409 us (1.038)
  local copies, waits for them, and re-layouts: 69.1 us -> 106 us
  waiting for transfers between devices: 196 us -> 177 us
  starting transfers between devices: 41.2 us -> 28.4 us
  other arithmetic: 13.6 us -> 24.3 us
    ppermute x0 -> x3, waiting for transfers between devices: none -> 67.2 us  [local(): lax.ppermute(outgoing, 'dp', [(j, (j + shift) % dp_count) for j in range(...]
    all_to_all x1, waiting for transfers between devices: 43.4 us -> 0.01 us  [local(): lax.all_to_all(pair_grad.reshape(flat_shape), ('outer', 'inner'), split_a...]
    all_to_all x1, waiting for transfers between devices: 45 us -> 17.2 us  [local(): lax.all_to_all(expert_out.reshape(flat_shape), ('outer', 'inner'), split_...]
    all_to_all x2 -> x0, waiting for transfers between devices: 24.3 us -> none  [spread_columns(): lax.all_to_all(block.reshape(slot_total, dp_count, piece), 'dp', split_ax...]
    dynamic_slice x0 -> x1, local copies, waits for them, and re-layouts: none -> 19.7 us  [local(): lax.dynamic_index_in_dim(both_in, dp_index, axis=1, keepdims=False)]
    all_to_all x2 -> x0, starting transfers between devices: 18.6 us -> none  [spread_columns(): lax.all_to_all(block.reshape(slot_total, dp_count, piece), 'dp', split_ax...]
    unnamed x20 -> x29, local copies, waits for them, and re-layouts: 0.88 us -> 11.5 us
    all_to_all x1, waiting for transfers between devices: 34.5 us -> 43.9 us  [local(): lax.all_to_all(send_rows.reshape(flat_shape), ('outer', 'inner'), split_a...]
  transfers between devices with their start and end apart: 8 -> 9, of which waited for: 6 -> 5; matrix products, arithmetic and copies ran while one was open for 27% -> 32% of each run, Pallas kernels for 0% -> 0%
where the time goes in v4:
time: 409 us; the launch traced here: 401 us
  waiting for transfers between devices  177 us (43%)
  local copies, waits for them, and re-layouts  106 us (26%)
  matrix products  50.8 us (12%)
  starting transfers between devices  28.4 us (7%)
  other arithmetic  24.3 us (6%)
  between operations  14.6 us (4%)
    ppermute x3, waiting for transfers between devices, local(): lax.ppermute(outgoing, 'dp', [(j, (j + shift) % dp_count) for j in range(...  67.2 us
    all_to_all x1, waiting for transfers between devices, local(): lax.all_to_all(send_grads.reshape(flat_shape), ('outer', 'inner'), split_...  48.5 us
    all_to_all x1, waiting for transfers between devices, local(): lax.all_to_all(send_rows.reshape(flat_shape), ('outer', 'inner'), split_a...  43.9 us
    dynamic_slice x1, local copies, waits for them, and re-layouts, local(): lax.dynamic_index_in_dim(both_in, dp_index, axis=1, keepdims=False)  19.7 us
    dot_general x3, matrix products, contract_last(): lax.dot_general(left, right, (((1,), (1,)), ((), ())), preferred_element_...  18.6 us
    all_to_all x1, waiting for transfers between devices, local(): lax.all_to_all(expert_out.reshape(flat_shape), ('outer', 'inner'), split_...  17.2 us
    unnamed x29, local copies, waits for them, and re-layouts  11.5 us
    dot_general x2, matrix products, contract_first(): lax.dot_general(left, right, (((0,), (0,)), ((), ())), preferred_element_...  11 us
  transfers between devices with their start and end apart: 9, of which 5 were waited for; matrix products, arithmetic and copies ran while one was open for 32% of the time, Pallas kernels for 0%

profile of v4, /device:TPU:8, one launch (start us, length us, event | category | flops | bytes accessed | tf_op | source)
XLA Modules:
  0.0 401.2 jit_solution(613315356057448808)
XLA Ops:
  22.4 6.6 %multiply_convert_fusion = bf16[32,12,4096]{2,1,0:T(8,128)(2,1)} fusion(f32[32,12,4096]{2,1,0:T(8,128)} %reshape.170, f32[32,12]{1,0:T(8,128)S(1)} %mul.67), kind=kLoop, calls=%fused_computation.8 | loop fusion | flops 3145728 | bytes 9438720 | tf_op jit(solution)/shard_map/convert_element_type | solution.py:65
  28.9 7.7 %all-to-all-start.2 = ((bf16[32,12,4096]{2,1,0:T(8,128)(2,1)}), bf16[32,12,4096]{2,1,0:T(8,128)(2,1)}, u32[]{:S(2)}, u32[]{:S(2)}) async-start(bf16[32,12,4096]{2,1,0:T(8,128)(2,1)} %multiply_convert_fusion), calls=%async_computation.2 | async-start | bytes 8388608 | tf_op jit(solution)/shard_map/all_to_all | solution.py:75
  42.7 48.5 %all-to-all-done.2 = bf16[32,12,4096]{2,1,0:T(8,128)(2,1)} async-done(((bf16[32,12,4096]{2,1,0:T(8,128)(2,1)}), bf16[32,12,4096]{2,1,0:T(8,128)(2,1)}, u32[]{:S(2)}, u32[]{:S(2)}) %all-to-all-start.2) | async-done | bytes 3145760 | tf_op jit(solution)/shard_map/all_to_all | solution.py:75
  91.2 4.8 %all-to-all-start = ((bf16[32,12,4096]{2,1,0:T(8,128)(2,1)}), bf16[32,12,4096]{2,1,0:T(8,128)(2,1)}, u32[]{:S(2)}, u32[]{:S(2)}) async-start(bf16[32,12,4096]{2,1,0:T(8,128)(2,1)} %reshape.160), calls=%async_computation | async-start | bytes 8388608 | tf_op jit(solution)/shard_map/all_to_all | solution.py:68
  100.3 6.4 %fusion = f32[384,768]{1,0:T(8,128)} fusion(bf16[384,4096]{1,0:T(8,128)(2,1)S(1)} %reshape.166, bf16[1,768,4096]{2,1,0:T(8,128)(2,1)} %param.13), kind=kOutput, calls=%fused_computation.10 | convolution fusion | flops 2415919104 | bytes 10616832 | tf_op jit(solution)/shard_map/dot_general | solution.py:8
  106.7 43.9 %all-to-all-done = bf16[32,12,4096]{2,1,0:T(8,128)(2,1)} async-done(((bf16[32,12,4096]{2,1,0:T(8,128)(2,1)}), bf16[32,12,4096]{2,1,0:T(8,128)(2,1)}, u32[]{:S(2)}, u32[]{:S(2)}) %all-to-all-start) | async-done | bytes 3145760 | tf_op jit(solution)/shard_map/all_to_all | solution.py:68
  154.6 5.5 %fusion.6 = f32[384,768]{1,0:T(8,128)S(1)} fusion(bf16[384,4096]{1,0:T(8,128)(2,1)S(1)} %reshape.161, bf16[1,4096,768]{2,1,0:T(8,128)(2,1)} %param.12), kind=kOutput, calls=%fused_computation.16 | convolution fusion | flops 2415919104 | bytes 10616832 | tf_op jit(solution)/shard_map/dot_general | solution.py:21
  160.1 7.0 %multiply_convert_fusion.2 = (bf16[384,768]{1,0:T(8,128)(2,1)}, bf16[384,768]{1,0:T(8,128)(2,1)}, bf16[384,768]{1,0:T(8,128)(2,1)}) fusion(f32[384,768]{1,0:T(8,128)S(1)} %copy-done.8, f32[384,768]{1,0:T(8,128)S(1)} %fusion.6, bf16[384,4096]{1,0:T(8,128)(2,1)S(1)} %reshape.161, bf16[1,4096,768]{2,1,0:T(8,128)(2,1)} %param.11), kind=kOutput, calls=%fused_computation.44 | convolution fusion | flops 2420342784 | bytes 13565952 | tf_op jit(solution)/shard_map/dot_general | solution.py:20
  167.0 5.6 %fusion.14 = bf16[384,4096]{1,0:T(8,128)(2,1)S(1)} fusion(bf16[384,768]{1,0:T(8,128)(2,1)} %get-tuple-element.14, bf16[1,768,4096]{2,1,0:T(8,128)(2,1)} %param.13), kind=kOutput, calls=%fused_computation.23 | convolution fusion | flops 2417491968 | bytes 10027008 | tf_op jit(solution)/shard_map/dot_general | solution.py:25
  175.4 5.0 %all-to-all-start.1 = ((bf16[32,12,4096]{2,1,0:T(8,128)(2,1)}), bf16[32,12,4096]{2,1,0:T(8,128)(2,1)}, u32[]{:S(2)}, u32[]{:S(2)}) async-start(bf16[32,12,4096]{2,1,0:T(8,128)(2,1)} %reshape.162), calls=%async_computation.1 | async-start | bytes 8388608 | tf_op jit(solution)/shard_map/all_to_all | solution.py:89
  182.0 4.8 %fusion.4 = f32[384,4096]{1,0:T(8,128)S(1)} fusion(bf16[384,768]{1,0:T(8,128)(2,1)S(1)} %copy-done.4, bf16[1,4096,768]{2,1,0:T(8,128)(2,1)} %param.12), kind=kOutput, calls=%fused_computation.14 | convolution fusion | flops 2415919104 | bytes 13172736 | tf_op jit(solution)/shard_map/dot_general | solution.py:8
  186.8 7.3 %add_convert_fusion = bf16[384,4096]{1,0:T(8,128)(2,1)S(1)} fusion(f32[384,4096]{1,0:T(8,128)S(1)} %fusion.4, bf16[384,768]{1,0:T(8,128)(2,1)S(1)} %copy-done.3, bf16[1,4096,768]{2,1,0:T(8,128)(2,1)} %param.11), kind=kOutput, calls=%fused_computation.22 | convolution fusion | flops 2419064832 | bytes 16318464 | tf_op jit(solution)/shard_map/dot_general | solution.py:8
  196.9 6.9 %reshape_reshape.6 = bf16[384,4,1024]{2,1,0:T(4,128)(2,1)S(1)} reshape(bf16[32,12,4096]{2,1,0:T(8,128)(2,1)} %all-to-all-done) | data formatting | bytes 6291456 | tf_op jit(solution)/shard_map/reshape;reshape | solution.py:109
  203.8 8.2 %reshape_reshape.7 = bf16[384,4,1024]{2,1,0:T(4,128)(2,1)} reshape(bf16[32,12,4096]{2,1,0:T(8,128)(2,1)} %all-to-all-done.2) | data formatting | bytes 6291456 | tf_op jit(solution)/shard_map/reshape;reshape | solution.py:109
  217.7 17.2 %all-to-all-done.1 = bf16[32,12,4096]{2,1,0:T(8,128)(2,1)} async-done(((bf16[32,12,4096]{2,1,0:T(8,128)(2,1)}), bf16[32,12,4096]{2,1,0:T(8,128)(2,1)}, u32[]{:S(2)}, u32[]{:S(2)}) %all-to-all-start.1) | async-done | bytes 3145760 | tf_op jit(solution)/shard_map/all_to_all | solution.py:89
  234.9 4.9 %all-to-all-start.3 = ((bf16[32,12,4096]{2,1,0:T(8,128)(2,1)}), bf16[32,12,4096]{2,1,0:T(8,128)(2,1)}, u32[]{:S(2)}, u32[]{:S(2)}) async-start(bf16[32,12,4096]{2,1,0:T(8,128)(2,1)} %reshape.167), calls=%async_computation.3 | async-start | bytes 8388608 | tf_op jit(solution)/shard_map/all_to_all | solution.py:96
  239.7 19.7 %constant_dynamic-slice_fusion.3 = (bf16[384,1,2048]{2,1,0:T(2,128)(2,1)S(1)}, bf16[384,1,2048]{2,1,0:T(2,128)(2,1)S(1)}, bf16[384,1,2048]{2,1,0:T(2,128)(2,1)S(1)}, bf16[384,1,2048]{2,1,0:T(2,128)(2,1)S(1)}) fusion(bf16[384,4,2048]{2,1,0:T(4,128)(2,1)} %constant_dynamic-update-slice_fusion, s32[]{:T(128)S(6)} %select_n.106, s32[]{:T(128)S(6)} %select_n.112, ...), kind=kLoop, calls=%fused_computation.89 | loop fusion | bytes 12582928 | tf_op jit(solution)/shard_map/jit(dynamic_index_in_dim)/dynamic_slice | solution.py:111
  261.5 4.0 %collective-permute-start.2 = (bf16[384,2048]{1,0:T(8,128)(2,1)}, bf16[384,2048]{1,0:T(8,128)(2,1)}, u32[]{:S(2)}, u32[]{:S(2)}) collective-permute-start(bf16[384,2048]{1,0:T(8,128)(2,1)} %bitcast.80), channel_id=1, source_target_pairs={{0,96},{32,0},{64,32},{96,64},{1,97},{33,1},{65,33},{97,65},{2,98}... | collective-permute-start | bytes 4718600 | tf_op jit(solution)/shard_map/ppermute | solution.py:115
  272.1 61.5 %collective-permute-done.2 = bf16[384,2048]{1,0:T(8,128)(2,1)} collective-permute-done((bf16[384,2048]{1,0:T(8,128)(2,1)}, bf16[384,2048]{1,0:T(8,128)(2,1)}, u32[]{:S(2)}, u32[]{:S(2)}) %collective-permute-start.2) | collective-permute-done | bytes 1572896 | tf_op jit(solution)/shard_map/ppermute | solution.py:115
  333.6 5.8 %collective-permute-done = bf16[384,2048]{1,0:T(8,128)(2,1)} collective-permute-done((bf16[384,2048]{1,0:T(8,128)(2,1)}, bf16[384,2048]{1,0:T(8,128)(2,1)}, u32[]{:S(2)}, u32[]{:S(2)}) %collective-permute-start) | collective-permute-done | bytes 1572896 | tf_op jit(solution)/shard_map/ppermute | solution.py:115
  339.3 5.7 %pad_maximum_fusion = bf16[1536,2048]{1,0:T(8,128)(2,1)} fusion(bf16[384,2048]{1,0:T(8,128)(2,1)} %collective-permute-done.2, bf16[384,2048]{1,0:T(8,128)(2,1)} %collective-permute-done.1, bf16[384,2048]{1,0:T(8,128)(2,1)} %collective-permute-done, bf16[384,2048]{1,0:T(8,128)(2,1)S(1)} %bitcast.86), kind=kLoop, calls=%fused_computation.9 | loop fusion | flops 25165824 | bytes 12582912 | tf_op jit(solution)/shard_map/concatenate | solution.py:117
  372.1 5.7 %fusion.25 = bf16[1,768,1024]{2,1,0:T(8,128)(2,1)} fusion(bf16[1536,768]{1,0:T(8,128)(2,1)S(1)} %bitcast_select_fusion.1, bf16[1536,2048]{1,0:T(8,128)(2,1)} %pad_maximum_fusion), kind=kOutput, calls=%fused_computation.41 | convolution fusion | flops 2416705536 | bytes 7077888 | tf_op jit(solution)/shard_map/dot_general | solution.py:14
  377.8 5.5 %gather_fusion.5 = bf16[4,384,1536]{2,1,0:T(8,128)(2,1)} fusion(bf16[4,384,1536]{2,1,0:T(8,128)(2,1)} %bitcast.87, s32[1024]{0:T(1024)S(1)} %pad_clamp_fusion), kind=kCustom, calls=%fused_computation.5 | custom fusion | bytes 9437200 | tf_op jit(solution)/shard_map/jit(_take)/gather | solution.py:120
  386.9 5.3 %convolution_convert_fusion = bf16[1024,1536]{1,0:T(8,128)(2,1)S(1)} fusion(bf16[1536,1536]{1,0:T(8,128)(2,1)S(1)} %bitcast_select_fusion, bf16[1536,2048]{1,0:T(8,128)(2,1)S(1)} %bitcast.85), kind=kOutput, calls=%fused_computation.26 | convolution fusion | flops 4833411072 | bytes 11010048 | tf_op jit(solution)/shard_map/dot_general | solution.py:14
  (90 shorter events, 83.1 us)
Async XLA Ops:
  15.6 3.6 copy-start.7
  28.9 7.7 %copy-start.5 = (bf16[32,4096]{1,0:T(8,128)(2,1)S(1)}, bf16[32,4096]{1,0:T(8,128)(2,1)}, u32[]{:S(2)}) copy-start(bf16[32,4096]{1,0:T(8,128)(2,1)} %param.7) | copy-start | bytes 786436
  28.9 62.3 %all-to-all-start.2 = ((bf16[32,12,4096]{2,1,0:T(8,128)(2,1)}), bf16[32,12,4096]{2,1,0:T(8,128)(2,1)}, u32[]{:S(2)}, u32[]{:S(2)}) async-start(bf16[32,12,4096]{2,1,0:T(8,128)(2,1)} %multiply_convert_fusion), calls=%async_computation.2 | async-start | bytes 8388608 | tf_op jit(solution)/shard_map/all_to_all | solution.py:75
  91.2 59.4 %all-to-all-start = ((bf16[32,12,4096]{2,1,0:T(8,128)(2,1)}), bf16[32,12,4096]{2,1,0:T(8,128)(2,1)}, u32[]{:S(2)}, u32[]{:S(2)}) async-start(bf16[32,12,4096]{2,1,0:T(8,128)(2,1)} %reshape.160), calls=%async_computation | async-start | bytes 8388608 | tf_op jit(solution)/shard_map/all_to_all | solution.py:68
  96.0 273.3 %all-gather.7.cloned.1.call-start = ((), (), s32[]{:S(2)}) async-start(), calls=%async_computation.5 | async-start | bytes 2949120 | tf_op jit(solution)/shard_map/all_gather | solution.py:124
  154.6 5.5 %copy-start.8 = (f32[384,768]{1,0:T(8,128)S(1)}, f32[384,768]{1,0:T(8,128)}, u32[]{:S(2)}) copy-start(f32[384,768]{1,0:T(8,128)} %fusion) | copy-start | bytes 3538948
  175.3 5.5 %copy-start.2 = (bf16[384,768]{1,0:T(8,128)(2,1)S(1)}, bf16[384,768]{1,0:T(8,128)(2,1)}, u32[]{:S(2)}) copy-start(bf16[384,768]{1,0:T(8,128)(2,1)} %get-tuple-element.12) | copy-start | bytes 1769476
  175.4 5.5 %copy-start.4 = (bf16[384,768]{1,0:T(8,128)(2,1)S(1)}, bf16[384,768]{1,0:T(8,128)(2,1)}, u32[]{:S(2)}) copy-start(bf16[384,768]{1,0:T(8,128)(2,1)} %get-tuple-element.13) | copy-start | bytes 1769476
  175.4 59.5 %all-to-all-start.1 = ((bf16[32,12,4096]{2,1,0:T(8,128)(2,1)}), bf16[32,12,4096]{2,1,0:T(8,128)(2,1)}, u32[]{:S(2)}, u32[]{:S(2)}) async-start(bf16[32,12,4096]{2,1,0:T(8,128)(2,1)} %reshape.162), calls=%async_computation.1 | async-start | bytes 8388608 | tf_op jit(solution)/shard_map/all_to_all | solution.py:89
  180.3 197.4 %all-gather.5.cloned.1.call-start = ((), (), s32[]{:S(2)}) async-start(), calls=%async_computation.4 | async-start | bytes 5898240 | tf_op jit(solution)/shard_map/all_gather | solution.py:121
  182.0 4.8 %copy-start.3 = (bf16[384,768]{1,0:T(8,128)(2,1)S(1)}, bf16[384,768]{1,0:T(8,128)(2,1)}, u32[]{:S(2)}) copy-start(bf16[384,768]{1,0:T(8,128)(2,1)} %get-tuple-element.12) | copy-start | bytes 1769476
  212.0 2.8 copy-start
  234.9 117.4 %all-to-all-start.3 = ((bf16[32,12,4096]{2,1,0:T(8,128)(2,1)}), bf16[32,12,4096]{2,1,0:T(8,128)(2,1)}, u32[]{:S(2)}, u32[]{:S(2)}) async-start(bf16[32,12,4096]{2,1,0:T(8,128)(2,1)} %reshape.167), calls=%async_computation.3 | async-start | bytes 8388608 | tf_op jit(solution)/shard_map/all_to_all | solution.py:96
  261.5 72.0 %collective-permute-start.2 = (bf16[384,2048]{1,0:T(8,128)(2,1)}, bf16[384,2048]{1,0:T(8,128)(2,1)}, u32[]{:S(2)}, u32[]{:S(2)}) collective-permute-start(bf16[384,2048]{1,0:T(8,128)(2,1)} %bitcast.80), channel_id=1, source_target_pairs={{0,96},{32,0},{64,32},{96,64},{1,97},{33,1},{65,33},{97,65},{2,98}... | collective-permute-start | bytes 4718600 | tf_op jit(solution)/shard_map/ppermute | solution.py:115
  267.7 65.9 %collective-permute-start.1 = (bf16[384,2048]{1,0:T(8,128)(2,1)}, bf16[384,2048]{1,0:T(8,128)(2,1)}, u32[]{:S(2)}, u32[]{:S(2)}) collective-permute-start(bf16[384,2048]{1,0:T(8,128)(2,1)} %bitcast.81), channel_id=1, source_target_pairs={{0,64},{32,96},{64,0},{96,32},{1,65},{33,97},{65,1},{97,33},{2,66}... | collective-permute-start | bytes 4718600 | tf_op jit(solution)/shard_map/ppermute | solution.py:115
  269.7 69.6 %collective-permute-start = (bf16[384,2048]{1,0:T(8,128)(2,1)}, bf16[384,2048]{1,0:T(8,128)(2,1)}, u32[]{:S(2)}, u32[]{:S(2)}) collective-permute-start(bf16[384,2048]{1,0:T(8,128)(2,1)} %bitcast.82), channel_id=1, source_target_pairs={{0,32},{32,64},{64,96},{96,0},{1,33},{33,65},{65,97},{97,1},{2,34}... | collective-permute-start | bytes 4718600 | tf_op jit(solution)/shard_map/ppermute | solution.py:115
  356.2 3.2 copy-start.6
  359.4 7.6 %copy-start.1 = (bf16[256,4096]{1,0:T(8,128)(2,1)S(1)}, bf16[256,4096]{1,0:T(8,128)(2,1)}, u32[]{:S(2)}) copy-start(bf16[256,4096]{1,0:T(8,128)(2,1)} %gather_fusion.1) | copy-start | bytes 6291460
  377.8 8.5 %slice-start = ((s8[6291456]{0:T(1024)(128)(4,1)}), s8[2097152]{0:T(1024)(128)(4,1)S(1)}, s32[]{:S(2)}) async-start(s8[6291456]{0:T(1024)(128)(4,1)} %bitcast.84), calls=%async_computation.6 | async-start | bytes 4194304
  383.3 3.6 slice-start.1
Sparse Core Ops, SparseCore 0:
  167.2 32.7 all-gather.6
  201.6 52.7 all-gather.4

commit v5 on v0

--- a/solution.py
+++ b/solution.py
@@ -101,14 +101,17 @@
             tiled=True,
         ),
     )
+    dp_count = lax.axis_size("dp")
+    piece = width // dp_count
+    column_pieces = jnp.stack(
+        [rows_in[:, part * piece:(part + 1) * piece] for part in range(dp_count)], axis=0
+    )
+    rows_all = lax.all_to_all(column_pieces, "dp", split_axis=0, concat_axis=0, tiled=True)
     joined_grads = jnp.concatenate([grad_gate_pre, grad_up_pre], axis=1)
-    columns = rows_in
-    grad_joined = lax.psum_scatter(
-        contract_first(columns, joined_grads).astype(jnp.bfloat16),
-        "dp",
-        scatter_dimension=0,
-        tiled=True,
-    ).astype(jnp.float32)
+    joined_all = lax.all_gather(joined_grads, "dp", axis=0, tiled=False)
+    grad_joined = lax.dot_general(
+        rows_all, joined_all, (((0, 1), (0, 1)), ((), ())), preferred_element_type=jnp.float32
+    )
     columns = grads_in
     grad_down = (
         lax.psum_scatter(

time: 358 us -> 379 us (1.059)
  local copies, waits for them, and re-layouts: 56.8 us -> 65.6 us
  starting transfers between devices: 23.4 us -> 28 us
    reduce_scatter x1 -> x0, waiting for transfers between devices: 26.2 us -> none  [local(): lax.psum_scatter(contract_first(columns, joined_grads).astype(jnp.bfloat1...]
    all_to_all x0 -> x1, waiting for transfers between devices: none -> 15.4 us  [local(): lax.all_to_all(column_pieces, 'dp', split_axis=0, concat_axis=0, tiled=True)]
    dot_general x2 -> x1, matrix products: 16.3 us -> 8.15 us  [contract_first(): lax.dot_general(left, right, (((0,), (0,)), ((), ())), preferred_element_...]
    dot_general x0 -> x1, matrix products: none -> 7.84 us  [local(): lax.dot_general(rows_all, joined_all, (((0, 1), (0, 1)), ((), ())), prefe...]
    all_to_all x1, waiting for transfers between devices: 39.5 us -> 45.1 us  [local(): lax.all_to_all(expert_out.reshape(flat_shape), ('outer', 'inner'), split_...]
    all_to_all x0 -> x1, starting transfers between devices: none -> 5.29 us  [local(): lax.all_to_all(column_pieces, 'dp', split_axis=0, concat_axis=0, tiled=True)]
    unnamed x21 -> x31, local copies, waits for them, and re-layouts: 4.26 us -> 9.1 us
    all_to_all x1, waiting for transfers between devices: 37.9 us -> 42.7 us  [local(): lax.all_to_all(send_rows.reshape(flat_shape), ('outer', 'inner'), split_a...]
  transfers between devices with their start and end apart: 6 -> 7, of which waited for: 5 -> 5; matrix products, arithmetic and copies ran while one was open for 25% -> 26% of each run, Pallas kernels for 0% -> 0%
where the time goes in v5:
time: 379 us; the launch traced here: 378 us
  waiting for transfers between devices  194 us (51%)
  local copies, waits for them, and re-layouts  65.6 us (17%)
  matrix products  59.9 us (16%)
  starting transfers between devices  28 us (7%)
  other arithmetic  16.5 us (4%)
  between operations  14.3 us (4%)
    all_to_all x1, waiting for transfers between devices, local(): lax.all_to_all(send_grads.reshape(flat_shape), ('outer', 'inner'), split_...  48.5 us
    all_to_all x1, waiting for transfers between devices, local(): lax.all_to_all(expert_out.reshape(flat_shape), ('outer', 'inner'), split_...  45.1 us
    all_to_all x1, waiting for transfers between devices, local(): lax.all_to_all(send_rows.reshape(flat_shape), ('outer', 'inner'), split_a...  42.7 us
    all_to_all x1, waiting for transfers between devices, local(): lax.all_to_all(pair_grad.reshape(flat_shape), ('outer', 'inner'), split_a...  41.7 us
    dot_general x3, matrix products, contract_last(): lax.dot_general(left, right, (((1,), (1,)), ((), ())), preferred_element_...  21.3 us
    all_to_all x1, waiting for transfers between devices, local(): lax.all_to_all(column_pieces, 'dp', split_axis=0, concat_axis=0, tiled=True)  15.4 us
    unnamed x31, local copies, waits for them, and re-layouts  9.1 us
    dot_general x1, matrix products, contract_first(): lax.dot_general(left, right, (((0,), (0,)), ((), ())), preferred_element_...  8.15 us
  transfers between devices with their start and end apart: 7, of which 5 were waited for; matrix products, arithmetic and copies ran while one was open for 26% of the time, Pallas kernels for 0%

profile of v5, /device:TPU:8, one launch (start us, length us, event | category | flops | bytes accessed | tf_op | source)
XLA Modules:
  0.0 377.7 jit_solution(11054077749244219025)
XLA Ops:
  22.4 6.5 %multiply_convert_fusion = bf16[32,12,4096]{2,1,0:T(8,128)(2,1)} fusion(f32[32,12,4096]{2,1,0:T(8,128)} %reshape.110, f32[32,12]{1,0:T(8,128)S(1)} %mul.67), kind=kLoop, calls=%fused_computation.6 | loop fusion | flops 3145728 | bytes 9438720 | tf_op jit(solution)/shard_map/convert_element_type | solution.py:65
  28.9 7.7 %all-to-all-start.2 = ((bf16[32,12,4096]{2,1,0:T(8,128)(2,1)}), bf16[32,12,4096]{2,1,0:T(8,128)(2,1)}, u32[]{:S(2)}, u32[]{:S(2)}) async-start(bf16[32,12,4096]{2,1,0:T(8,128)(2,1)} %multiply_convert_fusion), calls=%async_computation.2 | async-start | bytes 8388608 | tf_op jit(solution)/shard_map/all_to_all | solution.py:75
  42.7 48.5 %all-to-all-done.2 = bf16[32,12,4096]{2,1,0:T(8,128)(2,1)} async-done(((bf16[32,12,4096]{2,1,0:T(8,128)(2,1)}), bf16[32,12,4096]{2,1,0:T(8,128)(2,1)}, u32[]{:S(2)}, u32[]{:S(2)}) %all-to-all-start.2) | async-done | bytes 3145760 | tf_op jit(solution)/shard_map/all_to_all | solution.py:75
  91.2 4.8 %all-to-all-start = ((bf16[32,12,4096]{2,1,0:T(8,128)(2,1)}), bf16[32,12,4096]{2,1,0:T(8,128)(2,1)}, u32[]{:S(2)}, u32[]{:S(2)}) async-start(bf16[32,12,4096]{2,1,0:T(8,128)(2,1)} %reshape.100), calls=%async_computation | async-start | bytes 8388608 | tf_op jit(solution)/shard_map/all_to_all | solution.py:68
  96.2 4.0 %reshape.106 = bf16[384,4096]{1,0:T(8,128)(2,1)S(1)} reshape(bf16[32,12,4096]{2,1,0:T(8,128)(2,1)} %all-to-all-done.2) | data formatting | bytes 6291456 | tf_op jit(solution)/shard_map/reshape | solution.py:84
  100.2 7.6 %fusion = f32[384,768]{1,0:T(8,128)} fusion(bf16[384,4096]{1,0:T(8,128)(2,1)S(1)} %reshape.106, bf16[1,768,4096]{2,1,0:T(8,128)(2,1)} %param.13), kind=kOutput, calls=%fused_computation.9 | convolution fusion | flops 2415919104 | bytes 10616832 | tf_op jit(solution)/shard_map/dot_general | solution.py:8
  107.8 42.7 %all-to-all-done = bf16[32,12,4096]{2,1,0:T(8,128)(2,1)} async-done(((bf16[32,12,4096]{2,1,0:T(8,128)(2,1)}), bf16[32,12,4096]{2,1,0:T(8,128)(2,1)}, u32[]{:S(2)}, u32[]{:S(2)}) %all-to-all-start) | async-done | bytes 3145760 | tf_op jit(solution)/shard_map/all_to_all | solution.py:68
  150.5 4.0 %reshape.101 = bf16[384,4096]{1,0:T(8,128)(2,1)S(1)} reshape(bf16[32,12,4096]{2,1,0:T(8,128)(2,1)} %all-to-all-done) | data formatting | bytes 6291456 | tf_op jit(solution)/shard_map/reshape | solution.py:83
  154.5 5.5 %fusion.6 = f32[384,768]{1,0:T(8,128)S(1)} fusion(bf16[384,4096]{1,0:T(8,128)(2,1)S(1)} %reshape.101, bf16[1,4096,768]{2,1,0:T(8,128)(2,1)} %param.12), kind=kOutput, calls=%fused_computation.15 | convolution fusion | flops 2415919104 | bytes 10616832 | tf_op jit(solution)/shard_map/dot_general | solution.py:21
  160.0 6.6 %multiply_convert_fusion.2 = (bf16[384,768]{1,0:T(8,128)(2,1)S(1)}, bf16[384,768]{1,0:T(8,128)(2,1)S(1)}, bf16[384,768]{1,0:T(8,128)(2,1)}) fusion(f32[384,768]{1,0:T(8,128)S(1)} %copy-done.11, f32[384,768]{1,0:T(8,128)S(1)} %fusion.6, bf16[384,4096]{1,0:T(8,128)(2,1)S(1)} %reshape.101, bf16[1,4096,768]{2,1,0:T(8,128)(2,1)} %param.11), kind=kOutput, calls=%fused_computation.32 | convolution fusion | flops 2420342784 | bytes 13565952 | tf_op jit(solution)/shard_map/dot_general | solution.py:20
  169.0 8.2 %convolution_convert_fusion = bf16[4096,768]{1,0:T(8,128)(2,1)} fusion(bf16[384,4096]{1,0:T(8,128)(2,1)} %copy-done.2, bf16[384,768]{1,0:T(8,128)(2,1)} %get-tuple-element.26), kind=kOutput, calls=%fused_computation.7 | convolution fusion | flops 2419064832 | bytes 10027008 | tf_op jit(solution)/shard_map/dot_general | solution.py:14
  177.2 5.4 %fusion.4 = f32[384,4096]{1,0:T(8,128)S(1)} fusion(bf16[384,768]{1,0:T(8,128)(2,1)} %copy-done.7, bf16[1,4096,768]{2,1,0:T(8,128)(2,1)} %param.12), kind=kOutput, calls=%fused_computation.13 | convolution fusion | flops 2415919104 | bytes 13172736 | tf_op jit(solution)/shard_map/dot_general | solution.py:8
  182.6 8.4 %add_convert_fusion = bf16[384,4096]{1,0:T(8,128)(2,1)} fusion(f32[384,4096]{1,0:T(8,128)S(1)} %fusion.4, bf16[384,768]{1,0:T(8,128)(2,1)S(1)} %copy-done.6, bf16[1,4096,768]{2,1,0:T(8,128)(2,1)} %param.11), kind=kOutput, calls=%fused_computation.21 | convolution fusion | flops 2419064832 | bytes 16318464 | tf_op jit(solution)/shard_map/dot_general | solution.py:8
  191.0 5.5 %reshape.107 = bf16[32,12,4096]{2,1,0:T(8,128)(2,1)} reshape(bf16[384,4096]{1,0:T(8,128)(2,1)} %add_convert_fusion) | data formatting | bytes 6291456 | tf_op jit(solution)/shard_map/reshape | solution.py:97
  196.5 4.8 %all-to-all-start.3 = ((bf16[32,12,4096]{2,1,0:T(8,128)(2,1)}), bf16[32,12,4096]{2,1,0:T(8,128)(2,1)}, u32[]{:S(2)}, u32[]{:S(2)}) async-start(bf16[32,12,4096]{2,1,0:T(8,128)(2,1)} %reshape.107), calls=%async_computation.3 | async-start | bytes 8388608 | tf_op jit(solution)/shard_map/all_to_all | solution.py:96
  201.2 7.3 %fusion.14 = bf16[384,4096]{1,0:T(8,128)(2,1)} fusion(bf16[384,768]{1,0:T(8,128)(2,1)} %get-tuple-element.26, bf16[1,768,4096]{2,1,0:T(8,128)(2,1)} %param.13), kind=kOutput, calls=%fused_computation.22 | convolution fusion | flops 2417491968 | bytes 10027008 | tf_op jit(solution)/shard_map/dot_general | solution.py:25
  208.6 5.5 %reshape.102 = bf16[32,12,4096]{2,1,0:T(8,128)(2,1)} reshape(bf16[384,4096]{1,0:T(8,128)(2,1)} %fusion.14) | data formatting | bytes 6291456 | tf_op jit(solution)/shard_map/reshape | solution.py:90
  214.1 41.7 %all-to-all-done.3 = bf16[32,12,4096]{2,1,0:T(8,128)(2,1)} async-done(((bf16[32,12,4096]{2,1,0:T(8,128)(2,1)}), bf16[32,12,4096]{2,1,0:T(8,128)(2,1)}, u32[]{:S(2)}, u32[]{:S(2)}) %all-to-all-start.3) | async-done | bytes 3145760 | tf_op jit(solution)/shard_map/all_to_all | solution.py:96
  255.8 4.9 %all-to-all-start.1 = ((bf16[32,12,4096]{2,1,0:T(8,128)(2,1)}), bf16[32,12,4096]{2,1,0:T(8,128)(2,1)}, u32[]{:S(2)}, u32[]{:S(2)}) async-start(bf16[32,12,4096]{2,1,0:T(8,128)(2,1)} %reshape.102), calls=%async_computation.1 | async-start | bytes 8388608 | tf_op jit(solution)/shard_map/all_to_all | solution.py:89
  270.0 45.1 %all-to-all-done.1 = bf16[32,12,4096]{2,1,0:T(8,128)(2,1)} async-done(((bf16[32,12,4096]{2,1,0:T(8,128)(2,1)}), bf16[32,12,4096]{2,1,0:T(8,128)(2,1)}, u32[]{:S(2)}, u32[]{:S(2)}) %all-to-all-start.1) | async-done | bytes 3145760 | tf_op jit(solution)/shard_map/all_to_all | solution.py:89
  315.2 5.3 %all-to-all-start.4 = ((bf16[4,384,1024]{1,2,0:T(8,128)(2,1)}), bf16[4,384,1024]{1,2,0:T(8,128)(2,1)}, u32[]{:S(2)}, u32[]{:S(2)}) async-start(bf16[4,384,1024]{1,2,0:T(8,128)(2,1)} %pad_maximum_fusion), calls=%async_computation.4 | async-start | bytes 6291456 | tf_op jit(solution)/shard_map/all_to_all | solution.py:109
  320.5 4.0 %reshape.108 = bf16[384,4096]{1,0:T(8,128)(2,1)S(1)} reshape(bf16[32,12,4096]{2,1,0:T(8,128)(2,1)} %all-to-all-done.3) | data formatting | bytes 6291456 | tf_op jit(solution)/shard_map/reshape | solution.py:127
  343.2 15.4 %all-to-all-done.4 = bf16[4,384,1024]{1,2,0:T(8,128)(2,1)} async-done(((bf16[4,384,1024]{1,2,0:T(8,128)(2,1)}), bf16[4,384,1024]{1,2,0:T(8,128)(2,1)}, u32[]{:S(2)}, u32[]{:S(2)}) %all-to-all-start.4) | async-done | bytes 3145760 | tf_op jit(solution)/shard_map/all_to_all | solution.py:109
  358.6 7.8 %bitcast_convert_fusion = bf16[1024,1536]{1,0:T(8,128)(2,1)S(1)} fusion(bf16[4,384,1024]{1,2,0:T(8,128)(2,1)} %all-to-all-done.4, bf16[4,384,1536]{2,1,0:T(8,128)(2,1)} %bitcast.84), kind=kOutput, calls=%fused_computation.8 | convolution fusion | flops 4833411072 | bytes 11010048 | tf_op jit(solution)/shard_map/dot_general | solution.py:112
  (75 shorter events, 56.3 us)
Async XLA Ops:
  15.6 3.6 copy-start.10
  28.9 7.7 %copy-start.8 = (bf16[32,4096]{1,0:T(8,128)(2,1)S(1)}, bf16[32,4096]{1,0:T(8,128)(2,1)}, u32[]{:S(2)}) copy-start(bf16[32,4096]{1,0:T(8,128)(2,1)} %param.7) | copy-start | bytes 786436
  28.9 62.3 %all-to-all-start.2 = ((bf16[32,12,4096]{2,1,0:T(8,128)(2,1)}), bf16[32,12,4096]{2,1,0:T(8,128)(2,1)}, u32[]{:S(2)}, u32[]{:S(2)}) async-start(bf16[32,12,4096]{2,1,0:T(8,128)(2,1)} %multiply_convert_fusion), calls=%async_computation.2 | async-start | bytes 8388608 | tf_op jit(solution)/shard_map/all_to_all | solution.py:75
  91.2 59.4 %all-to-all-start = ((bf16[32,12,4096]{2,1,0:T(8,128)(2,1)}), bf16[32,12,4096]{2,1,0:T(8,128)(2,1)}, u32[]{:S(2)}, u32[]{:S(2)}) async-start(bf16[32,12,4096]{2,1,0:T(8,128)(2,1)} %reshape.100), calls=%async_computation | async-start | bytes 8388608 | tf_op jit(solution)/shard_map/all_to_all | solution.py:68
  96.0 262.6 %all-gather.3.cloned.1.call-start = ((), (), s32[]{:S(2)}) async-start(), calls=%async_computation.7 | async-start | bytes 5898240 | tf_op jit(solution)/shard_map/all_gather | solution.py:111
  100.2 7.6 %copy-start.2 = (bf16[384,4096]{1,0:T(8,128)(2,1)}, bf16[384,4096]{1,0:T(8,128)(2,1)S(1)}, u32[]{:S(2)}) copy-start(bf16[384,4096]{1,0:T(8,128)(2,1)S(1)} %reshape.106) | copy-start | bytes 9437188
  154.5 5.5 %copy-start.11 = (f32[384,768]{1,0:T(8,128)S(1)}, f32[384,768]{1,0:T(8,128)}, u32[]{:S(2)}) copy-start(f32[384,768]{1,0:T(8,128)} %fusion) | copy-start | bytes 3538948
  166.6 0.8 copy-start.5
  166.6 1.0 copy-start.7
  168.7 199.6 %reduce-scatter.2.cloned.1.call-start = ((), (), s32[]{:S(2)}) async-start(), calls=%async_computation.6 | async-start | bytes 7864320 | tf_op jit(solution)/shard_map/reduce_scatter | solution.py:117
  177.2 5.4 %copy-start.6 = (bf16[384,768]{1,0:T(8,128)(2,1)S(1)}, bf16[384,768]{1,0:T(8,128)(2,1)}, u32[]{:S(2)}) copy-start(bf16[384,768]{1,0:T(8,128)(2,1)} %copy-done.5) | copy-start | bytes 1769476
  196.5 59.3 %all-to-all-start.3 = ((bf16[32,12,4096]{2,1,0:T(8,128)(2,1)}), bf16[32,12,4096]{2,1,0:T(8,128)(2,1)}, u32[]{:S(2)}, u32[]{:S(2)}) async-start(bf16[32,12,4096]{2,1,0:T(8,128)(2,1)} %reshape.107), calls=%async_computation.3 | async-start | bytes 8388608 | tf_op jit(solution)/shard_map/all_to_all | solution.py:96
  255.8 59.4 %all-to-all-start.1 = ((bf16[32,12,4096]{2,1,0:T(8,128)(2,1)}), bf16[32,12,4096]{2,1,0:T(8,128)(2,1)}, u32[]{:S(2)}, u32[]{:S(2)}) async-start(bf16[32,12,4096]{2,1,0:T(8,128)(2,1)} %reshape.102), calls=%async_computation.1 | async-start | bytes 8388608 | tf_op jit(solution)/shard_map/all_to_all | solution.py:89
  262.4 3.1 copy-start.4
  262.4 4.3 %copy-start.3 = (bf16[384,1024]{1,0:T(8,128)(2,1)S(1)}, bf16[384,1024]{1,0:T(8,128)(2,1)}, u32[]{:S(2)}) copy-start(bf16[384,1024]{1,0:T(8,128)(2,1)} %get-tuple-element.23) | copy-start | bytes 2359300
  315.2 43.4 %all-to-all-start.4 = ((bf16[4,384,1024]{1,2,0:T(8,128)(2,1)}), bf16[4,384,1024]{1,2,0:T(8,128)(2,1)}, u32[]{:S(2)}, u32[]{:S(2)}) async-start(bf16[4,384,1024]{1,2,0:T(8,128)(2,1)} %pad_maximum_fusion), calls=%async_computation.4 | async-start | bytes 6291456 | tf_op jit(solution)/shard_map/all_to_all | solution.py:109
  331.7 3.2 copy-start.9
  334.8 3.9 %copy-start = (bf16[256,4096]{1,0:T(8,128)(2,1)S(1)}, bf16[256,4096]{1,0:T(8,128)(2,1)}, u32[]{:S(2)}) copy-start(bf16[256,4096]{1,0:T(8,128)(2,1)} %gather_fusion.4) | copy-start | bytes 6291460
  338.7 2.1 copy-start.1
Sparse Core Ops, SparseCore 0:
  168.8 52.3 all-gather.2
  223.7 64.4 reduce-scatter.1

commit v6 on v5

--- a/solution.py
+++ b/solution.py
@@ -63,7 +63,12 @@
     send_grads = (
         gate_pad[slot_pair][:, None] * upstream_pad[slot_token].astype(jnp.float32)
     ).astype(jnp.bfloat16)
-    flat_shape = (expert_count, capacity, width)
+    fold = 1
+    while (capacity * fold) % 16 or (width // fold) % 128 or width % fold:
+        fold += 1
+    if (width // fold) % 128 or width % fold:
+        fold = 1
+    flat_shape = (expert_count, capacity * fold, width // fold)
     got_rows, got_grads = (
         lax.all_to_all(
             send_rows.reshape(flat_shape),
@@ -85,6 +90,16 @@
     hidden, expert_out, grad_gate_pre, grad_up_pre, pair_grad = expert_rows(
         rows_in, grads_in, w_gate[0], w_up[0], w_down[0]
     )
+    dp_count = lax.axis_size("dp")
+    piece = width // dp_count
+    rows_all = lax.all_to_all(
+        jnp.stack([rows_in[:, part * piece:(part + 1) * piece] for part in range(dp_count)], axis=0),
+        "dp",
+        split_axis=0,
+        concat_axis=0,
+        tiled=True,
+    )
+    expert_out, pair_grad, rows_all = lax.optimization_barrier((expert_out, pair_grad, rows_all))
     back_out, back_grad = (
         lax.all_to_all(
             expert_out.reshape(flat_shape),
@@ -101,12 +116,6 @@
             tiled=True,
         ),
     )
-    dp_count = lax.axis_size("dp")
-    piece = width // dp_count
-    column_pieces = jnp.stack(
-        [rows_in[:, part * piece:(part + 1) * piece] for part in range(dp_count)], axis=0
-    )
-    rows_all = lax.all_to_all(column_pieces, "dp", split_axis=0, concat_axis=0, tiled=True)
     joined_grads = jnp.concatenate([grad_gate_pre, grad_up_pre], axis=1)
     joined_all = lax.all_gather(joined_grads, "dp", axis=0, tiled=False)
     grad_joined = lax.dot_general(

time: 379 us -> 364 us (0.960)
  waiting for transfers between devices: 194 us -> 175 us
    all_to_all x1, waiting for transfers between devices: 15.4 us -> 50.1 us  [local(): lax.all_to_all(jnp.stack([rows_in[:, part * piece:(part + 1) * piece] for...]
    all_to_all x1, waiting for transfers between devices: 48.5 us -> 32.5 us  [local(): lax.all_to_all(send_grads.reshape(flat_shape), ('outer', 'inner'), split_...]
    all_to_all x1, waiting for transfers between devices: 42.7 us -> 27.2 us  [local(): lax.all_to_all(send_rows.reshape(flat_shape), ('outer', 'inner'), split_a...]
    all_to_all x1, waiting for transfers between devices: 45.1 us -> 33.5 us  [local(): lax.all_to_all(expert_out.reshape(flat_shape), ('outer', 'inner'), split_...]
    all_to_all x1, waiting for transfers between devices: 41.7 us -> 31.8 us  [local(): lax.all_to_all(pair_grad.reshape(flat_shape), ('outer', 'inner'), split_a...]
    unnamed x31 -> x27, local copies, waits for them, and re-layouts: 9.1 us -> 6.15 us
  transfers between devices with their start and end apart: 7 -> 7, of which waited for: 5 -> 5; matrix products, arithmetic and copies ran while one was open for 26% -> 27% of each run, Pallas kernels for 0% -> 0%
where the time goes in v6:
time: 364 us; the launch traced here: 361 us
  waiting for transfers between devices  175 us (48%)
  local copies, waits for them, and re-layouts  66.2 us (18%)
  matrix products  59.7 us (16%)
  starting transfers between devices  30.6 us (8%)
  other arithmetic  15.5 us (4%)
  between operations  14.3 us (4%)
    all_to_all x1, waiting for transfers between devices, local(): lax.all_to_all(jnp.stack([rows_in[:, part * piece:(part + 1) * piece] for...  50.1 us
    all_to_all x1, waiting for transfers between devices, local(): lax.all_to_all(expert_out.reshape(flat_shape), ('outer', 'inner'), split_...  33.5 us
    all_to_all x1, waiting for transfers between devices, local(): lax.all_to_all(send_grads.reshape(flat_shape), ('outer', 'inner'), split_...  32.5 us
    all_to_all x1, waiting for transfers between devices, local(): lax.all_to_all(pair_grad.reshape(flat_shape), ('outer', 'inner'), split_a...  31.8 us
    all_to_all x1, waiting for transfers between devices, local(): lax.all_to_all(send_rows.reshape(flat_shape), ('outer', 'inner'), split_a...  27.2 us
    dot_general x3, matrix products, contract_last(): lax.dot_general(left, right, (((1,), (1,)), ((), ())), preferred_element_...  20.9 us
    dot_general x1, matrix products, contract_first(): lax.dot_general(left, right, (((0,), (0,)), ((), ())), preferred_element_...  8.15 us
    dot_general x1, matrix products, local(): lax.dot_general(rows_all, joined_all, (((0, 1), (0, 1)), ((), ())), prefe...  8.13 us
  transfers between devices with their start and end apart: 7, of which 5 were waited for; matrix products, arithmetic and copies ran while one was open for 27% of the time, Pallas kernels for 0%

profile of v6, /device:TPU:8, one launch (start us, length us, event | category | flops | bytes accessed | tf_op | source)
XLA Modules:
  0.0 361.4 jit_solution(15035026848561233419)
XLA Ops:
  23.1 4.9 %multiply_convert_fusion = bf16[32,48,1024]{2,1,0:T(8,128)(2,1)} fusion(f32[32,48,1024]{2,1,0:T(8,128)} %reshape.108, f32[32,48]{1,0:T(8,128)S(1)} %copy.22), kind=kLoop, calls=%fused_computation.21 | loop fusion | flops 3145728 | bytes 9443328 | tf_op jit(solution)/shard_map/convert_element_type | solution.py:65
  28.0 7.7 %all-to-all-start.1 = ((bf16[32,48,1024]{2,1,0:T(8,128)(2,1)}), bf16[32,48,1024]{2,1,0:T(8,128)(2,1)}, u32[]{:S(2)}, u32[]{:S(2)}) async-start(bf16[32,48,1024]{2,1,0:T(8,128)(2,1)} %multiply_convert_fusion), calls=%async_computation.1 | async-start | bytes 6291456 | tf_op jit(solution)/shard_map/all_to_all | solution.py:80
  42.8 32.5 %all-to-all-done.1 = bf16[32,48,1024]{2,1,0:T(8,128)(2,1)} async-done(((bf16[32,48,1024]{2,1,0:T(8,128)(2,1)}), bf16[32,48,1024]{2,1,0:T(8,128)(2,1)}, u32[]{:S(2)}, u32[]{:S(2)}) %all-to-all-start.1) | async-done | bytes 3145760 | tf_op jit(solution)/shard_map/all_to_all | solution.py:80
  75.3 5.3 %all-to-all-start = ((bf16[32,48,1024]{2,1,0:T(8,128)(2,1)}), bf16[32,48,1024]{2,1,0:T(8,128)(2,1)}, u32[]{:S(2)}, u32[]{:S(2)}) async-start(bf16[32,48,1024]{2,1,0:T(8,128)(2,1)} %reshape.98), calls=%async_computation | async-start | bytes 6291456 | tf_op jit(solution)/shard_map/all_to_all | solution.py:73
  80.8 4.5 %reshape.101 = bf16[384,4096]{1,0:T(8,128)(2,1)S(1)} reshape(bf16[32,48,1024]{2,1,0:T(8,128)(2,1)} %all-to-all-done.1) | data formatting | bytes 6291456 | tf_op jit(solution)/shard_map/reshape | solution.py:89
  85.3 7.6 %fusion = f32[384,768]{1,0:T(8,128)} fusion(bf16[384,4096]{1,0:T(8,128)(2,1)S(1)} %reshape.101, bf16[1,768,4096]{2,1,0:T(8,128)(2,1)} %param.13), kind=kOutput, calls=%fused_computation.8 | convolution fusion | flops 2415919104 | bytes 10616832 | tf_op jit(solution)/shard_map/dot_general | solution.py:8
  92.9 27.2 %all-to-all-done = bf16[32,48,1024]{2,1,0:T(8,128)(2,1)} async-done(((bf16[32,48,1024]{2,1,0:T(8,128)(2,1)}), bf16[32,48,1024]{2,1,0:T(8,128)(2,1)}, u32[]{:S(2)}, u32[]{:S(2)}) %all-to-all-start) | async-done | bytes 3145760 | tf_op jit(solution)/shard_map/all_to_all | solution.py:73
  124.6 5.5 %fusion.6 = f32[384,768]{1,0:T(8,128)S(1)} fusion(bf16[384,4096]{1,0:T(8,128)(2,1)S(1)} %reshape.99, bf16[1,4096,768]{2,1,0:T(8,128)(2,1)} %param.12), kind=kOutput, calls=%fused_computation.14 | convolution fusion | flops 2415919104 | bytes 10616832 | tf_op jit(solution)/shard_map/dot_general | solution.py:21
  130.1 6.6 %multiply_convert_fusion.2 = (bf16[384,768]{1,0:T(8,128)(2,1)S(1)}, bf16[384,768]{1,0:T(8,128)(2,1)S(1)}, bf16[384,768]{1,0:T(8,128)(2,1)}) fusion(f32[384,768]{1,0:T(8,128)S(1)} %copy-done.11, f32[384,768]{1,0:T(8,128)S(1)} %fusion.6, bf16[384,4096]{1,0:T(8,128)(2,1)S(1)} %reshape.99, bf16[1,4096,768]{2,1,0:T(8,128)(2,1)} %param.11), kind=kOutput, calls=%fused_computation.32 | convolution fusion | flops 2420342784 | bytes 13565952 | tf_op jit(solution)/shard_map/dot_general | solution.py:20
  138.9 8.2 %convolution_convert_fusion = bf16[4096,768]{1,0:T(8,128)(2,1)} fusion(bf16[384,4096]{1,0:T(8,128)(2,1)} %copy-done.3, bf16[384,768]{1,0:T(8,128)(2,1)} %get-tuple-element.32), kind=kOutput, calls=%fused_computation.6 | convolution fusion | flops 2419064832 | bytes 10027008 | tf_op jit(solution)/shard_map/dot_general | solution.py:14
  149.3 5.3 %all-to-all-start.2 = ((bf16[4,384,1024]{2,1,0:T(8,128)(2,1)}), bf16[4,384,1024]{2,1,0:T(8,128)(2,1)S(1)}, u32[]{:S(2)}, u32[]{:S(2)}) async-start(bf16[4,384,1024]{2,1,0:T(8,128)(2,1)} %pad_maximum_fusion), calls=%async_computation.2 | async-start | bytes 6291456 | tf_op jit(solution)/shard_map/all_to_all | solution.py:95
  154.7 7.3 %fusion.14 = bf16[384,4096]{1,0:T(8,128)(2,1)} fusion(bf16[384,768]{1,0:T(8,128)(2,1)} %get-tuple-element.32, bf16[1,768,4096]{2,1,0:T(8,128)(2,1)} %param.13), kind=kOutput, calls=%fused_computation.22 | convolution fusion | flops 2417491968 | bytes 10027008 | tf_op jit(solution)/shard_map/dot_general | solution.py:25
  161.9 4.9 %fusion.4 = f32[384,4096]{1,0:T(8,128)S(1)} fusion(bf16[384,768]{1,0:T(8,128)(2,1)S(1)} %copy-done.7, bf16[1,4096,768]{2,1,0:T(8,128)(2,1)} %param.12), kind=kOutput, calls=%fused_computation.12 | convolution fusion | flops 2415919104 | bytes 13172736 | tf_op jit(solution)/shard_map/dot_general | solution.py:8
  166.8 8.4 %add_convert_fusion = bf16[384,4096]{1,0:T(8,128)(2,1)} fusion(f32[384,4096]{1,0:T(8,128)S(1)} %fusion.4, bf16[384,768]{1,0:T(8,128)(2,1)S(1)} %copy-done.5, bf16[1,4096,768]{2,1,0:T(8,128)(2,1)} %param.11), kind=kOutput, calls=%fused_computation.20 | convolution fusion | flops 2419064832 | bytes 16318464 | tf_op jit(solution)/shard_map/dot_general | solution.py:8
  175.3 50.1 %all-to-all-done.2 = bf16[4,384,1024]{2,1,0:T(8,128)(2,1)S(1)} async-done(((bf16[4,384,1024]{2,1,0:T(8,128)(2,1)}), bf16[4,384,1024]{2,1,0:T(8,128)(2,1)S(1)}, u32[]{:S(2)}, u32[]{:S(2)}) %all-to-all-start.2) | async-done | bytes 3145760 | tf_op jit(solution)/shard_map/all_to_all | solution.py:95
  225.3 6.3 %reshape.102 = bf16[32,48,1024]{2,1,0:T(8,128)(2,1)} reshape(bf16[384,4096]{1,0:T(8,128)(2,1)} %fusion.14) | data formatting | bytes 6291456 | tf_op jit(solution)/shard_map/reshape | solution.py:105
  231.7 6.7 %all-to-all-start.3 = ((bf16[32,48,1024]{2,1,0:T(8,128)(2,1)}), bf16[32,48,1024]{2,1,0:T(8,128)(2,1)S(1)}, u32[]{:S(2)}, u32[]{:S(2)}) async-start(bf16[32,48,1024]{2,1,0:T(8,128)(2,1)} %reshape.102), calls=%async_computation.3 | async-start | bytes 6291456 | tf_op jit(solution)/shard_map/all_to_all | solution.py:104
  238.3 6.0 %reshape.105 = bf16[32,48,1024]{2,1,0:T(8,128)(2,1)} reshape(bf16[384,4096]{1,0:T(8,128)(2,1)} %add_convert_fusion) | data formatting | bytes 6291456 | tf_op jit(solution)/shard_map/reshape | solution.py:112
  244.3 33.5 %all-to-all-done.3 = bf16[32,48,1024]{2,1,0:T(8,128)(2,1)S(1)} async-done(((bf16[32,48,1024]{2,1,0:T(8,128)(2,1)}), bf16[32,48,1024]{2,1,0:T(8,128)(2,1)S(1)}, u32[]{:S(2)}, u32[]{:S(2)}) %all-to-all-start.3) | async-done | bytes 3145760 | tf_op jit(solution)/shard_map/all_to_all | solution.py:104
  279.5 5.3 %all-to-all-start.4 = ((bf16[32,48,1024]{2,1,0:T(8,128)(2,1)}), bf16[32,48,1024]{2,1,0:T(8,128)(2,1)}, u32[]{:S(2)}, u32[]{:S(2)}) async-start(bf16[32,48,1024]{2,1,0:T(8,128)(2,1)} %reshape.105), calls=%async_computation.4 | async-start | bytes 6291456 | tf_op jit(solution)/shard_map/all_to_all | solution.py:111
  284.8 4.5 %reshape.103 = bf16[384,4096]{1,0:T(8,128)(2,1)S(1)} reshape(bf16[32,48,1024]{2,1,0:T(8,128)(2,1)} %copy-done) | data formatting | bytes 6291456 | tf_op jit(solution)/shard_map/reshape | solution.py:135
  292.6 31.8 %all-to-all-done.4 = bf16[32,48,1024]{2,1,0:T(8,128)(2,1)} async-done(((bf16[32,48,1024]{2,1,0:T(8,128)(2,1)}), bf16[32,48,1024]{2,1,0:T(8,128)(2,1)}, u32[]{:S(2)}, u32[]{:S(2)}) %all-to-all-start.4) | async-done | bytes 3145760 | tf_op jit(solution)/shard_map/all_to_all | solution.py:111
  324.4 4.5 %reshape.106 = bf16[384,4096]{1,0:T(8,128)(2,1)S(1)} reshape(bf16[32,48,1024]{2,1,0:T(8,128)(2,1)} %all-to-all-done.4) | data formatting | bytes 6291456 | tf_op jit(solution)/shard_map/reshape | solution.py:136
  342.0 8.1 %bitcast_convert_fusion = bf16[1024,1536]{1,0:T(8,128)(2,1)S(1)} fusion(bf16[4,384,1024]{2,1,0:T(8,128)(2,1)} %copy-done.2, bf16[4,384,1536]{2,1,0:T(8,128)(2,1)} %bitcast.86), kind=kOutput, calls=%fused_computation.7 | convolution fusion | flops 4833411072 | bytes 11010048 | tf_op jit(solution)/shard_map/dot_general | solution.py:121
  (74 shorter events, 54.5 us)
Async XLA Ops:
  15.6 4.2 %copy-start.10 = (f32[32,8]{0,1:T(8,128)S(1)}, f32[32,8]{0,1:T(8,128)}, u32[]{:S(2)}) copy-start(f32[32,8]{0,1:T(8,128)} %param.9) | copy-start | bytes 3076
  28.0 7.7 %copy-start.8 = (bf16[32,4096]{1,0:T(8,128)(2,1)S(1)}, bf16[32,4096]{1,0:T(8,128)(2,1)}, u32[]{:S(2)}) copy-start(bf16[32,4096]{1,0:T(8,128)(2,1)} %param.7) | copy-start | bytes 786436
  28.0 47.3 %all-to-all-start.1 = ((bf16[32,48,1024]{2,1,0:T(8,128)(2,1)}), bf16[32,48,1024]{2,1,0:T(8,128)(2,1)}, u32[]{:S(2)}, u32[]{:S(2)}) async-start(bf16[32,48,1024]{2,1,0:T(8,128)(2,1)} %multiply_convert_fusion), calls=%async_computation.1 | async-start | bytes 6291456 | tf_op jit(solution)/shard_map/all_to_all | solution.py:80
  75.3 44.9 %all-to-all-start = ((bf16[32,48,1024]{2,1,0:T(8,128)(2,1)}), bf16[32,48,1024]{2,1,0:T(8,128)(2,1)}, u32[]{:S(2)}, u32[]{:S(2)}) async-start(bf16[32,48,1024]{2,1,0:T(8,128)(2,1)} %reshape.98), calls=%async_computation | async-start | bytes 6291456 | tf_op jit(solution)/shard_map/all_to_all | solution.py:73
  80.6 261.4 %all-gather.3.cloned.1.call-start = ((), (), s32[]{:S(2)}) async-start(), calls=%async_computation.7 | async-start | bytes 5898240 | tf_op jit(solution)/shard_map/all_gather | solution.py:120
  85.3 7.6 %copy-start.3 = (bf16[384,4096]{1,0:T(8,128)(2,1)}, bf16[384,4096]{1,0:T(8,128)(2,1)S(1)}, u32[]{:S(2)}) copy-start(bf16[384,4096]{1,0:T(8,128)(2,1)S(1)} %reshape.101) | copy-start | bytes 9437188
  124.6 5.5 %copy-start.11 = (f32[384,768]{1,0:T(8,128)S(1)}, f32[384,768]{1,0:T(8,128)}, u32[]{:S(2)}) copy-start(f32[384,768]{1,0:T(8,128)} %fusion) | copy-start | bytes 3538948
  136.7 0.8 copy-start.4
  136.7 1.0 copy-start.6
  138.8 213.2 %reduce-scatter.2.cloned.1.call-start = ((), (), s32[]{:S(2)}) async-start(), calls=%async_computation.6 | async-start | bytes 7864320 | tf_op jit(solution)/shard_map/reduce_scatter | solution.py:126
  149.3 76.0 %all-to-all-start.2 = ((bf16[4,384,1024]{2,1,0:T(8,128)(2,1)}), bf16[4,384,1024]{2,1,0:T(8,128)(2,1)S(1)}, u32[]{:S(2)}, u32[]{:S(2)}) async-start(bf16[4,384,1024]{2,1,0:T(8,128)(2,1)} %pad_maximum_fusion), calls=%async_computation.2 | async-start | bytes 6291456 | tf_op jit(solution)/shard_map/all_to_all | solution.py:95
  154.7 7.3 %copy-start.7 = (bf16[384,768]{1,0:T(8,128)(2,1)S(1)}, bf16[384,768]{1,0:T(8,128)(2,1)}, u32[]{:S(2)}) copy-start(bf16[384,768]{1,0:T(8,128)(2,1)} %copy-done.6) | copy-start | bytes 1769476
  161.9 4.9 %copy-start.5 = (bf16[384,768]{1,0:T(8,128)(2,1)S(1)}, bf16[384,768]{1,0:T(8,128)(2,1)}, u32[]{:S(2)}) copy-start(bf16[384,768]{1,0:T(8,128)(2,1)} %copy-done.4) | copy-start | bytes 1769476
  225.3 6.3 %copy-start.2 = (bf16[4,384,1024]{2,1,0:T(8,128)(2,1)}, bf16[4,384,1024]{2,1,0:T(8,128)(2,1)S(1)}, u32[]{:S(2)}) copy-start(bf16[4,384,1024]{2,1,0:T(8,128)(2,1)S(1)} %all-to-all-done.2) | copy-start | bytes 9437188
  231.7 46.2 %all-to-all-start.3 = ((bf16[32,48,1024]{2,1,0:T(8,128)(2,1)}), bf16[32,48,1024]{2,1,0:T(8,128)(2,1)S(1)}, u32[]{:S(2)}, u32[]{:S(2)}) async-start(bf16[32,48,1024]{2,1,0:T(8,128)(2,1)} %reshape.102), calls=%async_computation.3 | async-start | bytes 6291456 | tf_op jit(solution)/shard_map/all_to_all | solution.py:104
  277.8 1.7 copy-start
  279.5 44.9 %all-to-all-start.4 = ((bf16[32,48,1024]{2,1,0:T(8,128)(2,1)}), bf16[32,48,1024]{2,1,0:T(8,128)(2,1)}, u32[]{:S(2)}, u32[]{:S(2)}) async-start(bf16[32,48,1024]{2,1,0:T(8,128)(2,1)} %reshape.105), calls=%async_computation.4 | async-start | bytes 6291456 | tf_op jit(solution)/shard_map/all_to_all | solution.py:111
  328.9 3.2 copy-start.9
  332.1 7.6 %copy-start.1 = (bf16[256,4096]{1,0:T(8,128)(2,1)S(1)}, bf16[256,4096]{1,0:T(8,128)(2,1)}, u32[]{:S(2)}) copy-start(bf16[256,4096]{1,0:T(8,128)(2,1)} %gather_fusion.3) | copy-start | bytes 6291460
Sparse Core Ops, SparseCore 0:
  138.9 85.5 all-gather.2
  226.9 65.4 reduce-scatter.1

commit v7 on v6

--- a/solution.py
+++ b/solution.py
@@ -87,9 +87,6 @@
     )
     rows_in = got_rows.reshape(-1, width)
     grads_in = got_grads.reshape(-1, width)
-    hidden, expert_out, grad_gate_pre, grad_up_pre, pair_grad = expert_rows(
-        rows_in, grads_in, w_gate[0], w_up[0], w_down[0]
-    )
     dp_count = lax.axis_size("dp")
     piece = width // dp_count
     rows_all = lax.all_to_all(
@@ -99,7 +96,21 @@
         concat_axis=0,
         tiled=True,
     )
-    expert_out, pair_grad, rows_all = lax.optimization_barrier((expert_out, pair_grad, rows_all))
+    gate_mat, up_mat, down_mat = w_gate[0], w_up[0], w_down[0]
+    gate_pre = jnp.dot(rows_in, gate_mat, preferred_element_type=jnp.float32)
+    up_pre = jnp.dot(rows_in, up_mat, preferred_element_type=jnp.float32)
+    sigma = jax.nn.sigmoid(gate_pre)
+    silu_value = gate_pre * sigma
+    hidden = (silu_value * up_pre).astype(jnp.bfloat16)
+    expert_out = jnp.dot(hidden, down_mat, preferred_element_type=jnp.float32).astype(jnp.bfloat16)
+    grads_in, rows_all = lax.optimization_barrier((grads_in, rows_all))
+    grad_hidden = contract_last(grads_in, down_mat)
+    slope = sigma * (1.0 + gate_pre * (1.0 - sigma))
+    grad_gate_pre = (grad_hidden * up_pre * slope).astype(jnp.bfloat16)
+    grad_up_pre = (grad_hidden * silu_value).astype(jnp.bfloat16)
+    pair_grad = (
+        contract_last(grad_gate_pre, gate_mat) + contract_last(grad_up_pre, up_mat)
+    ).astype(jnp.bfloat16)
     back_out, back_grad = (
         lax.all_to_all(
             expert_out.reshape(flat_shape),

time: 364 us -> 323 us (0.89)
  waiting for transfers between devices: 175 us -> 135 us
  local copies, waits for them, and re-layouts: 66.2 us -> 71.9 us
    all_to_all x1, waiting for transfers between devices: 50.1 us -> 25.4 us  [local(): lax.all_to_all(jnp.stack([rows_in[:, part * piece:(part + 1) * piece] for...]
    all_to_all x1, waiting for transfers between devices: 27.2 us -> 19.8 us  [local(): lax.all_to_all(send_rows.reshape(flat_shape), ('outer', 'inner'), split_a...]
    all_to_all x1, waiting for transfers between devices: 31.8 us -> 26.2 us  [local(): lax.all_to_all(pair_grad.reshape(flat_shape), ('outer', 'inner'), split_a...]
  transfers between devices with their start and end apart: 7 -> 7, of which waited for: 5 -> 5; matrix products, arithmetic and copies ran while one was open for 27% -> 34% of each run, Pallas kernels for 0% -> 0%
where the time goes in v7:
time: 323 us; the launch traced here: 321 us
  waiting for transfers between devices  135 us (42%)
  local copies, waits for them, and re-layouts  71.9 us (22%)
  matrix products  56.9 us (18%)
  starting transfers between devices  28.8 us (9%)
  between operations  14.3 us (4%)
  other arithmetic  13.8 us (4%)
    all_to_all x1, waiting for transfers between devices, local(): lax.all_to_all(expert_out.reshape(flat_shape), ('outer', 'inner'), split_...  31.8 us
    all_to_all x1, waiting for transfers between devices, local(): lax.all_to_all(send_grads.reshape(flat_shape), ('outer', 'inner'), split_...  31.8 us
    all_to_all x1, waiting for transfers between devices, local(): lax.all_to_all(pair_grad.reshape(flat_shape), ('outer', 'inner'), split_a...  26.2 us
    all_to_all x1, waiting for transfers between devices, local(): lax.all_to_all(jnp.stack([rows_in[:, part * piece:(part + 1) * piece] for...  25.4 us
    all_to_all x1, waiting for transfers between devices, local(): lax.all_to_all(send_rows.reshape(flat_shape), ('outer', 'inner'), split_a...  19.8 us
    dot_general x3, matrix products, contract_last(): lax.dot_general(left, right, (((1,), (1,)), ((), ())), preferred_element_...  18.8 us
    dot_general x1, matrix products, local(): lax.dot_general(rows_all, joined_all, (((0, 1), (0, 1)), ((), ())), prefe...  8.13 us
    unnamed x27, local copies, waits for them, and re-layouts  7.82 us
  transfers between devices with their start and end apart: 7, of which 5 were waited for; matrix products, arithmetic and copies ran while one was open for 34% of the time, Pallas kernels for 0%

profile of v7, /device:TPU:8, one launch (start us, length us, event | category | flops | bytes accessed | tf_op | source)
XLA Modules:
  0.0 320.7 jit_solution(9298119070367567472)
XLA Ops:
  19.3 7.5 %all-to-all-start = ((bf16[32,48,1024]{2,1,0:T(8,128)(2,1)}), bf16[32,48,1024]{2,1,0:T(8,128)(2,1)S(1)}, u32[]{:S(2)}, u32[]{:S(2)}) async-start(bf16[32,48,1024]{2,1,0:T(8,128)(2,1)} %reshape.98), calls=%async_computation | async-start | bytes 6291456 | tf_op jit(solution)/shard_map/all_to_all | solution.py:73
  32.0 6.4 %reshape.108 = f32[32,48,1024]{2,1,0:T(8,128)} reshape(bf16[384,4096]{1,0:T(8,128)(2,1)} %gather_fusion.3) | data formatting | bytes 9437184 | tf_op jit(solution)/shard_map/convert_element_type | solution.py:64
  41.7 5.0 %multiply_convert_fusion = bf16[32,48,1024]{2,1,0:T(8,128)(2,1)} fusion(f32[32,48,1024]{2,1,0:T(8,128)} %reshape.108, f32[32,48]{1,0:T(8,128)S(1)} %copy.22), kind=kLoop, calls=%fused_computation.21 | loop fusion | flops 3145728 | bytes 9443328 | tf_op jit(solution)/shard_map/convert_element_type | solution.py:65
  46.6 19.8 %all-to-all-done = bf16[32,48,1024]{2,1,0:T(8,128)(2,1)S(1)} async-done(((bf16[32,48,1024]{2,1,0:T(8,128)(2,1)}), bf16[32,48,1024]{2,1,0:T(8,128)(2,1)S(1)}, u32[]{:S(2)}, u32[]{:S(2)}) %all-to-all-start) | async-done | bytes 3145760 | tf_op jit(solution)/shard_map/all_to_all | solution.py:73
  66.4 5.3 %all-to-all-start.2 = ((bf16[32,48,1024]{2,1,0:T(8,128)(2,1)}), bf16[32,48,1024]{2,1,0:T(8,128)(2,1)}, u32[]{:S(2)}, u32[]{:S(2)}) async-start(bf16[32,48,1024]{2,1,0:T(8,128)(2,1)} %multiply_convert_fusion), calls=%async_computation.2 | async-start | bytes 6291456 | tf_op jit(solution)/shard_map/all_to_all | solution.py:80
  79.4 31.8 %all-to-all-done.2 = bf16[32,48,1024]{2,1,0:T(8,128)(2,1)} async-done(((bf16[32,48,1024]{2,1,0:T(8,128)(2,1)}), bf16[32,48,1024]{2,1,0:T(8,128)(2,1)}, u32[]{:S(2)}, u32[]{:S(2)}) %all-to-all-start.2) | async-done | bytes 3145760 | tf_op jit(solution)/shard_map/all_to_all | solution.py:80
  111.3 5.3 %all-to-all-start.3 = ((bf16[4,384,1024]{2,1,0:T(8,128)(2,1)}), bf16[4,384,1024]{2,1,0:T(8,128)(2,1)}, u32[]{:S(2)}, u32[]{:S(2)}) async-start(bf16[4,384,1024]{2,1,0:T(8,128)(2,1)} %pad_maximum_fusion), calls=%async_computation.3 | async-start | bytes 6291456 | tf_op jit(solution)/shard_map/all_to_all | solution.py:92
  116.6 6.1 %reshape.104 = bf16[384,4096]{1,0:T(8,128)(2,1)} reshape(bf16[32,48,1024]{2,1,0:T(8,128)(2,1)} %all-to-all-done.2) | data formatting | bytes 6291456 | tf_op jit(solution)/shard_map/reshape | solution.py:89
  122.7 6.4 %fusion.6 = f32[384,768]{1,0:T(8,128)} fusion(bf16[384,4096]{1,0:T(8,128)(2,1)S(1)} %copy-done, bf16[1,4096,768]{2,1,0:T(8,128)(2,1)} %param.12), kind=kOutput, calls=%fused_computation.14 | convolution fusion | flops 2415919104 | bytes 10616832 | tf_op jit(solution)/shard_map/dot_general | solution.py:101
  129.0 25.4 %all-to-all-done.3 = bf16[4,384,1024]{2,1,0:T(8,128)(2,1)} async-done(((bf16[4,384,1024]{2,1,0:T(8,128)(2,1)}), bf16[4,384,1024]{2,1,0:T(8,128)(2,1)}, u32[]{:S(2)}, u32[]{:S(2)}) %all-to-all-start.3) | async-done | bytes 3145760 | tf_op jit(solution)/shard_map/all_to_all | solution.py:92
  154.4 6.5 %fusion = f32[384,768]{1,0:T(8,128)S(1)} fusion(bf16[384,4096]{1,0:T(8,128)(2,1)} %reshape.104, bf16[1,768,4096]{2,1,0:T(8,128)(2,1)} %param.13), kind=kOutput, calls=%fused_computation.8 | convolution fusion | flops 2415919104 | bytes 10616832 | tf_op jit(solution)/shard_map/dot_general | solution.py:8
  160.9 6.6 %multiply_convert_fusion.2 = (bf16[384,768]{1,0:T(8,128)(2,1)S(1)}, bf16[384,768]{1,0:T(8,128)(2,1)S(1)}, bf16[384,768]{1,0:T(8,128)(2,1)}) fusion(f32[384,768]{1,0:T(8,128)S(1)} %fusion, f32[384,768]{1,0:T(8,128)S(1)} %copy-done.11, bf16[384,4096]{1,0:T(8,128)(2,1)S(1)} %copy-done, bf16[1,4096,768]{2,1,0:T(8,128)(2,1)} %param.11), kind=kOutput, calls=%fused_computation.32 | convolution fusion | flops 2420342784 | bytes 13565952 | tf_op jit(solution)/shard_map/dot_general | solution.py:100
  170.3 6.4 %convolution_convert_fusion = bf16[4096,768]{1,0:T(8,128)(2,1)} fusion(bf16[384,4096]{1,0:T(8,128)(2,1)S(1)} %copy-done.4, bf16[384,768]{1,0:T(8,128)(2,1)} %get-tuple-element.30), kind=kOutput, calls=%fused_computation.6 | convolution fusion | flops 2419064832 | bytes 10027008 | tf_op jit(solution)/shard_map/dot_general | solution.py:14
  177.8 5.1 %fusion.4 = f32[384,4096]{1,0:T(8,128)S(1)} fusion(bf16[384,768]{1,0:T(8,128)(2,1)S(1)} %copy-done.8, bf16[1,4096,768]{2,1,0:T(8,128)(2,1)} %param.12), kind=kOutput, calls=%fused_computation.12 | convolution fusion | flops 2415919104 | bytes 13172736 | tf_op jit(solution)/shard_map/dot_general | solution.py:8
  182.9 7.3 %add_convert_fusion = bf16[384,4096]{1,0:T(8,128)(2,1)S(1)} fusion(f32[384,4096]{1,0:T(8,128)S(1)} %fusion.4, bf16[384,768]{1,0:T(8,128)(2,1)S(1)} %copy-done.6, bf16[1,4096,768]{2,1,0:T(8,128)(2,1)} %param.11), kind=kOutput, calls=%fused_computation.20 | convolution fusion | flops 2419064832 | bytes 16318464 | tf_op jit(solution)/shard_map/dot_general | solution.py:8
  193.9 5.3 %all-to-all-start.4 = ((bf16[32,48,1024]{2,1,0:T(8,128)(2,1)}), bf16[32,48,1024]{2,1,0:T(8,128)(2,1)S(1)}, u32[]{:S(2)}, u32[]{:S(2)}) async-start(bf16[32,48,1024]{2,1,0:T(8,128)(2,1)} %reshape.105), calls=%async_computation.4 | async-start | bytes 6291456 | tf_op jit(solution)/shard_map/all_to_all | solution.py:122
  199.2 7.3 %fusion.14 = bf16[384,4096]{1,0:T(8,128)(2,1)} fusion(bf16[384,768]{1,0:T(8,128)(2,1)} %get-tuple-element.30, bf16[1,768,4096]{2,1,0:T(8,128)(2,1)} %param.13), kind=kOutput, calls=%fused_computation.22 | convolution fusion | flops 2417491968 | bytes 10027008 | tf_op jit(solution)/shard_map/dot_general | solution.py:105
  206.5 6.0 %reshape.100 = bf16[32,48,1024]{2,1,0:T(8,128)(2,1)} reshape(bf16[384,4096]{1,0:T(8,128)(2,1)} %fusion.14) | data formatting | bytes 6291456 | tf_op jit(solution)/shard_map/reshape | solution.py:116
  212.5 26.2 %all-to-all-done.4 = bf16[32,48,1024]{2,1,0:T(8,128)(2,1)S(1)} async-done(((bf16[32,48,1024]{2,1,0:T(8,128)(2,1)}), bf16[32,48,1024]{2,1,0:T(8,128)(2,1)S(1)}, u32[]{:S(2)}, u32[]{:S(2)}) %all-to-all-start.4) | async-done | bytes 3145760 | tf_op jit(solution)/shard_map/all_to_all | solution.py:122
  240.3 5.4 %all-to-all-start.1 = ((bf16[32,48,1024]{2,1,0:T(8,128)(2,1)}), bf16[32,48,1024]{2,1,0:T(8,128)(2,1)}, u32[]{:S(2)}, u32[]{:S(2)}) async-start(bf16[32,48,1024]{2,1,0:T(8,128)(2,1)} %reshape.100), calls=%async_computation.1 | async-start | bytes 6291456 | tf_op jit(solution)/shard_map/all_to_all | solution.py:115
  245.7 4.5 %reshape.106 = bf16[384,4096]{1,0:T(8,128)(2,1)S(1)} reshape(bf16[32,48,1024]{2,1,0:T(8,128)(2,1)} %copy-done.1) | data formatting | bytes 6291456 | tf_op jit(solution)/shard_map/reshape | solution.py:147
  253.4 31.8 %all-to-all-done.1 = bf16[32,48,1024]{2,1,0:T(8,128)(2,1)} async-done(((bf16[32,48,1024]{2,1,0:T(8,128)(2,1)}), bf16[32,48,1024]{2,1,0:T(8,128)(2,1)}, u32[]{:S(2)}, u32[]{:S(2)}) %all-to-all-start.1) | async-done | bytes 3145760 | tf_op jit(solution)/shard_map/all_to_all | solution.py:115
  285.3 4.5 %reshape.101 = bf16[384,4096]{1,0:T(8,128)(2,1)S(1)} reshape(bf16[32,48,1024]{2,1,0:T(8,128)(2,1)} %all-to-all-done.1) | data formatting | bytes 6291456 | tf_op jit(solution)/shard_map/reshape | solution.py:146
  301.3 8.1 %bitcast_convert_fusion = bf16[1024,1536]{1,0:T(8,128)(2,1)S(1)} fusion(bf16[4,384,1024]{2,1,0:T(8,128)(2,1)} %all-to-all-done.3, bf16[4,384,1536]{2,1,0:T(8,128)(2,1)} %bitcast.86), kind=kOutput, calls=%fused_computation.7 | convolution fusion | flops 4833411072 | bytes 11010048 | tf_op jit(solution)/shard_map/dot_general | solution.py:132
  (74 shorter events, 56.6 us)
Async XLA Ops:
  19.3 47.0 %all-to-all-start = ((bf16[32,48,1024]{2,1,0:T(8,128)(2,1)}), bf16[32,48,1024]{2,1,0:T(8,128)(2,1)S(1)}, u32[]{:S(2)}, u32[]{:S(2)}) async-start(bf16[32,48,1024]{2,1,0:T(8,128)(2,1)} %reshape.98), calls=%async_computation | async-start | bytes 6291456 | tf_op jit(solution)/shard_map/all_to_all | solution.py:73
  32.0 6.4 %copy-start.10 = (f32[32,8]{0,1:T(8,128)S(1)}, f32[32,8]{0,1:T(8,128)}, u32[]{:S(2)}) copy-start(f32[32,8]{0,1:T(8,128)} %param.9) | copy-start | bytes 3076
  66.4 44.9 %all-to-all-start.2 = ((bf16[32,48,1024]{2,1,0:T(8,128)(2,1)}), bf16[32,48,1024]{2,1,0:T(8,128)(2,1)}, u32[]{:S(2)}, u32[]{:S(2)}) async-start(bf16[32,48,1024]{2,1,0:T(8,128)(2,1)} %multiply_convert_fusion), calls=%async_computation.2 | async-start | bytes 6291456 | tf_op jit(solution)/shard_map/all_to_all | solution.py:80
  111.3 43.2 %all-to-all-start.3 = ((bf16[4,384,1024]{2,1,0:T(8,128)(2,1)}), bf16[4,384,1024]{2,1,0:T(8,128)(2,1)}, u32[]{:S(2)}, u32[]{:S(2)}) async-start(bf16[4,384,1024]{2,1,0:T(8,128)(2,1)} %pad_maximum_fusion), calls=%async_computation.3 | async-start | bytes 6291456 | tf_op jit(solution)/shard_map/all_to_all | solution.py:92
  116.6 6.1 %copy-start = (bf16[384,4096]{1,0:T(8,128)(2,1)S(1)}, bf16[384,4096]{1,0:T(8,128)(2,1)}, u32[]{:S(2)}) copy-start(bf16[384,4096]{1,0:T(8,128)(2,1)} %reshape.99) | copy-start | bytes 9437188
  116.6 184.7 %all-gather.3.cloned.1.call-start = ((), (), s32[]{:S(2)}) async-start(), calls=%async_computation.7 | async-start | bytes 5898240 | tf_op jit(solution)/shard_map/all_gather | solution.py:131
  154.4 6.5 %copy-start.11 = (f32[384,768]{1,0:T(8,128)S(1)}, f32[384,768]{1,0:T(8,128)}, u32[]{:S(2)}) copy-start(f32[384,768]{1,0:T(8,128)} %fusion.6) | copy-start | bytes 3538948
  167.5 0.8 copy-start.5
  167.5 1.0 copy-start.7
  167.5 2.7 copy-start.4
  169.6 141.7 %reduce-scatter.2.cloned.1.call-start = ((), (), s32[]{:S(2)}) async-start(), calls=%async_computation.6 | async-start | bytes 7864320 | tf_op jit(solution)/shard_map/reduce_scatter | solution.py:137
  176.7 1.1 copy-start.8
  177.8 5.1 %copy-start.6 = (bf16[384,768]{1,0:T(8,128)(2,1)S(1)}, bf16[384,768]{1,0:T(8,128)(2,1)}, u32[]{:S(2)}) copy-start(bf16[384,768]{1,0:T(8,128)(2,1)} %copy-done.5) | copy-start | bytes 1769476
  193.9 44.7 %all-to-all-start.4 = ((bf16[32,48,1024]{2,1,0:T(8,128)(2,1)}), bf16[32,48,1024]{2,1,0:T(8,128)(2,1)S(1)}, u32[]{:S(2)}, u32[]{:S(2)}) async-start(bf16[32,48,1024]{2,1,0:T(8,128)(2,1)} %reshape.105), calls=%async_computation.4 | async-start | bytes 6291456 | tf_op jit(solution)/shard_map/all_to_all | solution.py:122
  238.7 1.7 copy-start.1
  240.3 44.9 %all-to-all-start.1 = ((bf16[32,48,1024]{2,1,0:T(8,128)(2,1)}), bf16[32,48,1024]{2,1,0:T(8,128)(2,1)}, u32[]{:S(2)}, u32[]{:S(2)}) async-start(bf16[32,48,1024]{2,1,0:T(8,128)(2,1)} %reshape.100), calls=%async_computation.1 | async-start | bytes 6291456 | tf_op jit(solution)/shard_map/all_to_all | solution.py:115
  289.8 3.2 copy-start.9
  293.0 3.9 %copy-start.2 = (bf16[256,4096]{1,0:T(8,128)(2,1)S(1)}, bf16[256,4096]{1,0:T(8,128)(2,1)}, u32[]{:S(2)}) copy-start(bf16[256,4096]{1,0:T(8,128)(2,1)} %gather_fusion.4) | copy-start | bytes 6291460
  296.8 2.1 copy-start.3
Sparse Core Ops, SparseCore 0:
  169.8 49.6 all-gather.2
  221.9 64.5 reduce-scatter.1

commit v8 on v7

--- a/solution.py
+++ b/solution.py
@@ -89,13 +89,12 @@
     grads_in = got_grads.reshape(-1, width)
     dp_count = lax.axis_size("dp")
     piece = width // dp_count
-    rows_all = lax.all_to_all(
-        jnp.stack([rows_in[:, part * piece:(part + 1) * piece] for part in range(dp_count)], axis=0),
-        "dp",
-        split_axis=0,
-        concat_axis=0,
-        tiled=True,
-    )
+    dp_index = lax.axis_index("dp")
+    arrived = [lax.dynamic_slice_in_dim(rows_in, dp_index * piece, piece, axis=1)]
+    for shift in range(1, dp_count):
+        outgoing = lax.dynamic_slice_in_dim(rows_in, ((dp_index + shift) % dp_count) * piece, piece, axis=1)
+        arrived.append(lax.ppermute(outgoing, "dp", [(j, (j + shift) % dp_count) for j in range(dp_count)]))
+    rows_all = jnp.stack(arrived, axis=0)
     gate_mat, up_mat, down_mat = w_gate[0], w_up[0], w_down[0]
     gate_pre = jnp.dot(rows_in, gate_mat, preferred_element_type=jnp.float32)
     up_pre = jnp.dot(rows_in, up_mat, preferred_element_type=jnp.float32)
@@ -128,7 +127,8 @@
         ),
     )
     joined_grads = jnp.concatenate([grad_gate_pre, grad_up_pre], axis=1)
-    joined_all = lax.all_gather(joined_grads, "dp", axis=0, tiled=False)
+    source_order = (dp_index - jnp.arange(dp_count)) % dp_count
+    joined_all = jnp.take(lax.all_gather(joined_grads, "dp", axis=0, tiled=False), source_order, axis=0)
     grad_joined = lax.dot_general(
         rows_all, joined_all, (((0, 1), (0, 1)), ((), ())), preferred_element_type=jnp.float32
     )

time: 323 us -> 297 us (0.920)
  waiting for transfers between devices: 135 us -> 104 us
  local copies, waits for them, and re-layouts: 71.9 us -> 78.6 us
  matrix products: 56.9 us -> 52.8 us
    all_to_all x1 -> x0, waiting for transfers between devices: 25.4 us -> none  [local(): lax.all_to_all(jnp.stack([rows_in[:, part * piece:(part + 1) * piece] for...]
    ppermute x0 -> x3, starting transfers between devices: none -> 5.9 us  [local(): lax.ppermute(outgoing, 'dp', [(j, (j + shift) % dp_count) for j in range(...]
    all_to_all x1, waiting for transfers between devices: 31.8 us -> 26.2 us  [local(): lax.all_to_all(send_grads.reshape(flat_shape), ('outer', 'inner'), split_...]
    gather x0 -> x1, local copies, waits for them, and re-layouts: none -> 5.44 us  [local(): jnp.take(lax.all_gather(joined_grads, 'dp', axis=0, tiled=False), source_...]
    all_to_all x1 -> x0, starting transfers between devices: 5.31 us -> none  [local(): lax.all_to_all(jnp.stack([rows_in[:, part * piece:(part + 1) * piece] for...]
    unnamed x27 -> x35, local copies, waits for them, and re-layouts: 7.82 us -> 7.74 us
  transfers between devices with their start and end apart: 7 -> 9, of which waited for: 5 -> 4; matrix products, arithmetic and copies ran while one was open for 34% -> 38% of each run, Pallas kernels for 0% -> 0%
where the time goes in v8:
time: 297 us; the launch traced here: 295 us
  waiting for transfers between devices  104 us (35%)
  local copies, waits for them, and re-layouts  78.6 us (26%)
  matrix products  52.8 us (18%)
  starting transfers between devices  29.5 us (10%)
  other arithmetic  15.2 us (5%)
  between operations  14.4 us (5%)
    all_to_all x1, waiting for transfers between devices, local(): lax.all_to_all(expert_out.reshape(flat_shape), ('outer', 'inner'), split_...  31.8 us
    all_to_all x1, waiting for transfers between devices, local(): lax.all_to_all(send_grads.reshape(flat_shape), ('outer', 'inner'), split_...  26.2 us
    all_to_all x1, waiting for transfers between devices, local(): lax.all_to_all(pair_grad.reshape(flat_shape), ('outer', 'inner'), split_a...  26.2 us
    all_to_all x1, waiting for transfers between devices, local(): lax.all_to_all(send_rows.reshape(flat_shape), ('outer', 'inner'), split_a...  19.9 us
    dot_general x3, matrix products, contract_last(): lax.dot_general(left, right, (((1,), (1,)), ((), ())), preferred_element_...  18.5 us
    dot_general x1, matrix products, local(): lax.dot_general(rows_all, joined_all, (((0, 1), (0, 1)), ((), ())), prefe...  8.01 us
    unnamed x35, local copies, waits for them, and re-layouts  7.74 us
    all_to_all x1, starting transfers between devices, local(): lax.all_to_all(send_rows.reshape(flat_shape), ('outer', 'inner'), split_a...  7.54 us
  transfers between devices with their start and end apart: 9, of which 4 were waited for; matrix products, arithmetic and copies ran while one was open for 38% of the time, Pallas kernels for 0%

profile of v8, /device:TPU:8, one launch (start us, length us, event | category | flops | bytes accessed | tf_op | source)
XLA Modules:
  0.0 294.6 jit_solution(7835931170010077268)
XLA Ops:
  19.4 7.5 %all-to-all-start = ((bf16[32,48,1024]{2,1,0:T(8,128)(2,1)}), bf16[32,48,1024]{2,1,0:T(8,128)(2,1)S(1)}, u32[]{:S(2)}, u32[]{:S(2)}) async-start(bf16[32,48,1024]{2,1,0:T(8,128)(2,1)} %reshape.152), calls=%async_computation | async-start | bytes 6291456 | tf_op jit(solution)/shard_map/all_to_all | solution.py:73
  27.9 4.0 %gather_fusion.3 = bf16[384,4096]{1,0:T(8,128)(2,1)} fusion(bf16[33,4096]{1,0:T(8,128)(2,1)S(1)} %concatenate.14, s32[1024]{0:T(1024)S(1)} %get-tuple-element.34), kind=kCustom, calls=%fused_computation.3 | custom fusion | bytes 6292992 | tf_op jit(solution)/shard_map/gather | solution.py:64
  31.9 6.4 %reshape.162 = f32[32,48,1024]{2,1,0:T(8,128)} reshape(bf16[384,4096]{1,0:T(8,128)(2,1)} %gather_fusion.3) | data formatting | bytes 9437184 | tf_op jit(solution)/shard_map/convert_element_type | solution.py:64
  41.6 4.9 %multiply_convert_fusion = bf16[32,48,1024]{2,1,0:T(8,128)(2,1)} fusion(f32[32,48,1024]{2,1,0:T(8,128)} %reshape.162, f32[32,48]{1,0:T(8,128)S(1)} %copy.22), kind=kLoop, calls=%fused_computation.22 | loop fusion | flops 3145728 | bytes 9443328 | tf_op jit(solution)/shard_map/convert_element_type | solution.py:65
  46.5 19.9 %all-to-all-done = bf16[32,48,1024]{2,1,0:T(8,128)(2,1)S(1)} async-done(((bf16[32,48,1024]{2,1,0:T(8,128)(2,1)}), bf16[32,48,1024]{2,1,0:T(8,128)(2,1)S(1)}, u32[]{:S(2)}, u32[]{:S(2)}) %all-to-all-start) | async-done | bytes 3145760 | tf_op jit(solution)/shard_map/all_to_all | solution.py:73
  66.4 5.3 %all-to-all-start.2 = ((bf16[32,48,1024]{2,1,0:T(8,128)(2,1)}), bf16[32,48,1024]{2,1,0:T(8,128)(2,1)}, u32[]{:S(2)}, u32[]{:S(2)}) async-start(bf16[32,48,1024]{2,1,0:T(8,128)(2,1)} %multiply_convert_fusion), calls=%async_computation.2 | async-start | bytes 6291456 | tf_op jit(solution)/shard_map/all_to_all | solution.py:80
  85.0 26.2 %all-to-all-done.2 = bf16[32,48,1024]{2,1,0:T(8,128)(2,1)} async-done(((bf16[32,48,1024]{2,1,0:T(8,128)(2,1)}), bf16[32,48,1024]{2,1,0:T(8,128)(2,1)}, u32[]{:S(2)}, u32[]{:S(2)}) %all-to-all-start.2) | async-done | bytes 3145760 | tf_op jit(solution)/shard_map/all_to_all | solution.py:80
  111.3 5.9 %reshape.158 = bf16[384,4096]{1,0:T(8,128)(2,1)} reshape(bf16[32,48,1024]{2,1,0:T(8,128)(2,1)} %all-to-all-done.2) | data formatting | bytes 6291456 | tf_op jit(solution)/shard_map/reshape | solution.py:89
  117.2 5.4 %fusion.6 = f32[384,768]{1,0:T(8,128)S(1)} fusion(bf16[384,4096]{1,0:T(8,128)(2,1)S(1)} %copy-done, bf16[1,4096,768]{2,1,0:T(8,128)(2,1)} %param.12), kind=kOutput, calls=%fused_computation.15 | convolution fusion | flops 2415919104 | bytes 10616832 | tf_op jit(solution)/shard_map/dot_general | solution.py:100
  126.0 6.1 %fusion = f32[384,768]{1,0:T(8,128)S(1)} fusion(bf16[384,4096]{1,0:T(8,128)(2,1)S(1)} %copy-done.5, bf16[1,768,4096]{2,1,0:T(8,128)(2,1)} %param.13), kind=kOutput, calls=%fused_computation.9 | convolution fusion | flops 2415919104 | bytes 10616832 | tf_op jit(solution)/shard_map/dot_general | solution.py:8
  132.2 3.9 %multiply_convert_fusion.2 = (bf16[384,768]{1,0:T(8,128)(2,1)S(1)}, bf16[384,768]{1,0:T(8,128)(2,1)S(1)}, bf16[384,768]{1,0:T(8,128)(2,1)}) fusion(f32[384,768]{1,0:T(8,128)S(1)} %fusion, f32[384,768]{1,0:T(8,128)S(1)} %fusion.6, bf16[384,4096]{1,0:T(8,128)(2,1)S(1)} %copy-done, bf16[1,4096,768]{2,1,0:T(8,128)(2,1)S(1)} %bitcast.86), kind=kOutput, calls=%fused_computation.37 | convolution fusion | flops 2420342784 | bytes 13565952 | tf_op jit(solution)/shard_map/dot_general | solution.py:99
  138.8 6.5 %convolution_convert_fusion = bf16[4096,768]{1,0:T(8,128)(2,1)} fusion(bf16[384,4096]{1,0:T(8,128)(2,1)S(1)} %copy-done.6, bf16[384,768]{1,0:T(8,128)(2,1)} %get-tuple-element.30), kind=kOutput, calls=%fused_computation.7 | convolution fusion | flops 2419064832 | bytes 10027008 | tf_op jit(solution)/shard_map/dot_general | solution.py:14
  146.3 5.1 %fusion.4 = f32[384,4096]{1,0:T(8,128)S(1)} fusion(bf16[384,768]{1,0:T(8,128)(2,1)S(1)} %copy-done.11, bf16[1,4096,768]{2,1,0:T(8,128)(2,1)} %param.12), kind=kOutput, calls=%fused_computation.13 | convolution fusion | flops 2415919104 | bytes 13172736 | tf_op jit(solution)/shard_map/dot_general | solution.py:8
  151.5 7.3 %add_convert_fusion = bf16[384,4096]{1,0:T(8,128)(2,1)S(1)} fusion(f32[384,4096]{1,0:T(8,128)S(1)} %fusion.4, bf16[384,768]{1,0:T(8,128)(2,1)S(1)} %copy-done.9, bf16[1,4096,768]{2,1,0:T(8,128)(2,1)} %param.11), kind=kOutput, calls=%fused_computation.21 | convolution fusion | flops 2419064832 | bytes 16318464 | tf_op jit(solution)/shard_map/dot_general | solution.py:8
  162.4 5.3 %all-to-all-start.3 = ((bf16[32,48,1024]{2,1,0:T(8,128)(2,1)}), bf16[32,48,1024]{2,1,0:T(8,128)(2,1)S(1)}, u32[]{:S(2)}, u32[]{:S(2)}) async-start(bf16[32,48,1024]{2,1,0:T(8,128)(2,1)} %reshape.159), calls=%async_computation.3 | async-start | bytes 6291456 | tf_op jit(solution)/shard_map/all_to_all | solution.py:121
  167.8 7.3 %fusion.14 = bf16[384,4096]{1,0:T(8,128)(2,1)} fusion(bf16[384,768]{1,0:T(8,128)(2,1)} %get-tuple-element.30, bf16[1,768,4096]{2,1,0:T(8,128)(2,1)} %param.13), kind=kOutput, calls=%fused_computation.23 | convolution fusion | flops 2417491968 | bytes 10027008 | tf_op jit(solution)/shard_map/dot_general | solution.py:104
  175.1 6.0 %reshape.154 = bf16[32,48,1024]{2,1,0:T(8,128)(2,1)} reshape(bf16[384,4096]{1,0:T(8,128)(2,1)} %fusion.14) | data formatting | bytes 6291456 | tf_op jit(solution)/shard_map/reshape | solution.py:115
  181.1 26.2 %all-to-all-done.3 = bf16[32,48,1024]{2,1,0:T(8,128)(2,1)S(1)} async-done(((bf16[32,48,1024]{2,1,0:T(8,128)(2,1)}), bf16[32,48,1024]{2,1,0:T(8,128)(2,1)S(1)}, u32[]{:S(2)}, u32[]{:S(2)}) %all-to-all-start.3) | async-done | bytes 3145760 | tf_op jit(solution)/shard_map/all_to_all | solution.py:121
  208.9 5.3 %all-to-all-start.1 = ((bf16[32,48,1024]{2,1,0:T(8,128)(2,1)}), bf16[32,48,1024]{2,1,0:T(8,128)(2,1)}, u32[]{:S(2)}, u32[]{:S(2)}) async-start(bf16[32,48,1024]{2,1,0:T(8,128)(2,1)} %reshape.154), calls=%async_computation.1 | async-start | bytes 6291456 | tf_op jit(solution)/shard_map/all_to_all | solution.py:114
  214.3 4.5 %reshape.160 = bf16[384,4096]{1,0:T(8,128)(2,1)S(1)} reshape(bf16[32,48,1024]{2,1,0:T(8,128)(2,1)} %copy-done.1) | data formatting | bytes 6291456 | tf_op jit(solution)/shard_map/reshape | solution.py:147
  222.1 31.8 %all-to-all-done.1 = bf16[32,48,1024]{2,1,0:T(8,128)(2,1)} async-done(((bf16[32,48,1024]{2,1,0:T(8,128)(2,1)}), bf16[32,48,1024]{2,1,0:T(8,128)(2,1)}, u32[]{:S(2)}, u32[]{:S(2)}) %all-to-all-start.1) | async-done | bytes 3145760 | tf_op jit(solution)/shard_map/all_to_all | solution.py:114
  253.8 4.5 %reshape.155 = bf16[384,4096]{1,0:T(8,128)(2,1)S(1)} reshape(bf16[32,48,1024]{2,1,0:T(8,128)(2,1)} %all-to-all-done.1) | data formatting | bytes 6291456 | tf_op jit(solution)/shard_map/reshape | solution.py:146
  269.9 5.4 %gather_fusion.5 = bf16[4,384,1536]{2,1,0:T(8,128)(2,1)} fusion(bf16[4,384,1536]{2,1,0:T(8,128)(2,1)} %bitcast.77, s32[1024]{0:T(1024)S(1)} %pad_clamp_fusion), kind=kCustom, calls=%fused_computation.5 | custom fusion | bytes 9437200 | tf_op jit(solution)/shard_map/jit(_take)/gather | solution.py:131
  275.3 8.0 %bitcast_convert_fusion = bf16[1024,1536]{1,0:T(8,128)(2,1)S(1)} fusion(bf16[4,384,1024]{2,1,0:T(8,128)(2,1)S(1)} %copy-done.4, bf16[4,384,1536]{2,1,0:T(8,128)(2,1)} %gather_fusion.5, pred[4]{0:T(512)(128)(4,1)S(1)} %compare_and_fusion), kind=kOutput, calls=%fused_computation.8 | convolution fusion | flops 4835770368 | bytes 11010052 | tf_op jit(solution)/shard_map/dot_general | solution.py:132
  (91 shorter events, 61.3 us)
Async XLA Ops:
  19.4 47.0 %all-to-all-start = ((bf16[32,48,1024]{2,1,0:T(8,128)(2,1)}), bf16[32,48,1024]{2,1,0:T(8,128)(2,1)S(1)}, u32[]{:S(2)}, u32[]{:S(2)}) async-start(bf16[32,48,1024]{2,1,0:T(8,128)(2,1)} %reshape.152), calls=%async_computation | async-start | bytes 6291456 | tf_op jit(solution)/shard_map/all_to_all | solution.py:73
  31.9 6.4 %copy-start.13 = (f32[32,8]{0,1:T(8,128)S(1)}, f32[32,8]{0,1:T(8,128)}, u32[]{:S(2)}) copy-start(f32[32,8]{0,1:T(8,128)} %param.9) | copy-start | bytes 3076
  66.4 44.9 %all-to-all-start.2 = ((bf16[32,48,1024]{2,1,0:T(8,128)(2,1)}), bf16[32,48,1024]{2,1,0:T(8,128)(2,1)}, u32[]{:S(2)}, u32[]{:S(2)}) async-start(bf16[32,48,1024]{2,1,0:T(8,128)(2,1)} %multiply_convert_fusion), calls=%async_computation.2 | async-start | bytes 6291456 | tf_op jit(solution)/shard_map/all_to_all | solution.py:80
  71.7 198.2 %all-gather.3.cloned.1.call-start = ((), (), s32[]{:S(2)}) async-start(), calls=%async_computation.6 | async-start | bytes 5898240 | tf_op jit(solution)/shard_map/all_gather | solution.py:131
  79.1 43.5 %collective-permute-start.1 = (bf16[384,1024]{1,0:T(8,128)(2,1)}, bf16[384,1024]{1,0:T(8,128)(2,1)}, u32[]{:S(2)}, u32[]{:S(2)}) collective-permute-start(bf16[384,1024]{1,0:T(8,128)(2,1)} %get-tuple-element.26), channel_id=1, source_target_pairs={{0,64},{32,96},{64,0},{96,32},{1,65},{33,97},{65,1},{97,33},{2,66}... | collective-permute-start | bytes 2359304 | tf_op jit(solution)/shard_map/ppermute | solution.py:96
  83.0 39.7 %collective-permute-start.2 = (bf16[384,1024]{1,0:T(8,128)(2,1)}, bf16[384,1024]{1,0:T(8,128)(2,1)}, u32[]{:S(2)}, u32[]{:S(2)}) collective-permute-start(bf16[384,1024]{1,0:T(8,128)(2,1)} %get-tuple-element.25), channel_id=1, source_target_pairs={{0,96},{32,0},{64,32},{96,64},{1,97},{33,1},{65,33},{97,65},{2,98}... | collective-permute-start | bytes 2359304 | tf_op jit(solution)/shard_map/ppermute | solution.py:96
  83.7 33.5 %copy-start = (bf16[384,4096]{1,0:T(8,128)(2,1)S(1)}, bf16[384,4096]{1,0:T(8,128)(2,1)}, u32[]{:S(2)}) copy-start(bf16[384,4096]{1,0:T(8,128)(2,1)} %reshape.153) | copy-start | bytes 9437188
  83.7 39.0 %collective-permute-start = (bf16[384,1024]{1,0:T(8,128)(2,1)}, bf16[384,1024]{1,0:T(8,128)(2,1)}, u32[]{:S(2)}, u32[]{:S(2)}) collective-permute-start(bf16[384,1024]{1,0:T(8,128)(2,1)} %get-tuple-element.27), channel_id=1, source_target_pairs={{0,32},{32,64},{64,96},{96,0},{1,33},{33,65},{65,97},{97,1},{2,34}... | collective-permute-start | bytes 2359304 | tf_op jit(solution)/shard_map/ppermute | solution.py:96
  117.2 5.5 %copy-start.7 = (bf16[1,384,1024]{2,1,0:T(8,128)(2,1)S(1)}, bf16[1,384,1024]{2,1,0:T(8,128)(2,1)}, u32[]{:S(2)}) copy-start(bf16[1,384,1024]{2,1,0:T(8,128)(2,1)} %get-tuple-element.24) | copy-start | bytes 2359300
  122.7 3.3 %copy-start.5 = (bf16[384,4096]{1,0:T(8,128)(2,1)S(1)}, bf16[384,4096]{1,0:T(8,128)(2,1)}, u32[]{:S(2)}) copy-start(bf16[384,4096]{1,0:T(8,128)(2,1)} %reshape.158) | copy-start | bytes 9437188
  122.7 9.4 %slice-start = ((s8[6291456]{0:T(1024)(128)(4,1)}), s8[4194304]{0:T(1024)(128)(4,1)S(1)}, s32[]{:S(2)}) async-start(s8[6291456]{0:T(1024)(128)(4,1)} %bitcast.85), calls=%async_computation.7 | async-start | bytes 8388608
  126.0 6.2 %slice-start.1 = ((s8[6291456]{0:T(1024)(128)(4,1)}), s8[2097152]{0:T(1024)(128)(4,1)S(1)}, s32[]{:S(2)}) async-start(s8[6291456]{0:T(1024)(128)(4,1)} %bitcast.85), calls=%async_computation.8 | async-start | bytes 4194304
  136.1 1.0 copy-start.10
  136.1 2.7 copy-start.6
  138.2 147.0 %reduce-scatter.2.cloned.1.call-start = ((), (), s32[]{:S(2)}) async-start(), calls=%async_computation.5 | async-start | bytes 7864320 | tf_op jit(solution)/shard_map/reduce_scatter | solution.py:137
  145.3 1.1 copy-start.11
  146.3 5.1 %copy-start.9 = (bf16[384,768]{1,0:T(8,128)(2,1)S(1)}, bf16[384,768]{1,0:T(8,128)(2,1)}, u32[]{:S(2)}) copy-start(bf16[384,768]{1,0:T(8,128)(2,1)} %copy-done.8) | copy-start | bytes 1769476
  162.4 44.8 %all-to-all-start.3 = ((bf16[32,48,1024]{2,1,0:T(8,128)(2,1)}), bf16[32,48,1024]{2,1,0:T(8,128)(2,1)S(1)}, u32[]{:S(2)}, u32[]{:S(2)}) async-start(bf16[32,48,1024]{2,1,0:T(8,128)(2,1)} %reshape.159), calls=%async_computation.3 | async-start | bytes 6291456 | tf_op jit(solution)/shard_map/all_to_all | solution.py:121
  207.3 1.7 copy-start.1
  208.9 44.9 %all-to-all-start.1 = ((bf16[32,48,1024]{2,1,0:T(8,128)(2,1)}), bf16[32,48,1024]{2,1,0:T(8,128)(2,1)}, u32[]{:S(2)}, u32[]{:S(2)}) async-start(bf16[32,48,1024]{2,1,0:T(8,128)(2,1)} %reshape.154), calls=%async_computation.1 | async-start | bytes 6291456 | tf_op jit(solution)/shard_map/all_to_all | solution.py:114
  258.3 3.2 %copy-start.12 = (bf16[32,4096]{1,0:T(8,128)(2,1)S(1)}, bf16[32,4096]{1,0:T(8,128)(2,1)}, u32[]{:S(2)}) copy-start(bf16[32,4096]{1,0:T(8,128)(2,1)} %param.10) | copy-start | bytes 786436
  261.5 3.9 %copy-start.2 = (bf16[256,4096]{1,0:T(8,128)(2,1)S(1)}, bf16[256,4096]{1,0:T(8,128)(2,1)}, u32[]{:S(2)}) copy-start(bf16[256,4096]{1,0:T(8,128)(2,1)} %gather_fusion.4) | copy-start | bytes 6291460
  265.4 2.1 copy-start.3
  269.9 5.4 %copy-start.4 = (bf16[4,384,1024]{2,1,0:T(8,128)(2,1)S(1)}, bf16[4,384,1024]{2,1,0:T(8,128)(2,1)}, u32[]{:S(2)}) copy-start(bf16[4,384,1024]{2,1,0:T(8,128)(2,1)} %pad_maximum_fusion) | copy-start | bytes 9437188
  (1 other events, 0.8 us)
Sparse Core Ops, SparseCore 0:
  138.3 52.8 all-gather.2
  193.6 64.4 reduce-scatter.1

commit v9 on v8

--- a/solution.py
+++ b/solution.py
@@ -102,7 +102,7 @@
     silu_value = gate_pre * sigma
     hidden = (silu_value * up_pre).astype(jnp.bfloat16)
     expert_out = jnp.dot(hidden, down_mat, preferred_element_type=jnp.float32).astype(jnp.bfloat16)
-    grads_in, rows_all = lax.optimization_barrier((grads_in, rows_all))
+    grads_in, rows_all, expert_out = lax.optimization_barrier((grads_in, rows_all, expert_out))
     grad_hidden = contract_last(grads_in, down_mat)
     slope = sigma * (1.0 + gate_pre * (1.0 - sigma))
     grad_gate_pre = (grad_hidden * up_pre * slope).astype(jnp.bfloat16)

time: 297 us -> 281 us (0.946)
  waiting for transfers between devices: 104 us -> 83.6 us
    all_to_all x1, waiting for transfers between devices: 31.8 us -> 20 us  [local(): lax.all_to_all(expert_out.reshape(flat_shape), ('outer', 'inner'), split_...]
    all_to_all x1, waiting for transfers between devices: 26.2 us -> 15.9 us  [local(): lax.all_to_all(send_grads.reshape(flat_shape), ('outer', 'inner'), split_...]
  transfers between devices with their start and end apart: 9 -> 9, of which waited for: 4 -> 4; matrix products, arithmetic and copies ran while one was open for 38% -> 43% of each run, Pallas kernels for 0% -> 0%
where the time goes in v9:
time: 281 us; the launch traced here: 278 us
  waiting for transfers between devices  83.6 us (30%)
  local copies, waits for them, and re-layouts  79.6 us (28%)
  matrix products  54.1 us (19%)
  starting transfers between devices  29.3 us (10%)
  other arithmetic  16.9 us (6%)
  between operations  14.4 us (5%)
    all_to_all x1, waiting for transfers between devices, local(): lax.all_to_all(pair_grad.reshape(flat_shape), ('outer', 'inner'), split_a...  27.8 us
    all_to_all x1, waiting for transfers between devices, local(): lax.all_to_all(expert_out.reshape(flat_shape), ('outer', 'inner'), split_...  20 us
    all_to_all x1, waiting for transfers between devices, local(): lax.all_to_all(send_rows.reshape(flat_shape), ('outer', 'inner'), split_a...  19.8 us
    dot_general x3, matrix products, contract_last(): lax.dot_general(left, right, (((1,), (1,)), ((), ())), preferred_element_...  19.4 us
    all_to_all x1, waiting for transfers between devices, local(): lax.all_to_all(send_grads.reshape(flat_shape), ('outer', 'inner'), split_...  15.9 us
    unnamed x35, local copies, waits for them, and re-layouts  8.26 us
    dot_general x1, matrix products, contract_first(): lax.dot_general(left, right, (((0,), (0,)), ((), ())), preferred_element_...  8.15 us
    dot_general x1, matrix products, local(): lax.dot_general(rows_all, joined_all, (((0, 1), (0, 1)), ((), ())), prefe...  8 us
  transfers between devices with their start and end apart: 9, of which 4 were waited for; matrix products, arithmetic and copies ran while one was open for 43% of the time, Pallas kernels for 0%

profile of v9, /device:TPU:8, one launch (start us, length us, event | category | flops | bytes accessed | tf_op | source)
XLA Modules:
  0.0 277.9 jit_solution(13582877376663010519)
XLA Ops:
  19.4 7.7 %all-to-all-start.1 = ((bf16[32,48,1024]{2,1,0:T(8,128)(2,1)}), bf16[32,48,1024]{2,1,0:T(8,128)(2,1)S(1)}, u32[]{:S(2)}, u32[]{:S(2)}) async-start(bf16[32,48,1024]{2,1,0:T(8,128)(2,1)} %reshape.154), calls=%async_computation.1 | async-start | bytes 6291456 | tf_op jit(solution)/shard_map/all_to_all | solution.py:73
  31.3 4.1 %gather_fusion.1 = bf16[384,4096]{1,0:T(8,128)(2,1)} fusion(bf16[33,4096]{1,0:T(8,128)(2,1)S(1)} %concatenate.13, s32[1024]{0:T(1024)S(1)} %get-tuple-element.36), kind=kCustom, calls=%fused_computation.1 | custom fusion | bytes 6292992 | tf_op jit(solution)/shard_map/gather | solution.py:64
  35.4 6.4 %reshape.162 = f32[32,48,1024]{2,1,0:T(8,128)} reshape(bf16[384,4096]{1,0:T(8,128)(2,1)} %gather_fusion.1) | data formatting | bytes 9437184 | tf_op jit(solution)/shard_map/convert_element_type | solution.py:64
  41.8 4.9 %multiply_convert_fusion = bf16[32,48,1024]{2,1,0:T(8,128)(2,1)} fusion(f32[32,48,1024]{2,1,0:T(8,128)} %reshape.162, f32[32,48]{1,0:T(8,128)S(1)} %copy.22), kind=kLoop, calls=%fused_computation.22 | loop fusion | flops 3145728 | bytes 9443328 | tf_op jit(solution)/shard_map/convert_element_type | solution.py:65
  46.7 19.8 %all-to-all-done.1 = bf16[32,48,1024]{2,1,0:T(8,128)(2,1)S(1)} async-done(((bf16[32,48,1024]{2,1,0:T(8,128)(2,1)}), bf16[32,48,1024]{2,1,0:T(8,128)(2,1)S(1)}, u32[]{:S(2)}, u32[]{:S(2)}) %all-to-all-start.1) | async-done | bytes 3145760 | tf_op jit(solution)/shard_map/all_to_all | solution.py:73
  66.5 5.3 %all-to-all-start = ((bf16[32,48,1024]{2,1,0:T(8,128)(2,1)}), bf16[32,48,1024]{2,1,0:T(8,128)(2,1)}, u32[]{:S(2)}, u32[]{:S(2)}) async-start(bf16[32,48,1024]{2,1,0:T(8,128)(2,1)} %multiply_convert_fusion), calls=%async_computation | async-start | bytes 6291456 | tf_op jit(solution)/shard_map/all_to_all | solution.py:80
  79.4 4.0 %collective-permute-start.2 = (bf16[384,1024]{1,0:T(8,128)(2,1)}, bf16[384,1024]{1,0:T(8,128)(2,1)}, u32[]{:S(2)}, u32[]{:S(2)}) collective-permute-start(bf16[384,1024]{1,0:T(8,128)(2,1)} %get-tuple-element.27), channel_id=1, source_target_pairs={{0,96},{32,0},{64,32},{96,64},{1,97},{33,1},{65,33},{97,65},{2,98}... | collective-permute-start | bytes 2359304 | tf_op jit(solution)/shard_map/ppermute | solution.py:96
  84.7 6.0 %fusion.10 = f32[384,768]{1,0:T(8,128)S(1)} fusion(bf16[384,4096]{1,0:T(8,128)(2,1)S(1)} %copy-done.1, bf16[1,4096,768]{2,1,0:T(8,128)(2,1)} %param.11), kind=kOutput, calls=%fused_computation.19 | convolution fusion | flops 2415919104 | bytes 10616832 | tf_op jit(solution)/shard_map/dot_general | solution.py:99
  95.5 15.9 %all-to-all-done = bf16[32,48,1024]{2,1,0:T(8,128)(2,1)} async-done(((bf16[32,48,1024]{2,1,0:T(8,128)(2,1)}), bf16[32,48,1024]{2,1,0:T(8,128)(2,1)}, u32[]{:S(2)}, u32[]{:S(2)}) %all-to-all-start) | async-done | bytes 3145760 | tf_op jit(solution)/shard_map/all_to_all | solution.py:80
  111.4 6.0 %reshape.153 = bf16[384,4096]{1,0:T(8,128)(2,1)} reshape(bf16[32,48,1024]{2,1,0:T(8,128)(2,1)} %all-to-all-done) | data formatting | bytes 6291456 | tf_op jit(solution)/shard_map/reshape | solution.py:89
  117.3 5.6 %fusion.14 = bf16[384,4096]{1,0:T(8,128)(2,1)S(1)} fusion(bf16[384,768]{1,0:T(8,128)(2,1)} %get-tuple-element.34, bf16[1,768,4096]{2,1,0:T(8,128)(2,1)} %param.13), kind=kOutput, calls=%fused_computation.23 | convolution fusion | flops 2417491968 | bytes 10027008 | tf_op jit(solution)/shard_map/dot_general | solution.py:104
  127.5 6.0 %multiply_convert_fusion.2 = (bf16[384,768]{1,0:T(8,128)(2,1)S(1)}, bf16[384,768]{1,0:T(8,128)(2,1)S(1)}) fusion(f32[384,768]{1,0:T(8,128)S(1)} %copy-done.12, f32[384,768]{1,0:T(8,128)S(1)} %copy-done.13, bf16[384,4096]{1,0:T(8,128)(2,1)S(1)} %copy-done.4, bf16[1,768,4096]{2,1,0:T(8,128)(2,1)} %param.13), kind=kOutput, calls=%fused_computation.37 | convolution fusion | flops 2419752960 | bytes 12976128 | tf_op jit(solution)/shard_map/dot_general | solution.py:8
  135.8 8.1 %convolution_convert_fusion = bf16[4096,768]{1,0:T(8,128)(2,1)} fusion(bf16[384,4096]{1,0:T(8,128)(2,1)} %reshape.153, bf16[384,768]{1,0:T(8,128)(2,1)} %get-tuple-element.34), kind=kOutput, calls=%fused_computation.7 | convolution fusion | flops 2419064832 | bytes 10027008 | tf_op jit(solution)/shard_map/dot_general | solution.py:14
  147.7 5.5 %all-to-all-start.2 = ((bf16[32,48,1024]{2,1,0:T(8,128)(2,1)}), bf16[32,48,1024]{2,1,0:T(8,128)(2,1)S(1)}, u32[]{:S(2)}, u32[]{:S(2)}) async-start(bf16[32,48,1024]{2,1,0:T(8,128)(2,1)} %reshape.156), calls=%async_computation.2 | async-start | bytes 6291456 | tf_op jit(solution)/shard_map/all_to_all | solution.py:114
  153.2 5.0 %fusion.4 = f32[384,4096]{1,0:T(8,128)S(1)} fusion(bf16[384,768]{1,0:T(8,128)(2,1)} %copy-done.8, bf16[1,4096,768]{2,1,0:T(8,128)(2,1)} %param.12), kind=kOutput, calls=%fused_computation.13 | convolution fusion | flops 2415919104 | bytes 13172736 | tf_op jit(solution)/shard_map/dot_general | solution.py:8
  158.2 8.5 %add_convert_fusion = bf16[384,4096]{1,0:T(8,128)(2,1)} fusion(f32[384,4096]{1,0:T(8,128)S(1)} %fusion.4, bf16[384,768]{1,0:T(8,128)(2,1)S(1)} %copy-done.7, bf16[1,4096,768]{2,1,0:T(8,128)(2,1)} %param.11), kind=kOutput, calls=%fused_computation.21 | convolution fusion | flops 2419064832 | bytes 16318464 | tf_op jit(solution)/shard_map/dot_general | solution.py:8
  166.6 6.0 %reshape.159 = bf16[32,48,1024]{2,1,0:T(8,128)(2,1)} reshape(bf16[384,4096]{1,0:T(8,128)(2,1)} %add_convert_fusion) | data formatting | bytes 6291456 | tf_op jit(solution)/shard_map/reshape | solution.py:122
  172.6 20.0 %all-to-all-done.2 = bf16[32,48,1024]{2,1,0:T(8,128)(2,1)S(1)} async-done(((bf16[32,48,1024]{2,1,0:T(8,128)(2,1)}), bf16[32,48,1024]{2,1,0:T(8,128)(2,1)S(1)}, u32[]{:S(2)}, u32[]{:S(2)}) %all-to-all-start.2) | async-done | bytes 3145760 | tf_op jit(solution)/shard_map/all_to_all | solution.py:114
  194.3 5.3 %all-to-all-start.3 = ((bf16[32,48,1024]{2,1,0:T(8,128)(2,1)}), bf16[32,48,1024]{2,1,0:T(8,128)(2,1)}, u32[]{:S(2)}, u32[]{:S(2)}) async-start(bf16[32,48,1024]{2,1,0:T(8,128)(2,1)} %reshape.159), calls=%async_computation.3 | async-start | bytes 6291456 | tf_op jit(solution)/shard_map/all_to_all | solution.py:121
  199.7 4.7 %reshape.157 = bf16[384,4096]{1,0:T(8,128)(2,1)S(1)} reshape(bf16[32,48,1024]{2,1,0:T(8,128)(2,1)} %copy-done) | data formatting | bytes 6291456 | tf_op jit(solution)/shard_map/reshape | solution.py:146
  211.3 27.8 %all-to-all-done.3 = bf16[32,48,1024]{2,1,0:T(8,128)(2,1)} async-done(((bf16[32,48,1024]{2,1,0:T(8,128)(2,1)}), bf16[32,48,1024]{2,1,0:T(8,128)(2,1)}, u32[]{:S(2)}, u32[]{:S(2)}) %all-to-all-start.3) | async-done | bytes 3145760 | tf_op jit(solution)/shard_map/all_to_all | solution.py:121
  239.1 4.5 %reshape.160 = bf16[384,4096]{1,0:T(8,128)(2,1)S(1)} reshape(bf16[32,48,1024]{2,1,0:T(8,128)(2,1)} %all-to-all-done.3) | data formatting | bytes 6291456 | tf_op jit(solution)/shard_map/reshape | solution.py:147
  253.0 5.6 %gather_fusion.5 = bf16[4,384,1536]{2,1,0:T(8,128)(2,1)} fusion(bf16[4,384,1536]{2,1,0:T(8,128)(2,1)} %bitcast.80, s32[1024]{0:T(1024)S(1)} %pad_clamp_fusion), kind=kCustom, calls=%fused_computation.5 | custom fusion | bytes 9437200 | tf_op jit(solution)/shard_map/jit(_take)/gather | solution.py:131
  258.6 8.0 %bitcast_convert_fusion = bf16[1024,1536]{1,0:T(8,128)(2,1)S(1)} fusion(bf16[4,384,1024]{2,1,0:T(8,128)(2,1)S(1)} %copy-done.3, bf16[4,384,1536]{2,1,0:T(8,128)(2,1)} %gather_fusion.5, pred[4]{0:T(512)(128)(4,1)S(1)} %compare_and_fusion), kind=kOutput, calls=%fused_computation.8 | convolution fusion | flops 4835770368 | bytes 11010052 | tf_op jit(solution)/shard_map/dot_general | solution.py:132
  (91 shorter events, 62.9 us)
Async XLA Ops:
  19.4 7.7 %copy-start.10 = (f32[32,8]{0,1:T(8,128)S(1)}, f32[32,8]{0,1:T(8,128)}, u32[]{:S(2)}) copy-start(f32[32,8]{0,1:T(8,128)} %param.9) | copy-start | bytes 3076
  19.4 47.2 %all-to-all-start.1 = ((bf16[32,48,1024]{2,1,0:T(8,128)(2,1)}), bf16[32,48,1024]{2,1,0:T(8,128)(2,1)S(1)}, u32[]{:S(2)}, u32[]{:S(2)}) async-start(bf16[32,48,1024]{2,1,0:T(8,128)(2,1)} %reshape.154), calls=%async_computation.1 | async-start | bytes 6291456 | tf_op jit(solution)/shard_map/all_to_all | solution.py:73
  66.5 44.9 %all-to-all-start = ((bf16[32,48,1024]{2,1,0:T(8,128)(2,1)}), bf16[32,48,1024]{2,1,0:T(8,128)(2,1)}, u32[]{:S(2)}, u32[]{:S(2)}) async-start(bf16[32,48,1024]{2,1,0:T(8,128)(2,1)} %multiply_convert_fusion), calls=%async_computation | async-start | bytes 6291456 | tf_op jit(solution)/shard_map/all_to_all | solution.py:80
  71.8 181.2 %all-gather.3.cloned.1.call-start = ((), (), s32[]{:S(2)}) async-start(), calls=%async_computation.6 | async-start | bytes 5898240 | tf_op jit(solution)/shard_map/all_gather | solution.py:131
  75.6 9.0 %copy-start.1 = (bf16[384,4096]{1,0:T(8,128)(2,1)S(1)}, bf16[384,4096]{1,0:T(8,128)(2,1)}, u32[]{:S(2)}) copy-start(bf16[384,4096]{1,0:T(8,128)(2,1)} %reshape.155) | copy-start | bytes 9437188
  79.4 43.6 %collective-permute-start.2 = (bf16[384,1024]{1,0:T(8,128)(2,1)}, bf16[384,1024]{1,0:T(8,128)(2,1)}, u32[]{:S(2)}, u32[]{:S(2)}) collective-permute-start(bf16[384,1024]{1,0:T(8,128)(2,1)} %get-tuple-element.27), channel_id=1, source_target_pairs={{0,96},{32,0},{64,32},{96,64},{1,97},{33,1},{65,33},{97,65},{2,98}... | collective-permute-start | bytes 2359304 | tf_op jit(solution)/shard_map/ppermute | solution.py:96
  83.4 39.6 %collective-permute-start.1 = (bf16[384,1024]{1,0:T(8,128)(2,1)}, bf16[384,1024]{1,0:T(8,128)(2,1)}, u32[]{:S(2)}, u32[]{:S(2)}) collective-permute-start(bf16[384,1024]{1,0:T(8,128)(2,1)} %get-tuple-element.28), channel_id=1, source_target_pairs={{0,64},{32,96},{64,0},{96,32},{1,65},{33,97},{65,1},{97,33},{2,66}... | collective-permute-start | bytes 2359304 | tf_op jit(solution)/shard_map/ppermute | solution.py:96
  83.4 8.3 %slice-start = ((s8[6291456]{0:T(1024)(128)(4,1)}), s8[4194304]{0:T(1024)(128)(4,1)S(1)}, s32[]{:S(2)}) async-start(s8[6291456]{0:T(1024)(128)(4,1)} %bitcast.88), calls=%async_computation.7 | async-start | bytes 8388608
  83.4 8.3 %slice-start.1 = ((s8[6291456]{0:T(1024)(128)(4,1)}), s8[2097152]{0:T(1024)(128)(4,1)S(1)}, s32[]{:S(2)}) async-start(s8[6291456]{0:T(1024)(128)(4,1)} %bitcast.88), calls=%async_computation.8 | async-start | bytes 4194304
  83.4 39.6 %collective-permute-start = (bf16[384,1024]{1,0:T(8,128)(2,1)}, bf16[384,1024]{1,0:T(8,128)(2,1)}, u32[]{:S(2)}, u32[]{:S(2)}) collective-permute-start(bf16[384,1024]{1,0:T(8,128)(2,1)} %get-tuple-element.29), channel_id=1, source_target_pairs={{0,32},{32,64},{64,96},{96,0},{1,33},{33,65},{65,97},{97,1},{2,34}... | collective-permute-start | bytes 2359304 | tf_op jit(solution)/shard_map/ppermute | solution.py:96
  90.7 1.0 copy-start.11
  117.3 5.7 %copy-start.5 = (bf16[1,384,1024]{2,1,0:T(8,128)(2,1)S(1)}, bf16[1,384,1024]{2,1,0:T(8,128)(2,1)}, u32[]{:S(2)}) copy-start(bf16[1,384,1024]{2,1,0:T(8,128)(2,1)} %get-tuple-element.26) | copy-start | bytes 2359300
  123.0 3.3 %copy-start.4 = (bf16[384,4096]{1,0:T(8,128)(2,1)S(1)}, bf16[384,4096]{1,0:T(8,128)(2,1)}, u32[]{:S(2)}) copy-start(bf16[384,4096]{1,0:T(8,128)(2,1)} %reshape.153) | copy-start | bytes 9437188
  123.1 3.8 %copy-start.12 = (f32[384,768]{1,0:T(8,128)S(1)}, f32[384,768]{1,0:T(8,128)}, u32[]{:S(2)}) copy-start(f32[384,768]{1,0:T(8,128)} %copy-done.11) | copy-start | bytes 3538948
  123.1 4.4 %copy-start.13 = (f32[384,768]{1,0:T(8,128)S(1)}, f32[384,768]{1,0:T(8,128)}, u32[]{:S(2)}) copy-start(f32[384,768]{1,0:T(8,128)} %get-tuple-element.35) | copy-start | bytes 3538948
  133.4 1.0 copy-start.8
  135.6 133.0 %reduce-scatter.2.cloned.1.call-start = ((), (), s32[]{:S(2)}) async-start(), calls=%async_computation.5 | async-start | bytes 7864320 | tf_op jit(solution)/shard_map/reduce_scatter | solution.py:137
  147.7 45.0 %all-to-all-start.2 = ((bf16[32,48,1024]{2,1,0:T(8,128)(2,1)}), bf16[32,48,1024]{2,1,0:T(8,128)(2,1)S(1)}, u32[]{:S(2)}, u32[]{:S(2)}) async-start(bf16[32,48,1024]{2,1,0:T(8,128)(2,1)} %reshape.156), calls=%async_computation.2 | async-start | bytes 6291456 | tf_op jit(solution)/shard_map/all_to_all | solution.py:114
  153.2 5.0 %copy-start.7 = (bf16[384,768]{1,0:T(8,128)(2,1)S(1)}, bf16[384,768]{1,0:T(8,128)(2,1)}, u32[]{:S(2)}) copy-start(bf16[384,768]{1,0:T(8,128)(2,1)} %copy-done.6) | copy-start | bytes 1769476
  192.7 1.7 copy-start
  194.3 44.8 %all-to-all-start.3 = ((bf16[32,48,1024]{2,1,0:T(8,128)(2,1)}), bf16[32,48,1024]{2,1,0:T(8,128)(2,1)}, u32[]{:S(2)}, u32[]{:S(2)}) async-start(bf16[32,48,1024]{2,1,0:T(8,128)(2,1)} %reshape.159), calls=%async_computation.3 | async-start | bytes 6291456 | tf_op jit(solution)/shard_map/all_to_all | solution.py:121
  204.4 3.2 %copy-start.9 = (bf16[32,4096]{1,0:T(8,128)(2,1)S(1)}, bf16[32,4096]{1,0:T(8,128)(2,1)}, u32[]{:S(2)}) copy-start(bf16[32,4096]{1,0:T(8,128)(2,1)} %param.10) | copy-start | bytes 786436
  246.8 3.9 %copy-start.2 = (bf16[256,4096]{1,0:T(8,128)(2,1)S(1)}, bf16[256,4096]{1,0:T(8,128)(2,1)}, u32[]{:S(2)}) copy-start(bf16[256,4096]{1,0:T(8,128)(2,1)} %gather_fusion.3) | copy-start | bytes 6291460
  253.0 5.6 %copy-start.3 = (bf16[4,384,1024]{2,1,0:T(8,128)(2,1)S(1)}, bf16[4,384,1024]{2,1,0:T(8,128)(2,1)}, u32[]{:S(2)}) copy-start(bf16[4,384,1024]{2,1,0:T(8,128)(2,1)} %pad_maximum_fusion) | copy-start | bytes 9437188
  (1 other events, 0.8 us)
Sparse Core Ops, SparseCore 0:
  135.7 52.8 all-gather.2
  191.0 64.4 reduce-scatter.1

commit v10 on v9

--- a/solution.py
+++ b/solution.py
@@ -59,16 +59,19 @@
     token_pad = jnp.concatenate([tokens, jnp.zeros((1, width), jnp.bfloat16)], axis=0)
     upstream_pad = jnp.concatenate([upstream, jnp.zeros((1, width), jnp.bfloat16)], axis=0)
     gate_pad = jnp.concatenate([flat_gates, jnp.zeros((1,), jnp.float32)], axis=0)
-    send_rows = token_pad[slot_token]
-    send_grads = (
-        gate_pad[slot_pair][:, None] * upstream_pad[slot_token].astype(jnp.float32)
-    ).astype(jnp.bfloat16)
     fold = 1
     while (capacity * fold) % 16 or (width // fold) % 128 or width % fold:
         fold += 1
     if (width // fold) % 128 or width % fold:
         fold = 1
-    flat_shape = (expert_count, capacity * fold, width // fold)
+    narrow = width // fold
+    flat_shape = (expert_count, capacity * fold, narrow)
+    row_index = (slot_token[:, None] * fold + jnp.arange(fold, dtype=jnp.int32)[None, :]).reshape(-1)
+    send_rows = token_pad.reshape(-1, narrow)[row_index]
+    send_grads = (
+        jnp.repeat(gate_pad[slot_pair], fold)[:, None]
+        * upstream_pad.reshape(-1, narrow)[row_index].astype(jnp.float32)
+    ).astype(jnp.bfloat16)
     got_rows, got_grads = (
         lax.all_to_all(
             send_rows.reshape(flat_shape),
@@ -143,13 +146,22 @@
         .astype(jnp.float32)
         .T
     )
-    pair_out = back_out.reshape(-1, width)[pair_slot].reshape(local_tokens, top_count, width)
-    pair_back = back_grad.reshape(-1, width)[pair_slot].reshape(local_tokens, top_count, width)
-    output = jnp.sum(gate_values[:, :, None] * pair_out.astype(jnp.float32), axis=1).astype(
-        jnp.bfloat16
+    pair_index = (
+        pair_slot.reshape(local_tokens, 1, top_count) * fold
+        + jnp.arange(fold, dtype=jnp.int32)[None, :, None]
+    ).reshape(local_tokens * fold, top_count)
+    pair_out = back_out.reshape(-1, narrow)[pair_index].astype(jnp.float32)
+    pair_back = back_grad.reshape(-1, narrow)[pair_index].astype(jnp.float32)
+    gate_rows = jnp.repeat(gate_values, fold, axis=0)
+    output = (
+        jnp.sum(gate_rows[:, :, None] * pair_out, axis=1).reshape(local_tokens, width).astype(jnp.bfloat16)
     )
-    grad_tokens = jnp.sum(pair_back.astype(jnp.float32), axis=1).astype(jnp.bfloat16)
-    grad_gates = jnp.einsum("tkd,td->tk", pair_out, upstream, preferred_element_type=jnp.float32)
+    grad_tokens = jnp.sum(pair_back, axis=1).reshape(local_tokens, width).astype(jnp.bfloat16)
+    upstream_rows = upstream.reshape(local_tokens * fold, narrow).astype(jnp.float32)
+    grad_gates = jnp.sum(
+        jnp.sum(upstream_rows[:, None, :] * pair_out, axis=2).reshape(local_tokens, fold, top_count),
+        axis=1,
+    )
     grad_w_gate = grad_joined[:, :ff_width].astype(jnp.bfloat16)[None]
     grad_w_up = grad_joined[:, ff_width:].astype(jnp.bfloat16)[None]
     grad_w_down = grad_down.astype(jnp.bfloat16)[None]

time: 281 us -> 274 us (0.975)
  local copies, waits for them, and re-layouts: 79.6 us -> 76.2 us
  matrix products: 54.1 us -> 51.2 us
    gather x5, local copies, waits for them, and re-layouts: 16.6 us -> 28.4 us  [the longest x1 8.55 us: local(): pair_out = back_out.reshape(-1, narrow)[pair_index].astype(jnp.float32)]
    reshape x3 -> x2, local copies, waits for them, and re-layouts: 12.9 us -> 1.33 us  [the longest x1 1.15 us: local(): upstream_pad.reshape(-1, narrow)[row_index].astype(jnp.float32)]
    all_to_all x1, waiting for transfers between devices: 19.8 us -> 24.3 us  [local(): lax.all_to_all(send_rows.reshape(flat_shape), ('outer', 'inner'), split_a...]
    convert_element_type x1 -> x3, local copies, waits for them, and re-layouts: 6.41 us -> 2.67 us  [the longest x1 0.94 us: local(): upstream.reshape(local_tokens * fold, narrow).astype(jnp.float32)]
    all_to_all x1, waiting for transfers between devices: 27.8 us -> 24.6 us  [local(): lax.all_to_all(pair_grad.reshape(flat_shape), ('outer', 'inner'), split_a...]
    dot_general x1 -> x0, matrix products: 3.03 us -> none  [local(): jnp.einsum('tkd,td->tk', pair_out, upstream, preferred_element_type=jnp.f...]
    unnamed x35 -> x36, local copies, waits for them, and re-layouts: 8.26 us -> 8.97 us
    reduce_sum x2 -> x3, other arithmetic: 6.21 us -> 6.43 us  [the longest x1 3.36 us: local(): jnp.sum(upstream_rows[:, None, :] * pair_out, axis=2)]
  transfers between devices with their start and end apart: 9 -> 9, of which waited for: 4 -> 4; matrix products, arithmetic and copies ran while one was open for 43% -> 42% of each run, Pallas kernels for 0% -> 0%
where the time goes in v10:
time: 274 us; the launch traced here: 272 us
  waiting for transfers between devices  84.8 us (31%)
  local copies, waits for them, and re-layouts  76.2 us (28%)
  matrix products  51.2 us (19%)
  starting transfers between devices  29.3 us (11%)
  other arithmetic  15.9 us (6%)
  between operations  14.5 us (5%)
    all_to_all x1, waiting for transfers between devices, local(): lax.all_to_all(pair_grad.reshape(flat_shape), ('outer', 'inner'), split_a...  24.6 us
    all_to_all x1, waiting for transfers between devices, local(): lax.all_to_all(send_rows.reshape(flat_shape), ('outer', 'inner'), split_a...  24.3 us
    all_to_all x1, waiting for transfers between devices, local(): lax.all_to_all(expert_out.reshape(flat_shape), ('outer', 'inner'), split_...  20.1 us
    dot_general x3, matrix products, contract_last(): lax.dot_general(left, right, (((1,), (1,)), ((), ())), preferred_element_...  19.4 us
    all_to_all x1, waiting for transfers between devices, local(): lax.all_to_all(send_grads.reshape(flat_shape), ('outer', 'inner'), split_...  15.8 us
    unnamed x36, local copies, waits for them, and re-layouts  8.97 us
    gather x1, local copies, waits for them, and re-layouts, local(): pair_out = back_out.reshape(-1, narrow)[pair_index].astype(jnp.float32)  8.55 us
    dot_general x1, matrix products, contract_first(): lax.dot_general(left, right, (((0,), (0,)), ((), ())), preferred_element_...  8.19 us
  transfers between devices with their start and end apart: 9, of which 4 were waited for; matrix products, arithmetic and copies ran while one was open for 42% of the time, Pallas kernels for 0%

profile of v10, /device:TPU:8, one launch (start us, length us, event | category | flops | bytes accessed | tf_op | source)
XLA Modules:
  0.0 271.8 jit_solution(7044331214346658851)
XLA Ops:
  12.2 5.8 %gather_fusion.2 = bf16[1536,1024]{1,0:T(8,128)(2,1)} fusion(bf16[132,1024]{1,0:T(8,128)(2,1)S(1)} %reshape.257, s32[2048]{0:T(1024)S(1)} %pad_clamp_fusion), kind=kCustom, calls=%fused_computation.2 | custom fusion | bytes 6297600 | tf_op jit(solution)/shard_map/gather | solution.py:70
  18.0 7.7 %all-to-all-start.1 = ((bf16[32,48,1024]{2,1,0:T(8,128)(2,1)}), bf16[32,48,1024]{2,1,0:T(8,128)(2,1)S(1)}, u32[]{:S(2)}, u32[]{:S(2)}) async-start(bf16[32,48,1024]{2,1,0:T(8,128)(2,1)} %bitcast.90), calls=%async_computation.1 | async-start | bytes 6291456 | tf_op jit(solution)/shard_map/all_to_all | solution.py:76
  30.8 5.9 %gather_fusion.1 = bf16[1536,1024]{1,0:T(8,128)(2,1)} fusion(bf16[132,1024]{1,0:T(8,128)(2,1)S(1)} %reshape.255, s32[2048]{0:T(1024)S(1)} %pad_clamp_fusion), kind=kCustom, calls=%fused_computation.1 | custom fusion | bytes 6297600 | tf_op jit(solution)/shard_map/gather | solution.py:73
  36.8 4.1 %fusion = bf16[32,48,1024]{2,1,0:T(8,128)(2,1)} fusion(bf16[32,48,1024]{2,1,0:T(8,128)(2,1)} %bitcast.91, f32[32,48]{1,0:T(8,128)S(1)} %copy.43), kind=kLoop, calls=%fused_computation.9 | loop fusion | flops 4718592 | bytes 6297600 | tf_op jit(solution)/shard_map/convert_element_type | solution.py:74
  40.9 24.3 %all-to-all-done.1 = bf16[32,48,1024]{2,1,0:T(8,128)(2,1)S(1)} async-done(((bf16[32,48,1024]{2,1,0:T(8,128)(2,1)}), bf16[32,48,1024]{2,1,0:T(8,128)(2,1)S(1)}, u32[]{:S(2)}, u32[]{:S(2)}) %all-to-all-start.1) | async-done | bytes 3145760 | tf_op jit(solution)/shard_map/all_to_all | solution.py:76
  65.2 5.3 %all-to-all-start = ((bf16[32,48,1024]{2,1,0:T(8,128)(2,1)}), bf16[32,48,1024]{2,1,0:T(8,128)(2,1)}, u32[]{:S(2)}, u32[]{:S(2)}) async-start(bf16[32,48,1024]{2,1,0:T(8,128)(2,1)} %fusion), calls=%async_computation | async-start | bytes 6291456 | tf_op jit(solution)/shard_map/all_to_all | solution.py:83
  78.0 4.0 %collective-permute-start.2 = (bf16[384,1024]{1,0:T(8,128)(2,1)}, bf16[384,1024]{1,0:T(8,128)(2,1)}, u32[]{:S(2)}, u32[]{:S(2)}) collective-permute-start(bf16[384,1024]{1,0:T(8,128)(2,1)} %get-tuple-element.41), channel_id=1, source_target_pairs={{0,96},{32,0},{64,32},{96,64},{1,97},{33,1},{65,33},{97,65},{2,98}... | collective-permute-start | bytes 2359304 | tf_op jit(solution)/shard_map/ppermute | solution.py:99
  83.3 6.0 %fusion.11 = f32[384,768]{1,0:T(8,128)S(1)} fusion(bf16[384,4096]{1,0:T(8,128)(2,1)S(1)} %copy-done.1, bf16[1,4096,768]{2,1,0:T(8,128)(2,1)} %param.11), kind=kOutput, calls=%fused_computation.21 | convolution fusion | flops 2415919104 | bytes 10616832 | tf_op jit(solution)/shard_map/dot_general | solution.py:102
  94.2 15.8 %all-to-all-done = bf16[32,48,1024]{2,1,0:T(8,128)(2,1)} async-done(((bf16[32,48,1024]{2,1,0:T(8,128)(2,1)}), bf16[32,48,1024]{2,1,0:T(8,128)(2,1)}, u32[]{:S(2)}, u32[]{:S(2)}) %all-to-all-start) | async-done | bytes 3145760 | tf_op jit(solution)/shard_map/all_to_all | solution.py:83
  110.0 6.0 %reshape.256 = bf16[384,4096]{1,0:T(8,128)(2,1)} reshape(bf16[32,48,1024]{2,1,0:T(8,128)(2,1)} %all-to-all-done) | data formatting | bytes 6291456 | tf_op jit(solution)/shard_map/reshape | solution.py:92
  116.0 5.6 %fusion.15 = bf16[384,4096]{1,0:T(8,128)(2,1)S(1)} fusion(bf16[384,768]{1,0:T(8,128)(2,1)} %get-tuple-element.50, bf16[1,768,4096]{2,1,0:T(8,128)(2,1)} %param.13), kind=kOutput, calls=%fused_computation.24 | convolution fusion | flops 2417491968 | bytes 10027008 | tf_op jit(solution)/shard_map/dot_general | solution.py:107
  126.1 6.0 %multiply_convert_fusion.1 = (bf16[384,768]{1,0:T(8,128)(2,1)S(1)}, bf16[384,768]{1,0:T(8,128)(2,1)S(1)}) fusion(f32[384,768]{1,0:T(8,128)S(1)} %copy-done.12, f32[384,768]{1,0:T(8,128)S(1)} %copy-done.13, bf16[384,4096]{1,0:T(8,128)(2,1)S(1)} %copy-done.3, bf16[1,768,4096]{2,1,0:T(8,128)(2,1)} %param.13), kind=kOutput, calls=%fused_computation.39 | convolution fusion | flops 2419752960 | bytes 12976128 | tf_op jit(solution)/shard_map/dot_general | solution.py:8
  134.5 8.2 %convolution_convert_fusion = bf16[4096,768]{1,0:T(8,128)(2,1)} fusion(bf16[384,4096]{1,0:T(8,128)(2,1)} %reshape.256, bf16[384,768]{1,0:T(8,128)(2,1)} %get-tuple-element.50), kind=kOutput, calls=%fused_computation.7 | convolution fusion | flops 2419064832 | bytes 10027008 | tf_op jit(solution)/shard_map/dot_general | solution.py:14
  146.4 5.4 %all-to-all-start.2 = ((bf16[32,48,1024]{2,1,0:T(8,128)(2,1)}), bf16[32,48,1024]{2,1,0:T(8,128)(2,1)S(1)}, u32[]{:S(2)}, u32[]{:S(2)}) async-start(bf16[32,48,1024]{2,1,0:T(8,128)(2,1)} %reshape.260), calls=%async_computation.2 | async-start | bytes 6291456 | tf_op jit(solution)/shard_map/all_to_all | solution.py:117
  151.8 5.0 %fusion.5 = f32[384,4096]{1,0:T(8,128)S(1)} fusion(bf16[384,768]{1,0:T(8,128)(2,1)} %copy-done.9, bf16[1,4096,768]{2,1,0:T(8,128)(2,1)} %param.12), kind=kOutput, calls=%fused_computation.15 | convolution fusion | flops 2415919104 | bytes 13172736 | tf_op jit(solution)/shard_map/dot_general | solution.py:8
  156.8 8.5 %add_convert_fusion = bf16[384,4096]{1,0:T(8,128)(2,1)} fusion(f32[384,4096]{1,0:T(8,128)S(1)} %fusion.5, bf16[384,768]{1,0:T(8,128)(2,1)S(1)} %copy-done.8, bf16[1,4096,768]{2,1,0:T(8,128)(2,1)} %param.11), kind=kOutput, calls=%fused_computation.23 | convolution fusion | flops 2419064832 | bytes 16318464 | tf_op jit(solution)/shard_map/dot_general | solution.py:8
  165.3 6.0 %reshape.262 = bf16[32,48,1024]{2,1,0:T(8,128)(2,1)} reshape(bf16[384,4096]{1,0:T(8,128)(2,1)} %add_convert_fusion) | data formatting | bytes 6291456 | tf_op jit(solution)/shard_map/reshape | solution.py:125
  171.3 20.1 %all-to-all-done.2 = bf16[32,48,1024]{2,1,0:T(8,128)(2,1)S(1)} async-done(((bf16[32,48,1024]{2,1,0:T(8,128)(2,1)}), bf16[32,48,1024]{2,1,0:T(8,128)(2,1)S(1)}, u32[]{:S(2)}, u32[]{:S(2)}) %all-to-all-start.2) | async-done | bytes 3145760 | tf_op jit(solution)/shard_map/all_to_all | solution.py:117
  193.0 5.3 %all-to-all-start.3 = ((bf16[32,48,1024]{2,1,0:T(8,128)(2,1)}), bf16[32,48,1024]{2,1,0:T(8,128)(2,1)S(1)}, u32[]{:S(2)}, u32[]{:S(2)}) async-start(bf16[32,48,1024]{2,1,0:T(8,128)(2,1)} %reshape.262), calls=%async_computation.3 | async-start | bytes 6291456 | tf_op jit(solution)/shard_map/all_to_all | solution.py:124
  199.6 8.5 %gather_fusion.3 = bf16[1024,1024]{1,0:T(8,128)(2,1)} fusion(bf16[1536,1024]{1,0:T(8,128)(2,1)} %bitcast.89, s32[1024]{0:T(1024)S(1)} %broadcast_clamp_fusion), kind=kCustom, calls=%fused_computation.3 | custom fusion | bytes 4198400 | tf_op jit(solution)/shard_map/gather | solution.py:153
  213.1 24.6 %all-to-all-done.3 = bf16[32,48,1024]{2,1,0:T(8,128)(2,1)S(1)} async-done(((bf16[32,48,1024]{2,1,0:T(8,128)(2,1)}), bf16[32,48,1024]{2,1,0:T(8,128)(2,1)S(1)}, u32[]{:S(2)}, u32[]{:S(2)}) %all-to-all-start.3) | async-done | bytes 3145760 | tf_op jit(solution)/shard_map/all_to_all | solution.py:124
  237.7 5.4 %gather_fusion.4 = bf16[1024,1024]{1,0:T(8,128)(2,1)} fusion(bf16[1536,1024]{1,0:T(8,128)(2,1)S(1)} %bitcast.88, s32[1024]{0:T(1024)S(1)} %broadcast_clamp_fusion), kind=kCustom, calls=%fused_computation.4 | custom fusion | bytes 4198400 | tf_op jit(solution)/shard_map/gather | solution.py:154
  246.9 5.5 %gather_fusion.5 = bf16[4,384,1536]{2,1,0:T(8,128)(2,1)} fusion(bf16[4,384,1536]{2,1,0:T(8,128)(2,1)} %bitcast.92, s32[1024]{0:T(1024)S(1)} %pad_clamp_fusion.1), kind=kCustom, calls=%fused_computation.5 | custom fusion | bytes 9437200 | tf_op jit(solution)/shard_map/jit(_take)/gather | solution.py:134
  252.4 8.1 %bitcast_convert_fusion = bf16[1024,1536]{1,0:T(8,128)(2,1)S(1)} fusion(bf16[4,384,1024]{2,1,0:T(8,128)(2,1)S(1)} %copy-done.2, bf16[4,384,1536]{2,1,0:T(8,128)(2,1)} %gather_fusion.5, pred[4]{0:T(512)(128)(4,1)S(1)} %compare_and_fusion), kind=kOutput, calls=%fused_computation.10 | convolution fusion | flops 4835770368 | bytes 11010052 | tf_op jit(solution)/shard_map/dot_general | solution.py:135
  (102 shorter events, 50.4 us)
Async XLA Ops:
  18.0 7.7 %copy-start.10 = (f32[32,8]{0,1:T(8,128)S(1)}, f32[32,8]{0,1:T(8,128)}, u32[]{:S(2)}) copy-start(f32[32,8]{0,1:T(8,128)} %param.9) | copy-start | bytes 3076
  18.0 10.9 %copy-start.5 = (bf16[32,4096]{1,0:T(8,128)(2,1)S(1)}, bf16[32,4096]{1,0:T(8,128)(2,1)}, u32[]{:S(2)}) copy-start(bf16[32,4096]{1,0:T(8,128)(2,1)} %param.10) | copy-start | bytes 786436
  18.0 47.2 %all-to-all-start.1 = ((bf16[32,48,1024]{2,1,0:T(8,128)(2,1)}), bf16[32,48,1024]{2,1,0:T(8,128)(2,1)S(1)}, u32[]{:S(2)}, u32[]{:S(2)}) async-start(bf16[32,48,1024]{2,1,0:T(8,128)(2,1)} %bitcast.90), calls=%async_computation.1 | async-start | bytes 6291456 | tf_op jit(solution)/shard_map/all_to_all | solution.py:76
  65.2 44.9 %all-to-all-start = ((bf16[32,48,1024]{2,1,0:T(8,128)(2,1)}), bf16[32,48,1024]{2,1,0:T(8,128)(2,1)}, u32[]{:S(2)}, u32[]{:S(2)}) async-start(bf16[32,48,1024]{2,1,0:T(8,128)(2,1)} %fusion), calls=%async_computation | async-start | bytes 6291456 | tf_op jit(solution)/shard_map/all_to_all | solution.py:83
  70.5 176.5 %all-gather.3.cloned.1.call-start = ((), (), s32[]{:S(2)}) async-start(), calls=%async_computation.6 | async-start | bytes 5898240 | tf_op jit(solution)/shard_map/all_gather | solution.py:134
  74.3 9.0 %copy-start.1 = (bf16[384,4096]{1,0:T(8,128)(2,1)S(1)}, bf16[384,4096]{1,0:T(8,128)(2,1)}, u32[]{:S(2)}) copy-start(bf16[384,4096]{1,0:T(8,128)(2,1)} %reshape.259) | copy-start | bytes 9437188
  78.0 43.6 %collective-permute-start.2 = (bf16[384,1024]{1,0:T(8,128)(2,1)}, bf16[384,1024]{1,0:T(8,128)(2,1)}, u32[]{:S(2)}, u32[]{:S(2)}) collective-permute-start(bf16[384,1024]{1,0:T(8,128)(2,1)} %get-tuple-element.41), channel_id=1, source_target_pairs={{0,96},{32,0},{64,32},{96,64},{1,97},{33,1},{65,33},{97,65},{2,98}... | collective-permute-start | bytes 2359304 | tf_op jit(solution)/shard_map/ppermute | solution.py:99
  82.0 39.6 %collective-permute-start.1 = (bf16[384,1024]{1,0:T(8,128)(2,1)}, bf16[384,1024]{1,0:T(8,128)(2,1)}, u32[]{:S(2)}, u32[]{:S(2)}) collective-permute-start(bf16[384,1024]{1,0:T(8,128)(2,1)} %get-tuple-element.42), channel_id=1, source_target_pairs={{0,64},{32,96},{64,0},{96,32},{1,65},{33,97},{65,1},{97,33},{2,66}... | collective-permute-start | bytes 2359304 | tf_op jit(solution)/shard_map/ppermute | solution.py:99
  82.0 8.3 %slice-start = ((s8[6291456]{0:T(1024)(128)(4,1)}), s8[4194304]{0:T(1024)(128)(4,1)S(1)}, s32[]{:S(2)}) async-start(s8[6291456]{0:T(1024)(128)(4,1)} %bitcast.100), calls=%async_computation.7 | async-start | bytes 8388608
  82.0 8.3 %slice-start.1 = ((s8[6291456]{0:T(1024)(128)(4,1)}), s8[2097152]{0:T(1024)(128)(4,1)S(1)}, s32[]{:S(2)}) async-start(s8[6291456]{0:T(1024)(128)(4,1)} %bitcast.100), calls=%async_computation.8 | async-start | bytes 4194304
  82.0 39.6 %collective-permute-start = (bf16[384,1024]{1,0:T(8,128)(2,1)}, bf16[384,1024]{1,0:T(8,128)(2,1)}, u32[]{:S(2)}, u32[]{:S(2)}) collective-permute-start(bf16[384,1024]{1,0:T(8,128)(2,1)} %get-tuple-element.43), channel_id=1, source_target_pairs={{0,32},{32,64},{64,96},{96,0},{1,33},{33,65},{65,97},{97,1},{2,34}... | collective-permute-start | bytes 2359304 | tf_op jit(solution)/shard_map/ppermute | solution.py:99
  89.3 1.0 copy-start.11
  116.0 5.7 %copy-start.4 = (bf16[1,384,1024]{2,1,0:T(8,128)(2,1)S(1)}, bf16[1,384,1024]{2,1,0:T(8,128)(2,1)}, u32[]{:S(2)}) copy-start(bf16[1,384,1024]{2,1,0:T(8,128)(2,1)} %get-tuple-element.40) | copy-start | bytes 2359300
  121.7 3.2 %copy-start.3 = (bf16[384,4096]{1,0:T(8,128)(2,1)S(1)}, bf16[384,4096]{1,0:T(8,128)(2,1)}, u32[]{:S(2)}) copy-start(bf16[384,4096]{1,0:T(8,128)(2,1)} %reshape.256) | copy-start | bytes 9437188
  121.7 3.8 %copy-start.12 = (f32[384,768]{1,0:T(8,128)S(1)}, f32[384,768]{1,0:T(8,128)}, u32[]{:S(2)}) copy-start(f32[384,768]{1,0:T(8,128)} %copy-done.11) | copy-start | bytes 3538948
  121.7 4.4 %copy-start.13 = (f32[384,768]{1,0:T(8,128)S(1)}, f32[384,768]{1,0:T(8,128)}, u32[]{:S(2)}) copy-start(f32[384,768]{1,0:T(8,128)} %get-tuple-element.51) | copy-start | bytes 3538948
  132.1 1.0 copy-start.9
  134.2 128.2 %reduce-scatter.2.cloned.1.call-start = ((), (), s32[]{:S(2)}) async-start(), calls=%async_computation.5 | async-start | bytes 7864320 | tf_op jit(solution)/shard_map/reduce_scatter | solution.py:140
  146.4 45.0 %all-to-all-start.2 = ((bf16[32,48,1024]{2,1,0:T(8,128)(2,1)}), bf16[32,48,1024]{2,1,0:T(8,128)(2,1)S(1)}, u32[]{:S(2)}, u32[]{:S(2)}) async-start(bf16[32,48,1024]{2,1,0:T(8,128)(2,1)} %reshape.260), calls=%async_computation.2 | async-start | bytes 6291456 | tf_op jit(solution)/shard_map/all_to_all | solution.py:117
  151.8 5.0 %copy-start.8 = (bf16[384,768]{1,0:T(8,128)(2,1)S(1)}, bf16[384,768]{1,0:T(8,128)(2,1)}, u32[]{:S(2)}) copy-start(bf16[384,768]{1,0:T(8,128)(2,1)} %copy-done.7) | copy-start | bytes 1769476
  171.3 27.0 %copy-start.6 = (bf16[32,4096]{1,0:T(8,128)(2,1)S(1)}, bf16[32,4096]{1,0:T(8,128)(2,1)}, u32[]{:S(2)}) copy-start(bf16[32,4096]{1,0:T(8,128)(2,1)} %param.10) | copy-start | bytes 786436
  191.3 1.7 copy-start
  193.0 44.7 %all-to-all-start.3 = ((bf16[32,48,1024]{2,1,0:T(8,128)(2,1)}), bf16[32,48,1024]{2,1,0:T(8,128)(2,1)S(1)}, u32[]{:S(2)}, u32[]{:S(2)}) async-start(bf16[32,48,1024]{2,1,0:T(8,128)(2,1)} %reshape.262), calls=%async_computation.3 | async-start | bytes 6291456 | tf_op jit(solution)/shard_map/all_to_all | solution.py:124
  246.9 5.5 %copy-start.2 = (bf16[4,384,1024]{2,1,0:T(8,128)(2,1)S(1)}, bf16[4,384,1024]{2,1,0:T(8,128)(2,1)}, u32[]{:S(2)}) copy-start(bf16[4,384,1024]{2,1,0:T(8,128)(2,1)} %pad_maximum_fusion) | copy-start | bytes 9437188
  (1 other events, 0.8 us)
Sparse Core Ops, SparseCore 0:
  134.3 52.8 all-gather.2
  189.6 64.4 reduce-scatter.1

commit v11 on v10

--- a/solution.py
+++ b/solution.py
@@ -130,8 +130,12 @@
         ),
     )
     joined_grads = jnp.concatenate([grad_gate_pre, grad_up_pre], axis=1)
-    source_order = (dp_index - jnp.arange(dp_count)) % dp_count
-    joined_all = jnp.take(lax.all_gather(joined_grads, "dp", axis=0, tiled=False), source_order, axis=0)
+    joined_arrived = [joined_grads]
+    for shift in range(1, dp_count):
+        joined_arrived.append(
+            lax.ppermute(joined_grads, "dp", [(j, (j + shift) % dp_count) for j in range(dp_count)])
+        )
+    joined_all = jnp.stack(joined_arrived, axis=0)
     grad_joined = lax.dot_general(
         rows_all, joined_all, (((0, 1), (0, 1)), ((), ())), preferred_element_type=jnp.float32
     )
@@ -151,6 +155,7 @@
         + jnp.arange(fold, dtype=jnp.int32)[None, :, None]
     ).reshape(local_tokens * fold, top_count)
     pair_out = back_out.reshape(-1, narrow)[pair_index].astype(jnp.float32)
+    grad_joined, back_grad = lax.optimization_barrier((grad_joined, back_grad))
     pair_back = back_grad.reshape(-1, narrow)[pair_index].astype(jnp.float32)
     gate_rows = jnp.repeat(gate_values, fold, axis=0)
     output = (

time: 274 us -> 291 us (1.062)
  waiting for transfers between devices: 84.8 us -> 101 us
  local copies, waits for them, and re-layouts: 76.2 us -> 68 us
  starting transfers between devices: 29.3 us -> 36 us
    ppermute x0 -> x3, waiting for transfers between devices: none -> 48.2 us  [local(): lax.ppermute(joined_grads, 'dp', [(j, (j + shift) % dp_count) for j in ra...]
    all_to_all x1, waiting for transfers between devices: 24.6 us -> 0.01 us  [local(): lax.all_to_all(pair_grad.reshape(flat_shape), ('outer', 'inner'), split_a...]
    all_to_all x1, waiting for transfers between devices: 20.1 us -> 12.6 us  [local(): lax.all_to_all(expert_out.reshape(flat_shape), ('outer', 'inner'), split_...]
    ppermute x0 -> x3, starting transfers between devices: none -> 7.08 us  [local(): lax.ppermute(joined_grads, 'dp', [(j, (j + shift) % dp_count) for j in ra...]
    gather x1 -> x0, local copies, waits for them, and re-layouts: 5.46 us -> none  [local(): jnp.take(lax.all_gather(joined_grads, 'dp', axis=0, tiled=False), source_...]
    gather x1, local copies, waits for them, and re-layouts: 8.55 us -> 5.4 us  [local(): pair_out = back_out.reshape(-1, narrow)[pair_index].astype(jnp.float32)]
    unnamed x36 -> x30, local copies, waits for them, and re-layouts: 8.97 us -> 7 us
  transfers between devices with their start and end apart: 9 -> 11, of which waited for: 4 -> 6; matrix products, arithmetic and copies ran while one was open for 42% -> 39% of each run, Pallas kernels for 0% -> 0%
where the time goes in v11:
time: 291 us; the launch traced here: 289 us
  waiting for transfers between devices  101 us (35%)
  local copies, waits for them, and re-layouts  68 us (23%)
  matrix products  54 us (19%)
  starting transfers between devices  36 us (12%)
  other arithmetic  16 us (5%)
  between operations  14.4 us (5%)
    ppermute x3, waiting for transfers between devices, local(): lax.ppermute(joined_grads, 'dp', [(j, (j + shift) % dp_count) for j in ra...  48.2 us
    all_to_all x1, waiting for transfers between devices, local(): lax.all_to_all(send_rows.reshape(flat_shape), ('outer', 'inner'), split_a...  24.3 us
    dot_general x3, matrix products, contract_last(): lax.dot_general(left, right, (((1,), (1,)), ((), ())), preferred_element_...  20.9 us
    all_to_all x1, waiting for transfers between devices, local(): lax.all_to_all(send_grads.reshape(flat_shape), ('outer', 'inner'), split_...  15.8 us
    all_to_all x1, waiting for transfers between devices, local(): lax.all_to_all(expert_out.reshape(flat_shape), ('outer', 'inner'), split_...  12.6 us
    dot_general x1, matrix products, local(): lax.dot_general(rows_all, joined_all, (((0, 1), (0, 1)), ((), ())), prefe...  9.49 us
    dot_general x1, matrix products, local(): jnp.dot(hidden, down_mat, preferred_element_type=jnp.float32)  8.36 us
    all_to_all x1, starting transfers between devices, local(): lax.all_to_all(send_rows.reshape(flat_shape), ('outer', 'inner'), split_a...  7.66 us
  transfers between devices with their start and end apart: 11, of which 6 were waited for; matrix products, arithmetic and copies ran while one was open for 39% of the time, Pallas kernels for 0%

profile of v11, /device:TPU:8, one launch (start us, length us, event | category | flops | bytes accessed | tf_op | source)
XLA Modules:
  0.0 289.2 jit_solution(17549715101258377792)
XLA Ops:
  12.2 5.8 %gather_fusion.2 = bf16[1536,1024]{1,0:T(8,128)(2,1)} fusion(bf16[132,1024]{1,0:T(8,128)(2,1)S(1)} %reshape.203, s32[2048]{0:T(1024)S(1)} %pad_clamp_fusion), kind=kCustom, calls=%fused_computation.2 | custom fusion | bytes 6297600 | tf_op jit(solution)/shard_map/gather | solution.py:70
  18.0 7.7 %all-to-all-start.1 = ((bf16[32,48,1024]{2,1,0:T(8,128)(2,1)}), bf16[32,48,1024]{2,1,0:T(8,128)(2,1)S(1)}, u32[]{:S(2)}, u32[]{:S(2)}) async-start(bf16[32,48,1024]{2,1,0:T(8,128)(2,1)} %bitcast.91), calls=%async_computation.1 | async-start | bytes 6291456 | tf_op jit(solution)/shard_map/all_to_all | solution.py:76
  30.8 5.9 %gather_fusion.1 = bf16[1536,1024]{1,0:T(8,128)(2,1)} fusion(bf16[132,1024]{1,0:T(8,128)(2,1)S(1)} %reshape.201, s32[2048]{0:T(1024)S(1)} %pad_clamp_fusion), kind=kCustom, calls=%fused_computation.1 | custom fusion | bytes 6297600 | tf_op jit(solution)/shard_map/gather | solution.py:73
  36.7 4.1 %fusion = bf16[32,48,1024]{2,1,0:T(8,128)(2,1)} fusion(bf16[32,48,1024]{2,1,0:T(8,128)(2,1)} %bitcast.92, f32[32,48]{1,0:T(8,128)S(1)} %copy.43), kind=kLoop, calls=%fused_computation.8 | loop fusion | flops 4718592 | bytes 6297600 | tf_op jit(solution)/shard_map/convert_element_type | solution.py:74
  40.8 24.3 %all-to-all-done.1 = bf16[32,48,1024]{2,1,0:T(8,128)(2,1)S(1)} async-done(((bf16[32,48,1024]{2,1,0:T(8,128)(2,1)}), bf16[32,48,1024]{2,1,0:T(8,128)(2,1)S(1)}, u32[]{:S(2)}, u32[]{:S(2)}) %all-to-all-start.1) | async-done | bytes 3145760 | tf_op jit(solution)/shard_map/all_to_all | solution.py:76
  65.1 5.3 %all-to-all-start = ((bf16[32,48,1024]{2,1,0:T(8,128)(2,1)}), bf16[32,48,1024]{2,1,0:T(8,128)(2,1)}, u32[]{:S(2)}, u32[]{:S(2)}) async-start(bf16[32,48,1024]{2,1,0:T(8,128)(2,1)} %fusion), calls=%async_computation | async-start | bytes 6291456 | tf_op jit(solution)/shard_map/all_to_all | solution.py:83
  78.1 4.0 %collective-permute-start.2 = (bf16[384,1024]{1,0:T(8,128)(2,1)}, bf16[384,1024]{1,0:T(8,128)(2,1)}, u32[]{:S(2)}, u32[]{:S(2)}) collective-permute-start(bf16[384,1024]{1,0:T(8,128)(2,1)} %get-tuple-element.45), channel_id=1, source_target_pairs={{0,96},{32,0},{64,32},{96,64},{1,97},{33,1},{65,33},{97,65},{2,98}... | collective-permute-start | bytes 2359304 | tf_op jit(solution)/shard_map/ppermute | solution.py:99
  83.4 6.0 %fusion.11 = f32[384,768]{1,0:T(8,128)S(1)} fusion(bf16[384,4096]{1,0:T(8,128)(2,1)S(1)} %copy-done, bf16[1,4096,768]{2,1,0:T(8,128)(2,1)} %param.11), kind=kOutput, calls=%fused_computation.19 | convolution fusion | flops 2415919104 | bytes 10616832 | tf_op jit(solution)/shard_map/dot_general | solution.py:102
  94.2 15.8 %all-to-all-done = bf16[32,48,1024]{2,1,0:T(8,128)(2,1)} async-done(((bf16[32,48,1024]{2,1,0:T(8,128)(2,1)}), bf16[32,48,1024]{2,1,0:T(8,128)(2,1)}, u32[]{:S(2)}, u32[]{:S(2)}) %all-to-all-start) | async-done | bytes 3145760 | tf_op jit(solution)/shard_map/all_to_all | solution.py:83
  110.0 4.5 %reshape.202 = bf16[384,4096]{1,0:T(8,128)(2,1)S(1)} reshape(bf16[32,48,1024]{2,1,0:T(8,128)(2,1)} %all-to-all-done) | data formatting | bytes 6291456 | tf_op jit(solution)/shard_map/reshape | solution.py:92
  114.5 8.4 %fusion.15 = bf16[384,4096]{1,0:T(8,128)(2,1)} fusion(bf16[384,768]{1,0:T(8,128)(2,1)} %get-tuple-element.56, bf16[1,768,4096]{2,1,0:T(8,128)(2,1)} %param.13), kind=kOutput, calls=%fused_computation.22 | convolution fusion | flops 2417491968 | bytes 10027008 | tf_op jit(solution)/shard_map/dot_general | solution.py:107
  126.1 5.4 %convolution_convert_fusion = bf16[4096,768]{1,0:T(8,128)(2,1)} fusion(bf16[384,4096]{1,0:T(8,128)(2,1)S(1)} %reshape.202, bf16[384,768]{1,0:T(8,128)(2,1)S(1)} %copy-done.9), kind=kOutput, calls=%fused_computation.6 | convolution fusion | flops 2419064832 | bytes 10027008 | tf_op jit(solution)/shard_map/dot_general | solution.py:14
  137.1 5.3 %all-to-all-start.2 = ((bf16[32,48,1024]{2,1,0:T(8,128)(2,1)}), bf16[32,48,1024]{2,1,0:T(8,128)(2,1)S(1)}, u32[]{:S(2)}, u32[]{:S(2)}) async-start(bf16[32,48,1024]{2,1,0:T(8,128)(2,1)} %reshape.206), calls=%async_computation.2 | async-start | bytes 6291456 | tf_op jit(solution)/shard_map/all_to_all | solution.py:117
  142.4 7.2 %multiply_convert_fusion.1 = (bf16[384,768]{1,0:T(8,128)(2,1)S(1)}, bf16[384,768]{1,0:T(8,128)(2,1)S(1)}) fusion(f32[384,768]{1,0:T(8,128)} %copy-done.10, f32[384,768]{1,0:T(8,128)} %get-tuple-element.57, bf16[384,4096]{1,0:T(8,128)(2,1)} %copy-done.1, bf16[1,768,4096]{2,1,0:T(8,128)(2,1)} %param.13), kind=kOutput, calls=%fused_computation.42 | convolution fusion | flops 2419752960 | bytes 12976128 | tf_op jit(solution)/shard_map/dot_general | solution.py:8
  149.7 5.2 %fusion.5 = f32[384,4096]{1,0:T(8,128)S(1)} fusion(bf16[384,768]{1,0:T(8,128)(2,1)S(1)} %get-tuple-element.49, bf16[1,4096,768]{2,1,0:T(8,128)(2,1)} %param.12), kind=kOutput, calls=%fused_computation.13 | convolution fusion | flops 2415919104 | bytes 13172736 | tf_op jit(solution)/shard_map/dot_general | solution.py:8
  154.9 8.4 %add_convert_fusion = bf16[384,4096]{1,0:T(8,128)(2,1)} fusion(f32[384,4096]{1,0:T(8,128)S(1)} %fusion.5, bf16[384,768]{1,0:T(8,128)(2,1)S(1)} %get-tuple-element.48, bf16[1,4096,768]{2,1,0:T(8,128)(2,1)} %param.11), kind=kOutput, calls=%fused_computation.21 | convolution fusion | flops 2419064832 | bytes 16318464 | tf_op jit(solution)/shard_map/dot_general | solution.py:8
  163.3 5.9 %reshape.208 = bf16[32,48,1024]{2,1,0:T(8,128)(2,1)} reshape(bf16[384,4096]{1,0:T(8,128)(2,1)} %add_convert_fusion) | data formatting | bytes 6291456 | tf_op jit(solution)/shard_map/reshape | solution.py:125
  169.3 12.6 %all-to-all-done.2 = bf16[32,48,1024]{2,1,0:T(8,128)(2,1)S(1)} async-done(((bf16[32,48,1024]{2,1,0:T(8,128)(2,1)}), bf16[32,48,1024]{2,1,0:T(8,128)(2,1)S(1)}, u32[]{:S(2)}, u32[]{:S(2)}) %all-to-all-start.2) | async-done | bytes 3145760 | tf_op jit(solution)/shard_map/all_to_all | solution.py:117
  181.8 5.4 %all-to-all-start.3 = ((bf16[32,48,1024]{2,1,0:T(8,128)(2,1)}), bf16[32,48,1024]{2,1,0:T(8,128)(2,1)}, u32[]{:S(2)}, u32[]{:S(2)}) async-start(bf16[32,48,1024]{2,1,0:T(8,128)(2,1)} %reshape.208), calls=%async_computation.3 | async-start | bytes 6291456 | tf_op jit(solution)/shard_map/all_to_all | solution.py:124
  198.4 22.6 %collective-permute-done.4 = bf16[384,1536]{1,0:T(8,128)(2,1)} collective-permute-done((bf16[384,1536]{1,0:T(8,128)(2,1)}, bf16[384,1536]{1,0:T(8,128)(2,1)}, u32[]{:S(2)}, u32[]{:S(2)}) %collective-permute-start.4) | collective-permute-done | bytes 1179680 | tf_op jit(solution)/shard_map/ppermute | solution.py:136
  221.0 24.8 %collective-permute-done.3 = bf16[384,1536]{1,0:T(8,128)(2,1)} collective-permute-done((bf16[384,1536]{1,0:T(8,128)(2,1)}, bf16[384,1536]{1,0:T(8,128)(2,1)}, u32[]{:S(2)}, u32[]{:S(2)}) %collective-permute-start.3) | collective-permute-done | bytes 1179680 | tf_op jit(solution)/shard_map/ppermute | solution.py:136
  246.6 9.5 %fusion.26 = bf16[1024,1536]{1,0:T(8,128)(2,1)} fusion(bf16[4,384,1024]{2,1,0:T(8,128)(2,1)} %pad_maximum_fusion, bf16[1,384,1536]{2,1,0:T(8,128)(2,1)} %bitcast.20, bf16[1,384,1536]{2,1,0:T(8,128)(2,1)} %bitcast.19, bf16[1,384,1536]{2,1,0:T(8,128)(2,1)} %bitcast.18, bf16[1,384,1536]{2,1,0:T(8,128)(2,1)} %get-tuple-element.50), kind=kOutput, calls=%fused_computation.33 | convolution fusion | flops 4838916096 | bytes 11010048 | tf_op jit(solution)/shard_map/dot_general | solution.py:139
  256.1 5.4 %gather_fusion.3 = bf16[1024,1024]{1,0:T(8,128)(2,1)} fusion(bf16[1536,1024]{1,0:T(8,128)(2,1)S(1)} %bitcast.90, s32[1024]{0:T(1024)S(1)} %broadcast_clamp_fusion), kind=kCustom, calls=%fused_computation.3 | custom fusion | bytes 4198400 | tf_op jit(solution)/shard_map/gather | solution.py:157
  266.5 7.3 %gather_fusion.4 = bf16[1024,1024]{1,0:T(8,128)(2,1)S(1)} fusion(bf16[1536,1024]{1,0:T(8,128)(2,1)} %bitcast.22, s32[1024]{0:T(1024)S(1)} %broadcast_clamp_fusion), kind=kCustom, calls=%fused_computation.4 | custom fusion | bytes 4198400 | tf_op jit(solution)/shard_map/gather | solution.py:159
  (95 shorter events, 58.1 us)
Async XLA Ops:
  18.0 7.7 %copy-start.8 = (f32[32,8]{0,1:T(8,128)S(1)}, f32[32,8]{0,1:T(8,128)}, u32[]{:S(2)}) copy-start(f32[32,8]{0,1:T(8,128)} %param.9) | copy-start | bytes 3076
  18.0 10.9 %copy-start.4 = (bf16[32,4096]{1,0:T(8,128)(2,1)S(1)}, bf16[32,4096]{1,0:T(8,128)(2,1)}, u32[]{:S(2)}) copy-start(bf16[32,4096]{1,0:T(8,128)(2,1)} %param.10) | copy-start | bytes 786436
  18.0 47.2 %all-to-all-start.1 = ((bf16[32,48,1024]{2,1,0:T(8,128)(2,1)}), bf16[32,48,1024]{2,1,0:T(8,128)(2,1)S(1)}, u32[]{:S(2)}, u32[]{:S(2)}) async-start(bf16[32,48,1024]{2,1,0:T(8,128)(2,1)} %bitcast.91), calls=%async_computation.1 | async-start | bytes 6291456 | tf_op jit(solution)/shard_map/all_to_all | solution.py:76
  65.1 44.9 %all-to-all-start = ((bf16[32,48,1024]{2,1,0:T(8,128)(2,1)}), bf16[32,48,1024]{2,1,0:T(8,128)(2,1)}, u32[]{:S(2)}, u32[]{:S(2)}) async-start(bf16[32,48,1024]{2,1,0:T(8,128)(2,1)} %fusion), calls=%async_computation | async-start | bytes 6291456 | tf_op jit(solution)/shard_map/all_to_all | solution.py:83
  70.4 209.4 %reduce-scatter.2.cloned.1.call-start = ((), (), s32[]{:S(2)}) async-start(), calls=%async_computation.5 | async-start | bytes 7864320 | tf_op jit(solution)/shard_map/reduce_scatter | solution.py:144
  74.3 9.0 %copy-start = (bf16[384,4096]{1,0:T(8,128)(2,1)S(1)}, bf16[384,4096]{1,0:T(8,128)(2,1)}, u32[]{:S(2)}) copy-start(bf16[384,4096]{1,0:T(8,128)(2,1)} %reshape.205) | copy-start | bytes 9437188
  78.1 44.8 %collective-permute-start.2 = (bf16[384,1024]{1,0:T(8,128)(2,1)}, bf16[384,1024]{1,0:T(8,128)(2,1)}, u32[]{:S(2)}, u32[]{:S(2)}) collective-permute-start(bf16[384,1024]{1,0:T(8,128)(2,1)} %get-tuple-element.45), channel_id=1, source_target_pairs={{0,96},{32,0},{64,32},{96,64},{1,97},{33,1},{65,33},{97,65},{2,98}... | collective-permute-start | bytes 2359304 | tf_op jit(solution)/shard_map/ppermute | solution.py:99
  82.1 40.8 %collective-permute-start.1 = (bf16[384,1024]{1,0:T(8,128)(2,1)}, bf16[384,1024]{1,0:T(8,128)(2,1)}, u32[]{:S(2)}, u32[]{:S(2)}) collective-permute-start(bf16[384,1024]{1,0:T(8,128)(2,1)} %get-tuple-element.46), channel_id=1, source_target_pairs={{0,64},{32,96},{64,0},{96,32},{1,65},{33,97},{65,1},{97,33},{2,66}... | collective-permute-start | bytes 2359304 | tf_op jit(solution)/shard_map/ppermute | solution.py:99
  82.1 8.3 %slice-start = ((s8[6291456]{0:T(1024)(128)(4,1)}), s8[4194304]{0:T(1024)(128)(4,1)S(1)}, s32[]{:S(2)}) async-start(s8[6291456]{0:T(1024)(128)(4,1)} %bitcast.100), calls=%async_computation.6 | async-start | bytes 8388608
  82.1 8.3 %slice-start.1 = ((s8[6291456]{0:T(1024)(128)(4,1)}), s8[2097152]{0:T(1024)(128)(4,1)S(1)}, s32[]{:S(2)}) async-start(s8[6291456]{0:T(1024)(128)(4,1)} %bitcast.100), calls=%async_computation.7 | async-start | bytes 4194304
  82.1 40.8 %collective-permute-start = (bf16[384,1024]{1,0:T(8,128)(2,1)}, bf16[384,1024]{1,0:T(8,128)(2,1)}, u32[]{:S(2)}, u32[]{:S(2)}) collective-permute-start(bf16[384,1024]{1,0:T(8,128)(2,1)} %get-tuple-element.47), channel_id=1, source_target_pairs={{0,32},{32,64},{64,96},{96,0},{1,33},{33,65},{65,97},{97,1},{2,34}... | collective-permute-start | bytes 2359304 | tf_op jit(solution)/shard_map/ppermute | solution.py:99
  89.4 1.0 copy-start.10
  114.5 11.6 %copy-start.1 = (bf16[384,4096]{1,0:T(8,128)(2,1)}, bf16[384,4096]{1,0:T(8,128)(2,1)S(1)}, u32[]{:S(2)}) copy-start(bf16[384,4096]{1,0:T(8,128)(2,1)S(1)} %reshape.202) | copy-start | bytes 9437188
  114.5 8.4 %copy-start.3 = (bf16[1,384,1024]{2,1,0:T(8,128)(2,1)S(1)}, bf16[1,384,1024]{2,1,0:T(8,128)(2,1)}, u32[]{:S(2)}) copy-start(bf16[1,384,1024]{2,1,0:T(8,128)(2,1)} %get-tuple-element.44) | copy-start | bytes 2359300
  122.9 3.2 %copy-start.9 = (bf16[384,768]{1,0:T(8,128)(2,1)S(1)}, bf16[384,768]{1,0:T(8,128)(2,1)}, u32[]{:S(2)}) copy-start(bf16[384,768]{1,0:T(8,128)(2,1)} %get-tuple-element.56) | copy-start | bytes 1769476
  131.6 1.9 copy-start.2
  137.1 44.7 %all-to-all-start.2 = ((bf16[32,48,1024]{2,1,0:T(8,128)(2,1)}), bf16[32,48,1024]{2,1,0:T(8,128)(2,1)S(1)}, u32[]{:S(2)}, u32[]{:S(2)}) async-start(bf16[32,48,1024]{2,1,0:T(8,128)(2,1)} %reshape.206), calls=%async_computation.2 | async-start | bytes 6291456 | tf_op jit(solution)/shard_map/all_to_all | solution.py:117
  149.6 5.2 %copy-start.7 = (bf16[384,768]{1,0:T(8,128)(2,1)}, bf16[384,768]{1,0:T(8,128)(2,1)S(1)}, u32[]{:S(2)}) copy-start(bf16[384,768]{1,0:T(8,128)(2,1)S(1)} %get-tuple-element.49) | copy-start | bytes 1769476
  149.7 5.2 %copy-start.6 = (bf16[384,768]{1,0:T(8,128)(2,1)}, bf16[384,768]{1,0:T(8,128)(2,1)S(1)}, u32[]{:S(2)}) copy-start(bf16[384,768]{1,0:T(8,128)(2,1)S(1)} %get-tuple-element.48) | copy-start | bytes 1769476
  181.8 84.7 %all-to-all-start.3 = ((bf16[32,48,1024]{2,1,0:T(8,128)(2,1)}), bf16[32,48,1024]{2,1,0:T(8,128)(2,1)}, u32[]{:S(2)}, u32[]{:S(2)}) async-start(bf16[32,48,1024]{2,1,0:T(8,128)(2,1)} %reshape.208), calls=%async_computation.3 | async-start | bytes 6291456 | tf_op jit(solution)/shard_map/all_to_all | solution.py:124
  187.2 10.0 %copy-start.5 = (bf16[32,4096]{1,0:T(8,128)(2,1)S(1)}, bf16[32,4096]{1,0:T(8,128)(2,1)}, u32[]{:S(2)}) copy-start(bf16[32,4096]{1,0:T(8,128)(2,1)} %param.10) | copy-start | bytes 786436
  190.1 31.0 %collective-permute-start.4 = (bf16[384,1536]{1,0:T(8,128)(2,1)}, bf16[384,1536]{1,0:T(8,128)(2,1)}, u32[]{:S(2)}, u32[]{:S(2)}) collective-permute-start(bf16[384,1536]{1,0:T(8,128)(2,1)} %get-tuple-element.51), channel_id=1, source_target_pairs={{0,64},{32,96},{64,0},{96,32},{1,65},{33,97},{65,1},{97,33},{2,66}... | collective-permute-start | bytes 3538952 | tf_op jit(solution)/shard_map/ppermute | solution.py:136
  193.9 51.9 %collective-permute-start.3 = (bf16[384,1536]{1,0:T(8,128)(2,1)}, bf16[384,1536]{1,0:T(8,128)(2,1)}, u32[]{:S(2)}, u32[]{:S(2)}) collective-permute-start(bf16[384,1536]{1,0:T(8,128)(2,1)} %get-tuple-element.51), channel_id=1, source_target_pairs={{0,32},{32,64},{64,96},{96,0},{1,33},{33,65},{65,97},{97,1},{2,34}... | collective-permute-start | bytes 3538952 | tf_op jit(solution)/shard_map/ppermute | solution.py:136
  195.0 51.7 %collective-permute-start.5 = (bf16[384,1536]{1,0:T(8,128)(2,1)}, bf16[384,1536]{1,0:T(8,128)(2,1)}, u32[]{:S(2)}, u32[]{:S(2)}) collective-permute-start(bf16[384,1536]{1,0:T(8,128)(2,1)} %get-tuple-element.51), channel_id=1, source_target_pairs={{0,96},{32,0},{64,32},{96,64},{1,97},{33,1},{65,33},{97,65},{2,98}... | collective-permute-start | bytes 3538952 | tf_op jit(solution)/shard_map/ppermute | solution.py:136
Sparse Core Ops, SparseCore 0:
  131.7 64.1 reduce-scatter.1

commit v12 on v10

--- a/solution.py
+++ b/solution.py
@@ -151,6 +151,7 @@
         + jnp.arange(fold, dtype=jnp.int32)[None, :, None]
     ).reshape(local_tokens * fold, top_count)
     pair_out = back_out.reshape(-1, narrow)[pair_index].astype(jnp.float32)
+    grad_joined, back_grad = lax.optimization_barrier((grad_joined, back_grad))
     pair_back = back_grad.reshape(-1, narrow)[pair_index].astype(jnp.float32)
     gate_rows = jnp.repeat(gate_values, fold, axis=0)
     output = (

time: 274 us -> 265 us (0.967)
  waiting for transfers between devices: 84.8 us -> 73.4 us
    all_to_all x1, waiting for transfers between devices: 24.6 us -> 9.94 us  [local(): lax.all_to_all(pair_grad.reshape(flat_shape), ('outer', 'inner'), split_a...]
    reduce_scatter x1, waiting for transfers between devices: 0.01 us -> 3.3 us  [local(): lax.psum_scatter(contract_first(columns, hidden).astype(jnp.bfloat16), 'd...]
    unnamed x36 -> x34, local copies, waits for them, and re-layouts: 8.97 us -> 8.88 us
  transfers between devices with their start and end apart: 9 -> 9, of which waited for: 4 -> 5; matrix products, arithmetic and copies ran while one was open for 42% -> 45% of each run, Pallas kernels for 0% -> 0%
where the time goes in v12:
time: 265 us; the launch traced here: 263 us
  local copies, waits for them, and re-layouts  77.8 us (29%)
  waiting for transfers between devices  73.4 us (28%)
  matrix products  52.3 us (20%)
  starting transfers between devices  29.4 us (11%)
  other arithmetic  16 us (6%)
  between operations  14.5 us (5%)
    all_to_all x1, waiting for transfers between devices, local(): lax.all_to_all(send_rows.reshape(flat_shape), ('outer', 'inner'), split_a...  24.3 us
    all_to_all x1, waiting for transfers between devices, local(): lax.all_to_all(expert_out.reshape(flat_shape), ('outer', 'inner'), split_...  20.1 us
    dot_general x3, matrix products, contract_last(): lax.dot_general(left, right, (((1,), (1,)), ((), ())), preferred_element_...  19.4 us
    all_to_all x1, waiting for transfers between devices, local(): lax.all_to_all(send_grads.reshape(flat_shape), ('outer', 'inner'), split_...  15.7 us
    all_to_all x1, waiting for transfers between devices, local(): lax.all_to_all(pair_grad.reshape(flat_shape), ('outer', 'inner'), split_a...  9.94 us
    dot_general x1, matrix products, local(): lax.dot_general(rows_all, joined_all, (((0, 1), (0, 1)), ((), ())), prefe...  9.32 us
    unnamed x34, local copies, waits for them, and re-layouts  8.88 us
    gather x1, local copies, waits for them, and re-layouts, local(): pair_out = back_out.reshape(-1, narrow)[pair_index].astype(jnp.float32)  8.52 us
  transfers between devices with their start and end apart: 9, of which 5 were waited for; matrix products, arithmetic and copies ran while one was open for 45% of the time, Pallas kernels for 0%

profile of v12, /device:TPU:8, one launch (start us, length us, event | category | flops | bytes accessed | tf_op | source)
XLA Modules:
  0.0 263.4 jit_solution(12816260635576294409)
XLA Ops:
  12.2 5.8 %gather_fusion.2 = bf16[1536,1024]{1,0:T(8,128)(2,1)} fusion(bf16[132,1024]{1,0:T(8,128)(2,1)S(1)} %reshape.257, s32[2048]{0:T(1024)S(1)} %pad_clamp_fusion), kind=kCustom, calls=%fused_computation.2 | custom fusion | bytes 6297600 | tf_op jit(solution)/shard_map/gather | solution.py:70
  18.0 7.7 %all-to-all-start.1 = ((bf16[32,48,1024]{2,1,0:T(8,128)(2,1)}), bf16[32,48,1024]{2,1,0:T(8,128)(2,1)S(1)}, u32[]{:S(2)}, u32[]{:S(2)}) async-start(bf16[32,48,1024]{2,1,0:T(8,128)(2,1)} %bitcast.90), calls=%async_computation.1 | async-start | bytes 6291456 | tf_op jit(solution)/shard_map/all_to_all | solution.py:76
  30.8 5.9 %gather_fusion.1 = bf16[1536,1024]{1,0:T(8,128)(2,1)} fusion(bf16[132,1024]{1,0:T(8,128)(2,1)S(1)} %reshape.255, s32[2048]{0:T(1024)S(1)} %pad_clamp_fusion), kind=kCustom, calls=%fused_computation.1 | custom fusion | bytes 6297600 | tf_op jit(solution)/shard_map/gather | solution.py:73
  36.7 4.1 %fusion = bf16[32,48,1024]{2,1,0:T(8,128)(2,1)} fusion(bf16[32,48,1024]{2,1,0:T(8,128)(2,1)} %bitcast.91, f32[32,48]{1,0:T(8,128)S(1)} %copy.43), kind=kLoop, calls=%fused_computation.9 | loop fusion | flops 4718592 | bytes 6297600 | tf_op jit(solution)/shard_map/convert_element_type | solution.py:74
  40.8 24.3 %all-to-all-done.1 = bf16[32,48,1024]{2,1,0:T(8,128)(2,1)S(1)} async-done(((bf16[32,48,1024]{2,1,0:T(8,128)(2,1)}), bf16[32,48,1024]{2,1,0:T(8,128)(2,1)S(1)}, u32[]{:S(2)}, u32[]{:S(2)}) %all-to-all-start.1) | async-done | bytes 3145760 | tf_op jit(solution)/shard_map/all_to_all | solution.py:76
  65.1 5.3 %all-to-all-start = ((bf16[32,48,1024]{2,1,0:T(8,128)(2,1)}), bf16[32,48,1024]{2,1,0:T(8,128)(2,1)}, u32[]{:S(2)}, u32[]{:S(2)}) async-start(bf16[32,48,1024]{2,1,0:T(8,128)(2,1)} %fusion), calls=%async_computation | async-start | bytes 6291456 | tf_op jit(solution)/shard_map/all_to_all | solution.py:83
  78.1 4.0 %collective-permute-start.2 = (bf16[384,1024]{1,0:T(8,128)(2,1)}, bf16[384,1024]{1,0:T(8,128)(2,1)}, u32[]{:S(2)}, u32[]{:S(2)}) collective-permute-start(bf16[384,1024]{1,0:T(8,128)(2,1)} %get-tuple-element.45), channel_id=1, source_target_pairs={{0,96},{32,0},{64,32},{96,64},{1,97},{33,1},{65,33},{97,65},{2,98}... | collective-permute-start | bytes 2359304 | tf_op jit(solution)/shard_map/ppermute | solution.py:99
  83.4 6.0 %fusion.11 = f32[384,768]{1,0:T(8,128)S(1)} fusion(bf16[384,4096]{1,0:T(8,128)(2,1)S(1)} %copy-done.1, bf16[1,4096,768]{2,1,0:T(8,128)(2,1)} %param.11), kind=kOutput, calls=%fused_computation.20 | convolution fusion | flops 2415919104 | bytes 10616832 | tf_op jit(solution)/shard_map/dot_general | solution.py:102
  94.2 15.7 %all-to-all-done = bf16[32,48,1024]{2,1,0:T(8,128)(2,1)} async-done(((bf16[32,48,1024]{2,1,0:T(8,128)(2,1)}), bf16[32,48,1024]{2,1,0:T(8,128)(2,1)}, u32[]{:S(2)}, u32[]{:S(2)}) %all-to-all-start) | async-done | bytes 3145760 | tf_op jit(solution)/shard_map/all_to_all | solution.py:83
  110.0 5.9 %reshape.256 = bf16[384,4096]{1,0:T(8,128)(2,1)} reshape(bf16[32,48,1024]{2,1,0:T(8,128)(2,1)} %all-to-all-done) | data formatting | bytes 6291456 | tf_op jit(solution)/shard_map/reshape | solution.py:92
  115.9 5.6 %fusion.15 = bf16[384,4096]{1,0:T(8,128)(2,1)S(1)} fusion(bf16[384,768]{1,0:T(8,128)(2,1)} %get-tuple-element.54, bf16[1,768,4096]{2,1,0:T(8,128)(2,1)} %param.13), kind=kOutput, calls=%fused_computation.23 | convolution fusion | flops 2417491968 | bytes 10027008 | tf_op jit(solution)/shard_map/dot_general | solution.py:107
  126.0 6.0 %multiply_convert_fusion.1 = (bf16[384,768]{1,0:T(8,128)(2,1)S(1)}, bf16[384,768]{1,0:T(8,128)(2,1)S(1)}) fusion(f32[384,768]{1,0:T(8,128)S(1)} %copy-done.11, f32[384,768]{1,0:T(8,128)S(1)} %copy-done.12, bf16[384,4096]{1,0:T(8,128)(2,1)S(1)} %copy-done.2, bf16[1,768,4096]{2,1,0:T(8,128)(2,1)} %param.13), kind=kOutput, calls=%fused_computation.39 | convolution fusion | flops 2419752960 | bytes 12976128 | tf_op jit(solution)/shard_map/dot_general | solution.py:8
  134.4 8.2 %convolution_convert_fusion = bf16[4096,768]{1,0:T(8,128)(2,1)} fusion(bf16[384,4096]{1,0:T(8,128)(2,1)} %reshape.256, bf16[384,768]{1,0:T(8,128)(2,1)} %get-tuple-element.54), kind=kOutput, calls=%fused_computation.7 | convolution fusion | flops 2419064832 | bytes 10027008 | tf_op jit(solution)/shard_map/dot_general | solution.py:14
  146.3 5.6 %all-to-all-start.2 = ((bf16[32,48,1024]{2,1,0:T(8,128)(2,1)}), bf16[32,48,1024]{2,1,0:T(8,128)(2,1)S(1)}, u32[]{:S(2)}, u32[]{:S(2)}) async-start(bf16[32,48,1024]{2,1,0:T(8,128)(2,1)} %reshape.260), calls=%async_computation.2 | async-start | bytes 6291456 | tf_op jit(solution)/shard_map/all_to_all | solution.py:117
  151.9 5.0 %fusion.5 = f32[384,4096]{1,0:T(8,128)S(1)} fusion(bf16[384,768]{1,0:T(8,128)(2,1)} %copy-done.8, bf16[1,4096,768]{2,1,0:T(8,128)(2,1)} %param.12), kind=kOutput, calls=%fused_computation.14 | convolution fusion | flops 2415919104 | bytes 13172736 | tf_op jit(solution)/shard_map/dot_general | solution.py:8
  156.9 8.4 %add_convert_fusion = bf16[384,4096]{1,0:T(8,128)(2,1)} fusion(f32[384,4096]{1,0:T(8,128)S(1)} %fusion.5, bf16[384,768]{1,0:T(8,128)(2,1)S(1)} %copy-done.7, bf16[1,4096,768]{2,1,0:T(8,128)(2,1)} %param.11), kind=kOutput, calls=%fused_computation.22 | convolution fusion | flops 2419064832 | bytes 16318464 | tf_op jit(solution)/shard_map/dot_general | solution.py:8
  165.3 6.0 %reshape.262 = bf16[32,48,1024]{2,1,0:T(8,128)(2,1)} reshape(bf16[384,4096]{1,0:T(8,128)(2,1)} %add_convert_fusion) | data formatting | bytes 6291456 | tf_op jit(solution)/shard_map/reshape | solution.py:125
  171.3 20.1 %all-to-all-done.2 = bf16[32,48,1024]{2,1,0:T(8,128)(2,1)S(1)} async-done(((bf16[32,48,1024]{2,1,0:T(8,128)(2,1)}), bf16[32,48,1024]{2,1,0:T(8,128)(2,1)S(1)}, u32[]{:S(2)}, u32[]{:S(2)}) %all-to-all-start.2) | async-done | bytes 3145760 | tf_op jit(solution)/shard_map/all_to_all | solution.py:117
  193.0 5.3 %all-to-all-start.3 = ((bf16[32,48,1024]{2,1,0:T(8,128)(2,1)}), bf16[32,48,1024]{2,1,0:T(8,128)(2,1)S(1)}, u32[]{:S(2)}, u32[]{:S(2)}) async-start(bf16[32,48,1024]{2,1,0:T(8,128)(2,1)} %reshape.262), calls=%async_computation.3 | async-start | bytes 6291456 | tf_op jit(solution)/shard_map/all_to_all | solution.py:124
  199.6 8.5 %gather_fusion.3 = bf16[1024,1024]{1,0:T(8,128)(2,1)} fusion(bf16[1536,1024]{1,0:T(8,128)(2,1)} %bitcast.89, s32[1024]{0:T(1024)S(1)} %broadcast_clamp_fusion), kind=kCustom, calls=%fused_computation.3 | custom fusion | bytes 4198400 | tf_op jit(solution)/shard_map/gather | solution.py:153
  213.1 5.3 %gather_fusion.4 = bf16[4,384,1536]{2,1,0:T(8,128)(2,1)} fusion(bf16[4,384,1536]{2,1,0:T(8,128)(2,1)} %bitcast.92, s32[1024]{0:T(1024)S(1)} %pad_clamp_fusion.1), kind=kCustom, calls=%fused_computation.4 | custom fusion | bytes 9437200 | tf_op jit(solution)/shard_map/jit(_take)/gather | solution.py:134
  218.4 9.3 %fusion.21 = bf16[1024,1536]{1,0:T(8,128)(2,1)} fusion(bf16[4,384,1024]{2,1,0:T(8,128)(2,1)} %pad_maximum_fusion, bf16[4,384,1536]{2,1,0:T(8,128)(2,1)} %gather_fusion.4, pred[4]{0:T(512)(128)(4,1)S(1)} %compare_and_fusion), kind=kOutput, calls=%fused_computation.29 | convolution fusion | flops 4834197504 | bytes 11010052 | tf_op jit(solution)/shard_map/dot_general | solution.py:135
  227.8 9.9 %all-to-all-done.3 = bf16[32,48,1024]{2,1,0:T(8,128)(2,1)S(1)} async-done(((bf16[32,48,1024]{2,1,0:T(8,128)(2,1)}), bf16[32,48,1024]{2,1,0:T(8,128)(2,1)S(1)}, u32[]{:S(2)}, u32[]{:S(2)}) %all-to-all-start.3) | async-done | bytes 3145760 | tf_op jit(solution)/shard_map/all_to_all | solution.py:124
  237.7 5.4 %gather_fusion.5 = bf16[1024,1024]{1,0:T(8,128)(2,1)} fusion(bf16[1536,1024]{1,0:T(8,128)(2,1)S(1)} %bitcast.88, s32[1024]{0:T(1024)S(1)} %broadcast_clamp_fusion), kind=kCustom, calls=%fused_computation.5 | custom fusion | bytes 4198400 | tf_op jit(solution)/shard_map/gather | solution.py:155
  (100 shorter events, 55.6 us)
Async XLA Ops:
  18.0 7.7 %copy-start.9 = (f32[32,8]{0,1:T(8,128)S(1)}, f32[32,8]{0,1:T(8,128)}, u32[]{:S(2)}) copy-start(f32[32,8]{0,1:T(8,128)} %param.9) | copy-start | bytes 3076
  18.0 10.9 %copy-start.4 = (bf16[32,4096]{1,0:T(8,128)(2,1)S(1)}, bf16[32,4096]{1,0:T(8,128)(2,1)}, u32[]{:S(2)}) copy-start(bf16[32,4096]{1,0:T(8,128)(2,1)} %param.10) | copy-start | bytes 786436
  18.0 47.2 %all-to-all-start.1 = ((bf16[32,48,1024]{2,1,0:T(8,128)(2,1)}), bf16[32,48,1024]{2,1,0:T(8,128)(2,1)S(1)}, u32[]{:S(2)}, u32[]{:S(2)}) async-start(bf16[32,48,1024]{2,1,0:T(8,128)(2,1)} %bitcast.90), calls=%async_computation.1 | async-start | bytes 6291456 | tf_op jit(solution)/shard_map/all_to_all | solution.py:76
  65.1 44.9 %all-to-all-start = ((bf16[32,48,1024]{2,1,0:T(8,128)(2,1)}), bf16[32,48,1024]{2,1,0:T(8,128)(2,1)}, u32[]{:S(2)}, u32[]{:S(2)}) async-start(bf16[32,48,1024]{2,1,0:T(8,128)(2,1)} %fusion), calls=%async_computation | async-start | bytes 6291456 | tf_op jit(solution)/shard_map/all_to_all | solution.py:83
  70.4 142.7 %all-gather.3.cloned.1.call-start = ((), (), s32[]{:S(2)}) async-start(), calls=%async_computation.6 | async-start | bytes 5898240 | tf_op jit(solution)/shard_map/all_gather | solution.py:134
  74.3 9.1 %copy-start.1 = (bf16[384,4096]{1,0:T(8,128)(2,1)S(1)}, bf16[384,4096]{1,0:T(8,128)(2,1)}, u32[]{:S(2)}) copy-start(bf16[384,4096]{1,0:T(8,128)(2,1)} %reshape.259) | copy-start | bytes 9437188
  78.1 43.5 %collective-permute-start.2 = (bf16[384,1024]{1,0:T(8,128)(2,1)}, bf16[384,1024]{1,0:T(8,128)(2,1)}, u32[]{:S(2)}, u32[]{:S(2)}) collective-permute-start(bf16[384,1024]{1,0:T(8,128)(2,1)} %get-tuple-element.45), channel_id=1, source_target_pairs={{0,96},{32,0},{64,32},{96,64},{1,97},{33,1},{65,33},{97,65},{2,98}... | collective-permute-start | bytes 2359304 | tf_op jit(solution)/shard_map/ppermute | solution.py:99
  82.1 39.5 %collective-permute-start.1 = (bf16[384,1024]{1,0:T(8,128)(2,1)}, bf16[384,1024]{1,0:T(8,128)(2,1)}, u32[]{:S(2)}, u32[]{:S(2)}) collective-permute-start(bf16[384,1024]{1,0:T(8,128)(2,1)} %get-tuple-element.46), channel_id=1, source_target_pairs={{0,64},{32,96},{64,0},{96,32},{1,65},{33,97},{65,1},{97,33},{2,66}... | collective-permute-start | bytes 2359304 | tf_op jit(solution)/shard_map/ppermute | solution.py:99
  82.1 8.3 %slice-start = ((s8[6291456]{0:T(1024)(128)(4,1)}), s8[4194304]{0:T(1024)(128)(4,1)S(1)}, s32[]{:S(2)}) async-start(s8[6291456]{0:T(1024)(128)(4,1)} %bitcast.100), calls=%async_computation.7 | async-start | bytes 8388608
  82.1 8.3 %slice-start.1 = ((s8[6291456]{0:T(1024)(128)(4,1)}), s8[2097152]{0:T(1024)(128)(4,1)S(1)}, s32[]{:S(2)}) async-start(s8[6291456]{0:T(1024)(128)(4,1)} %bitcast.100), calls=%async_computation.8 | async-start | bytes 4194304
  82.1 39.5 %collective-permute-start = (bf16[384,1024]{1,0:T(8,128)(2,1)}, bf16[384,1024]{1,0:T(8,128)(2,1)}, u32[]{:S(2)}, u32[]{:S(2)}) collective-permute-start(bf16[384,1024]{1,0:T(8,128)(2,1)} %get-tuple-element.47), channel_id=1, source_target_pairs={{0,32},{32,64},{64,96},{96,0},{1,33},{33,65},{65,97},{97,1},{2,34}... | collective-permute-start | bytes 2359304 | tf_op jit(solution)/shard_map/ppermute | solution.py:99
  89.4 1.0 copy-start.10
  115.9 5.7 %copy-start.3 = (bf16[1,384,1024]{2,1,0:T(8,128)(2,1)S(1)}, bf16[1,384,1024]{2,1,0:T(8,128)(2,1)}, u32[]{:S(2)}) copy-start(bf16[1,384,1024]{2,1,0:T(8,128)(2,1)} %get-tuple-element.44) | copy-start | bytes 2359300
  121.6 3.3 %copy-start.2 = (bf16[384,4096]{1,0:T(8,128)(2,1)S(1)}, bf16[384,4096]{1,0:T(8,128)(2,1)}, u32[]{:S(2)}) copy-start(bf16[384,4096]{1,0:T(8,128)(2,1)} %reshape.256) | copy-start | bytes 9437188
  121.6 3.8 %copy-start.11 = (f32[384,768]{1,0:T(8,128)S(1)}, f32[384,768]{1,0:T(8,128)}, u32[]{:S(2)}) copy-start(f32[384,768]{1,0:T(8,128)} %copy-done.10) | copy-start | bytes 3538948
  121.6 4.4 %copy-start.12 = (f32[384,768]{1,0:T(8,128)S(1)}, f32[384,768]{1,0:T(8,128)}, u32[]{:S(2)}) copy-start(f32[384,768]{1,0:T(8,128)} %get-tuple-element.55) | copy-start | bytes 3538948
  132.0 0.8 copy-start.6
  132.0 1.0 copy-start.8
  134.1 119.9 %reduce-scatter.2.cloned.1.call-start = ((), (), s32[]{:S(2)}) async-start(), calls=%async_computation.5 | async-start | bytes 7864320 | tf_op jit(solution)/shard_map/reduce_scatter | solution.py:140
  146.3 45.1 %all-to-all-start.2 = ((bf16[32,48,1024]{2,1,0:T(8,128)(2,1)}), bf16[32,48,1024]{2,1,0:T(8,128)(2,1)S(1)}, u32[]{:S(2)}, u32[]{:S(2)}) async-start(bf16[32,48,1024]{2,1,0:T(8,128)(2,1)} %reshape.260), calls=%async_computation.2 | async-start | bytes 6291456 | tf_op jit(solution)/shard_map/all_to_all | solution.py:117
  151.9 5.0 %copy-start.7 = (bf16[384,768]{1,0:T(8,128)(2,1)S(1)}, bf16[384,768]{1,0:T(8,128)(2,1)}, u32[]{:S(2)}) copy-start(bf16[384,768]{1,0:T(8,128)(2,1)} %copy-done.6) | copy-start | bytes 1769476
  171.3 27.0 %copy-start.5 = (bf16[32,4096]{1,0:T(8,128)(2,1)S(1)}, bf16[32,4096]{1,0:T(8,128)(2,1)}, u32[]{:S(2)}) copy-start(bf16[32,4096]{1,0:T(8,128)(2,1)} %param.10) | copy-start | bytes 786436
  191.4 1.7 copy-start
  193.0 44.7 %all-to-all-start.3 = ((bf16[32,48,1024]{2,1,0:T(8,128)(2,1)}), bf16[32,48,1024]{2,1,0:T(8,128)(2,1)S(1)}, u32[]{:S(2)}, u32[]{:S(2)}) async-start(bf16[32,48,1024]{2,1,0:T(8,128)(2,1)} %reshape.262), calls=%async_computation.3 | async-start | bytes 6291456 | tf_op jit(solution)/shard_map/all_to_all | solution.py:124
Sparse Core Ops, SparseCore 0:
  134.2 52.8 all-gather.2
  189.5 64.4 reduce-scatter.1

commit v13 on v10

--- a/solution.py
+++ b/solution.py
@@ -105,7 +105,8 @@
     silu_value = gate_pre * sigma
     hidden = (silu_value * up_pre).astype(jnp.bfloat16)
     expert_out = jnp.dot(hidden, down_mat, preferred_element_type=jnp.float32).astype(jnp.bfloat16)
-    grads_in, rows_all, expert_out = lax.optimization_barrier((grads_in, rows_all, expert_out))
+    out_send = expert_out.reshape(flat_shape)
+    grads_in, rows_all, out_send = lax.optimization_barrier((grads_in, rows_all, out_send))
     grad_hidden = contract_last(grads_in, down_mat)
     slope = sigma * (1.0 + gate_pre * (1.0 - sigma))
     grad_gate_pre = (grad_hidden * up_pre * slope).astype(jnp.bfloat16)
@@ -115,7 +116,7 @@
     ).astype(jnp.bfloat16)
     back_out, back_grad = (
         lax.all_to_all(
-            expert_out.reshape(flat_shape),
+            out_send,
             ("outer", "inner"),
             split_axis=0,
             concat_axis=0,
@@ -151,6 +152,9 @@
         + jnp.arange(fold, dtype=jnp.int32)[None, :, None]
     ).reshape(local_tokens * fold, top_count)
     pair_out = back_out.reshape(-1, narrow)[pair_index].astype(jnp.float32)
+    grad_w_gate = grad_joined[:, :ff_width].astype(jnp.bfloat16)[None]
+    grad_w_up = grad_joined[:, ff_width:].astype(jnp.bfloat16)[None]
+    grad_w_gate, grad_w_up, back_grad = lax.optimization_barrier((grad_w_gate, grad_w_up, back_grad))
     pair_back = back_grad.reshape(-1, narrow)[pair_index].astype(jnp.float32)
     gate_rows = jnp.repeat(gate_values, fold, axis=0)
     output = (
@@ -162,8 +166,6 @@
         jnp.sum(upstream_rows[:, None, :] * pair_out, axis=2).reshape(local_tokens, fold, top_count),
         axis=1,
     )
-    grad_w_gate = grad_joined[:, :ff_width].astype(jnp.bfloat16)[None]
-    grad_w_up = grad_joined[:, ff_width:].astype(jnp.bfloat16)[None]
     grad_w_down = grad_down.astype(jnp.bfloat16)[None]
     return (output, grad_tokens, grad_gates, grad_w_gate, grad_w_up, grad_w_down)
 

time: 274 us -> 261 us (0.953)
  waiting for transfers between devices: 84.8 us -> 77.8 us
  matrix products: 51.2 us -> 46.1 us
    all_to_all x1, waiting for transfers between devices: 24.6 us -> 8.97 us  [local(): lax.all_to_all(pair_grad.reshape(flat_shape), ('outer', 'inner'), split_a...]
    reduce_scatter x1, waiting for transfers between devices: 0.01 us -> 9.33 us  [local(): lax.psum_scatter(contract_first(columns, hidden).astype(jnp.bfloat16), 'd...]
    all_to_all x1, waiting for transfers between devices: 15.8 us -> 9.58 us  [local(): lax.all_to_all(send_grads.reshape(flat_shape), ('outer', 'inner'), split_...]
    ppermute x3, waiting for transfers between devices: 0.01 us -> 5.53 us  [local(): lax.ppermute(outgoing, 'dp', [(j, (j + shift) % dp_count) for j in range(...]
    dot_general x1, matrix products: 5.65 us -> 2.8 us  [local(): jnp.dot(hidden, down_mat, preferred_element_type=jnp.float32)]
  transfers between devices with their start and end apart: 9 -> 9, of which waited for: 4 -> 7; matrix products, arithmetic and copies ran while one was open for 42% -> 42% of each run, Pallas kernels for 0% -> 0%
where the time goes in v13:
time: 261 us; the launch traced here: 259 us
  waiting for transfers between devices  77.8 us (30%)
  local copies, waits for them, and re-layouts  73.8 us (28%)
  matrix products  46.1 us (18%)
  starting transfers between devices  31 us (12%)
  other arithmetic  16.1 us (6%)
  between operations  14.5 us (6%)
    all_to_all x1, waiting for transfers between devices, local(): lax.all_to_all(send_rows.reshape(flat_shape), ('outer', 'inner'), split_a...  24.3 us
    all_to_all x1, waiting for transfers between devices, local(): lax.all_to_all(out_send, ('outer', 'inner'), split_axis=0, concat_axis=0,...  20 us
    dot_general x3, matrix products, contract_last(): lax.dot_general(left, right, (((1,), (1,)), ((), ())), preferred_element_...  19.1 us
    all_to_all x1, waiting for transfers between devices, local(): lax.all_to_all(send_grads.reshape(flat_shape), ('outer', 'inner'), split_...  9.58 us
    reduce_scatter x1, waiting for transfers between devices, local(): lax.psum_scatter(contract_first(columns, hidden).astype(jnp.bfloat16), 'd...  9.33 us
    all_to_all x1, waiting for transfers between devices, local(): lax.all_to_all(pair_grad.reshape(flat_shape), ('outer', 'inner'), split_a...  8.97 us
    gather x1, local copies, waits for them, and re-layouts, local(): pair_out = back_out.reshape(-1, narrow)[pair_index].astype(jnp.float32)  8.75 us
    dot_general x1, matrix products, local(): lax.dot_general(rows_all, joined_all, (((0, 1), (0, 1)), ((), ())), prefe...  8.09 us
  transfers between devices with their start and end apart: 9, of which 7 were waited for; matrix products, arithmetic and copies ran while one was open for 42% of the time, Pallas kernels for 0%

profile of v13, /device:TPU:8, one launch (start us, length us, event | category | flops | bytes accessed | tf_op | source)
XLA Modules:
  0.0 259.3 jit_solution(16850525532553247143)
XLA Ops:
  12.2 5.8 %gather_fusion.2 = bf16[1536,1024]{1,0:T(8,128)(2,1)} fusion(bf16[132,1024]{1,0:T(8,128)(2,1)S(1)} %reshape.257, s32[2048]{0:T(1024)S(1)} %pad_clamp_fusion), kind=kCustom, calls=%fused_computation.2 | custom fusion | bytes 6297600 | tf_op jit(solution)/shard_map/gather | solution.py:70
  18.0 7.7 %all-to-all-start.1 = ((bf16[32,48,1024]{2,1,0:T(8,128)(2,1)}), bf16[32,48,1024]{2,1,0:T(8,128)(2,1)S(1)}, u32[]{:S(2)}, u32[]{:S(2)}) async-start(bf16[32,48,1024]{2,1,0:T(8,128)(2,1)} %bitcast.90), calls=%async_computation.1 | async-start | bytes 6291456 | tf_op jit(solution)/shard_map/all_to_all | solution.py:76
  30.8 5.9 %gather_fusion.1 = bf16[1536,1024]{1,0:T(8,128)(2,1)} fusion(bf16[132,1024]{1,0:T(8,128)(2,1)S(1)} %reshape.255, s32[2048]{0:T(1024)S(1)} %pad_clamp_fusion), kind=kCustom, calls=%fused_computation.1 | custom fusion | bytes 6297600 | tf_op jit(solution)/shard_map/gather | solution.py:73
  36.7 4.1 %fusion = bf16[32,48,1024]{2,1,0:T(8,128)(2,1)} fusion(bf16[32,48,1024]{2,1,0:T(8,128)(2,1)} %bitcast.91, f32[32,48]{1,0:T(8,128)S(1)} %copy.43), kind=kLoop, calls=%fused_computation.9 | loop fusion | flops 4718592 | bytes 6297600 | tf_op jit(solution)/shard_map/convert_element_type | solution.py:74
  40.8 24.3 %all-to-all-done.1 = bf16[32,48,1024]{2,1,0:T(8,128)(2,1)S(1)} async-done(((bf16[32,48,1024]{2,1,0:T(8,128)(2,1)}), bf16[32,48,1024]{2,1,0:T(8,128)(2,1)S(1)}, u32[]{:S(2)}, u32[]{:S(2)}) %all-to-all-start.1) | async-done | bytes 3145760 | tf_op jit(solution)/shard_map/all_to_all | solution.py:76
  65.2 5.3 %all-to-all-start = ((bf16[32,48,1024]{2,1,0:T(8,128)(2,1)}), bf16[32,48,1024]{2,1,0:T(8,128)(2,1)}, u32[]{:S(2)}, u32[]{:S(2)}) async-start(bf16[32,48,1024]{2,1,0:T(8,128)(2,1)} %fusion), calls=%async_computation | async-start | bytes 6291456 | tf_op jit(solution)/shard_map/all_to_all | solution.py:83
  78.1 4.0 %collective-permute-start.2 = (bf16[384,1024]{1,0:T(8,128)(2,1)}, bf16[384,1024]{1,0:T(8,128)(2,1)}, u32[]{:S(2)}, u32[]{:S(2)}) collective-permute-start(bf16[384,1024]{1,0:T(8,128)(2,1)} %get-tuple-element.47), channel_id=1, source_target_pairs={{0,96},{32,0},{64,32},{96,64},{1,97},{33,1},{65,33},{97,65},{2,98}... | collective-permute-start | bytes 2359304 | tf_op jit(solution)/shard_map/ppermute | solution.py:99
  83.4 6.0 %fusion.11 = f32[384,768]{1,0:T(8,128)S(1)} fusion(bf16[384,4096]{1,0:T(8,128)(2,1)S(1)} %copy-done.1, bf16[1,4096,768]{2,1,0:T(8,128)(2,1)} %param.11), kind=kOutput, calls=%fused_computation.21 | convolution fusion | flops 2415919104 | bytes 10616832 | tf_op jit(solution)/shard_map/dot_general | solution.py:102
  100.4 9.6 %all-to-all-done = bf16[32,48,1024]{2,1,0:T(8,128)(2,1)} async-done(((bf16[32,48,1024]{2,1,0:T(8,128)(2,1)}), bf16[32,48,1024]{2,1,0:T(8,128)(2,1)}, u32[]{:S(2)}, u32[]{:S(2)}) %all-to-all-start) | async-done | bytes 3145760 | tf_op jit(solution)/shard_map/all_to_all | solution.py:83
  110.0 4.5 %reshape.256 = bf16[384,4096]{1,0:T(8,128)(2,1)S(1)} reshape(bf16[32,48,1024]{2,1,0:T(8,128)(2,1)} %all-to-all-done) | data formatting | bytes 6291456 | tf_op jit(solution)/shard_map/reshape | solution.py:92
  123.4 5.8 %multiply_convert_fusion.1 = (bf16[384,768]{1,0:T(8,128)(2,1)S(1)}, bf16[384,768]{1,0:T(8,128)(2,1)S(1)}) fusion(f32[384,768]{1,0:T(8,128)S(1)} %copy-done.10, f32[384,768]{1,0:T(8,128)S(1)} %copy-done.11, bf16[384,4096]{1,0:T(8,128)(2,1)S(1)} %reshape.256, bf16[1,768,4096]{2,1,0:T(8,128)(2,1)} %param.13), kind=kOutput, calls=%fused_computation.39 | convolution fusion | flops 2419752960 | bytes 12976128 | tf_op jit(solution)/shard_map/dot_general | solution.py:8
  131.4 6.4 %convolution_convert_fusion = bf16[4096,768]{1,0:T(8,128)(2,1)} fusion(bf16[384,4096]{1,0:T(8,128)(2,1)S(1)} %reshape.256, bf16[384,768]{1,0:T(8,128)(2,1)} %copy-done.8), kind=kOutput, calls=%fused_computation.7 | convolution fusion | flops 2419064832 | bytes 10027008 | tf_op jit(solution)/shard_map/dot_general | solution.py:14
  137.8 7.4 %all-to-all-start.2 = ((bf16[32,48,1024]{2,1,0:T(8,128)(2,1)}), bf16[32,48,1024]{2,1,0:T(8,128)(2,1)S(1)}, u32[]{:S(2)}, u32[]{:S(2)}) async-start(bf16[32,48,1024]{2,1,0:T(8,128)(2,1)} %reshape.260), calls=%async_computation.2 | async-start | bytes 6291456 | tf_op jit(solution)/shard_map/all_to_all | solution.py:118
  145.3 4.9 %fusion.5 = f32[384,4096]{1,0:T(8,128)S(1)} fusion(bf16[384,768]{1,0:T(8,128)(2,1)} %copy-done.6, bf16[1,4096,768]{2,1,0:T(8,128)(2,1)} %param.12), kind=kOutput, calls=%fused_computation.15 | convolution fusion | flops 2415919104 | bytes 13172736 | tf_op jit(solution)/shard_map/dot_general | solution.py:8
  150.2 8.4 %add_convert_fusion = bf16[384,4096]{1,0:T(8,128)(2,1)} fusion(f32[384,4096]{1,0:T(8,128)S(1)} %fusion.5, bf16[384,768]{1,0:T(8,128)(2,1)S(1)} %copy-done.5, bf16[1,4096,768]{2,1,0:T(8,128)(2,1)} %param.11), kind=kOutput, calls=%fused_computation.23 | convolution fusion | flops 2419064832 | bytes 16318464 | tf_op jit(solution)/shard_map/dot_general | solution.py:8
  158.7 6.0 %reshape.262 = bf16[32,48,1024]{2,1,0:T(8,128)(2,1)} reshape(bf16[384,4096]{1,0:T(8,128)(2,1)} %add_convert_fusion) | data formatting | bytes 6291456 | tf_op jit(solution)/shard_map/reshape | solution.py:126
  164.6 20.0 %all-to-all-done.2 = bf16[32,48,1024]{2,1,0:T(8,128)(2,1)S(1)} async-done(((bf16[32,48,1024]{2,1,0:T(8,128)(2,1)}), bf16[32,48,1024]{2,1,0:T(8,128)(2,1)S(1)}, u32[]{:S(2)}, u32[]{:S(2)}) %all-to-all-start.2) | async-done | bytes 3145760 | tf_op jit(solution)/shard_map/all_to_all | solution.py:118
  186.4 5.3 %all-to-all-start.3 = ((bf16[32,48,1024]{2,1,0:T(8,128)(2,1)}), bf16[32,48,1024]{2,1,0:T(8,128)(2,1)S(1)}, u32[]{:S(2)}, u32[]{:S(2)}) async-start(bf16[32,48,1024]{2,1,0:T(8,128)(2,1)} %reshape.262), calls=%async_computation.3 | async-start | bytes 6291456 | tf_op jit(solution)/shard_map/all_to_all | solution.py:125
  193.1 8.8 %gather_fusion.3 = bf16[1024,1024]{1,0:T(8,128)(2,1)} fusion(bf16[1536,1024]{1,0:T(8,128)(2,1)} %bitcast.89, s32[1024]{0:T(1024)S(1)} %broadcast_clamp_fusion), kind=kCustom, calls=%fused_computation.3 | custom fusion | bytes 4198400 | tf_op jit(solution)/shard_map/gather | solution.py:154
  206.8 5.5 %gather_fusion.4 = bf16[4,384,1536]{2,1,0:T(8,128)(2,1)} fusion(bf16[4,384,1536]{2,1,0:T(8,128)(2,1)} %bitcast.92, s32[1024]{0:T(1024)S(1)} %pad_clamp_fusion.1), kind=kCustom, calls=%fused_computation.4 | custom fusion | bytes 9437200 | tf_op jit(solution)/shard_map/jit(_take)/gather | solution.py:135
  212.3 8.1 %bitcast_convert_fusion = bf16[1024,1536]{1,0:T(8,128)(2,1)S(1)} fusion(bf16[4,384,1024]{2,1,0:T(8,128)(2,1)} %pad_maximum_fusion, bf16[4,384,1536]{2,1,0:T(8,128)(2,1)} %gather_fusion.4, pred[4]{0:T(512)(128)(4,1)S(1)} %compare_and_fusion), kind=kOutput, calls=%fused_computation.10 | convolution fusion | flops 4835770368 | bytes 11010052 | tf_op jit(solution)/shard_map/dot_general | solution.py:136
  222.3 9.0 %all-to-all-done.3 = bf16[32,48,1024]{2,1,0:T(8,128)(2,1)S(1)} async-done(((bf16[32,48,1024]{2,1,0:T(8,128)(2,1)}), bf16[32,48,1024]{2,1,0:T(8,128)(2,1)S(1)}, u32[]{:S(2)}, u32[]{:S(2)}) %all-to-all-start.3) | async-done | bytes 3145760 | tf_op jit(solution)/shard_map/all_to_all | solution.py:125
  231.2 5.4 %gather_fusion.5 = bf16[1024,1024]{1,0:T(8,128)(2,1)} fusion(bf16[1536,1024]{1,0:T(8,128)(2,1)S(1)} %bitcast.88, s32[1024]{0:T(1024)S(1)} %broadcast_clamp_fusion), kind=kCustom, calls=%fused_computation.5 | custom fusion | bytes 4198400 | tf_op jit(solution)/shard_map/gather | solution.py:158
  240.6 9.3 %reduce-scatter.2.cloned.1.call-done = bf16[1024,768]{1,0:T(8,128)(2,1)} async-done(((bf16[4096,768]{1,0:T(8,128)(2,1)}), bf16[1024,768]{1,0:T(8,128)(2,1)}) %reduce-scatter.2.cloned.1.call-update) | async-done | bytes 1572880 | tf_op jit(solution)/shard_map/reduce_scatter | solution.py:141
  (103 shorter events, 57.4 us)
Async XLA Ops:
  18.0 7.7 %copy-start.7 = (f32[32,8]{0,1:T(8,128)S(1)}, f32[32,8]{0,1:T(8,128)}, u32[]{:S(2)}) copy-start(f32[32,8]{0,1:T(8,128)} %param.9) | copy-start | bytes 3076
  18.0 10.9 %copy-start.2 = (bf16[32,4096]{1,0:T(8,128)(2,1)S(1)}, bf16[32,4096]{1,0:T(8,128)(2,1)}, u32[]{:S(2)}) copy-start(bf16[32,4096]{1,0:T(8,128)(2,1)} %param.10) | copy-start | bytes 786436
  18.0 47.2 %all-to-all-start.1 = ((bf16[32,48,1024]{2,1,0:T(8,128)(2,1)}), bf16[32,48,1024]{2,1,0:T(8,128)(2,1)S(1)}, u32[]{:S(2)}, u32[]{:S(2)}) async-start(bf16[32,48,1024]{2,1,0:T(8,128)(2,1)} %bitcast.90), calls=%async_computation.1 | async-start | bytes 6291456 | tf_op jit(solution)/shard_map/all_to_all | solution.py:76
  65.2 44.9 %all-to-all-start = ((bf16[32,48,1024]{2,1,0:T(8,128)(2,1)}), bf16[32,48,1024]{2,1,0:T(8,128)(2,1)}, u32[]{:S(2)}, u32[]{:S(2)}) async-start(bf16[32,48,1024]{2,1,0:T(8,128)(2,1)} %fusion), calls=%async_computation | async-start | bytes 6291456 | tf_op jit(solution)/shard_map/all_to_all | solution.py:83
  70.5 136.3 %all-gather.3.cloned.1.call-start = ((), (), s32[]{:S(2)}) async-start(), calls=%async_computation.6 | async-start | bytes 5898240 | tf_op jit(solution)/shard_map/all_gather | solution.py:135
  74.3 9.0 %copy-start.1 = (bf16[384,4096]{1,0:T(8,128)(2,1)S(1)}, bf16[384,4096]{1,0:T(8,128)(2,1)}, u32[]{:S(2)}) copy-start(bf16[384,4096]{1,0:T(8,128)(2,1)} %reshape.259) | copy-start | bytes 9437188
  74.3 19.6 %slice-start = ((s8[6291456]{0:T(1024)(128)(4,1)}), s8[4194304]{0:T(1024)(128)(4,1)S(1)}, s32[]{:S(2)}) async-start(s8[6291456]{0:T(1024)(128)(4,1)} %bitcast.100), calls=%async_computation.7 | async-start | bytes 8388608
  78.1 38.3 %collective-permute-start.2 = (bf16[384,1024]{1,0:T(8,128)(2,1)}, bf16[384,1024]{1,0:T(8,128)(2,1)}, u32[]{:S(2)}, u32[]{:S(2)}) collective-permute-start(bf16[384,1024]{1,0:T(8,128)(2,1)} %get-tuple-element.47), channel_id=1, source_target_pairs={{0,96},{32,0},{64,32},{96,64},{1,97},{33,1},{65,33},{97,65},{2,98}... | collective-permute-start | bytes 2359304 | tf_op jit(solution)/shard_map/ppermute | solution.py:99
  82.1 34.3 %collective-permute-start.1 = (bf16[384,1024]{1,0:T(8,128)(2,1)}, bf16[384,1024]{1,0:T(8,128)(2,1)}, u32[]{:S(2)}, u32[]{:S(2)}) collective-permute-start(bf16[384,1024]{1,0:T(8,128)(2,1)} %get-tuple-element.48), channel_id=1, source_target_pairs={{0,64},{32,96},{64,0},{96,32},{1,65},{33,97},{65,1},{97,33},{2,66}... | collective-permute-start | bytes 2359304 | tf_op jit(solution)/shard_map/ppermute | solution.py:99
  82.1 7.3 %slice-start.2 = ((s8[6291456]{0:T(1024)(128)(4,1)}), s8[4194304]{0:T(1024)(128)(4,1)S(1)}, s32[]{:S(2)}) async-start(s8[6291456]{0:T(1024)(128)(4,1)} %bitcast.102), calls=%async_computation.9 | async-start | bytes 8388608
  82.1 7.3 %slice-start.3 = ((s8[6291456]{0:T(1024)(128)(4,1)}), s8[2097152]{0:T(1024)(128)(4,1)S(1)}, s32[]{:S(2)}) async-start(s8[6291456]{0:T(1024)(128)(4,1)} %bitcast.102), calls=%async_computation.10 | async-start | bytes 4194304
  82.1 11.8 %slice-start.1 = ((s8[6291456]{0:T(1024)(128)(4,1)}), s8[2097152]{0:T(1024)(128)(4,1)S(1)}, s32[]{:S(2)}) async-start(s8[6291456]{0:T(1024)(128)(4,1)} %bitcast.100), calls=%async_computation.8 | async-start | bytes 4194304
  82.1 37.9 %collective-permute-start = (bf16[384,1024]{1,0:T(8,128)(2,1)}, bf16[384,1024]{1,0:T(8,128)(2,1)}, u32[]{:S(2)}, u32[]{:S(2)}) collective-permute-start(bf16[384,1024]{1,0:T(8,128)(2,1)} %get-tuple-element.49), channel_id=1, source_target_pairs={{0,32},{32,64},{64,96},{96,0},{1,33},{33,65},{65,97},{97,1},{2,34}... | collective-permute-start | bytes 2359304 | tf_op jit(solution)/shard_map/ppermute | solution.py:99
  89.4 3.7 %copy-start.9 = (f32[384,768]{1,0:T(8,128)}, f32[384,768]{1,0:T(8,128)S(1)}, u32[]{:S(2)}) copy-start(f32[384,768]{1,0:T(8,128)S(1)} %fusion.11) | copy-start | bytes 3538948
  93.1 0.8 copy-start.8
  120.1 3.4 %copy-start.10 = (f32[384,768]{1,0:T(8,128)S(1)}, f32[384,768]{1,0:T(8,128)}, u32[]{:S(2)}) copy-start(f32[384,768]{1,0:T(8,128)} %copy-done.9) | copy-start | bytes 3538948
  120.1 3.4 %copy-start.11 = (f32[384,768]{1,0:T(8,128)S(1)}, f32[384,768]{1,0:T(8,128)}, u32[]{:S(2)}) copy-start(f32[384,768]{1,0:T(8,128)} %get-tuple-element.57) | copy-start | bytes 3538948
  129.2 1.0 copy-start.6
  131.3 118.6 %reduce-scatter.2.cloned.1.call-start = ((), (), s32[]{:S(2)}) async-start(), calls=%async_computation.5 | async-start | bytes 7864320 | tf_op jit(solution)/shard_map/reduce_scatter | solution.py:141
  137.8 46.8 %all-to-all-start.2 = ((bf16[32,48,1024]{2,1,0:T(8,128)(2,1)}), bf16[32,48,1024]{2,1,0:T(8,128)(2,1)S(1)}, u32[]{:S(2)}, u32[]{:S(2)}) async-start(bf16[32,48,1024]{2,1,0:T(8,128)(2,1)} %reshape.260), calls=%async_computation.2 | async-start | bytes 6291456 | tf_op jit(solution)/shard_map/all_to_all | solution.py:118
  145.2 5.0 %copy-start.5 = (bf16[384,768]{1,0:T(8,128)(2,1)S(1)}, bf16[384,768]{1,0:T(8,128)(2,1)}, u32[]{:S(2)}) copy-start(bf16[384,768]{1,0:T(8,128)(2,1)} %copy-done.4) | copy-start | bytes 1769476
  164.6 27.1 %copy-start.3 = (bf16[32,4096]{1,0:T(8,128)(2,1)S(1)}, bf16[32,4096]{1,0:T(8,128)(2,1)}, u32[]{:S(2)}) copy-start(bf16[32,4096]{1,0:T(8,128)(2,1)} %param.10) | copy-start | bytes 786436
  184.7 1.7 copy-start
  186.4 44.8 %all-to-all-start.3 = ((bf16[32,48,1024]{2,1,0:T(8,128)(2,1)}), bf16[32,48,1024]{2,1,0:T(8,128)(2,1)S(1)}, u32[]{:S(2)}, u32[]{:S(2)}) async-start(bf16[32,48,1024]{2,1,0:T(8,128)(2,1)} %reshape.262), calls=%async_computation.3 | async-start | bytes 6291456 | tf_op jit(solution)/shard_map/all_to_all | solution.py:125
  (1 other events, 0.8 us)
Sparse Core Ops, SparseCore 0:
  131.4 51.5 all-gather.2
  185.5 64.4 reduce-scatter.1

commit v14 on v13

--- a/solution.py
+++ b/solution.py
@@ -136,16 +136,14 @@
     grad_joined = lax.dot_general(
         rows_all, joined_all, (((0, 1), (0, 1)), ((), ())), preferred_element_type=jnp.float32
     )
-    columns = grads_in
-    grad_down = (
-        lax.psum_scatter(
-            contract_first(columns, hidden).astype(jnp.bfloat16),
-            "dp",
-            scatter_dimension=0,
-            tiled=True,
-        )
-        .astype(jnp.float32)
-        .T
+    grads_arrived = [lax.dynamic_slice_in_dim(grads_in, dp_index * piece, piece, axis=1)]
+    for shift in range(1, dp_count):
+        outgoing = lax.dynamic_slice_in_dim(grads_in, ((dp_index + shift) % dp_count) * piece, piece, axis=1)
+        grads_arrived.append(lax.ppermute(outgoing, "dp", [(j, (j + shift) % dp_count) for j in range(dp_count)]))
+    grads_all = jnp.stack(grads_arrived, axis=0)
+    hidden_all = jnp.take(lax.all_gather(hidden, "dp", axis=0, tiled=False), source_order, axis=0)
+    grad_down = lax.dot_general(
+        hidden_all, grads_all, (((0, 1), (0, 1)), ((), ())), preferred_element_type=jnp.float32
     )
     pair_index = (
         pair_slot.reshape(local_tokens, 1, top_count) * fold
@@ -154,7 +152,10 @@
     pair_out = back_out.reshape(-1, narrow)[pair_index].astype(jnp.float32)
     grad_w_gate = grad_joined[:, :ff_width].astype(jnp.bfloat16)[None]
     grad_w_up = grad_joined[:, ff_width:].astype(jnp.bfloat16)[None]
-    grad_w_gate, grad_w_up, back_grad = lax.optimization_barrier((grad_w_gate, grad_w_up, back_grad))
+    grad_w_down = grad_down.astype(jnp.bfloat16)[None]
+    grad_w_gate, grad_w_up, grad_w_down, back_grad = lax.optimization_barrier(
+        (grad_w_gate, grad_w_up, grad_w_down, back_grad)
+    )
     pair_back = back_grad.reshape(-1, narrow)[pair_index].astype(jnp.float32)
     gate_rows = jnp.repeat(gate_values, fold, axis=0)
     output = (
@@ -166,7 +167,6 @@
         jnp.sum(upstream_rows[:, None, :] * pair_out, axis=2).reshape(local_tokens, fold, top_count),
         axis=1,
     )
-    grad_w_down = grad_down.astype(jnp.bfloat16)[None]
     return (output, grad_tokens, grad_gates, grad_w_gate, grad_w_up, grad_w_down)
 
 

time: 261 us -> 300 us (1.15)
  waiting for transfers between devices: 77.8 us -> 101 us
  local copies, waits for them, and re-layouts: 73.8 us -> 81.2 us
  matrix products: 46.1 us -> 50 us
  starting transfers between devices: 31 us -> 34.9 us
    ppermute x3 -> x6, waiting for transfers between devices: 5.53 us -> 60.2 us  [local(): lax.ppermute(outgoing, 'dp', [(j, (j + shift) % dp_count) for j in range(...]
    all_to_all x1, waiting for transfers between devices: 9.58 us -> 0.01 us  [local(): lax.all_to_all(send_grads.reshape(flat_shape), ('outer', 'inner'), split_...]
    reduce_scatter x1 -> x0, waiting for transfers between devices: 9.33 us -> none  [local(): lax.psum_scatter(contract_first(columns, hidden).astype(jnp.bfloat16), 'd...]
    all_to_all x1, waiting for transfers between devices: 8.97 us -> 0.01 us  [local(): lax.all_to_all(pair_grad.reshape(flat_shape), ('outer', 'inner'), split_a...]
    dot_general x1, matrix products: 2.8 us -> 6.93 us  [local(): jnp.dot(hidden, down_mat, preferred_element_type=jnp.float32)]
    dot_general x3, matrix products: 19.1 us -> 15.1 us  [contract_last(): lax.dot_general(left, right, (((1,), (1,)), ((), ())), preferred_element_...]
    ppermute x3 -> x6, starting transfers between devices: 5.29 us -> 9.17 us  [local(): lax.ppermute(outgoing, 'dp', [(j, (j + shift) % dp_count) for j in range(...]
    gather x0 -> x1, local copies, waits for them, and re-layouts: none -> 3.81 us  [local(): jnp.take(lax.all_gather(hidden, 'dp', axis=0, tiled=False), source_order,...]
  transfers between devices with their start and end apart: 9 -> 12, of which waited for: 7 -> 6; matrix products, arithmetic and copies ran while one was open for 42% -> 41% of each run, Pallas kernels for 0% -> 0%
where the time goes in v14:
time: 300 us; the launch traced here: 296 us
  waiting for transfers between devices  101 us (34%)
  local copies, waits for them, and re-layouts  81.2 us (27%)
  matrix products  50 us (17%)
  starting transfers between devices  34.9 us (12%)
  other arithmetic  14.5 us (5%)
  between operations  14.5 us (5%)
    ppermute x6, waiting for transfers between devices, local(): lax.ppermute(outgoing, 'dp', [(j, (j + shift) % dp_count) for j in range(...  60.2 us
    all_to_all x1, waiting for transfers between devices, local(): lax.all_to_all(send_rows.reshape(flat_shape), ('outer', 'inner'), split_a...  24.3 us
    all_to_all x1, waiting for transfers between devices, local(): lax.all_to_all(out_send, ('outer', 'inner'), split_axis=0, concat_axis=0,...  16.5 us
    dot_general x3, matrix products, contract_last(): lax.dot_general(left, right, (((1,), (1,)), ((), ())), preferred_element_...  15.1 us
    ppermute x6, starting transfers between devices, local(): lax.ppermute(outgoing, 'dp', [(j, (j + shift) % dp_count) for j in range(...  9.17 us
    dot_general x1, matrix products, local(): lax.dot_general(rows_all, joined_all, (((0, 1), (0, 1)), ((), ())), prefe...  8 us
    all_to_all x1, starting transfers between devices, local(): lax.all_to_all(send_rows.reshape(flat_shape), ('outer', 'inner'), split_a...  7.67 us
    all_to_all x1, starting transfers between devices, local(): lax.all_to_all(out_send, ('outer', 'inner'), split_axis=0, concat_axis=0,...  7.39 us
  transfers between devices with their start and end apart: 12, of which 6 were waited for; matrix products, arithmetic and copies ran while one was open for 41% of the time, Pallas kernels for 0%

profile of v14, /device:TPU:8, one launch (start us, length us, event | category | flops | bytes accessed | tf_op | source)
XLA Modules:
  0.0 296.1 jit_solution(5295477850603253750)
XLA Ops:
  12.2 5.8 %gather_fusion.2 = bf16[1536,1024]{1,0:T(8,128)(2,1)} fusion(bf16[132,1024]{1,0:T(8,128)(2,1)S(1)} %reshape.257, s32[2048]{0:T(1024)S(1)} %pad_clamp_fusion), kind=kCustom, calls=%fused_computation.2 | custom fusion | bytes 6297600 | tf_op jit(solution)/shard_map/gather | solution.py:70
  18.0 7.7 %all-to-all-start.1 = ((bf16[32,48,1024]{2,1,0:T(8,128)(2,1)}), bf16[32,48,1024]{2,1,0:T(8,128)(2,1)S(1)}, u32[]{:S(2)}, u32[]{:S(2)}) async-start(bf16[32,48,1024]{2,1,0:T(8,128)(2,1)} %bitcast.95), calls=%async_computation.1 | async-start | bytes 6291456 | tf_op jit(solution)/shard_map/all_to_all | solution.py:76
  27.6 5.9 %gather_fusion.1 = bf16[1536,1024]{1,0:T(8,128)(2,1)} fusion(bf16[132,1024]{1,0:T(8,128)(2,1)S(1)} %reshape.255, s32[2048]{0:T(1024)S(1)} %pad_clamp_fusion), kind=kCustom, calls=%fused_computation.1 | custom fusion | bytes 6297600 | tf_op jit(solution)/shard_map/gather | solution.py:73
  40.8 24.3 %all-to-all-done.1 = bf16[32,48,1024]{2,1,0:T(8,128)(2,1)S(1)} async-done(((bf16[32,48,1024]{2,1,0:T(8,128)(2,1)}), bf16[32,48,1024]{2,1,0:T(8,128)(2,1)S(1)}, u32[]{:S(2)}, u32[]{:S(2)}) %all-to-all-start.1) | async-done | bytes 3145760 | tf_op jit(solution)/shard_map/all_to_all | solution.py:76
  66.9 5.2 %all-to-all-start = ((bf16[32,48,1024]{2,1,0:T(8,128)(2,1)}), bf16[32,48,1024]{2,1,0:T(8,128)(2,1)S(1)}, u32[]{:S(2)}, u32[]{:S(2)}) async-start(bf16[32,48,1024]{2,1,0:T(8,128)(2,1)} %fusion), calls=%async_computation | async-start | bytes 6291456 | tf_op jit(solution)/shard_map/all_to_all | solution.py:83
  72.2 5.9 %reshape.259 = bf16[384,4096]{1,0:T(8,128)(2,1)} reshape(bf16[32,48,1024]{2,1,0:T(8,128)(2,1)} %copy-done.2) | data formatting | bytes 6291456 | tf_op jit(solution)/shard_map/reshape | solution.py:91
  78.1 6.5 %fusion.11 = f32[384,768]{1,0:T(8,128)S(1)} fusion(bf16[384,4096]{1,0:T(8,128)(2,1)} %reshape.259, bf16[1,4096,768]{2,1,0:T(8,128)(2,1)} %param.11), kind=kOutput, calls=%fused_computation.21 | convolution fusion | flops 2415919104 | bytes 10616832 | tf_op jit(solution)/shard_map/dot_general | solution.py:102
  84.6 7.1 %multiply_convert_fusion.2 = (bf16[384,768]{1,0:T(8,128)(2,1)}, f32[384,768]{1,0:T(8,128)}) fusion(f32[384,768]{1,0:T(8,128)S(1)} %fusion.11, bf16[384,4096]{1,0:T(8,128)(2,1)S(1)} %copy-done, bf16[1,4096,768]{2,1,0:T(8,128)(2,1)} %param.12), kind=kOutput, calls=%fused_computation.53 | convolution fusion | flops 2417688576 | bytes 12386304 | tf_op jit(solution)/shard_map/dot_general | solution.py:103
  100.8 6.9 %fusion.15 = bf16[384,4096]{1,0:T(8,128)(2,1)} fusion(bf16[384,768]{1,0:T(8,128)(2,1)S(1)} %copy-done.6, bf16[1,768,4096]{2,1,0:T(8,128)(2,1)} %param.13), kind=kOutput, calls=%fused_computation.24 | convolution fusion | flops 2417491968 | bytes 10027008 | tf_op jit(solution)/shard_map/dot_general | solution.py:107
  107.7 6.0 %reshape.260 = bf16[32,48,1024]{2,1,0:T(8,128)(2,1)} reshape(bf16[384,4096]{1,0:T(8,128)(2,1)} %fusion.15) | data formatting | bytes 6291456 | tf_op jit(solution)/shard_map/reshape | solution.py:108
  117.4 12.3 %collective-permute-done.2 = bf16[384,1024]{1,0:T(8,128)(2,1)} collective-permute-done((bf16[384,1024]{1,0:T(8,128)(2,1)}, bf16[384,1024]{1,0:T(8,128)(2,1)}, u32[]{:S(2)}, u32[]{:S(2)}) %collective-permute-start.2) | collective-permute-done | bytes 786464 | tf_op jit(solution)/shard_map/ppermute | solution.py:99
  131.3 22.8 %collective-permute-done = bf16[384,1024]{1,0:T(8,128)(2,1)} collective-permute-done((bf16[384,1024]{1,0:T(8,128)(2,1)}, bf16[384,1024]{1,0:T(8,128)(2,1)}, u32[]{:S(2)}, u32[]{:S(2)}) %collective-permute-start) | collective-permute-done | bytes 786464 | tf_op jit(solution)/shard_map/ppermute | solution.py:99
  158.7 6.0 %multiply_convert_fusion.1 = (bf16[384,768]{1,0:T(8,128)(2,1)S(1)}, bf16[384,768]{1,0:T(8,128)(2,1)S(1)}) fusion(f32[384,768]{1,0:T(8,128)S(1)} %copy-done.13, f32[384,768]{1,0:T(8,128)S(1)} %copy-done.14, bf16[384,4096]{1,0:T(8,128)(2,1)S(1)} %copy-done.1, bf16[1,768,4096]{2,1,0:T(8,128)(2,1)} %param.13), kind=kOutput, calls=%fused_computation.52 | convolution fusion | flops 2419752960 | bytes 12976128 | tf_op jit(solution)/shard_map/dot_general | solution.py:8
  166.8 7.4 %all-to-all-start.2 = ((bf16[32,48,1024]{2,1,0:T(8,128)(2,1)}), bf16[32,48,1024]{2,1,0:T(8,128)(2,1)S(1)}, u32[]{:S(2)}, u32[]{:S(2)}) async-start(bf16[32,48,1024]{2,1,0:T(8,128)(2,1)} %reshape.260), calls=%async_computation.2 | async-start | bytes 6291456 | tf_op jit(solution)/shard_map/all_to_all | solution.py:118
  182.0 5.1 %fusion.5 = f32[384,4096]{1,0:T(8,128)S(1)} fusion(bf16[384,768]{1,0:T(8,128)(2,1)S(1)} %copy-done.10, bf16[1,4096,768]{2,1,0:T(8,128)(2,1)} %param.12), kind=kOutput, calls=%fused_computation.15 | convolution fusion | flops 2415919104 | bytes 13172736 | tf_op jit(solution)/shard_map/dot_general | solution.py:8
  191.2 6.0 %reshape.262 = bf16[32,48,1024]{2,1,0:T(8,128)(2,1)} reshape(bf16[384,4096]{1,0:T(8,128)(2,1)} %add_convert_fusion) | data formatting | bytes 6291456 | tf_op jit(solution)/shard_map/reshape | solution.py:126
  197.2 16.5 %all-to-all-done.2 = bf16[32,48,1024]{2,1,0:T(8,128)(2,1)S(1)} async-done(((bf16[32,48,1024]{2,1,0:T(8,128)(2,1)}), bf16[32,48,1024]{2,1,0:T(8,128)(2,1)S(1)}, u32[]{:S(2)}, u32[]{:S(2)}) %all-to-all-start.2) | async-done | bytes 3145760 | tf_op jit(solution)/shard_map/all_to_all | solution.py:118
  213.7 5.3 %all-to-all-start.3 = ((bf16[32,48,1024]{2,1,0:T(8,128)(2,1)}), bf16[32,48,1024]{2,1,0:T(8,128)(2,1)}, u32[]{:S(2)}, u32[]{:S(2)}) async-start(bf16[32,48,1024]{2,1,0:T(8,128)(2,1)} %reshape.262), calls=%async_computation.3 | async-start | bytes 6291456 | tf_op jit(solution)/shard_map/all_to_all | solution.py:125
  223.9 23.6 %collective-permute-done.3 = bf16[384,1024]{1,0:T(8,128)(2,1)} collective-permute-done((bf16[384,1024]{1,0:T(8,128)(2,1)}, bf16[384,1024]{1,0:T(8,128)(2,1)}, u32[]{:S(2)}, u32[]{:S(2)}) %collective-permute-start.3) | collective-permute-done | bytes 786464 | tf_op jit(solution)/shard_map/ppermute | solution.py:142
  247.5 6.4 %fusion.40 = bf16[1,768,1024]{2,1,0:T(8,128)(2,1)} fusion(bf16[1,384,1024]{2,1,0:T(8,128)(2,1)} %bitcast.26, bf16[1,384,1024]{2,1,0:T(8,128)(2,1)} %bitcast.25, bf16[1,384,1024]{2,1,0:T(8,128)(2,1)} %bitcast.24, bf16[1,384,1024]{2,1,0:T(8,128)(2,1)} %get-tuple-element.22, bf16[4,384,768]{2,1,0:T(8,128)(2,1)} %gather_fusion.5, ...), kind=kOutput, calls=%fused_computation.48 | convolution fusion | flops 2422603776 | bytes 7077892 | tf_op jit(solution)/shard_map/dot_general | solution.py:145
  254.0 5.4 %gather_fusion.3 = bf16[1024,1024]{1,0:T(8,128)(2,1)} fusion(bf16[1536,1024]{1,0:T(8,128)(2,1)S(1)} %bitcast.94, s32[1024]{0:T(1024)S(1)} %broadcast_clamp_fusion), kind=kCustom, calls=%fused_computation.3 | custom fusion | bytes 4198400 | tf_op jit(solution)/shard_map/gather | solution.py:152
  264.3 5.5 %gather_fusion.4 = bf16[4,384,1536]{2,1,0:T(8,128)(2,1)} fusion(bf16[4,384,1536]{2,1,0:T(8,128)(2,1)} %bitcast.97, s32[1024]{0:T(1024)S(1)} %pad_clamp_fusion.1), kind=kCustom, calls=%fused_computation.4 | custom fusion | bytes 9437200 | tf_op jit(solution)/shard_map/jit(_take)/gather | solution.py:135
  269.8 8.0 %bitcast_convert_fusion = bf16[1024,1536]{1,0:T(8,128)(2,1)S(1)} fusion(bf16[4,384,1024]{2,1,0:T(8,128)(2,1)S(1)} %copy-done.3, bf16[4,384,1536]{2,1,0:T(8,128)(2,1)} %gather_fusion.4, pred[4]{0:T(512)(128)(4,1)S(1)} %compare_and_fusion), kind=kOutput, calls=%fused_computation.10 | convolution fusion | flops 4835770368 | bytes 11010052 | tf_op jit(solution)/shard_map/dot_general | solution.py:136
  279.7 7.3 %gather_fusion.6 = bf16[1024,1024]{1,0:T(8,128)(2,1)S(1)} fusion(bf16[1536,1024]{1,0:T(8,128)(2,1)} %bitcast.29, s32[1024]{0:T(1024)S(1)} %broadcast_clamp_fusion), kind=kCustom, calls=%fused_computation.6 | custom fusion | bytes 4198400 | tf_op jit(solution)/shard_map/gather | solution.py:159
  (111 shorter events, 62.9 us)
Async XLA Ops:
  18.0 7.7 %copy-start.4 = (bf16[32,4096]{1,0:T(8,128)(2,1)S(1)}, bf16[32,4096]{1,0:T(8,128)(2,1)}, u32[]{:S(2)}) copy-start(bf16[32,4096]{1,0:T(8,128)(2,1)} %param.10) | copy-start | bytes 786436
  18.0 47.2 %all-to-all-start.1 = ((bf16[32,48,1024]{2,1,0:T(8,128)(2,1)}), bf16[32,48,1024]{2,1,0:T(8,128)(2,1)S(1)}, u32[]{:S(2)}, u32[]{:S(2)}) async-start(bf16[32,48,1024]{2,1,0:T(8,128)(2,1)} %bitcast.95), calls=%async_computation.1 | async-start | bytes 6291456 | tf_op jit(solution)/shard_map/all_to_all | solution.py:76
  27.6 5.9 %copy-start.11 = (f32[32,8]{0,1:T(8,128)S(1)}, f32[32,8]{0,1:T(8,128)}, u32[]{:S(2)}) copy-start(f32[32,8]{0,1:T(8,128)} %param.9) | copy-start | bytes 3076
  66.9 46.8 %all-to-all-start = ((bf16[32,48,1024]{2,1,0:T(8,128)(2,1)}), bf16[32,48,1024]{2,1,0:T(8,128)(2,1)S(1)}, u32[]{:S(2)}, u32[]{:S(2)}) async-start(bf16[32,48,1024]{2,1,0:T(8,128)(2,1)} %fusion), calls=%async_computation | async-start | bytes 6291456 | tf_op jit(solution)/shard_map/all_to_all | solution.py:83
  72.1 148.0 %all-gather.7.cloned.1.call-start = ((), (), s32[]{:S(2)}) async-start(), calls=%async_computation.5 | async-start | bytes 2949120 | tf_op jit(solution)/shard_map/all_gather | solution.py:144
  78.1 6.5 %copy-start = (bf16[384,4096]{1,0:T(8,128)(2,1)S(1)}, bf16[384,4096]{1,0:T(8,128)(2,1)}, u32[]{:S(2)}) copy-start(bf16[384,4096]{1,0:T(8,128)(2,1)} %reshape.259) | copy-start | bytes 9437188
  84.6 7.1 %copy-start.12 = (f32[384,768]{1,0:T(8,128)}, f32[384,768]{1,0:T(8,128)S(1)}, u32[]{:S(2)}) copy-start(f32[384,768]{1,0:T(8,128)S(1)} %fusion.11) | copy-start | bytes 3538948
  91.7 172.6 %all-gather.5.cloned.1.call-start = ((), (), s32[]{:S(2)}) async-start(), calls=%async_computation.4 | async-start | bytes 5898240 | tf_op jit(solution)/shard_map/all_gather | solution.py:135
  91.8 9.0 %copy-start.6 = (bf16[384,768]{1,0:T(8,128)(2,1)S(1)}, bf16[384,768]{1,0:T(8,128)(2,1)}, u32[]{:S(2)}) copy-start(bf16[384,768]{1,0:T(8,128)(2,1)} %get-tuple-element.38) | copy-start | bytes 1769476
  95.5 34.2 %collective-permute-start.2 = (bf16[384,1024]{1,0:T(8,128)(2,1)}, bf16[384,1024]{1,0:T(8,128)(2,1)}, u32[]{:S(2)}, u32[]{:S(2)}) collective-permute-start(bf16[384,1024]{1,0:T(8,128)(2,1)} %get-tuple-element.29), channel_id=1, source_target_pairs={{0,96},{32,0},{64,32},{96,64},{1,97},{33,1},{65,33},{97,65},{2,98}... | collective-permute-start | bytes 2359304 | tf_op jit(solution)/shard_map/ppermute | solution.py:99
  99.5 31.8 %collective-permute-start.1 = (bf16[384,1024]{1,0:T(8,128)(2,1)}, bf16[384,1024]{1,0:T(8,128)(2,1)}, u32[]{:S(2)}, u32[]{:S(2)}) collective-permute-start(bf16[384,1024]{1,0:T(8,128)(2,1)} %get-tuple-element.30), channel_id=1, source_target_pairs={{0,64},{32,96},{64,0},{96,32},{1,65},{33,97},{65,1},{97,33},{2,66}... | collective-permute-start | bytes 2359304 | tf_op jit(solution)/shard_map/ppermute | solution.py:99
  99.5 54.5 %collective-permute-start = (bf16[384,1024]{1,0:T(8,128)(2,1)}, bf16[384,1024]{1,0:T(8,128)(2,1)}, u32[]{:S(2)}, u32[]{:S(2)}) collective-permute-start(bf16[384,1024]{1,0:T(8,128)(2,1)} %get-tuple-element.31), channel_id=1, source_target_pairs={{0,32},{32,64},{64,96},{96,0},{1,33},{33,65},{65,97},{97,1},{2,34}... | collective-permute-start | bytes 2359304 | tf_op jit(solution)/shard_map/ppermute | solution.py:99
  154.0 4.6 %copy-start.14 = (f32[384,768]{1,0:T(8,128)S(1)}, f32[384,768]{1,0:T(8,128)}, u32[]{:S(2)}) copy-start(f32[384,768]{1,0:T(8,128)} %get-tuple-element.39) | copy-start | bytes 3538948
  166.8 46.9 %all-to-all-start.2 = ((bf16[32,48,1024]{2,1,0:T(8,128)(2,1)}), bf16[32,48,1024]{2,1,0:T(8,128)(2,1)S(1)}, u32[]{:S(2)}, u32[]{:S(2)}) async-start(bf16[32,48,1024]{2,1,0:T(8,128)(2,1)} %reshape.260), calls=%async_computation.2 | async-start | bytes 6291456 | tf_op jit(solution)/shard_map/all_to_all | solution.py:118
  174.4 7.6 %copy-start.10 = (bf16[384,768]{1,0:T(8,128)(2,1)S(1)}, bf16[384,768]{1,0:T(8,128)(2,1)}, u32[]{:S(2)}) copy-start(bf16[384,768]{1,0:T(8,128)(2,1)} %copy-done.9) | copy-start | bytes 1769476
  178.1 45.8 %collective-permute-start.5 = (bf16[384,1024]{1,0:T(8,128)(2,1)}, bf16[384,1024]{1,0:T(8,128)(2,1)}, u32[]{:S(2)}, u32[]{:S(2)}) collective-permute-start(bf16[384,1024]{1,0:T(8,128)(2,1)} %get-tuple-element.23), channel_id=1, source_target_pairs={{0,96},{32,0},{64,32},{96,64},{1,97},{33,1},{65,33},{97,65},{2,98}... | collective-permute-start | bytes 2359304 | tf_op jit(solution)/shard_map/ppermute | solution.py:142
  181.1 42.8 %collective-permute-start.4 = (bf16[384,1024]{1,0:T(8,128)(2,1)}, bf16[384,1024]{1,0:T(8,128)(2,1)}, u32[]{:S(2)}, u32[]{:S(2)}) collective-permute-start(bf16[384,1024]{1,0:T(8,128)(2,1)} %get-tuple-element.24), channel_id=1, source_target_pairs={{0,64},{32,96},{64,0},{96,32},{1,65},{33,97},{65,1},{97,33},{2,66}... | collective-permute-start | bytes 2359304 | tf_op jit(solution)/shard_map/ppermute | solution.py:142
  181.4 5.7 %slice-start = ((s8[6291456]{0:T(1024)(128)(4,1)}), s8[4194304]{0:T(1024)(128)(4,1)S(1)}, s32[]{:S(2)}) async-start(s8[6291456]{0:T(1024)(128)(4,1)} %bitcast.105), calls=%async_computation.6 | async-start | bytes 8388608
  181.4 5.7 %copy-start.8 = (bf16[384,768]{1,0:T(8,128)(2,1)S(1)}, bf16[384,768]{1,0:T(8,128)(2,1)}, u32[]{:S(2)}) copy-start(bf16[384,768]{1,0:T(8,128)(2,1)} %copy-done.7) | copy-start | bytes 1769476
  181.4 5.7 %slice-start.1 = ((s8[6291456]{0:T(1024)(128)(4,1)}), s8[2097152]{0:T(1024)(128)(4,1)S(1)}, s32[]{:S(2)}) async-start(s8[6291456]{0:T(1024)(128)(4,1)} %bitcast.105), calls=%async_computation.7 | async-start | bytes 4194304
  181.4 66.1 %collective-permute-start.3 = (bf16[384,1024]{1,0:T(8,128)(2,1)}, bf16[384,1024]{1,0:T(8,128)(2,1)}, u32[]{:S(2)}, u32[]{:S(2)}) collective-permute-start(bf16[384,1024]{1,0:T(8,128)(2,1)} %get-tuple-element.25), channel_id=1, source_target_pairs={{0,32},{32,64},{64,96},{96,0},{1,33},{33,65},{65,97},{97,1},{2,34}... | collective-permute-start | bytes 2359304 | tf_op jit(solution)/shard_map/ppermute | solution.py:142
  197.2 21.8 %copy-start.5 = (bf16[32,4096]{1,0:T(8,128)(2,1)S(1)}, bf16[32,4096]{1,0:T(8,128)(2,1)}, u32[]{:S(2)}) copy-start(bf16[32,4096]{1,0:T(8,128)(2,1)} %param.10) | copy-start | bytes 786436
  213.7 66.0 %all-to-all-start.3 = ((bf16[32,48,1024]{2,1,0:T(8,128)(2,1)}), bf16[32,48,1024]{2,1,0:T(8,128)(2,1)}, u32[]{:S(2)}, u32[]{:S(2)}) async-start(bf16[32,48,1024]{2,1,0:T(8,128)(2,1)} %reshape.262), calls=%async_computation.3 | async-start | bytes 6291456 | tf_op jit(solution)/shard_map/all_to_all | solution.py:125
  264.3 5.5 %copy-start.3 = (bf16[4,384,1024]{2,1,0:T(8,128)(2,1)S(1)}, bf16[4,384,1024]{2,1,0:T(8,128)(2,1)}, u32[]{:S(2)}) copy-start(bf16[4,384,1024]{2,1,0:T(8,128)(2,1)} %pad_maximum_fusion) | copy-start | bytes 9437188
  (5 other events, 11.2 us)
Sparse Core Ops, SparseCore 0:
  91.8 64.5 all-gather.6
  166.9 87.6 all-gather.4

commit v15 on v13

--- a/solution.py
+++ b/solution.py
@@ -136,17 +136,12 @@
     grad_joined = lax.dot_general(
         rows_all, joined_all, (((0, 1), (0, 1)), ((), ())), preferred_element_type=jnp.float32
     )
-    columns = grads_in
-    grad_down = (
-        lax.psum_scatter(
-            contract_first(columns, hidden).astype(jnp.bfloat16),
-            "dp",
-            scatter_dimension=0,
-            tiled=True,
-        )
-        .astype(jnp.float32)
-        .T
-    )
+    grad_down = lax.psum_scatter(
+        contract_first(hidden, grads_in).astype(jnp.bfloat16),
+        "dp",
+        scatter_dimension=1,
+        tiled=True,
+    ).astype(jnp.float32)
     pair_index = (
         pair_slot.reshape(local_tokens, 1, top_count) * fold
         + jnp.arange(fold, dtype=jnp.int32)[None, :, None]

time: 261 us -> 259 us (level)
  local copies, waits for them, and re-layouts: 73.8 us -> 70.7 us
    unnamed x36 -> x35, local copies, waits for them, and re-layouts: 7.71 us -> 5.13 us
where the time goes in v15:
time: 259 us; the launch traced here: 257 us
  waiting for transfers between devices  78.7 us (30%)
  local copies, waits for them, and re-layouts  70.7 us (27%)
  matrix products  46.3 us (18%)
  starting transfers between devices  31 us (12%)
  other arithmetic  16.1 us (6%)
  between operations  14.5 us (6%)
    all_to_all x1, waiting for transfers between devices, local(): lax.all_to_all(send_rows.reshape(flat_shape), ('outer', 'inner'), split_a...  24.3 us
    all_to_all x1, waiting for transfers between devices, local(): lax.all_to_all(out_send, ('outer', 'inner'), split_axis=0, concat_axis=0,...  20 us
    dot_general x3, matrix products, contract_last(): lax.dot_general(left, right, (((1,), (1,)), ((), ())), preferred_element_...  19.2 us
    reduce_scatter x1, waiting for transfers between devices, local(): lax.psum_scatter(contract_first(hidden, grads_in).astype(jnp.bfloat16), '...  9.88 us
    all_to_all x1, waiting for transfers between devices, local(): lax.all_to_all(send_grads.reshape(flat_shape), ('outer', 'inner'), split_...  9.58 us
    all_to_all x1, waiting for transfers between devices, local(): lax.all_to_all(pair_grad.reshape(flat_shape), ('outer', 'inner'), split_a...  9.37 us
    gather x1, local copies, waits for them, and re-layouts, local(): pair_out = back_out.reshape(-1, narrow)[pair_index].astype(jnp.float32)  8.33 us
    dot_general x1, matrix products, local(): lax.dot_general(rows_all, joined_all, (((0, 1), (0, 1)), ((), ())), prefe...  8.22 us
  transfers between devices with their start and end apart: 9, of which 7 were waited for; matrix products, arithmetic and copies ran while one was open for 42% of the time, Pallas kernels for 0%

profile of v15, /device:TPU:8, one launch (start us, length us, event | category | flops | bytes accessed | tf_op | source)
XLA Modules:
  0.0 257.3 jit_solution(5580855611038672268)
XLA Ops:
  12.2 5.8 %gather_fusion.2 = bf16[1536,1024]{1,0:T(8,128)(2,1)} fusion(bf16[132,1024]{1,0:T(8,128)(2,1)S(1)} %reshape.257, s32[2048]{0:T(1024)S(1)} %pad_clamp_fusion), kind=kCustom, calls=%fused_computation.2 | custom fusion | bytes 6297600 | tf_op jit(solution)/shard_map/gather | solution.py:70
  18.0 7.7 %all-to-all-start.1 = ((bf16[32,48,1024]{2,1,0:T(8,128)(2,1)}), bf16[32,48,1024]{2,1,0:T(8,128)(2,1)S(1)}, u32[]{:S(2)}, u32[]{:S(2)}) async-start(bf16[32,48,1024]{2,1,0:T(8,128)(2,1)} %bitcast.88), calls=%async_computation.1 | async-start | bytes 6291456 | tf_op jit(solution)/shard_map/all_to_all | solution.py:76
  30.8 5.9 %gather_fusion.1 = bf16[1536,1024]{1,0:T(8,128)(2,1)} fusion(bf16[132,1024]{1,0:T(8,128)(2,1)S(1)} %reshape.255, s32[2048]{0:T(1024)S(1)} %pad_clamp_fusion), kind=kCustom, calls=%fused_computation.1 | custom fusion | bytes 6297600 | tf_op jit(solution)/shard_map/gather | solution.py:73
  36.7 4.1 %fusion = bf16[32,48,1024]{2,1,0:T(8,128)(2,1)} fusion(bf16[32,48,1024]{2,1,0:T(8,128)(2,1)} %bitcast.89, f32[32,48]{1,0:T(8,128)S(1)} %copy.40), kind=kLoop, calls=%fused_computation.9 | loop fusion | flops 4718592 | bytes 6297600 | tf_op jit(solution)/shard_map/convert_element_type | solution.py:74
  40.8 24.3 %all-to-all-done.1 = bf16[32,48,1024]{2,1,0:T(8,128)(2,1)S(1)} async-done(((bf16[32,48,1024]{2,1,0:T(8,128)(2,1)}), bf16[32,48,1024]{2,1,0:T(8,128)(2,1)S(1)}, u32[]{:S(2)}, u32[]{:S(2)}) %all-to-all-start.1) | async-done | bytes 3145760 | tf_op jit(solution)/shard_map/all_to_all | solution.py:76
  65.2 5.3 %all-to-all-start = ((bf16[32,48,1024]{2,1,0:T(8,128)(2,1)}), bf16[32,48,1024]{2,1,0:T(8,128)(2,1)}, u32[]{:S(2)}, u32[]{:S(2)}) async-start(bf16[32,48,1024]{2,1,0:T(8,128)(2,1)} %fusion), calls=%async_computation | async-start | bytes 6291456 | tf_op jit(solution)/shard_map/all_to_all | solution.py:83
  78.1 4.0 %collective-permute-start.2 = (bf16[384,1024]{1,0:T(8,128)(2,1)}, bf16[384,1024]{1,0:T(8,128)(2,1)}, u32[]{:S(2)}, u32[]{:S(2)}) collective-permute-start(bf16[384,1024]{1,0:T(8,128)(2,1)} %get-tuple-element.23), channel_id=1, source_target_pairs={{0,96},{32,0},{64,32},{96,64},{1,97},{33,1},{65,33},{97,65},{2,98}... | collective-permute-start | bytes 2359304 | tf_op jit(solution)/shard_map/ppermute | solution.py:99
  83.4 6.0 %fusion.11 = f32[384,768]{1,0:T(8,128)S(1)} fusion(bf16[384,4096]{1,0:T(8,128)(2,1)S(1)} %copy-done.1, bf16[1,4096,768]{2,1,0:T(8,128)(2,1)} %param.11), kind=kOutput, calls=%fused_computation.21 | convolution fusion | flops 2415919104 | bytes 10616832 | tf_op jit(solution)/shard_map/dot_general | solution.py:102
  100.4 9.6 %all-to-all-done = bf16[32,48,1024]{2,1,0:T(8,128)(2,1)} async-done(((bf16[32,48,1024]{2,1,0:T(8,128)(2,1)}), bf16[32,48,1024]{2,1,0:T(8,128)(2,1)}, u32[]{:S(2)}, u32[]{:S(2)}) %all-to-all-start) | async-done | bytes 3145760 | tf_op jit(solution)/shard_map/all_to_all | solution.py:83
  110.0 4.5 %reshape.256 = bf16[384,4096]{1,0:T(8,128)(2,1)S(1)} reshape(bf16[32,48,1024]{2,1,0:T(8,128)(2,1)} %all-to-all-done) | data formatting | bytes 6291456 | tf_op jit(solution)/shard_map/reshape | solution.py:92
  123.4 5.8 %multiply_convert_fusion.1 = (bf16[384,768]{1,0:T(8,128)(2,1)S(1)}, bf16[384,768]{1,0:T(8,128)(2,1)S(1)}) fusion(f32[384,768]{1,0:T(8,128)S(1)} %copy-done.10, f32[384,768]{1,0:T(8,128)S(1)} %copy-done.11, bf16[384,4096]{1,0:T(8,128)(2,1)S(1)} %reshape.256, bf16[1,768,4096]{2,1,0:T(8,128)(2,1)} %param.13), kind=kOutput, calls=%fused_computation.39 | convolution fusion | flops 2419752960 | bytes 12976128 | tf_op jit(solution)/shard_map/dot_general | solution.py:8
  131.4 6.5 %convolution_convert_fusion = bf16[768,4096]{1,0:T(8,128)(2,1)} fusion(bf16[384,768]{1,0:T(8,128)(2,1)} %copy-done.8, bf16[384,4096]{1,0:T(8,128)(2,1)S(1)} %reshape.256), kind=kOutput, calls=%fused_computation.7 | convolution fusion | flops 2419064832 | bytes 10027008 | tf_op jit(solution)/shard_map/dot_general | solution.py:14
  137.9 7.4 %all-to-all-start.2 = ((bf16[32,48,1024]{2,1,0:T(8,128)(2,1)}), bf16[32,48,1024]{2,1,0:T(8,128)(2,1)S(1)}, u32[]{:S(2)}, u32[]{:S(2)}) async-start(bf16[32,48,1024]{2,1,0:T(8,128)(2,1)} %reshape.260), calls=%async_computation.2 | async-start | bytes 6291456 | tf_op jit(solution)/shard_map/all_to_all | solution.py:118
  145.3 5.0 %fusion.5 = f32[384,4096]{1,0:T(8,128)S(1)} fusion(bf16[384,768]{1,0:T(8,128)(2,1)} %copy-done.6, bf16[1,4096,768]{2,1,0:T(8,128)(2,1)} %param.12), kind=kOutput, calls=%fused_computation.15 | convolution fusion | flops 2415919104 | bytes 13172736 | tf_op jit(solution)/shard_map/dot_general | solution.py:8
  150.3 8.5 %add_convert_fusion = bf16[384,4096]{1,0:T(8,128)(2,1)} fusion(f32[384,4096]{1,0:T(8,128)S(1)} %fusion.5, bf16[384,768]{1,0:T(8,128)(2,1)S(1)} %copy-done.5, bf16[1,4096,768]{2,1,0:T(8,128)(2,1)} %param.11), kind=kOutput, calls=%fused_computation.23 | convolution fusion | flops 2419064832 | bytes 16318464 | tf_op jit(solution)/shard_map/dot_general | solution.py:8
  158.7 6.0 %reshape.262 = bf16[32,48,1024]{2,1,0:T(8,128)(2,1)} reshape(bf16[384,4096]{1,0:T(8,128)(2,1)} %add_convert_fusion) | data formatting | bytes 6291456 | tf_op jit(solution)/shard_map/reshape | solution.py:126
  164.7 20.0 %all-to-all-done.2 = bf16[32,48,1024]{2,1,0:T(8,128)(2,1)S(1)} async-done(((bf16[32,48,1024]{2,1,0:T(8,128)(2,1)}), bf16[32,48,1024]{2,1,0:T(8,128)(2,1)S(1)}, u32[]{:S(2)}, u32[]{:S(2)}) %all-to-all-start.2) | async-done | bytes 3145760 | tf_op jit(solution)/shard_map/all_to_all | solution.py:118
  186.5 5.3 %all-to-all-start.3 = ((bf16[32,48,1024]{2,1,0:T(8,128)(2,1)}), bf16[32,48,1024]{2,1,0:T(8,128)(2,1)S(1)}, u32[]{:S(2)}, u32[]{:S(2)}) async-start(bf16[32,48,1024]{2,1,0:T(8,128)(2,1)} %reshape.262), calls=%async_computation.3 | async-start | bytes 6291456 | tf_op jit(solution)/shard_map/all_to_all | solution.py:125
  193.1 8.3 %gather_fusion.3 = bf16[1024,1024]{1,0:T(8,128)(2,1)} fusion(bf16[1536,1024]{1,0:T(8,128)(2,1)} %bitcast.87, s32[1024]{0:T(1024)S(1)} %broadcast_clamp_fusion), kind=kCustom, calls=%fused_computation.3 | custom fusion | bytes 4198400 | tf_op jit(solution)/shard_map/gather | solution.py:149
  206.4 5.4 %gather_fusion.4 = bf16[4,384,1536]{2,1,0:T(8,128)(2,1)} fusion(bf16[4,384,1536]{2,1,0:T(8,128)(2,1)} %bitcast.90, s32[1024]{0:T(1024)S(1)} %pad_clamp_fusion.1), kind=kCustom, calls=%fused_computation.4 | custom fusion | bytes 9437200 | tf_op jit(solution)/shard_map/jit(_take)/gather | solution.py:135
  211.8 8.2 %bitcast_convert_fusion = bf16[1024,1536]{1,0:T(8,128)(2,1)S(1)} fusion(bf16[4,384,1024]{2,1,0:T(8,128)(2,1)} %pad_maximum_fusion, bf16[4,384,1536]{2,1,0:T(8,128)(2,1)} %gather_fusion.4, pred[4]{0:T(512)(128)(4,1)S(1)} %compare_and_fusion), kind=kOutput, calls=%fused_computation.10 | convolution fusion | flops 4835770368 | bytes 11010052 | tf_op jit(solution)/shard_map/dot_general | solution.py:136
  221.9 9.4 %all-to-all-done.3 = bf16[32,48,1024]{2,1,0:T(8,128)(2,1)S(1)} async-done(((bf16[32,48,1024]{2,1,0:T(8,128)(2,1)}), bf16[32,48,1024]{2,1,0:T(8,128)(2,1)S(1)}, u32[]{:S(2)}, u32[]{:S(2)}) %all-to-all-start.3) | async-done | bytes 3145760 | tf_op jit(solution)/shard_map/all_to_all | solution.py:125
  231.3 5.4 %gather_fusion.5 = bf16[1024,1024]{1,0:T(8,128)(2,1)} fusion(bf16[1536,1024]{1,0:T(8,128)(2,1)S(1)} %bitcast.86, s32[1024]{0:T(1024)S(1)} %broadcast_clamp_fusion), kind=kCustom, calls=%fused_computation.5 | custom fusion | bytes 4198400 | tf_op jit(solution)/shard_map/gather | solution.py:153
  240.6 9.9 %reduce-scatter.2.cloned.1.call-done = bf16[768,1024]{1,0:T(8,128)(2,1)} async-done(((bf16[768,4096]{1,0:T(8,128)(2,1)}), bf16[768,1024]{1,0:T(8,128)(2,1)}) %reduce-scatter.2.cloned.1.call-update) | async-done | bytes 1572880 | tf_op jit(solution)/shard_map/reduce_scatter | solution.py:139
  (102 shorter events, 54.7 us)
Async XLA Ops:
  18.0 7.7 %copy-start.7 = (f32[32,8]{0,1:T(8,128)S(1)}, f32[32,8]{0,1:T(8,128)}, u32[]{:S(2)}) copy-start(f32[32,8]{0,1:T(8,128)} %param.9) | copy-start | bytes 3076
  18.0 10.9 %copy-start.2 = (bf16[32,4096]{1,0:T(8,128)(2,1)S(1)}, bf16[32,4096]{1,0:T(8,128)(2,1)}, u32[]{:S(2)}) copy-start(bf16[32,4096]{1,0:T(8,128)(2,1)} %param.10) | copy-start | bytes 786436
  18.0 47.2 %all-to-all-start.1 = ((bf16[32,48,1024]{2,1,0:T(8,128)(2,1)}), bf16[32,48,1024]{2,1,0:T(8,128)(2,1)S(1)}, u32[]{:S(2)}, u32[]{:S(2)}) async-start(bf16[32,48,1024]{2,1,0:T(8,128)(2,1)} %bitcast.88), calls=%async_computation.1 | async-start | bytes 6291456 | tf_op jit(solution)/shard_map/all_to_all | solution.py:76
  65.2 44.9 %all-to-all-start = ((bf16[32,48,1024]{2,1,0:T(8,128)(2,1)}), bf16[32,48,1024]{2,1,0:T(8,128)(2,1)}, u32[]{:S(2)}, u32[]{:S(2)}) async-start(bf16[32,48,1024]{2,1,0:T(8,128)(2,1)} %fusion), calls=%async_computation | async-start | bytes 6291456 | tf_op jit(solution)/shard_map/all_to_all | solution.py:83
  70.5 136.0 %all-gather.3.cloned.1.call-start = ((), (), s32[]{:S(2)}) async-start(), calls=%async_computation.6 | async-start | bytes 5898240 | tf_op jit(solution)/shard_map/all_gather | solution.py:135
  74.3 9.0 %copy-start.1 = (bf16[384,4096]{1,0:T(8,128)(2,1)S(1)}, bf16[384,4096]{1,0:T(8,128)(2,1)}, u32[]{:S(2)}) copy-start(bf16[384,4096]{1,0:T(8,128)(2,1)} %reshape.259) | copy-start | bytes 9437188
  74.3 19.6 %slice-start = ((s8[6291456]{0:T(1024)(128)(4,1)}), s8[4194304]{0:T(1024)(128)(4,1)S(1)}, s32[]{:S(2)}) async-start(s8[6291456]{0:T(1024)(128)(4,1)} %bitcast.97), calls=%async_computation.7 | async-start | bytes 8388608
  78.1 38.3 %collective-permute-start.2 = (bf16[384,1024]{1,0:T(8,128)(2,1)}, bf16[384,1024]{1,0:T(8,128)(2,1)}, u32[]{:S(2)}, u32[]{:S(2)}) collective-permute-start(bf16[384,1024]{1,0:T(8,128)(2,1)} %get-tuple-element.23), channel_id=1, source_target_pairs={{0,96},{32,0},{64,32},{96,64},{1,97},{33,1},{65,33},{97,65},{2,98}... | collective-permute-start | bytes 2359304 | tf_op jit(solution)/shard_map/ppermute | solution.py:99
  82.1 34.3 %collective-permute-start.1 = (bf16[384,1024]{1,0:T(8,128)(2,1)}, bf16[384,1024]{1,0:T(8,128)(2,1)}, u32[]{:S(2)}, u32[]{:S(2)}) collective-permute-start(bf16[384,1024]{1,0:T(8,128)(2,1)} %get-tuple-element.24), channel_id=1, source_target_pairs={{0,64},{32,96},{64,0},{96,32},{1,65},{33,97},{65,1},{97,33},{2,66}... | collective-permute-start | bytes 2359304 | tf_op jit(solution)/shard_map/ppermute | solution.py:99
  82.1 7.3 %slice-start.2 = ((s8[6291456]{0:T(1024)(128)(4,1)}), s8[4194304]{0:T(1024)(128)(4,1)S(1)}, s32[]{:S(2)}) async-start(s8[6291456]{0:T(1024)(128)(4,1)} %bitcast.99), calls=%async_computation.9 | async-start | bytes 8388608
  82.1 7.3 %slice-start.3 = ((s8[6291456]{0:T(1024)(128)(4,1)}), s8[2097152]{0:T(1024)(128)(4,1)S(1)}, s32[]{:S(2)}) async-start(s8[6291456]{0:T(1024)(128)(4,1)} %bitcast.99), calls=%async_computation.10 | async-start | bytes 4194304
  82.1 11.8 %slice-start.1 = ((s8[6291456]{0:T(1024)(128)(4,1)}), s8[2097152]{0:T(1024)(128)(4,1)S(1)}, s32[]{:S(2)}) async-start(s8[6291456]{0:T(1024)(128)(4,1)} %bitcast.97), calls=%async_computation.8 | async-start | bytes 4194304
  82.1 37.9 %collective-permute-start = (bf16[384,1024]{1,0:T(8,128)(2,1)}, bf16[384,1024]{1,0:T(8,128)(2,1)}, u32[]{:S(2)}, u32[]{:S(2)}) collective-permute-start(bf16[384,1024]{1,0:T(8,128)(2,1)} %get-tuple-element.25), channel_id=1, source_target_pairs={{0,32},{32,64},{64,96},{96,0},{1,33},{33,65},{65,97},{97,1},{2,34}... | collective-permute-start | bytes 2359304 | tf_op jit(solution)/shard_map/ppermute | solution.py:99
  89.4 3.7 %copy-start.9 = (f32[384,768]{1,0:T(8,128)}, f32[384,768]{1,0:T(8,128)S(1)}, u32[]{:S(2)}) copy-start(f32[384,768]{1,0:T(8,128)S(1)} %fusion.11) | copy-start | bytes 3538948
  93.1 0.8 copy-start.8
  120.1 3.4 %copy-start.10 = (f32[384,768]{1,0:T(8,128)S(1)}, f32[384,768]{1,0:T(8,128)}, u32[]{:S(2)}) copy-start(f32[384,768]{1,0:T(8,128)} %copy-done.9) | copy-start | bytes 3538948
  120.1 3.4 %copy-start.11 = (f32[384,768]{1,0:T(8,128)S(1)}, f32[384,768]{1,0:T(8,128)}, u32[]{:S(2)}) copy-start(f32[384,768]{1,0:T(8,128)} %get-tuple-element.33) | copy-start | bytes 3538948
  129.2 1.0 copy-start.6
  131.3 119.2 %reduce-scatter.2.cloned.1.call-start = ((), (), s32[]{:S(2)}) async-start(), calls=%async_computation.5 | async-start | bytes 7864320 | tf_op jit(solution)/shard_map/reduce_scatter | solution.py:139
  137.9 46.8 %all-to-all-start.2 = ((bf16[32,48,1024]{2,1,0:T(8,128)(2,1)}), bf16[32,48,1024]{2,1,0:T(8,128)(2,1)S(1)}, u32[]{:S(2)}, u32[]{:S(2)}) async-start(bf16[32,48,1024]{2,1,0:T(8,128)(2,1)} %reshape.260), calls=%async_computation.2 | async-start | bytes 6291456 | tf_op jit(solution)/shard_map/all_to_all | solution.py:118
  145.3 5.0 %copy-start.5 = (bf16[384,768]{1,0:T(8,128)(2,1)S(1)}, bf16[384,768]{1,0:T(8,128)(2,1)}, u32[]{:S(2)}) copy-start(bf16[384,768]{1,0:T(8,128)(2,1)} %copy-done.4) | copy-start | bytes 1769476
  164.7 27.1 %copy-start.3 = (bf16[32,4096]{1,0:T(8,128)(2,1)S(1)}, bf16[32,4096]{1,0:T(8,128)(2,1)}, u32[]{:S(2)}) copy-start(bf16[32,4096]{1,0:T(8,128)(2,1)} %param.10) | copy-start | bytes 786436
  184.7 1.7 copy-start
  186.5 44.8 %all-to-all-start.3 = ((bf16[32,48,1024]{2,1,0:T(8,128)(2,1)}), bf16[32,48,1024]{2,1,0:T(8,128)(2,1)S(1)}, u32[]{:S(2)}, u32[]{:S(2)}) async-start(bf16[32,48,1024]{2,1,0:T(8,128)(2,1)} %reshape.262), calls=%async_computation.3 | async-start | bytes 6291456 | tf_op jit(solution)/shard_map/all_to_all | solution.py:125
  (1 other events, 0.8 us)
Sparse Core Ops, SparseCore 0:
  131.4 51.5 all-gather.2
  186.0 64.4 reduce-scatter.1

commit v16 on v15

--- a/solution.py
+++ b/solution.py
@@ -97,7 +97,6 @@
     for shift in range(1, dp_count):
         outgoing = lax.dynamic_slice_in_dim(rows_in, ((dp_index + shift) % dp_count) * piece, piece, axis=1)
         arrived.append(lax.ppermute(outgoing, "dp", [(j, (j + shift) % dp_count) for j in range(dp_count)]))
-    rows_all = jnp.stack(arrived, axis=0)
     gate_mat, up_mat, down_mat = w_gate[0], w_up[0], w_down[0]
     gate_pre = jnp.dot(rows_in, gate_mat, preferred_element_type=jnp.float32)
     up_pre = jnp.dot(rows_in, up_mat, preferred_element_type=jnp.float32)
@@ -106,7 +105,8 @@
     hidden = (silu_value * up_pre).astype(jnp.bfloat16)
     expert_out = jnp.dot(hidden, down_mat, preferred_element_type=jnp.float32).astype(jnp.bfloat16)
     out_send = expert_out.reshape(flat_shape)
-    grads_in, rows_all, out_send = lax.optimization_barrier((grads_in, rows_all, out_send))
+    grads_in, arrived, out_send = lax.optimization_barrier((grads_in, arrived, out_send))
+    rows_all = jnp.stack(arrived, axis=0)
     grad_hidden = contract_last(grads_in, down_mat)
     slope = sigma * (1.0 + gate_pre * (1.0 - sigma))
     grad_gate_pre = (grad_hidden * up_pre * slope).astype(jnp.bfloat16)

time: 259 us -> 268 us (1.035)
  local copies, waits for them, and re-layouts: 70.7 us -> 84.7 us
  waiting for transfers between devices: 78.7 us -> 66.1 us
  matrix products: 46.3 us -> 55.8 us
  other arithmetic: 16.1 us -> 12.7 us
    all_to_all x1, waiting for transfers between devices: 9.58 us -> 0.01 us  [local(): lax.all_to_all(send_grads.reshape(flat_shape), ('outer', 'inner'), split_...]
    unnamed x35 -> x28, local copies, waits for them, and re-layouts: 5.13 us -> 13.5 us
    dot_general x1, matrix products: 2.8 us -> 7.26 us  [local(): jnp.dot(hidden, down_mat, preferred_element_type=jnp.float32)]
    ppermute x3, waiting for transfers between devices: 5.53 us -> 1.18 us  [local(): lax.ppermute(outgoing, 'dp', [(j, (j + shift) % dp_count) for j in range(...]
    another operation x2 -> x1, local copies, waits for them, and re-layouts: 3.73 us -> 0.01 us  [the longest x1 3.73 us: local(): rows_all = jnp.stack(arrived, axis=0)]
    dynamic_slice x0 -> x1, local copies, waits for them, and re-layouts: none -> 3.65 us  [local(): lax.dynamic_slice_in_dim(rows_in, (dp_index + shift) % dp_count * piece,...]
    dot_general x1, matrix products: 3.66 us -> 7.04 us  [local(): up_pre = jnp.dot(rows_in, up_mat, preferred_element_type=jnp.float32)]
    another operation x3 -> x2, other arithmetic: 3.99 us -> 0.63 us  [the longest x1 3.36 us: local(): rows_all = jnp.stack(arrived, axis=0)]
  transfers between devices with their start and end apart: 9 -> 9, of which waited for: 7 -> 5; matrix products, arithmetic and copies ran while one was open for 42% -> 49% of each run, Pallas kernels for 0% -> 0%
where the time goes in v16:
time: 268 us; the launch traced here: 266 us
  local copies, waits for them, and re-layouts  84.7 us (32%)
  waiting for transfers between devices  66.1 us (25%)
  matrix products  55.8 us (21%)
  starting transfers between devices  32.2 us (12%)
  between operations  14.4 us (5%)
  other arithmetic  12.7 us (5%)
    all_to_all x1, waiting for transfers between devices, local(): lax.all_to_all(send_rows.reshape(flat_shape), ('outer', 'inner'), split_a...  24.3 us
    dot_general x3, matrix products, contract_last(): lax.dot_general(left, right, (((1,), (1,)), ((), ())), preferred_element_...  20.6 us
    all_to_all x1, waiting for transfers between devices, local(): lax.all_to_all(out_send, ('outer', 'inner'), split_axis=0, concat_axis=0,...  20.1 us
    unnamed x28, local copies, waits for them, and re-layouts  13.5 us
    reduce_scatter x1, waiting for transfers between devices, local(): lax.psum_scatter(contract_first(hidden, grads_in).astype(jnp.bfloat16), '...  11 us
    all_to_all x1, waiting for transfers between devices, local(): lax.all_to_all(pair_grad.reshape(flat_shape), ('outer', 'inner'), split_a...  9.5 us
    gather x1, local copies, waits for them, and re-layouts, local(): pair_out = back_out.reshape(-1, narrow)[pair_index].astype(jnp.float32)  8.35 us
    dot_general x1, matrix products, local(): lax.dot_general(rows_all, joined_all, (((0, 1), (0, 1)), ((), ())), prefe...  8.09 us
  transfers between devices with their start and end apart: 9, of which 5 were waited for; matrix products, arithmetic and copies ran while one was open for 49% of the time, Pallas kernels for 0%

profile of v16, /device:TPU:8, one launch (start us, length us, event | category | flops | bytes accessed | tf_op | source)
XLA Modules:
  0.0 266.0 jit_solution(5144851502189764805)
XLA Ops:
  12.2 5.8 %gather_fusion.2 = bf16[1536,1024]{1,0:T(8,128)(2,1)} fusion(bf16[132,1024]{1,0:T(8,128)(2,1)S(1)} %reshape.257, s32[2048]{0:T(1024)S(1)} %pad_clamp_fusion), kind=kCustom, calls=%fused_computation.2 | custom fusion | bytes 6297600 | tf_op jit(solution)/shard_map/gather | solution.py:70
  18.0 7.7 %all-to-all-start.1 = ((bf16[32,48,1024]{2,1,0:T(8,128)(2,1)}), bf16[32,48,1024]{2,1,0:T(8,128)(2,1)S(1)}, u32[]{:S(2)}, u32[]{:S(2)}) async-start(bf16[32,48,1024]{2,1,0:T(8,128)(2,1)} %bitcast.86), calls=%async_computation.1 | async-start | bytes 6291456 | tf_op jit(solution)/shard_map/all_to_all | solution.py:76
  30.8 5.9 %gather_fusion.1 = bf16[1536,1024]{1,0:T(8,128)(2,1)} fusion(bf16[132,1024]{1,0:T(8,128)(2,1)S(1)} %reshape.255, s32[2048]{0:T(1024)S(1)} %pad_clamp_fusion), kind=kCustom, calls=%fused_computation.1 | custom fusion | bytes 6297600 | tf_op jit(solution)/shard_map/gather | solution.py:73
  40.8 24.3 %all-to-all-done.1 = bf16[32,48,1024]{2,1,0:T(8,128)(2,1)S(1)} async-done(((bf16[32,48,1024]{2,1,0:T(8,128)(2,1)}), bf16[32,48,1024]{2,1,0:T(8,128)(2,1)S(1)}, u32[]{:S(2)}, u32[]{:S(2)}) %all-to-all-start.1) | async-done | bytes 3145760 | tf_op jit(solution)/shard_map/all_to_all | solution.py:76
  66.8 5.2 %all-to-all-start = ((bf16[32,48,1024]{2,1,0:T(8,128)(2,1)}), bf16[32,48,1024]{2,1,0:T(8,128)(2,1)S(1)}, u32[]{:S(2)}, u32[]{:S(2)}) async-start(bf16[32,48,1024]{2,1,0:T(8,128)(2,1)} %fusion), calls=%async_computation | async-start | bytes 6291456 | tf_op jit(solution)/shard_map/all_to_all | solution.py:83
  72.2 5.9 %reshape.259 = bf16[384,4096]{1,0:T(8,128)(2,1)} reshape(bf16[32,48,1024]{2,1,0:T(8,128)(2,1)} %copy-done.1) | data formatting | bytes 6291456 | tf_op jit(solution)/shard_map/reshape | solution.py:91
  95.2 6.3 %fusion.11 = f32[384,768]{1,0:T(8,128)S(1)} fusion(bf16[384,4096]{1,0:T(8,128)(2,1)} %reshape.259, bf16[1,4096,768]{2,1,0:T(8,128)(2,1)} %param.11), kind=kOutput, calls=%fused_computation.21 | convolution fusion | flops 2415919104 | bytes 10616832 | tf_op jit(solution)/shard_map/dot_general | solution.py:101
  101.6 7.0 %multiply_convert_fusion.2 = (bf16[384,768]{1,0:T(8,128)(2,1)}, f32[384,768]{1,0:T(8,128)}) fusion(f32[384,768]{1,0:T(8,128)S(1)} %fusion.11, bf16[384,4096]{1,0:T(8,128)(2,1)S(1)} %copy-done.2, bf16[1,4096,768]{2,1,0:T(8,128)(2,1)} %param.12), kind=kOutput, calls=%fused_computation.46 | convolution fusion | flops 2417688576 | bytes 12386304 | tf_op jit(solution)/shard_map/dot_general | solution.py:102
  110.9 7.3 %fusion.15 = bf16[384,4096]{1,0:T(8,128)(2,1)} fusion(bf16[384,768]{1,0:T(8,128)(2,1)} %get-tuple-element.38, bf16[1,768,4096]{2,1,0:T(8,128)(2,1)} %param.13), kind=kOutput, calls=%fused_computation.24 | convolution fusion | flops 2417491968 | bytes 10027008 | tf_op jit(solution)/shard_map/dot_general | solution.py:106
  118.2 5.9 %reshape.260 = bf16[32,48,1024]{2,1,0:T(8,128)(2,1)} reshape(bf16[384,4096]{1,0:T(8,128)(2,1)} %fusion.15) | data formatting | bytes 6291456 | tf_op jit(solution)/shard_map/reshape | solution.py:107
  128.9 7.2 %multiply_convert_fusion.1 = (bf16[384,768]{1,0:T(8,128)(2,1)S(1)}, bf16[384,768]{1,0:T(8,128)(2,1)S(1)}) fusion(f32[384,768]{1,0:T(8,128)} %copy-done.10, f32[384,768]{1,0:T(8,128)} %get-tuple-element.39, bf16[384,4096]{1,0:T(8,128)(2,1)} %reshape.256, bf16[1,768,4096]{2,1,0:T(8,128)(2,1)} %param.13), kind=kOutput, calls=%fused_computation.45 | convolution fusion | flops 2419752960 | bytes 12976128 | tf_op jit(solution)/shard_map/dot_general | solution.py:8
  138.9 6.4 %convolution_convert_fusion = bf16[768,4096]{1,0:T(8,128)(2,1)} fusion(bf16[384,768]{1,0:T(8,128)(2,1)} %get-tuple-element.38, bf16[384,4096]{1,0:T(8,128)(2,1)S(1)} %copy-done.3), kind=kOutput, calls=%fused_computation.7 | convolution fusion | flops 2419064832 | bytes 10027008 | tf_op jit(solution)/shard_map/dot_general | solution.py:14
  145.4 7.4 %all-to-all-start.2 = ((bf16[32,48,1024]{2,1,0:T(8,128)(2,1)}), bf16[32,48,1024]{2,1,0:T(8,128)(2,1)S(1)}, u32[]{:S(2)}, u32[]{:S(2)}) async-start(bf16[32,48,1024]{2,1,0:T(8,128)(2,1)} %reshape.260), calls=%async_computation.2 | async-start | bytes 6291456 | tf_op jit(solution)/shard_map/all_to_all | solution.py:118
  152.8 4.9 %fusion.5 = f32[384,4096]{1,0:T(8,128)S(1)} fusion(bf16[384,768]{1,0:T(8,128)(2,1)} %copy-done.8, bf16[1,4096,768]{2,1,0:T(8,128)(2,1)} %param.12), kind=kOutput, calls=%fused_computation.15 | convolution fusion | flops 2415919104 | bytes 13172736 | tf_op jit(solution)/shard_map/dot_general | solution.py:8
  157.7 8.5 %add_convert_fusion = bf16[384,4096]{1,0:T(8,128)(2,1)} fusion(f32[384,4096]{1,0:T(8,128)S(1)} %fusion.5, bf16[384,768]{1,0:T(8,128)(2,1)S(1)} %copy-done.7, bf16[1,4096,768]{2,1,0:T(8,128)(2,1)} %param.11), kind=kOutput, calls=%fused_computation.23 | convolution fusion | flops 2419064832 | bytes 16318464 | tf_op jit(solution)/shard_map/dot_general | solution.py:8
  166.2 5.9 %reshape.262 = bf16[32,48,1024]{2,1,0:T(8,128)(2,1)} reshape(bf16[384,4096]{1,0:T(8,128)(2,1)} %add_convert_fusion) | data formatting | bytes 6291456 | tf_op jit(solution)/shard_map/reshape | solution.py:126
  172.1 20.1 %all-to-all-done.2 = bf16[32,48,1024]{2,1,0:T(8,128)(2,1)S(1)} async-done(((bf16[32,48,1024]{2,1,0:T(8,128)(2,1)}), bf16[32,48,1024]{2,1,0:T(8,128)(2,1)S(1)}, u32[]{:S(2)}, u32[]{:S(2)}) %all-to-all-start.2) | async-done | bytes 3145760 | tf_op jit(solution)/shard_map/all_to_all | solution.py:118
  194.0 5.3 %all-to-all-start.3 = ((bf16[32,48,1024]{2,1,0:T(8,128)(2,1)}), bf16[32,48,1024]{2,1,0:T(8,128)(2,1)S(1)}, u32[]{:S(2)}, u32[]{:S(2)}) async-start(bf16[32,48,1024]{2,1,0:T(8,128)(2,1)} %reshape.262), calls=%async_computation.3 | async-start | bytes 6291456 | tf_op jit(solution)/shard_map/all_to_all | solution.py:125
  200.6 8.3 %gather_fusion.3 = bf16[1024,1024]{1,0:T(8,128)(2,1)} fusion(bf16[1536,1024]{1,0:T(8,128)(2,1)} %bitcast.85, s32[1024]{0:T(1024)S(1)} %broadcast_clamp_fusion), kind=kCustom, calls=%fused_computation.3 | custom fusion | bytes 4198400 | tf_op jit(solution)/shard_map/gather | solution.py:149
  213.9 5.4 %gather_fusion.4 = bf16[4,384,1536]{2,1,0:T(8,128)(2,1)} fusion(bf16[4,384,1536]{2,1,0:T(8,128)(2,1)} %bitcast.88, s32[1024]{0:T(1024)S(1)} %pad_clamp_fusion.1), kind=kCustom, calls=%fused_computation.4 | custom fusion | bytes 9437200 | tf_op jit(solution)/shard_map/jit(_take)/gather | solution.py:135
  219.3 8.1 %bitcast_convert_fusion = bf16[1024,1536]{1,0:T(8,128)(2,1)S(1)} fusion(bf16[4,384,1536]{2,1,0:T(8,128)(2,1)} %gather_fusion.4, pred[4]{0:T(512)(128)(4,1)S(1)} %compare_and_fusion, bf16[1,384,1024]{1,2,0:T(8,128)(2,1)} %bitcast.16, bf16[1,384,1024]{1,2,0:T(8,128)(2,1)} %bitcast.15, bf16[1,384,1024]{1,2,0:T(8,128)(2,1)} %bitcast.14, ...), kind=kOutput, calls=%fused_computation.10 | convolution fusion | flops 4840488960 | bytes 11010052 | tf_op jit(solution)/shard_map/dot_general | solution.py:136
  229.3 9.5 %all-to-all-done.3 = bf16[32,48,1024]{2,1,0:T(8,128)(2,1)S(1)} async-done(((bf16[32,48,1024]{2,1,0:T(8,128)(2,1)}), bf16[32,48,1024]{2,1,0:T(8,128)(2,1)S(1)}, u32[]{:S(2)}, u32[]{:S(2)}) %all-to-all-start.3) | async-done | bytes 3145760 | tf_op jit(solution)/shard_map/all_to_all | solution.py:125
  238.8 5.4 %gather_fusion.5 = bf16[1024,1024]{1,0:T(8,128)(2,1)} fusion(bf16[1536,1024]{1,0:T(8,128)(2,1)S(1)} %bitcast.84, s32[1024]{0:T(1024)S(1)} %broadcast_clamp_fusion), kind=kCustom, calls=%fused_computation.5 | custom fusion | bytes 4198400 | tf_op jit(solution)/shard_map/gather | solution.py:153
  248.1 11.0 %reduce-scatter.2.cloned.1.call-done = bf16[768,1024]{1,0:T(8,128)(2,1)} async-done(((bf16[768,4096]{1,0:T(8,128)(2,1)}), bf16[768,1024]{1,0:T(8,128)(2,1)}) %reduce-scatter.2.cloned.1.call-update) | async-done | bytes 1572880 | tf_op jit(solution)/shard_map/reduce_scatter | solution.py:139
  (93 shorter events, 56.6 us)
Async XLA Ops:
  18.0 7.7 %copy-start.9 = (f32[32,8]{0,1:T(8,128)S(1)}, f32[32,8]{0,1:T(8,128)}, u32[]{:S(2)}) copy-start(f32[32,8]{0,1:T(8,128)} %param.9) | copy-start | bytes 3076
  18.0 10.9 %copy-start.4 = (bf16[32,4096]{1,0:T(8,128)(2,1)S(1)}, bf16[32,4096]{1,0:T(8,128)(2,1)}, u32[]{:S(2)}) copy-start(bf16[32,4096]{1,0:T(8,128)(2,1)} %param.10) | copy-start | bytes 786436
  18.0 47.2 %all-to-all-start.1 = ((bf16[32,48,1024]{2,1,0:T(8,128)(2,1)}), bf16[32,48,1024]{2,1,0:T(8,128)(2,1)S(1)}, u32[]{:S(2)}, u32[]{:S(2)}) async-start(bf16[32,48,1024]{2,1,0:T(8,128)(2,1)} %bitcast.86), calls=%async_computation.1 | async-start | bytes 6291456 | tf_op jit(solution)/shard_map/all_to_all | solution.py:76
  65.1 1.7 copy-start.1
  66.8 57.2 %all-to-all-start = ((bf16[32,48,1024]{2,1,0:T(8,128)(2,1)}), bf16[32,48,1024]{2,1,0:T(8,128)(2,1)S(1)}, u32[]{:S(2)}, u32[]{:S(2)}) async-start(bf16[32,48,1024]{2,1,0:T(8,128)(2,1)} %fusion), calls=%async_computation | async-start | bytes 6291456 | tf_op jit(solution)/shard_map/all_to_all | solution.py:83
  72.1 141.8 %all-gather.3.cloned.1.call-start = ((), (), s32[]{:S(2)}) async-start(), calls=%async_computation.6 | async-start | bytes 5898240 | tf_op jit(solution)/shard_map/all_gather | solution.py:135
  88.7 12.9 %copy-start.2 = (bf16[384,4096]{1,0:T(8,128)(2,1)S(1)}, bf16[384,4096]{1,0:T(8,128)(2,1)}, u32[]{:S(2)}) copy-start(bf16[384,4096]{1,0:T(8,128)(2,1)} %reshape.259) | copy-start | bytes 9437188
  88.7 39.1 %collective-permute-start = (bf16[384,1024]{0,1:T(8,128)(2,1)}, bf16[384,1024]{0,1:T(8,128)(2,1)}, u32[]{:S(2)}, u32[]{:S(2)}) collective-permute-start(bf16[384,1024]{0,1:T(8,128)(2,1)} %copy.54), channel_id=1, source_target_pairs={{0,32},{32,64},{64,96},{96,0},{1,33},{33,65},{65,97},{97,1},{2,34}... | collective-permute-start | bytes 2359304 | tf_op jit(solution)/shard_map/ppermute | solution.py:99
  90.6 38.3 %collective-permute-start.1 = (bf16[384,1024]{0,1:T(8,128)(2,1)}, bf16[384,1024]{0,1:T(8,128)(2,1)}, u32[]{:S(2)}, u32[]{:S(2)}) collective-permute-start(bf16[384,1024]{0,1:T(8,128)(2,1)} %copy.55), channel_id=1, source_target_pairs={{0,64},{32,96},{64,0},{96,32},{1,65},{33,97},{65,1},{97,33},{2,66}... | collective-permute-start | bytes 2359304 | tf_op jit(solution)/shard_map/ppermute | solution.py:99
  94.2 34.7 %collective-permute-start.2 = (bf16[384,1024]{0,1:T(8,128)(2,1)}, bf16[384,1024]{0,1:T(8,128)(2,1)}, u32[]{:S(2)}, u32[]{:S(2)}) collective-permute-start(bf16[384,1024]{0,1:T(8,128)(2,1)} %copy.56), channel_id=1, source_target_pairs={{0,96},{32,0},{64,32},{96,64},{1,97},{33,1},{65,33},{97,65},{2,98}... | collective-permute-start | bytes 2359304 | tf_op jit(solution)/shard_map/ppermute | solution.py:99
  101.6 7.1 %copy-start.10 = (f32[384,768]{1,0:T(8,128)}, f32[384,768]{1,0:T(8,128)S(1)}, u32[]{:S(2)}) copy-start(f32[384,768]{1,0:T(8,128)S(1)} %fusion.11) | copy-start | bytes 3538948
  136.2 0.8 copy-start.6
  136.2 1.0 copy-start.8
  136.2 2.7 %copy-start.3 = (bf16[384,4096]{1,0:T(8,128)(2,1)S(1)}, bf16[384,4096]{1,0:T(8,128)(2,1)}, u32[]{:S(2)}) copy-start(bf16[384,4096]{1,0:T(8,128)(2,1)} %reshape.256) | copy-start | bytes 9437188
  138.3 120.8 %reduce-scatter.2.cloned.1.call-start = ((), (), s32[]{:S(2)}) async-start(), calls=%async_computation.5 | async-start | bytes 7864320 | tf_op jit(solution)/shard_map/reduce_scatter | solution.py:139
  145.4 46.8 %all-to-all-start.2 = ((bf16[32,48,1024]{2,1,0:T(8,128)(2,1)}), bf16[32,48,1024]{2,1,0:T(8,128)(2,1)S(1)}, u32[]{:S(2)}, u32[]{:S(2)}) async-start(bf16[32,48,1024]{2,1,0:T(8,128)(2,1)} %reshape.260), calls=%async_computation.2 | async-start | bytes 6291456 | tf_op jit(solution)/shard_map/all_to_all | solution.py:118
  152.8 5.0 %copy-start.7 = (bf16[384,768]{1,0:T(8,128)(2,1)S(1)}, bf16[384,768]{1,0:T(8,128)(2,1)}, u32[]{:S(2)}) copy-start(bf16[384,768]{1,0:T(8,128)(2,1)} %copy-done.6) | copy-start | bytes 1769476
  172.1 27.1 %copy-start.5 = (bf16[32,4096]{1,0:T(8,128)(2,1)S(1)}, bf16[32,4096]{1,0:T(8,128)(2,1)}, u32[]{:S(2)}) copy-start(bf16[32,4096]{1,0:T(8,128)(2,1)} %param.10) | copy-start | bytes 786436
  192.2 1.8 copy-start
  194.0 44.8 %all-to-all-start.3 = ((bf16[32,48,1024]{2,1,0:T(8,128)(2,1)}), bf16[32,48,1024]{2,1,0:T(8,128)(2,1)S(1)}, u32[]{:S(2)}, u32[]{:S(2)}) async-start(bf16[32,48,1024]{2,1,0:T(8,128)(2,1)} %reshape.262), calls=%async_computation.3 | async-start | bytes 6291456 | tf_op jit(solution)/shard_map/all_to_all | solution.py:125
Sparse Core Ops, SparseCore 0:
  138.5 53.1 all-gather.2
  194.6 64.4 reduce-scatter.1

commit v17 on v15

--- a/solution.py
+++ b/solution.py
@@ -67,7 +67,11 @@
     narrow = width // fold
     flat_shape = (expert_count, capacity * fold, narrow)
     row_index = (slot_token[:, None] * fold + jnp.arange(fold, dtype=jnp.int32)[None, :]).reshape(-1)
-    send_rows = token_pad.reshape(-1, narrow)[row_index]
+    token_view = token_pad.reshape(-1, narrow)
+    picker = (row_index[:, None] == jnp.arange(token_view.shape[0], dtype=jnp.int32)[None, :]).astype(
+        jnp.bfloat16
+    )
+    send_rows = jnp.dot(picker, token_view, preferred_element_type=jnp.float32).astype(jnp.bfloat16)
     send_grads = (
         jnp.repeat(gate_pad[slot_pair], fold)[:, None]
         * upstream_pad.reshape(-1, narrow)[row_index].astype(jnp.float32)

time: 259 us -> 256 us (0.988)
  local copies, waits for them, and re-layouts: 70.7 us -> 65.9 us
  matrix products: 46.3 us -> 48.9 us
    gather x1 -> x0, local copies, waits for them, and re-layouts: 5.81 us -> none  [local(): send_rows = token_pad.reshape(-1, narrow)[row_index]]
    dot_general x0 -> x1, matrix products: none -> 2.7 us  [local(): jnp.dot(picker, token_view, preferred_element_type=jnp.float32)]
  transfers between devices with their start and end apart: 9 -> 9, of which waited for: 7 -> 7; matrix products, arithmetic and copies ran while one was open for 42% -> 43% of each run, Pallas kernels for 0% -> 0%
where the time goes in v17:
time: 256 us; the launch traced here: 254 us
  waiting for transfers between devices  77.8 us (30%)
  local copies, waits for them, and re-layouts  65.9 us (26%)
  matrix products  48.9 us (19%)
  starting transfers between devices  31 us (12%)
  other arithmetic  16 us (6%)
  between operations  14.5 us (6%)
    all_to_all x1, waiting for transfers between devices, local(): lax.all_to_all(send_rows.reshape(flat_shape), ('outer', 'inner'), split_a...  23.2 us
    all_to_all x1, waiting for transfers between devices, local(): lax.all_to_all(out_send, ('outer', 'inner'), split_axis=0, concat_axis=0,...  20 us
    dot_general x3, matrix products, contract_last(): lax.dot_general(left, right, (((1,), (1,)), ((), ())), preferred_element_...  19.1 us
    reduce_scatter x1, waiting for transfers between devices, local(): lax.psum_scatter(contract_first(hidden, grads_in).astype(jnp.bfloat16), '...  10 us
    all_to_all x1, waiting for transfers between devices, local(): lax.all_to_all(send_grads.reshape(flat_shape), ('outer', 'inner'), split_...  9.6 us
    all_to_all x1, waiting for transfers between devices, local(): lax.all_to_all(pair_grad.reshape(flat_shape), ('outer', 'inner'), split_a...  9.4 us
    gather x1, local copies, waits for them, and re-layouts, local(): pair_out = back_out.reshape(-1, narrow)[pair_index].astype(jnp.float32)  8.31 us
    dot_general x1, matrix products, local(): lax.dot_general(rows_all, joined_all, (((0, 1), (0, 1)), ((), ())), prefe...  8.22 us
  transfers between devices with their start and end apart: 9, of which 7 were waited for; matrix products, arithmetic and copies ran while one was open for 43% of the time, Pallas kernels for 0%

profile of v17, /device:TPU:8, one launch (start us, length us, event | category | flops | bytes accessed | tf_op | source)
XLA Modules:
  0.0 254.2 jit_solution(15664278357069586378)
XLA Ops:
  14.8 7.7 %all-to-all-start.1 = ((bf16[32,48,1024]{2,1,0:T(8,128)(2,1)}), bf16[32,48,1024]{2,1,0:T(8,128)(2,1)S(1)}, u32[]{:S(2)}, u32[]{:S(2)}) async-start(bf16[32,48,1024]{2,1,0:T(8,128)(2,1)} %bitcast.89), calls=%async_computation.1 | async-start | bytes 6291456 | tf_op jit(solution)/shard_map/all_to_all | solution.py:80
  28.8 5.9 %gather_fusion.1 = bf16[1536,1024]{1,0:T(8,128)(2,1)} fusion(bf16[132,1024]{1,0:T(8,128)(2,1)S(1)} %reshape.266, s32[2048]{0:T(1024)S(1)} %pad_clamp_fusion), kind=kCustom, calls=%fused_computation.1 | custom fusion | bytes 6297600 | tf_op jit(solution)/shard_map/gather | solution.py:77
  34.7 4.1 %fusion = bf16[32,48,1024]{2,1,0:T(8,128)(2,1)} fusion(bf16[32,48,1024]{2,1,0:T(8,128)(2,1)} %bitcast.90, f32[32,48]{1,0:T(8,128)S(1)} %copy.40), kind=kLoop, calls=%fused_computation.8 | loop fusion | flops 4718592 | bytes 6297600 | tf_op jit(solution)/shard_map/convert_element_type | solution.py:78
  38.8 23.2 %all-to-all-done.1 = bf16[32,48,1024]{2,1,0:T(8,128)(2,1)S(1)} async-done(((bf16[32,48,1024]{2,1,0:T(8,128)(2,1)}), bf16[32,48,1024]{2,1,0:T(8,128)(2,1)S(1)}, u32[]{:S(2)}, u32[]{:S(2)}) %all-to-all-start.1) | async-done | bytes 3145760 | tf_op jit(solution)/shard_map/all_to_all | solution.py:80
  62.0 5.3 %all-to-all-start = ((bf16[32,48,1024]{2,1,0:T(8,128)(2,1)}), bf16[32,48,1024]{2,1,0:T(8,128)(2,1)}, u32[]{:S(2)}, u32[]{:S(2)}) async-start(bf16[32,48,1024]{2,1,0:T(8,128)(2,1)} %fusion), calls=%async_computation | async-start | bytes 6291456 | tf_op jit(solution)/shard_map/all_to_all | solution.py:87
  67.4 3.8 %reshape.270 = bf16[384,4096]{1,0:T(8,128)(2,1)} reshape(bf16[32,48,1024]{2,1,0:T(8,128)(2,1)S(1)} %all-to-all-done.1) | data formatting | bytes 6291456 | tf_op jit(solution)/shard_map/reshape | solution.py:95
  74.9 4.0 %collective-permute-start.2 = (bf16[384,1024]{1,0:T(8,128)(2,1)}, bf16[384,1024]{1,0:T(8,128)(2,1)}, u32[]{:S(2)}, u32[]{:S(2)}) collective-permute-start(bf16[384,1024]{1,0:T(8,128)(2,1)} %get-tuple-element.23), channel_id=1, source_target_pairs={{0,96},{32,0},{64,32},{96,64},{1,97},{33,1},{65,33},{97,65},{2,98}... | collective-permute-start | bytes 2359304 | tf_op jit(solution)/shard_map/ppermute | solution.py:103
  80.2 6.0 %fusion.11 = f32[384,768]{1,0:T(8,128)S(1)} fusion(bf16[384,4096]{1,0:T(8,128)(2,1)S(1)} %copy-done.1, bf16[1,4096,768]{2,1,0:T(8,128)(2,1)} %param.11), kind=kOutput, calls=%fused_computation.20 | convolution fusion | flops 2415919104 | bytes 10616832 | tf_op jit(solution)/shard_map/dot_general | solution.py:106
  97.2 9.6 %all-to-all-done = bf16[32,48,1024]{2,1,0:T(8,128)(2,1)} async-done(((bf16[32,48,1024]{2,1,0:T(8,128)(2,1)}), bf16[32,48,1024]{2,1,0:T(8,128)(2,1)}, u32[]{:S(2)}, u32[]{:S(2)}) %all-to-all-start) | async-done | bytes 3145760 | tf_op jit(solution)/shard_map/all_to_all | solution.py:87
  106.8 4.5 %reshape.267 = bf16[384,4096]{1,0:T(8,128)(2,1)S(1)} reshape(bf16[32,48,1024]{2,1,0:T(8,128)(2,1)} %all-to-all-done) | data formatting | bytes 6291456 | tf_op jit(solution)/shard_map/reshape | solution.py:96
  120.2 5.8 %multiply_convert_fusion.1 = (bf16[384,768]{1,0:T(8,128)(2,1)S(1)}, bf16[384,768]{1,0:T(8,128)(2,1)S(1)}) fusion(f32[384,768]{1,0:T(8,128)S(1)} %copy-done.9, f32[384,768]{1,0:T(8,128)S(1)} %copy-done.10, bf16[384,4096]{1,0:T(8,128)(2,1)S(1)} %reshape.267, bf16[1,768,4096]{2,1,0:T(8,128)(2,1)} %param.13), kind=kOutput, calls=%fused_computation.40 | convolution fusion | flops 2419752960 | bytes 12976128 | tf_op jit(solution)/shard_map/dot_general | solution.py:8
  128.2 6.4 %convolution_convert_fusion = bf16[768,4096]{1,0:T(8,128)(2,1)} fusion(bf16[384,768]{1,0:T(8,128)(2,1)} %copy-done.7, bf16[384,4096]{1,0:T(8,128)(2,1)S(1)} %reshape.267), kind=kOutput, calls=%fused_computation.6 | convolution fusion | flops 2419064832 | bytes 10027008 | tf_op jit(solution)/shard_map/dot_general | solution.py:14
  134.6 7.4 %all-to-all-start.2 = ((bf16[32,48,1024]{2,1,0:T(8,128)(2,1)}), bf16[32,48,1024]{2,1,0:T(8,128)(2,1)S(1)}, u32[]{:S(2)}, u32[]{:S(2)}) async-start(bf16[32,48,1024]{2,1,0:T(8,128)(2,1)} %reshape.271), calls=%async_computation.2 | async-start | bytes 6291456 | tf_op jit(solution)/shard_map/all_to_all | solution.py:122
  142.0 4.9 %fusion.5 = f32[384,4096]{1,0:T(8,128)S(1)} fusion(bf16[384,768]{1,0:T(8,128)(2,1)} %copy-done.5, bf16[1,4096,768]{2,1,0:T(8,128)(2,1)} %param.12), kind=kOutput, calls=%fused_computation.14 | convolution fusion | flops 2415919104 | bytes 13172736 | tf_op jit(solution)/shard_map/dot_general | solution.py:8
  147.0 8.4 %add_convert_fusion = bf16[384,4096]{1,0:T(8,128)(2,1)} fusion(f32[384,4096]{1,0:T(8,128)S(1)} %fusion.5, bf16[384,768]{1,0:T(8,128)(2,1)S(1)} %copy-done.4, bf16[1,4096,768]{2,1,0:T(8,128)(2,1)} %param.11), kind=kOutput, calls=%fused_computation.22 | convolution fusion | flops 2419064832 | bytes 16318464 | tf_op jit(solution)/shard_map/dot_general | solution.py:8
  155.4 6.0 %reshape.273 = bf16[32,48,1024]{2,1,0:T(8,128)(2,1)} reshape(bf16[384,4096]{1,0:T(8,128)(2,1)} %add_convert_fusion) | data formatting | bytes 6291456 | tf_op jit(solution)/shard_map/reshape | solution.py:130
  161.4 20.0 %all-to-all-done.2 = bf16[32,48,1024]{2,1,0:T(8,128)(2,1)S(1)} async-done(((bf16[32,48,1024]{2,1,0:T(8,128)(2,1)}), bf16[32,48,1024]{2,1,0:T(8,128)(2,1)S(1)}, u32[]{:S(2)}, u32[]{:S(2)}) %all-to-all-start.2) | async-done | bytes 3145760 | tf_op jit(solution)/shard_map/all_to_all | solution.py:122
  183.2 5.3 %all-to-all-start.3 = ((bf16[32,48,1024]{2,1,0:T(8,128)(2,1)}), bf16[32,48,1024]{2,1,0:T(8,128)(2,1)S(1)}, u32[]{:S(2)}, u32[]{:S(2)}) async-start(bf16[32,48,1024]{2,1,0:T(8,128)(2,1)} %reshape.273), calls=%async_computation.3 | async-start | bytes 6291456 | tf_op jit(solution)/shard_map/all_to_all | solution.py:129
  189.8 8.3 %gather_fusion.2 = bf16[1024,1024]{1,0:T(8,128)(2,1)} fusion(bf16[1536,1024]{1,0:T(8,128)(2,1)} %bitcast.88, s32[1024]{0:T(1024)S(1)} %broadcast_clamp_fusion), kind=kCustom, calls=%fused_computation.2 | custom fusion | bytes 4198400 | tf_op jit(solution)/shard_map/gather | solution.py:153
  203.1 5.4 %gather_fusion.3 = bf16[4,384,1536]{2,1,0:T(8,128)(2,1)} fusion(bf16[4,384,1536]{2,1,0:T(8,128)(2,1)} %bitcast.91, s32[1024]{0:T(1024)S(1)} %pad_clamp_fusion.1), kind=kCustom, calls=%fused_computation.3 | custom fusion | bytes 9437200 | tf_op jit(solution)/shard_map/jit(_take)/gather | solution.py:139
  208.5 8.2 %bitcast_convert_fusion = bf16[1024,1536]{1,0:T(8,128)(2,1)S(1)} fusion(bf16[4,384,1024]{2,1,0:T(8,128)(2,1)} %pad_maximum_fusion, bf16[4,384,1536]{2,1,0:T(8,128)(2,1)} %gather_fusion.3, pred[4]{0:T(512)(128)(4,1)S(1)} %compare_and_fusion), kind=kOutput, calls=%fused_computation.9 | convolution fusion | flops 4835770368 | bytes 11010052 | tf_op jit(solution)/shard_map/dot_general | solution.py:140
  218.6 9.4 %all-to-all-done.3 = bf16[32,48,1024]{2,1,0:T(8,128)(2,1)S(1)} async-done(((bf16[32,48,1024]{2,1,0:T(8,128)(2,1)}), bf16[32,48,1024]{2,1,0:T(8,128)(2,1)S(1)}, u32[]{:S(2)}, u32[]{:S(2)}) %all-to-all-start.3) | async-done | bytes 3145760 | tf_op jit(solution)/shard_map/all_to_all | solution.py:129
  228.0 5.4 %gather_fusion.4 = bf16[1024,1024]{1,0:T(8,128)(2,1)} fusion(bf16[1536,1024]{1,0:T(8,128)(2,1)S(1)} %bitcast.87, s32[1024]{0:T(1024)S(1)} %broadcast_clamp_fusion), kind=kCustom, calls=%fused_computation.4 | custom fusion | bytes 4198400 | tf_op jit(solution)/shard_map/gather | solution.py:157
  237.3 10.0 %reduce-scatter.2.cloned.1.call-done = bf16[768,1024]{1,0:T(8,128)(2,1)} async-done(((bf16[768,4096]{1,0:T(8,128)(2,1)}), bf16[768,1024]{1,0:T(8,128)(2,1)}) %reduce-scatter.2.cloned.1.call-update) | async-done | bytes 1572880 | tf_op jit(solution)/shard_map/reduce_scatter | solution.py:143
  (101 shorter events, 54.7 us)
Async XLA Ops:
  14.8 7.8 %copy-start.6 = (f32[32,8]{0,1:T(8,128)S(1)}, f32[32,8]{0,1:T(8,128)}, u32[]{:S(2)}) copy-start(f32[32,8]{0,1:T(8,128)} %param.9) | copy-start | bytes 3076
  14.8 47.2 %all-to-all-start.1 = ((bf16[32,48,1024]{2,1,0:T(8,128)(2,1)}), bf16[32,48,1024]{2,1,0:T(8,128)(2,1)S(1)}, u32[]{:S(2)}, u32[]{:S(2)}) async-start(bf16[32,48,1024]{2,1,0:T(8,128)(2,1)} %bitcast.89), calls=%async_computation.1 | async-start | bytes 6291456 | tf_op jit(solution)/shard_map/all_to_all | solution.py:80
  62.0 44.9 %all-to-all-start = ((bf16[32,48,1024]{2,1,0:T(8,128)(2,1)}), bf16[32,48,1024]{2,1,0:T(8,128)(2,1)}, u32[]{:S(2)}, u32[]{:S(2)}) async-start(bf16[32,48,1024]{2,1,0:T(8,128)(2,1)} %fusion), calls=%async_computation | async-start | bytes 6291456 | tf_op jit(solution)/shard_map/all_to_all | solution.py:87
  67.3 135.8 %all-gather.3.cloned.1.call-start = ((), (), s32[]{:S(2)}) async-start(), calls=%async_computation.6 | async-start | bytes 5898240 | tf_op jit(solution)/shard_map/all_gather | solution.py:139
  71.2 9.0 %copy-start.1 = (bf16[384,4096]{1,0:T(8,128)(2,1)S(1)}, bf16[384,4096]{1,0:T(8,128)(2,1)}, u32[]{:S(2)}) copy-start(bf16[384,4096]{1,0:T(8,128)(2,1)} %reshape.270) | copy-start | bytes 9437188
  71.2 19.5 %slice-start = ((s8[6291456]{0:T(1024)(128)(4,1)}), s8[4194304]{0:T(1024)(128)(4,1)S(1)}, s32[]{:S(2)}) async-start(s8[6291456]{0:T(1024)(128)(4,1)} %bitcast.98), calls=%async_computation.7 | async-start | bytes 8388608
  74.9 38.3 %collective-permute-start.2 = (bf16[384,1024]{1,0:T(8,128)(2,1)}, bf16[384,1024]{1,0:T(8,128)(2,1)}, u32[]{:S(2)}, u32[]{:S(2)}) collective-permute-start(bf16[384,1024]{1,0:T(8,128)(2,1)} %get-tuple-element.23), channel_id=1, source_target_pairs={{0,96},{32,0},{64,32},{96,64},{1,97},{33,1},{65,33},{97,65},{2,98}... | collective-permute-start | bytes 2359304 | tf_op jit(solution)/shard_map/ppermute | solution.py:103
  78.9 34.3 %collective-permute-start.1 = (bf16[384,1024]{1,0:T(8,128)(2,1)}, bf16[384,1024]{1,0:T(8,128)(2,1)}, u32[]{:S(2)}, u32[]{:S(2)}) collective-permute-start(bf16[384,1024]{1,0:T(8,128)(2,1)} %get-tuple-element.24), channel_id=1, source_target_pairs={{0,64},{32,96},{64,0},{96,32},{1,65},{33,97},{65,1},{97,33},{2,66}... | collective-permute-start | bytes 2359304 | tf_op jit(solution)/shard_map/ppermute | solution.py:103
  78.9 7.3 %slice-start.2 = ((s8[6291456]{0:T(1024)(128)(4,1)}), s8[4194304]{0:T(1024)(128)(4,1)S(1)}, s32[]{:S(2)}) async-start(s8[6291456]{0:T(1024)(128)(4,1)} %bitcast.100), calls=%async_computation.9 | async-start | bytes 8388608
  78.9 7.3 %slice-start.3 = ((s8[6291456]{0:T(1024)(128)(4,1)}), s8[2097152]{0:T(1024)(128)(4,1)S(1)}, s32[]{:S(2)}) async-start(s8[6291456]{0:T(1024)(128)(4,1)} %bitcast.100), calls=%async_computation.10 | async-start | bytes 4194304
  78.9 11.8 %slice-start.1 = ((s8[6291456]{0:T(1024)(128)(4,1)}), s8[2097152]{0:T(1024)(128)(4,1)S(1)}, s32[]{:S(2)}) async-start(s8[6291456]{0:T(1024)(128)(4,1)} %bitcast.98), calls=%async_computation.8 | async-start | bytes 4194304
  78.9 37.9 %collective-permute-start = (bf16[384,1024]{1,0:T(8,128)(2,1)}, bf16[384,1024]{1,0:T(8,128)(2,1)}, u32[]{:S(2)}, u32[]{:S(2)}) collective-permute-start(bf16[384,1024]{1,0:T(8,128)(2,1)} %get-tuple-element.25), channel_id=1, source_target_pairs={{0,32},{32,64},{64,96},{96,0},{1,33},{33,65},{65,97},{97,1},{2,34}... | collective-permute-start | bytes 2359304 | tf_op jit(solution)/shard_map/ppermute | solution.py:103
  86.2 3.7 %copy-start.8 = (f32[384,768]{1,0:T(8,128)}, f32[384,768]{1,0:T(8,128)S(1)}, u32[]{:S(2)}) copy-start(f32[384,768]{1,0:T(8,128)S(1)} %fusion.11) | copy-start | bytes 3538948
  89.9 0.8 copy-start.7
  116.9 3.3 %copy-start.9 = (f32[384,768]{1,0:T(8,128)S(1)}, f32[384,768]{1,0:T(8,128)}, u32[]{:S(2)}) copy-start(f32[384,768]{1,0:T(8,128)} %copy-done.8) | copy-start | bytes 3538948
  116.9 3.3 %copy-start.10 = (f32[384,768]{1,0:T(8,128)S(1)}, f32[384,768]{1,0:T(8,128)}, u32[]{:S(2)}) copy-start(f32[384,768]{1,0:T(8,128)} %get-tuple-element.33) | copy-start | bytes 3538948
  126.0 0.8 copy-start.3
  126.0 1.0 copy-start.5
  128.1 119.2 %reduce-scatter.2.cloned.1.call-start = ((), (), s32[]{:S(2)}) async-start(), calls=%async_computation.5 | async-start | bytes 7864320 | tf_op jit(solution)/shard_map/reduce_scatter | solution.py:143
  134.6 46.8 %all-to-all-start.2 = ((bf16[32,48,1024]{2,1,0:T(8,128)(2,1)}), bf16[32,48,1024]{2,1,0:T(8,128)(2,1)S(1)}, u32[]{:S(2)}, u32[]{:S(2)}) async-start(bf16[32,48,1024]{2,1,0:T(8,128)(2,1)} %reshape.271), calls=%async_computation.2 | async-start | bytes 6291456 | tf_op jit(solution)/shard_map/all_to_all | solution.py:122
  142.0 5.0 %copy-start.4 = (bf16[384,768]{1,0:T(8,128)(2,1)S(1)}, bf16[384,768]{1,0:T(8,128)(2,1)}, u32[]{:S(2)}) copy-start(bf16[384,768]{1,0:T(8,128)(2,1)} %copy-done.3) | copy-start | bytes 1769476
  161.4 27.1 %copy-start.2 = (bf16[32,4096]{1,0:T(8,128)(2,1)S(1)}, bf16[32,4096]{1,0:T(8,128)(2,1)}, u32[]{:S(2)}) copy-start(bf16[32,4096]{1,0:T(8,128)(2,1)} %param.10) | copy-start | bytes 786436
  181.4 1.7 copy-start
  183.2 44.8 %all-to-all-start.3 = ((bf16[32,48,1024]{2,1,0:T(8,128)(2,1)}), bf16[32,48,1024]{2,1,0:T(8,128)(2,1)S(1)}, u32[]{:S(2)}, u32[]{:S(2)}) async-start(bf16[32,48,1024]{2,1,0:T(8,128)(2,1)} %reshape.273), calls=%async_computation.3 | async-start | bytes 6291456 | tf_op jit(solution)/shard_map/all_to_all | solution.py:129
Sparse Core Ops, SparseCore 0:
  128.2 51.5 all-gather.2
  182.8 64.4 reduce-scatter.1
